TPU v7x, 512 devices: a whole 4x8x8 slice. The times are simulated.
512 devices in a mesh: pb: 32 (over x, y), kv: 16 (over z, core).
Axes of the slice: x: 4, y: 8, z: 8, core: 2. Of those that a mesh axis runs over, the one named last changes fastest.
Arguments:
- queries: bfloat16 [2, 8192, 128], P(None, 'pb'), may hold values from -600 to 600
- cache_keys: bfloat16 [2, 16384, 128], P(None, 'kv'), may hold values from -6 to 6
- cache_values: bfloat16 [2, 16384, 128], P(None, 'kv'), may hold values from -6 to 6
- selected: int32 [2, 2048], replicated, may hold values from 0 to 16383, as said below
Outputs:
- new_values: float32 [2, 2048, 128], P(None, 'kv')
- fit_residual: float32 [2, 2048, 128], P(None, 'kv')
Inputs may be any that keep to these rules, and one draw needn't show every extreme that they name: `selected`: each head's row holds 2048 different key positions; the cache's shards hold unequal numbers of them.
All inputs are finite; a program needn't handle non-finite values.
Results may differ from a plain program's by a relative error of at most 0.0049.
Values may be sent and summed in bfloat16 or wider, within the bound.
No kernel may reach another device: no remote copies, remote signals or barrier semaphores. Data moves between devices by JAX's collectives and lax.ppermute only.
A program may use at most 64 MiB of HBM per device.

v0:
```python
import math

import jax
import jax.numpy as jnp
from jax import lax
from jax.sharding import PartitionSpec as P

STEPS = 3


ridge_weight = 0.1
theta_mid = 1.1
delta_half = 1.0


def joined(part, axis, combine):
    gathered = jax.tree.map(lambda a: lax.all_gather(a, axis), part)

    def take(source):
        return jax.tree.map(lambda a: lax.dynamic_index_in_dim(a, source, 0, False), gathered)

    return lax.fori_loop(
        1, lax.axis_size(axis), lambda source, state: combine(state, take(source)), take(0)
    )


def combine_parts(first_part, second_part):
    peak_a, denom_a, numer_a = first_part
    peak_b, denom_b, numer_b = second_part
    peak = jnp.maximum(peak_a, peak_b)
    factor_a = jnp.exp(peak_a - peak)
    factor_b = jnp.exp(peak_b - peak)
    return (
        peak,
        denom_a * factor_a + denom_b * factor_b,
        numer_a * factor_a[..., None] + numer_b * factor_b[..., None],
    )


def per_device(queries, cache_keys, cache_values, selected):
    head_count, query_rows, head_width = queries.shape
    key_rows = cache_keys.shape[1]
    order_size = selected.shape[1]
    row_devices = lax.axis_size("pb")
    col_devices = lax.axis_size("kv")
    row_len = order_size // row_devices
    col_len = order_size // col_devices
    score_scale = head_width ** (-0.5)
    high = lax.Precision.HIGHEST
    col_start = lax.axis_index("kv") * col_len
    row_start = lax.axis_index("pb") * row_len
    offsets = selected - lax.axis_index("kv") * key_rows
    is_owned = (offsets >= 0) & (offsets < key_rows)
    picked = jnp.take_along_axis(cache_keys, jnp.clip(offsets, 0, key_rows - 1)[:, :, None], axis=1)
    picked = jnp.where(is_owned[:, :, None], picked, jnp.zeros_like(picked))
    chosen = lax.psum(picked, "kv").astype(jnp.float32).astype(jnp.bfloat16)
    block_rows = math.gcd(512, query_rows)
    block_count = query_rows // block_rows
    query_blocks = queries.reshape(head_count, block_count, block_rows, head_width).transpose(
        1, 0, 2, 3
    )

    def local_block(query_block):
        scores = (
            jnp.einsum("hqd,hkd->hqk", query_block, cache_keys, preferred_element_type=jnp.float32)
            * score_scale
        )
        block_peak = jnp.max(scores, axis=-1)
        weights = jnp.exp(scores - block_peak[..., None])
        block_denom = jnp.sum(weights, axis=-1)
        w_high = weights.astype(jnp.bfloat16)
        w_low = (weights - w_high.astype(jnp.float32)).astype(jnp.bfloat16)
        block_numer = jnp.einsum(
            "hqk,hkd->hqd", w_high, cache_values, preferred_element_type=jnp.float32
        )
        block_numer = block_numer + jnp.einsum(
            "hqk,hkd->hqd", w_low, cache_values, preferred_element_type=jnp.float32
        )
        compact = (
            jnp.einsum("hqd,hkd->hqk", query_block, chosen, preferred_element_type=jnp.float32)
            * score_scale
        )
        compact_w = jnp.exp(compact - jnp.max(compact, axis=-1, keepdims=True))
        block_probs = (compact_w / jnp.sum(compact_w, axis=-1, keepdims=True)).astype(jnp.bfloat16)
        return (block_peak, block_denom, block_numer, block_probs)

    peak_b, denom_b, numer_b, probs_b = lax.map(local_block, query_blocks)
    peak = peak_b.transpose(1, 0, 2).reshape(head_count, query_rows)
    denominator = denom_b.transpose(1, 0, 2).reshape(head_count, query_rows)
    numer = numer_b.transpose(1, 0, 2, 3).reshape(head_count, query_rows, head_width)
    compact_probs = probs_b.transpose(1, 0, 2, 3).reshape(head_count, query_rows, order_size)
    peak, denominator, numer = joined((peak, denominator, numer), "kv", combine_parts)
    attended = (numer / denominator[..., None]).astype(jnp.bfloat16)
    probs_cols = lax.dynamic_slice_in_dim(compact_probs, col_start, col_len, 2)
    product = jnp.einsum(
        "hqa,hqb->ahb", compact_probs, probs_cols, preferred_element_type=jnp.float32
    )
    gram_sum = lax.psum_scatter(
        product.reshape(lax.axis_size("pb") * row_len, head_count * col_len),
        "pb",
        scatter_dimension=0,
        tiled=True,
    )
    weighting = order_size / (query_rows * row_devices)
    row_ids = row_start + jnp.arange(row_len, dtype=jnp.int32)
    col_ids = col_start + jnp.arange(col_len, dtype=jnp.int32)
    identity = (row_ids[:, None] == col_ids[None, :]).astype(jnp.float32)
    gram_tile = gram_sum.reshape(row_len, head_count, col_len).transpose(1, 0, 2) * weighting
    gram_tile = gram_tile + ridge_weight * identity[None]
    rhs_part = jnp.einsum("hqa,hqd->had", probs_cols, attended, preferred_element_type=jnp.float32)
    rhs_col = lax.psum(rhs_part, "pb") * weighting
    sigma = theta_mid / delta_half
    solution = jnp.zeros_like(rhs_col)
    resid = rhs_col
    direction = rhs_col / theta_mid
    recur_now = 1.0 / sigma
    for iteration in range(STEPS):
        solution = solution + direction
        partial_rows = jnp.einsum("hrc,hcd->hrd", gram_tile, direction, precision=high)
        summed_rows = lax.psum(partial_rows, "kv")
        whole = lax.all_gather(summed_rows, "pb", axis=1, tiled=True)
        resid = resid - lax.dynamic_slice_in_dim(whole, col_start, col_len, 1)
        recur_next = 1.0 / (2.0 * sigma - recur_now)
        direction = recur_next * recur_now * direction + 2.0 * recur_next / delta_half * resid
        recur_now = recur_next
    return (solution, resid)


def solution(mesh):
    in_specs = (P(None, "pb", None), P(None, "kv", None), P(None, "kv", None), P())
    out_specs = (P(None, "kv", None), P(None, "kv", None))
    return jax.shard_map(
        per_device, mesh=mesh, in_specs=in_specs, out_specs=out_specs, check_vma=False
    )
```

profile of v0, /device:TPU:6, one launch (start us, length us, event | category | flops | bytes accessed | tf_op | source)
XLA Modules:
  0.0 1193.0 jit_solution(17051275337214577347)
XLA Ops:
  8.8 21.7 %gather_fusion = bf16[4096,128]{1,0:T(8,128)(2,1)S(1)} fusion(bf16[2,1024,128]{2,1,0:T(8,128)(2,1)S(1)} %copy-done, s32[4096]{0:T(1024)S(1)} %bitcast.60), kind=kCustom, calls=%fused_computation | custom fusion | bytes 2129920 | tf_op jit(solution)/shard_map/jit(take_along_axis)/gather | solution.py:54
  30.6 2.5 select_select_fusion
  33.1 123.1 %all-reduce.6.cloned.1.call-done = bf16[2,2048,128]{2,1,0:T(8,128)(2,1)} async-done(((bf16[2,2048,128]{2,1,0:T(8,128)(2,1)}), bf16[2,2048,128]{2,1,0:T(8,128)(2,1)}) %all-reduce.6.cloned.1.call-update) | async-done | bytes 1048592 | tf_op jit(solution)/shard_map/psum | solution.py:56
  156.2 4.6 fusion.45
  160.8 2.5 divide_convert_fusion
  164.7 1.9 copy.13
  168.2 1.3 fusion.14
  170.1 14.4 %all-gather.4 = f32[16,2,256]{2,1,0:T(2,128)S(1)} all-gather(f32[1,2,256]{2,1,0:T(2,128)S(1)} %bitcast.65), channel_id=3, replica_groups=mesh['pb'=32,'kv'=16] {'kv'}, dimensions={0}, use_global_device_ids=true | all-gather | bytes 34816 | tf_op jit(solution)/shard_map/all_gather | solution.py:17
  184.5 16.9 %all-gather.3 = f32[16,2,256]{2,1,0:T(2,128)S(1)} all-gather(f32[1,2,256]{2,1,0:T(2,128)S(1)} %bitcast.64), channel_id=2, replica_groups=mesh['pb'=32,'kv'=16] {'kv'}, dimensions={0}, use_global_device_ids=true | all-gather | bytes 34816 | tf_op jit(solution)/shard_map/all_gather | solution.py:17
  201.6 187.9 %reduce-scatter.2.cloned.1.call-done = f32[64,256]{1,0:T(8,128)} async-done(((f32[2048,256]{1,0:T(8,128)}), f32[64,256]{1,0:T(8,128)}) %reduce-scatter.2.cloned.1.call-update) | async-done | bytes 65552 | tf_op jit(solution)/shard_map/reduce_scatter | solution.py:98
  390.3 45.9 %all-gather.16.cloned.1.call-done = f32[32,256,128]{2,1,0:T(8,128)} async-done(((f32[2,256,128]{2,1,0:T(8,128)}), f32[32,256,128]{2,1,0:T(8,128)}) %all-gather.16.cloned.1.call-update) | async-done | bytes 4194320 | tf_op jit(solution)/shard_map/all_gather | solution.py:17
  437.2 18.9 %while.12 = (s32[]{:T(128)}, f32[2,256]{1,0:T(2,128)S(1)}, f32[2,256]{1,0:T(2,128)S(1)}, f32[2,256,128]{2,1,0:T(8,128)S(1)}, f32[16,2,256]{2,1,0:T(2,128)S(1)}, ...) while((s32[]{:T(128)}, f32[2,256]{1,0:T(2,128)S(1)}, ...), condition=%wide.region_6.7_spmd, body=%wide.region_5.6_spmd.sunk | while | flops 199685 | bytes 807063 | solution.py:22
  437.3 1.2 fusion.58
  438.5 1.2 fusion.58
  439.8 1.2 fusion.58
  441.0 1.2 fusion.58
  442.3 1.2 fusion.58
  443.6 1.2 fusion.58
  453.6 1.2 fusion.58
  456.1 1.9 fusion.22
  458.1 151.6 %all-reduce.8.cloned.1.call-done = f32[2,128,128]{2,1,0:T(8,128)} async-done(((f32[2,128,128]{2,1,0:T(8,128)}), f32[2,128,128]{2,1,0:T(8,128)}) %all-reduce.8.cloned.1.call-update) | async-done | bytes 131088 | tf_op jit(solution)/shard_map/psum | solution.py:111
  609.7 1.8 fusion.23
  611.6 106.0 %all-reduce.10.cloned.1.call-done = f32[2,64,128]{2,1,0:T(8,128)} async-done(((f32[2,64,128]{2,1,0:T(8,128)}), f32[2,64,128]{2,1,0:T(8,128)}) %all-reduce.10.cloned.1.call-update) | async-done | bytes 65552 | tf_op jit(solution)/shard_map/psum | solution.py:120
  717.7 83.0 %all-gather.10.cloned.1.call-done = f32[2,2048,128]{2,1,0:T(8,128)} async-done(((f32[2,64,128]{2,1,0:T(8,128)}), f32[2,2048,128]{2,1,0:T(8,128)}) %all-gather.10.cloned.1.call-update) | async-done | bytes 2097168 | tf_op jit(solution)/shard_map/all_gather | solution.py:121
  800.6 1.9 fusion.32
  802.6 106.5 %all-reduce.12.cloned.1.call-done = f32[2,64,128]{2,1,0:T(8,128)} async-done(((f32[2,64,128]{2,1,0:T(8,128)}), f32[2,64,128]{2,1,0:T(8,128)}) %all-reduce.12.cloned.1.call-update) | async-done | bytes 65552 | tf_op jit(solution)/shard_map/psum | solution.py:120
  909.2 83.1 %all-gather.12.cloned.1.call-done = f32[2,2048,128]{2,1,0:T(8,128)} async-done(((f32[2,64,128]{2,1,0:T(8,128)}), f32[2,2048,128]{2,1,0:T(8,128)}) %all-gather.12.cloned.1.call-update) | async-done | bytes 2097168 | tf_op jit(solution)/shard_map/all_gather | solution.py:121
  992.3 1.7 add_add_fusion
  994.0 1.9 fusion.28
  996.0 105.6 %all-reduce.14.cloned.1.call-done = f32[2,64,128]{2,1,0:T(8,128)} async-done(((f32[2,64,128]{2,1,0:T(8,128)}), f32[2,64,128]{2,1,0:T(8,128)}) %all-reduce.14.cloned.1.call-update) | async-done | bytes 65552 | tf_op jit(solution)/shard_map/psum | solution.py:120
  1101.6 83.0 %all-gather.14.cloned.1.call-done = f32[2,2048,128]{2,1,0:T(8,128)} async-done(((f32[2,64,128]{2,1,0:T(8,128)}), f32[2,2048,128]{2,1,0:T(8,128)}) %all-gather.14.cloned.1.call-update) | async-done | bytes 2097168 | tf_op jit(solution)/shard_map/all_gather | solution.py:121
  1184.6 1.6 dynamic-slice_subtract_fusion
  (67 shorter events, 17.6 us)
Async XLA Ops:
  7.2 1.7 copy-start
  7.2 149.1 %all-reduce.6.cloned.1.call-start = ((), (), s32[]{:S(2)}) async-start(), calls=%async_computation.1 | async-start | bytes 2097152 | tf_op jit(solution)/shard_map/psum | solution.py:56
  30.5 125.7 %copy-start.3 = (bf16[2,256,128]{2,1,0:T(8,128)(2,1)S(1)}, bf16[2,256,128]{2,1,0:T(8,128)(2,1)}, u32[]{:S(2)}) copy-start(bf16[2,256,128]{2,1,0:T(8,128)(2,1)} %param.6) | copy-start | bytes 393220
  33.0 356.4 %reduce-scatter.2.cloned.1.call-start = ((), (), s32[]{:S(2)}) async-start(), calls=%async_computation.3 | async-start | bytes 2162688 | tf_op jit(solution)/shard_map/reduce_scatter | solution.py:98
  163.4 1.3 copy-start.1
  166.6 1.0 copy-start.2
  166.6 269.6 %all-gather.16.cloned.1.call-start = ((), (), s32[]{:S(2)}) async-start(), calls=%async_computation.10 | async-start | bytes 4456448 | tf_op jit(solution)/shard_map/all_gather | solution.py:17
  169.6 440.1 %all-reduce.8.cloned.1.call-start = ((), (), s32[]{:S(2)}) async-start(), calls=%async_computation.2 | async-start | bytes 262144 | tf_op jit(solution)/shard_map/psum | solution.py:111
  458.0 259.6 %all-reduce.10.cloned.1.call-start = ((), (), s32[]{:S(2)}) async-start(), calls=%async_computation.4 | async-start | bytes 131072 | tf_op jit(solution)/shard_map/psum | solution.py:120
  611.5 189.1 %all-gather.10.cloned.1.call-start = ((), (), s32[]{:S(2)}) async-start(), calls=%async_computation.5 | async-start | bytes 2162688 | tf_op jit(solution)/shard_map/all_gather | solution.py:121
  717.6 191.5 %all-reduce.12.cloned.1.call-start = ((), (), s32[]{:S(2)}) async-start(), calls=%async_computation.6 | async-start | bytes 131072 | tf_op jit(solution)/shard_map/psum | solution.py:120
  802.5 189.8 %all-gather.12.cloned.1.call-start = ((), (), s32[]{:S(2)}) async-start(), calls=%async_computation.7 | async-start | bytes 2162688 | tf_op jit(solution)/shard_map/all_gather | solution.py:121
  909.1 192.5 %all-reduce.14.cloned.1.call-start = ((), (), s32[]{:S(2)}) async-start(), calls=%async_computation.8 | async-start | bytes 131072 | tf_op jit(solution)/shard_map/psum | solution.py:120
  995.9 188.7 %all-gather.14.cloned.1.call-start = ((), (), s32[]{:S(2)}) async-start(), calls=%async_computation.9 | async-start | bytes 2162688 | tf_op jit(solution)/shard_map/all_gather | solution.py:121
Sparse Core Ops, SparseCore 0:
  33.2 123.0 all-reduce.5
  166.7 222.7 reduce-scatter.1
  391.6 44.6 all-gather.15
  458.1 151.5 all-reduce.7
  612.5 105.0 all-reduce.9
  720.6 79.9 all-gather.9
  803.5 105.4 all-reduce.11
  912.3 79.9 all-gather.11
  996.0 105.4 all-reduce.13
  1104.6 79.9 all-gather.13
where the time goes:
time: 1200 us; the launch traced here: 1190 us
  waiting for transfers between devices  1080 us (90%)
  blocking collectives  31.3 us (3%)
  other arithmetic  29.8 us (2%)
  local copies, waits for them, and re-layouts  25.5 us (2%)
  matrix products  15.3 us (1%)
  between operations  14.3 us (1%)
    psum x3, waiting for transfers between devices, per_device(): summed_rows = lax.psum(partial_rows, 'kv')  318 us
    all_gather x3, waiting for transfers between devices, per_device(): whole = lax.all_gather(summed_rows, 'pb', axis=1, tiled=True)  249 us
    reduce_scatter x1, waiting for transfers between devices, per_device(): lax.psum_scatter(product.reshape(lax.axis_size('pb') * row_len, head_coun...  188 us
    psum x1, waiting for transfers between devices, per_device(): rhs_col = lax.psum(rhs_part, 'pb') * weighting  152 us
    psum x1, waiting for transfers between devices, per_device(): chosen = lax.psum(picked, 'kv').astype(jnp.float32).astype(jnp.bfloat16)  123 us
    all_gather x1, waiting for transfers between devices, joined(): gathered = jax.tree.map(lambda a: lax.all_gather(a, axis), part)  45.9 us
    all_gather x2, blocking collectives, joined(): gathered = jax.tree.map(lambda a: lax.all_gather(a, axis), part)  31.3 us
  transfers between devices with their start and end apart: 10, of which 10 were waited for; matrix products, arithmetic and copies ran while one was open for 0% of the time, Pallas kernels for 0%

commit v1 on v0

v1 whole, which is shorter than its diff:
```python
import jax
import jax.numpy as jnp
from jax import lax
from jax.sharding import PartitionSpec as P

STEPS = 3


ridge_weight = 0.1
theta_mid = 1.1
delta_half = 1.0

F32 = jnp.float32
BF16 = jnp.bfloat16


def exchange(tree, axis, bit):
    size = lax.axis_size(axis)
    pairs = [(s, s ^ bit) for s in range(size)]
    return jax.tree.map(lambda a: lax.ppermute(a, axis, pairs), tree)


def butterfly_sum(value, axis):
    bit = 1
    while bit < lax.axis_size(axis):
        value = value + exchange(value, axis, bit)
        bit *= 2
    return value


def butterfly(tree, axis, combine):
    bit = 1
    while bit < lax.axis_size(axis):
        tree = combine(tree, exchange(tree, axis, bit))
        bit *= 2
    return tree


def scatter_halving(blocks, axis):
    me = lax.axis_index(axis)
    bit = 1
    level = 0
    while bit < lax.axis_size(axis):
        rest = blocks.shape[0] // 2
        pair = blocks.reshape((rest, 2) + blocks.shape[1:])
        mine = (me >> level) & 1
        keep = jnp.where(mine == 0, pair[:, 0], pair[:, 1])
        give = jnp.where(mine == 0, pair[:, 1], pair[:, 0])
        blocks = keep + exchange(give, axis, bit)
        bit *= 2
        level += 1
    return blocks[0]


def split_dot(spec, low, wide):
    high = wide.astype(BF16)
    rest = (wide - high.astype(F32)).astype(BF16)
    return jnp.einsum(spec, low, high, preferred_element_type=F32) + jnp.einsum(
        spec, low, rest, preferred_element_type=F32
    )


def combine_stats(first, second):
    peak_a, denom_a, numer_a, cpeak_a, cdenom_a = first
    peak_b, denom_b, numer_b, cpeak_b, cdenom_b = second
    peak = jnp.maximum(peak_a, peak_b)
    fa = jnp.exp(peak_a - peak)
    fb = jnp.exp(peak_b - peak)
    cpeak = jnp.maximum(cpeak_a, cpeak_b)
    ga = jnp.exp(cpeak_a - cpeak)
    gb = jnp.exp(cpeak_b - cpeak)
    return (
        peak,
        denom_a * fa + denom_b * fb,
        numer_a * fa[..., None] + numer_b * fb[..., None],
        cpeak,
        cdenom_a * ga + cdenom_b * gb,
    )


def per_device(queries, cache_keys, cache_values, selected):
    head_count, query_rows, head_width = queries.shape
    key_rows = cache_keys.shape[1]
    order_size = selected.shape[1]
    row_devices = lax.axis_size("pb")
    col_devices = lax.axis_size("kv")
    col_len = order_size // col_devices
    score_scale = head_width ** (-0.5)
    me_kv = lax.axis_index("kv")

    local_pos = me_kv * key_rows + jnp.arange(key_rows, dtype=jnp.int32)
    owned = selected[:, :, None] == local_pos[None, None, :]
    picked = jnp.einsum(
        "hak,hkd->had", owned.astype(BF16), cache_keys, preferred_element_type=F32
    ).astype(BF16)
    kept_mask = jnp.any(owned, axis=1)
    blocks = picked.reshape(head_count, col_devices, col_len, head_width).transpose(1, 0, 2, 3)
    chosen_block = scatter_halving(blocks, "kv")

    scores = (
        jnp.einsum("hqd,hkd->hqk", queries, cache_keys, preferred_element_type=F32) * score_scale
    )
    peak = jnp.max(scores, axis=-1)
    weights = jnp.exp(scores - peak[..., None])
    denom = jnp.sum(weights, axis=-1)
    w_high = weights.astype(BF16)
    w_low = (weights - w_high.astype(F32)).astype(BF16)
    numer = jnp.einsum(
        "hqk,hkd->hqd", w_high, cache_values, preferred_element_type=F32
    ) + jnp.einsum("hqk,hkd->hqd", w_low, cache_values, preferred_element_type=F32)
    floor = jnp.float32(-1e30)
    kept_scores = jnp.where(kept_mask[:, None, :], scores, floor)
    cpeak = jnp.max(kept_scores, axis=-1)
    cweights = jnp.where(kept_mask[:, None, :], jnp.exp(kept_scores - cpeak[..., None]), 0.0)
    cdenom = jnp.sum(cweights, axis=-1)

    peak, denom, numer, cpeak, cdenom = butterfly(
        (peak, denom, numer, cpeak, cdenom), "kv", combine_stats
    )
    attended = (numer / denom[..., None]).astype(BF16)

    compact = (
        jnp.einsum("hqd,hkd->hqk", queries, chosen_block, preferred_element_type=F32)
        * score_scale
    )
    probs = (jnp.exp(compact - cpeak[..., None]) / cdenom[..., None]).astype(BF16)

    weighting = order_size / (query_rows * row_devices)
    rhs_part = jnp.einsum("hqa,hqd->had", probs, attended, preferred_element_type=F32)
    rhs = butterfly_sum(rhs_part, "pb") * weighting

    def gram_times(vec):
        across = butterfly_sum(split_dot("hqa,had->hqd", probs, vec), "kv")
        back = butterfly_sum(split_dot("hqa,hqd->had", probs, across), "pb")
        return back * weighting + ridge_weight * vec

    sigma = theta_mid / delta_half
    solution = jnp.zeros_like(rhs)
    resid = rhs
    direction = rhs / theta_mid
    recur_now = 1.0 / sigma
    for iteration in range(STEPS):
        solution = solution + direction
        resid = resid - gram_times(direction)
        recur_next = 1.0 / (2.0 * sigma - recur_now)
        direction = recur_next * recur_now * direction + 2.0 * recur_next / delta_half * resid
        recur_now = recur_next
    return (solution, resid)


def solution(mesh):
    in_specs = (P(None, "pb", None), P(None, "kv", None), P(None, "kv", None), P())
    out_specs = (P(None, "kv", None), P(None, "kv", None))
    return jax.shard_map(
        per_device, mesh=mesh, in_specs=in_specs, out_specs=out_specs, check_vma=False
    )
```

time: 1200 us -> 461 us (0.38)
  waiting for transfers between devices: 1080 us -> 239 us
  starting transfers between devices: 0.41 us -> 201 us
  blocking collectives: 31.3 us -> 0 us
  local copies, waits for them, and re-layouts: 25.5 us -> 1.15 us
  other arithmetic: 29.8 us -> 7.85 us
  between operations: 14.3 us -> 1.68 us
    psum x5 -> x0, waiting for transfers between devices: 593 us -> none  [the longest x3 318 us: per_device(): summed_rows = lax.psum(partial_rows, 'kv')]
    all_gather x4 -> x0, waiting for transfers between devices: 295 us -> none  [the longest x3 249 us: per_device(): whole = lax.all_gather(summed_rows, 'pb', axis=1, tiled=True)]
    ppermute x0 -> x56, waiting for transfers between devices: none -> 239 us  [exchange(): return jax.tree.map(lambda a: lax.ppermute(a, axis, pairs), tree)]
    ppermute x0 -> x56, starting transfers between devices: none -> 201 us  [exchange(): return jax.tree.map(lambda a: lax.ppermute(a, axis, pairs), tree)]
    reduce_scatter x1 -> x0, waiting for transfers between devices: 188 us -> none  [per_device(): lax.psum_scatter(product.reshape(lax.axis_size('pb') * row_len, head_coun...]
    all_gather x2 -> x0, blocking collectives: 31.3 us -> none  [joined(): gathered = jax.tree.map(lambda a: lax.all_gather(a, axis), part)]
    gather x1 -> x0, local copies, waits for them, and re-layouts: 21.7 us -> none  [per_device(): jnp.take_along_axis(cache_keys, jnp.clip(offsets, 0, key_rows - 1)[:, :,...]
    add x33 -> x41, other arithmetic: 18.6 us -> 1.59 us  [the longest x3 0.6 us: combine_stats(): numer_a * fa[..., None] + numer_b * fb[..., None]]
  transfers between devices with their start and end apart: 10 -> 56, of which waited for: 10 -> 37; matrix products, arithmetic and copies ran while one was open for 0% -> 2% of each run, Pallas kernels for 0% -> 0%
where the time goes in v1:
time: 461 us; the launch traced here: 459 us
  waiting for transfers between devices  239 us (52%)
  starting transfers between devices  201 us (44%)
  matrix products  8.83 us (2%)
  other arithmetic  7.85 us (2%)
    ppermute x56, waiting for transfers between devices, exchange(): return jax.tree.map(lambda a: lax.ppermute(a, axis, pairs), tree)  239 us
    ppermute x56, starting transfers between devices, exchange(): return jax.tree.map(lambda a: lax.ppermute(a, axis, pairs), tree)  201 us
  transfers between devices with their start and end apart: 56, of which 37 were waited for; matrix products, arithmetic and copies ran while one was open for 2% of the time, Pallas kernels for 0%

profile of v1, /device:TPU:6, one launch (start us, length us, event | category | flops | bytes accessed | tf_op | source)
XLA Modules:
  0.0 459.3 jit_solution(1036411666161579192)
XLA Ops:
  37.6 6.1 %collective-permute-start.10 = (f32[2,256]{1,0:T(2,128)S(1)}, f32[2,256]{1,0:T(2,128)S(1)}, u32[]{:S(2)}, u32[]{:S(2)}) collective-permute-start(f32[2,256]{1,0:T(2,128)S(1)} %get-tuple-element.27), channel_id=1, source_target_pairs={{0,4},{1,5},{2,6},{3,7},{4,0},{5,1},{6,2},{7,3},{8,12},{9,13},{10,... | collective-permute-start | bytes 6152 | tf_op jit(solution)/shard_map/ppermute | solution.py:20
  52.4 9.3 %collective-permute-start.11 = (f32[2,256]{1,0:T(2,128)S(1)}, f32[2,256]{1,0:T(2,128)S(1)}, u32[]{:S(2)}, u32[]{:S(2)}) collective-permute-start(f32[2,256]{1,0:T(2,128)S(1)} %get-tuple-element.25), channel_id=1, source_target_pairs={{0,8},{1,9},{2,10},{3,11},{4,12},{5,13},{6,14},{7,15},{8,0},{9,1},... | collective-permute-start | bytes 6152 | tf_op jit(solution)/shard_map/ppermute | solution.py:20
  63.7 7.8 %collective-permute-start.23 = (f32[2,256]{1,0:T(2,128)S(1)}, f32[2,256]{1,0:T(2,128)S(1)}, u32[]{:S(2)}, u32[]{:S(2)}) collective-permute-start(f32[2,256]{1,0:T(2,128)S(1)} %get-tuple-element.11), channel_id=1, source_target_pairs={{0,8},{1,9},{2,10},{3,11},{4,12},{5,13},{6,14},{7,15},{8,0},{9,1},... | collective-permute-start | bytes 6152 | tf_op jit(solution)/shard_map/ppermute | solution.py:20
  81.0 5.9 %collective-permute-done.15 = f32[2,256,128]{2,1,0:T(8,128)S(1)} collective-permute-done((f32[2,256,128]{2,1,0:T(8,128)S(1)}, f32[2,256,128]{2,1,0:T(8,128)S(1)}, u32[]{:S(2)}, u32[]{:S(2)}) %collective-permute-start.15) | collective-permute-done | bytes 262176 | tf_op jit(solution)/shard_map/ppermute | solution.py:20
  94.8 11.8 %collective-permute-done.17 = f32[2,256,128]{2,1,0:T(8,128)S(1)} collective-permute-done((f32[2,256,128]{2,1,0:T(8,128)S(1)}, f32[2,256,128]{2,1,0:T(8,128)S(1)}, u32[]{:S(2)}, u32[]{:S(2)}) %collective-permute-start.17) | collective-permute-done | bytes 262176 | tf_op jit(solution)/shard_map/ppermute | solution.py:20
  106.8 6.6 %collective-permute-start.19 = (f32[2,256,128]{2,1,0:T(8,128)S(1)}, f32[2,256,128]{2,1,0:T(8,128)S(1)}, u32[]{:S(2)}, u32[]{:S(2)}) collective-permute-start(f32[2,256,128]{2,1,0:T(8,128)S(1)} %multiply_add_fusion), channel_id=1, source_target_pairs={{0,8},{1,9},{2,10},{3,11},{4,12},{5,13},{6,14},{7,15},{8,0},{9,1},... | collective-permute-start | bytes 786440 | tf_op jit(solution)/shard_map/ppermute | solution.py:20
  116.6 6.9 %collective-permute-done.3 = bf16[1,2,128,128]{3,2,1,0:T(8,128)(2,1)S(1)} collective-permute-done((bf16[1,2,128,128]{3,2,1,0:T(8,128)(2,1)S(1)}, bf16[1,2,128,128]{3,2,1,0:T(8,128)(2,1)S(1)}, u32[]{:S(2)}, u32[]{:S(2)}) %collective-permute-start.3) | collective-permute-done | bytes 65568 | tf_op jit(solution)/shard_map/ppermute | solution.py:20
  132.5 5.4 %collective-permute-start.25 = (f32[2,128,128]{2,1,0:T(8,128)S(1)}, f32[2,128,128]{2,1,0:T(8,128)S(1)}, u32[]{:S(2)}, u32[]{:S(2)}) collective-permute-start(f32[2,128,128]{2,1,0:T(8,128)S(1)} %add.215), channel_id=1, source_target_pairs={{0,32},{16,48},{32,0},{48,16},{64,96},{80,112},{96,64},{112,80},{1... | collective-permute-start | bytes 393224 | tf_op jit(solution)/shard_map/ppermute | solution.py:20
  140.9 7.6 %collective-permute-start.26 = (f32[2,128,128]{2,1,0:T(8,128)S(1)}, f32[2,128,128]{2,1,0:T(8,128)S(1)}, u32[]{:S(2)}, u32[]{:S(2)}) collective-permute-start(f32[2,128,128]{2,1,0:T(8,128)S(1)} %add.216), channel_id=1, source_target_pairs={{0,64},{16,80},{32,96},{48,112},{64,0},{80,16},{96,32},{112,48},{1... | collective-permute-start | bytes 393224 | tf_op jit(solution)/shard_map/ppermute | solution.py:20
  176.2 6.6 %collective-permute-done.30 = f32[2,256,128]{2,1,0:T(8,128)S(1)} collective-permute-done((f32[2,256,128]{2,1,0:T(8,128)S(1)}, f32[2,256,128]{2,1,0:T(8,128)S(1)}, u32[]{:S(2)}, u32[]{:S(2)}) %collective-permute-start.30) | collective-permute-done | bytes 262176 | tf_op jit(solution)/shard_map/ppermute | solution.py:20
  182.8 5.4 %collective-permute-start.31 = (f32[2,256,128]{2,1,0:T(8,128)S(1)}, f32[2,256,128]{2,1,0:T(8,128)S(1)}, u32[]{:S(2)}, u32[]{:S(2)}) collective-permute-start(f32[2,256,128]{2,1,0:T(8,128)S(1)} %add.222), channel_id=1, source_target_pairs={{0,4},{1,5},{2,6},{3,7},{4,0},{5,1},{6,2},{7,3},{8,12},{9,13},{10,... | collective-permute-start | bytes 786440 | tf_op jit(solution)/shard_map/ppermute | solution.py:20
  188.2 11.6 %collective-permute-done.31 = f32[2,256,128]{2,1,0:T(8,128)S(1)} collective-permute-done((f32[2,256,128]{2,1,0:T(8,128)S(1)}, f32[2,256,128]{2,1,0:T(8,128)S(1)}, u32[]{:S(2)}, u32[]{:S(2)}) %collective-permute-start.31) | collective-permute-done | bytes 262176 | tf_op jit(solution)/shard_map/ppermute | solution.py:20
  199.8 6.7 %collective-permute-start.32 = (f32[2,256,128]{2,1,0:T(8,128)S(1)}, f32[2,256,128]{2,1,0:T(8,128)S(1)}, u32[]{:S(2)}, u32[]{:S(2)}) collective-permute-start(f32[2,256,128]{2,1,0:T(8,128)S(1)} %add.223), channel_id=1, source_target_pairs={{0,8},{1,9},{2,10},{3,11},{4,12},{5,13},{6,14},{7,15},{8,0},{9,1},... | collective-permute-start | bytes 786440 | tf_op jit(solution)/shard_map/ppermute | solution.py:20
  206.5 12.1 %collective-permute-done.32 = f32[2,256,128]{2,1,0:T(8,128)S(1)} collective-permute-done((f32[2,256,128]{2,1,0:T(8,128)S(1)}, f32[2,256,128]{2,1,0:T(8,128)S(1)}, u32[]{:S(2)}, u32[]{:S(2)}) %collective-permute-start.32) | collective-permute-done | bytes 262176 | tf_op jit(solution)/shard_map/ppermute | solution.py:20
  228.4 6.1 %collective-permute-done.34 = f32[2,128,128]{2,1,0:T(8,128)S(1)} collective-permute-done((f32[2,128,128]{2,1,0:T(8,128)S(1)}, f32[2,128,128]{2,1,0:T(8,128)S(1)}, u32[]{:S(2)}, u32[]{:S(2)}) %collective-permute-start.34) | collective-permute-done | bytes 131104 | tf_op jit(solution)/shard_map/ppermute | solution.py:20
  234.5 8.1 %collective-permute-start.35 = (f32[2,128,128]{2,1,0:T(8,128)S(1)}, f32[2,128,128]{2,1,0:T(8,128)S(1)}, u32[]{:S(2)}, u32[]{:S(2)}) collective-permute-start(f32[2,128,128]{2,1,0:T(8,128)S(1)} %add.227), channel_id=1, source_target_pairs={{0,64},{16,80},{32,96},{48,112},{64,0},{80,16},{96,32},{112,48},{1... | collective-permute-start | bytes 393224 | tf_op jit(solution)/shard_map/ppermute | solution.py:20
  242.7 6.4 %collective-permute-done.35 = f32[2,128,128]{2,1,0:T(8,128)S(1)} collective-permute-done((f32[2,128,128]{2,1,0:T(8,128)S(1)}, f32[2,128,128]{2,1,0:T(8,128)S(1)}, u32[]{:S(2)}, u32[]{:S(2)}) %collective-permute-start.35) | collective-permute-done | bytes 131104 | tf_op jit(solution)/shard_map/ppermute | solution.py:20
  259.3 5.8 %collective-permute-done.37 = f32[2,128,128]{2,1,0:T(8,128)S(1)} collective-permute-done((f32[2,128,128]{2,1,0:T(8,128)S(1)}, f32[2,128,128]{2,1,0:T(8,128)S(1)}, u32[]{:S(2)}, u32[]{:S(2)}) %collective-permute-start.37) | collective-permute-done | bytes 131104 | tf_op jit(solution)/shard_map/ppermute | solution.py:20
  271.0 8.3 %collective-permute-done.39 = f32[2,256,128]{2,1,0:T(8,128)S(1)} collective-permute-done((f32[2,256,128]{2,1,0:T(8,128)S(1)}, f32[2,256,128]{2,1,0:T(8,128)S(1)}, u32[]{:S(2)}, u32[]{:S(2)}) %collective-permute-start.39) | collective-permute-done | bytes 262176 | tf_op jit(solution)/shard_map/ppermute | solution.py:20
  284.1 11.6 %collective-permute-done.40 = f32[2,256,128]{2,1,0:T(8,128)S(1)} collective-permute-done((f32[2,256,128]{2,1,0:T(8,128)S(1)}, f32[2,256,128]{2,1,0:T(8,128)S(1)}, u32[]{:S(2)}, u32[]{:S(2)}) %collective-permute-start.40) | collective-permute-done | bytes 262176 | tf_op jit(solution)/shard_map/ppermute | solution.py:20
  300.8 13.5 %collective-permute-done.41 = f32[2,256,128]{2,1,0:T(8,128)S(1)} collective-permute-done((f32[2,256,128]{2,1,0:T(8,128)S(1)}, f32[2,256,128]{2,1,0:T(8,128)S(1)}, u32[]{:S(2)}, u32[]{:S(2)}) %collective-permute-start.41) | collective-permute-done | bytes 262176 | tf_op jit(solution)/shard_map/ppermute | solution.py:20
  316.6 5.4 %collective-permute-done.42 = f32[2,128,128]{2,1,0:T(8,128)S(1)} collective-permute-done((f32[2,128,128]{2,1,0:T(8,128)S(1)}, f32[2,128,128]{2,1,0:T(8,128)S(1)}, u32[]{:S(2)}, u32[]{:S(2)}) %collective-permute-start.42) | collective-permute-done | bytes 131104 | tf_op jit(solution)/shard_map/ppermute | solution.py:20
  324.6 7.6 %collective-permute-done.43 = f32[2,128,128]{2,1,0:T(8,128)S(1)} collective-permute-done((f32[2,128,128]{2,1,0:T(8,128)S(1)}, f32[2,128,128]{2,1,0:T(8,128)S(1)}, u32[]{:S(2)}, u32[]{:S(2)}) %collective-permute-start.43) | collective-permute-done | bytes 131104 | tf_op jit(solution)/shard_map/ppermute | solution.py:20
  337.0 8.7 %collective-permute-done.44 = f32[2,128,128]{2,1,0:T(8,128)S(1)} collective-permute-done((f32[2,128,128]{2,1,0:T(8,128)S(1)}, f32[2,128,128]{2,1,0:T(8,128)S(1)}, u32[]{:S(2)}, u32[]{:S(2)}) %collective-permute-start.44) | collective-permute-done | bytes 131104 | tf_op jit(solution)/shard_map/ppermute | solution.py:20
  356.4 5.1 %collective-permute-done.46 = f32[2,128,128]{2,1,0:T(8,128)S(1)} collective-permute-done((f32[2,128,128]{2,1,0:T(8,128)S(1)}, f32[2,128,128]{2,1,0:T(8,128)S(1)}, u32[]{:S(2)}, u32[]{:S(2)}) %collective-permute-start.46) | collective-permute-done | bytes 131104 | tf_op jit(solution)/shard_map/ppermute | solution.py:20
  368.0 8.3 %collective-permute-done.48 = f32[2,256,128]{2,1,0:T(8,128)S(1)} collective-permute-done((f32[2,256,128]{2,1,0:T(8,128)S(1)}, f32[2,256,128]{2,1,0:T(8,128)S(1)}, u32[]{:S(2)}, u32[]{:S(2)}) %collective-permute-start.48) | collective-permute-done | bytes 262176 | tf_op jit(solution)/shard_map/ppermute | solution.py:20
  376.4 5.2 %collective-permute-start.49 = (f32[2,256,128]{2,1,0:T(8,128)S(1)}, f32[2,256,128]{2,1,0:T(8,128)S(1)}, u32[]{:S(2)}, u32[]{:S(2)}) collective-permute-start(f32[2,256,128]{2,1,0:T(8,128)S(1)} %add.250), channel_id=1, source_target_pairs={{0,4},{1,5},{2,6},{3,7},{4,0},{5,1},{6,2},{7,3},{8,12},{9,13},{10,... | collective-permute-start | bytes 786440 | tf_op jit(solution)/shard_map/ppermute | solution.py:20
  381.6 11.6 %collective-permute-done.49 = f32[2,256,128]{2,1,0:T(8,128)S(1)} collective-permute-done((f32[2,256,128]{2,1,0:T(8,128)S(1)}, f32[2,256,128]{2,1,0:T(8,128)S(1)}, u32[]{:S(2)}, u32[]{:S(2)}) %collective-permute-start.49) | collective-permute-done | bytes 262176 | tf_op jit(solution)/shard_map/ppermute | solution.py:20
  398.1 13.5 %collective-permute-done.50 = f32[2,256,128]{2,1,0:T(8,128)S(1)} collective-permute-done((f32[2,256,128]{2,1,0:T(8,128)S(1)}, f32[2,256,128]{2,1,0:T(8,128)S(1)}, u32[]{:S(2)}, u32[]{:S(2)}) %collective-permute-start.50) | collective-permute-done | bytes 262176 | tf_op jit(solution)/shard_map/ppermute | solution.py:20
  413.9 5.4 %collective-permute-done.51 = f32[2,128,128]{2,1,0:T(8,128)S(1)} collective-permute-done((f32[2,128,128]{2,1,0:T(8,128)S(1)}, f32[2,128,128]{2,1,0:T(8,128)S(1)}, u32[]{:S(2)}, u32[]{:S(2)}) %collective-permute-start.51) | collective-permute-done | bytes 131104 | tf_op jit(solution)/shard_map/ppermute | solution.py:20
  422.0 7.4 %collective-permute-done.52 = f32[2,128,128]{2,1,0:T(8,128)S(1)} collective-permute-done((f32[2,128,128]{2,1,0:T(8,128)S(1)}, f32[2,128,128]{2,1,0:T(8,128)S(1)}, u32[]{:S(2)}, u32[]{:S(2)}) %collective-permute-start.52) | collective-permute-done | bytes 131104 | tf_op jit(solution)/shard_map/ppermute | solution.py:20
  434.2 8.7 %collective-permute-done.53 = f32[2,128,128]{2,1,0:T(8,128)S(1)} collective-permute-done((f32[2,128,128]{2,1,0:T(8,128)S(1)}, f32[2,128,128]{2,1,0:T(8,128)S(1)}, u32[]{:S(2)}, u32[]{:S(2)}) %collective-permute-start.53) | collective-permute-done | bytes 131104 | tf_op jit(solution)/shard_map/ppermute | solution.py:20
  (159 shorter events, 201.2 us)
Async XLA Ops:
  6.7 67.0 %collective-permute-start = (bf16[8,2,128,128]{3,2,1,0:T(8,128)(2,1)}, bf16[8,2,128,128]{3,2,1,0:T(8,128)(2,1)S(1)}, u32[]{:S(2)}, u32[]{:S(2)}) collective-permute-start(bf16[8,2,128,128]{3,2,1,0:T(8,128)(2,1)} %fusion.21), channel_id=1, source_target_pairs={{0,1},{1,0},{2,3},{3,2},{4,5},{5,4},{6,7},{7,6},{8,9},{9,8},{10,11... | collective-permute-start | bytes 1572872 | tf_op jit(solution)/shard_map/ppermute | solution.py:20
  11.7 13.6 %collective-permute-start.4 = (f32[2,256]{1,0:T(2,128)S(1)}, f32[2,256]{1,0:T(2,128)S(1)}, u32[]{:S(2)}, u32[]{:S(2)}) collective-permute-start(f32[2,256]{1,0:T(2,128)S(1)} %get-tuple-element.5), channel_id=1, source_target_pairs={{0,1},{1,0},{2,3},{3,2},{4,5},{5,4},{6,7},{7,6},{8,9},{9,8},{10,11... | collective-permute-start | bytes 6152 | tf_op jit(solution)/shard_map/ppermute | solution.py:20
  14.2 17.5 %collective-permute-start.12 = (f32[2,256]{1,0:T(2,128)S(1)}, f32[2,256]{1,0:T(2,128)S(1)}, u32[]{:S(2)}, u32[]{:S(2)}) collective-permute-start(f32[2,256]{1,0:T(2,128)S(1)} %get-tuple-element.4), channel_id=1, source_target_pairs={{0,1},{1,0},{2,3},{3,2},{4,5},{5,4},{6,7},{7,6},{8,9},{9,8},{10,11... | collective-permute-start | bytes 6152 | tf_op jit(solution)/shard_map/ppermute | solution.py:20
  17.4 12.3 %collective-permute-start.20 = (f32[2,256]{1,0:T(2,128)S(1)}, f32[2,256]{1,0:T(2,128)S(1)}, u32[]{:S(2)}, u32[]{:S(2)}) collective-permute-start(f32[2,256]{1,0:T(2,128)S(1)} %get-tuple-element.2), channel_id=1, source_target_pairs={{0,1},{1,0},{2,3},{3,2},{4,5},{5,4},{6,7},{7,6},{8,9},{9,8},{10,11... | collective-permute-start | bytes 6152 | tf_op jit(solution)/shard_map/ppermute | solution.py:20
  23.0 48.6 %collective-permute-start.13 = (f32[2,256,128]{2,1,0:T(8,128)S(1)}, f32[2,256,128]{2,1,0:T(8,128)S(1)}, u32[]{:S(2)}, u32[]{:S(2)}) collective-permute-start(f32[2,256,128]{2,1,0:T(8,128)S(1)} %fusion.11), channel_id=1, source_target_pairs={{0,1},{1,0},{2,3},{3,2},{4,5},{5,4},{6,7},{7,6},{8,9},{9,8},{10,11... | collective-permute-start | bytes 786440 | tf_op jit(solution)/shard_map/ppermute | solution.py:20
  25.4 10.2 %collective-permute-start.9 = (f32[2,256]{1,0:T(2,128)S(1)}, f32[2,256]{1,0:T(2,128)S(1)}, u32[]{:S(2)}, u32[]{:S(2)}) collective-permute-start(f32[2,256]{1,0:T(2,128)S(1)} %get-tuple-element.29), channel_id=1, source_target_pairs={{0,2},{1,3},{2,0},{3,1},{4,6},{5,7},{6,4},{7,5},{8,10},{9,11},{10,... | collective-permute-start | bytes 6152 | tf_op jit(solution)/shard_map/ppermute | solution.py:20
  31.7 12.0 %collective-permute-start.21 = (f32[2,256]{1,0:T(2,128)S(1)}, f32[2,256]{1,0:T(2,128)S(1)}, u32[]{:S(2)}, u32[]{:S(2)}) collective-permute-start(f32[2,256]{1,0:T(2,128)S(1)} %get-tuple-element.19), channel_id=1, source_target_pairs={{0,2},{1,3},{2,0},{3,1},{4,6},{5,7},{6,4},{7,5},{8,10},{9,11},{10,... | collective-permute-start | bytes 6152 | tf_op jit(solution)/shard_map/ppermute | solution.py:20
  37.6 12.9 %collective-permute-start.10 = (f32[2,256]{1,0:T(2,128)S(1)}, f32[2,256]{1,0:T(2,128)S(1)}, u32[]{:S(2)}, u32[]{:S(2)}) collective-permute-start(f32[2,256]{1,0:T(2,128)S(1)} %get-tuple-element.27), channel_id=1, source_target_pairs={{0,4},{1,5},{2,6},{3,7},{4,0},{5,1},{6,2},{7,3},{8,12},{9,13},{10,... | collective-permute-start | bytes 6152 | tf_op jit(solution)/shard_map/ppermute | solution.py:20
  45.6 16.1 %collective-permute-start.22 = (f32[2,256]{1,0:T(2,128)S(1)}, f32[2,256]{1,0:T(2,128)S(1)}, u32[]{:S(2)}, u32[]{:S(2)}) collective-permute-start(f32[2,256]{1,0:T(2,128)S(1)} %get-tuple-element.15), channel_id=1, source_target_pairs={{0,4},{1,5},{2,6},{3,7},{4,0},{5,1},{6,2},{7,3},{8,12},{9,13},{10,... | collective-permute-start | bytes 6152 | tf_op jit(solution)/shard_map/ppermute | solution.py:20
  50.5 13.2 %collective-permute-start.16 = (f32[2,256]{1,0:T(2,128)S(1)}, f32[2,256]{1,0:T(2,128)S(1)}, u32[]{:S(2)}, u32[]{:S(2)}) collective-permute-start(f32[2,256]{1,0:T(2,128)S(1)} %get-tuple-element.18), channel_id=1, source_target_pairs={{0,4},{1,5},{2,6},{3,7},{4,0},{5,1},{6,2},{7,3},{8,12},{9,13},{10,... | collective-permute-start | bytes 6152 | tf_op jit(solution)/shard_map/ppermute | solution.py:20
  52.4 64.2 %collective-permute-start.11 = (f32[2,256]{1,0:T(2,128)S(1)}, f32[2,256]{1,0:T(2,128)S(1)}, u32[]{:S(2)}, u32[]{:S(2)}) collective-permute-start(f32[2,256]{1,0:T(2,128)S(1)} %get-tuple-element.25), channel_id=1, source_target_pairs={{0,8},{1,9},{2,10},{3,11},{4,12},{5,13},{6,14},{7,15},{8,0},{9,1},... | collective-permute-start | bytes 6152 | tf_op jit(solution)/shard_map/ppermute | solution.py:20
  61.7 54.9 %collective-permute-start.7 = (f32[2,256]{1,0:T(2,128)S(1)}, f32[2,256]{1,0:T(2,128)S(1)}, u32[]{:S(2)}, u32[]{:S(2)}) collective-permute-start(f32[2,256]{1,0:T(2,128)S(1)} %get-tuple-element.26), channel_id=1, source_target_pairs={{0,8},{1,9},{2,10},{3,11},{4,12},{5,13},{6,14},{7,15},{8,0},{9,1},... | collective-permute-start | bytes 6152 | tf_op jit(solution)/shard_map/ppermute | solution.py:20
  63.7 13.7 %collective-permute-start.23 = (f32[2,256]{1,0:T(2,128)S(1)}, f32[2,256]{1,0:T(2,128)S(1)}, u32[]{:S(2)}, u32[]{:S(2)}) collective-permute-start(f32[2,256]{1,0:T(2,128)S(1)} %get-tuple-element.11), channel_id=1, source_target_pairs={{0,8},{1,9},{2,10},{3,11},{4,12},{5,13},{6,14},{7,15},{8,0},{9,1},... | collective-permute-start | bytes 6152 | tf_op jit(solution)/shard_map/ppermute | solution.py:20
  73.7 13.2 %collective-permute-start.15 = (f32[2,256,128]{2,1,0:T(8,128)S(1)}, f32[2,256,128]{2,1,0:T(8,128)S(1)}, u32[]{:S(2)}, u32[]{:S(2)}) collective-permute-start(f32[2,256,128]{2,1,0:T(8,128)S(1)} %multiply_add_fusion.2), channel_id=1, source_target_pairs={{0,2},{1,3},{2,0},{3,1},{4,6},{5,7},{6,4},{7,5},{8,10},{9,11},{10,... | collective-permute-start | bytes 786440 | tf_op jit(solution)/shard_map/ppermute | solution.py:20
  77.4 12.4 %collective-permute-start.1 = (bf16[4,2,128,128]{3,2,1,0:T(8,128)(2,1)S(1)}, bf16[4,2,128,128]{3,2,1,0:T(8,128)(2,1)S(1)}, u32[]{:S(2)}, u32[]{:S(2)}) collective-permute-start(bf16[4,2,128,128]{3,2,1,0:T(8,128)(2,1)S(1)} %fusion.22), channel_id=1, source_target_pairs={{0,2},{1,3},{2,0},{3,1},{4,6},{5,7},{6,4},{7,5},{8,10},{9,11},{10,... | collective-permute-start | bytes 786440 | tf_op jit(solution)/shard_map/ppermute | solution.py:20
  87.1 19.5 %collective-permute-start.17 = (f32[2,256,128]{2,1,0:T(8,128)S(1)}, f32[2,256,128]{2,1,0:T(8,128)S(1)}, u32[]{:S(2)}, u32[]{:S(2)}) collective-permute-start(f32[2,256,128]{2,1,0:T(8,128)S(1)} %multiply_add_fusion.1), channel_id=1, source_target_pairs={{0,4},{1,5},{2,6},{3,7},{4,0},{5,1},{6,2},{7,3},{8,12},{9,13},{10,... | collective-permute-start | bytes 786440 | tf_op jit(solution)/shard_map/ppermute | solution.py:20
  89.9 23.5 %collective-permute-start.2 = (bf16[2,2,128,128]{3,2,1,0:T(8,128)(2,1)S(1)}, bf16[2,2,128,128]{3,2,1,0:T(8,128)(2,1)S(1)}, u32[]{:S(2)}, u32[]{:S(2)}) collective-permute-start(bf16[2,2,128,128]{3,2,1,0:T(8,128)(2,1)S(1)} %fusion.25), channel_id=1, source_target_pairs={{0,4},{1,5},{2,6},{3,7},{4,0},{5,1},{6,2},{7,3},{8,12},{9,13},{10,... | collective-permute-start | bytes 393224 | tf_op jit(solution)/shard_map/ppermute | solution.py:20
  106.8 17.0 %collective-permute-start.19 = (f32[2,256,128]{2,1,0:T(8,128)S(1)}, f32[2,256,128]{2,1,0:T(8,128)S(1)}, u32[]{:S(2)}, u32[]{:S(2)}) collective-permute-start(f32[2,256,128]{2,1,0:T(8,128)S(1)} %multiply_add_fusion), channel_id=1, source_target_pairs={{0,8},{1,9},{2,10},{3,11},{4,12},{5,13},{6,14},{7,15},{8,0},{9,1},... | collective-permute-start | bytes 786440 | tf_op jit(solution)/shard_map/ppermute | solution.py:20
  140.9 11.6 %collective-permute-start.26 = (f32[2,128,128]{2,1,0:T(8,128)S(1)}, f32[2,128,128]{2,1,0:T(8,128)S(1)}, u32[]{:S(2)}, u32[]{:S(2)}) collective-permute-start(f32[2,128,128]{2,1,0:T(8,128)S(1)} %add.216), channel_id=1, source_target_pairs={{0,64},{16,80},{32,96},{48,112},{64,0},{80,16},{96,32},{112,48},{1... | collective-permute-start | bytes 393224 | tf_op jit(solution)/shard_map/ppermute | solution.py:20
  171.7 11.1 %collective-permute-start.30 = (f32[2,256,128]{2,1,0:T(8,128)S(1)}, f32[2,256,128]{2,1,0:T(8,128)S(1)}, u32[]{:S(2)}, u32[]{:S(2)}) collective-permute-start(f32[2,256,128]{2,1,0:T(8,128)S(1)} %add.221), channel_id=1, source_target_pairs={{0,2},{1,3},{2,0},{3,1},{4,6},{5,7},{6,4},{7,5},{8,10},{9,11},{10,... | collective-permute-start | bytes 786440 | tf_op jit(solution)/shard_map/ppermute | solution.py:20
  182.8 17.0 %collective-permute-start.31 = (f32[2,256,128]{2,1,0:T(8,128)S(1)}, f32[2,256,128]{2,1,0:T(8,128)S(1)}, u32[]{:S(2)}, u32[]{:S(2)}) collective-permute-start(f32[2,256,128]{2,1,0:T(8,128)S(1)} %add.222), channel_id=1, source_target_pairs={{0,4},{1,5},{2,6},{3,7},{4,0},{5,1},{6,2},{7,3},{8,12},{9,13},{10,... | collective-permute-start | bytes 786440 | tf_op jit(solution)/shard_map/ppermute | solution.py:20
  199.8 18.8 %collective-permute-start.32 = (f32[2,256,128]{2,1,0:T(8,128)S(1)}, f32[2,256,128]{2,1,0:T(8,128)S(1)}, u32[]{:S(2)}, u32[]{:S(2)}) collective-permute-start(f32[2,256,128]{2,1,0:T(8,128)S(1)} %add.223), channel_id=1, source_target_pairs={{0,8},{1,9},{2,10},{3,11},{4,12},{5,13},{6,14},{7,15},{8,0},{9,1},... | collective-permute-start | bytes 786440 | tf_op jit(solution)/shard_map/ppermute | solution.py:20
  234.5 14.5 %collective-permute-start.35 = (f32[2,128,128]{2,1,0:T(8,128)S(1)}, f32[2,128,128]{2,1,0:T(8,128)S(1)}, u32[]{:S(2)}, u32[]{:S(2)}) collective-permute-start(f32[2,128,128]{2,1,0:T(8,128)S(1)} %add.227), channel_id=1, source_target_pairs={{0,64},{16,80},{32,96},{48,112},{64,0},{80,16},{96,32},{112,48},{1... | collective-permute-start | bytes 393224 | tf_op jit(solution)/shard_map/ppermute | solution.py:20
  269.1 10.2 %collective-permute-start.39 = (f32[2,256,128]{2,1,0:T(8,128)S(1)}, f32[2,256,128]{2,1,0:T(8,128)S(1)}, u32[]{:S(2)}, u32[]{:S(2)}) collective-permute-start(f32[2,256,128]{2,1,0:T(8,128)S(1)} %add.235), channel_id=1, source_target_pairs={{0,2},{1,3},{2,0},{3,1},{4,6},{5,7},{6,4},{7,5},{8,10},{9,11},{10,... | collective-permute-start | bytes 786440 | tf_op jit(solution)/shard_map/ppermute | solution.py:20
  279.4 16.4 %collective-permute-start.40 = (f32[2,256,128]{2,1,0:T(8,128)S(1)}, f32[2,256,128]{2,1,0:T(8,128)S(1)}, u32[]{:S(2)}, u32[]{:S(2)}) collective-permute-start(f32[2,256,128]{2,1,0:T(8,128)S(1)} %add.236), channel_id=1, source_target_pairs={{0,4},{1,5},{2,6},{3,7},{4,0},{5,1},{6,2},{7,3},{8,12},{9,13},{10,... | collective-permute-start | bytes 786440 | tf_op jit(solution)/shard_map/ppermute | solution.py:20
  295.8 18.5 %collective-permute-start.41 = (f32[2,256,128]{2,1,0:T(8,128)S(1)}, f32[2,256,128]{2,1,0:T(8,128)S(1)}, u32[]{:S(2)}, u32[]{:S(2)}) collective-permute-start(f32[2,256,128]{2,1,0:T(8,128)S(1)} %add.237), channel_id=1, source_target_pairs={{0,8},{1,9},{2,10},{3,11},{4,12},{5,13},{6,14},{7,15},{8,0},{9,1},... | collective-permute-start | bytes 786440 | tf_op jit(solution)/shard_map/ppermute | solution.py:20
  322.0 10.2 %collective-permute-start.43 = (f32[2,128,128]{2,1,0:T(8,128)S(1)}, f32[2,128,128]{2,1,0:T(8,128)S(1)}, u32[]{:S(2)}, u32[]{:S(2)}) collective-permute-start(f32[2,128,128]{2,1,0:T(8,128)S(1)} %add.240), channel_id=1, source_target_pairs={{0,32},{16,48},{32,0},{48,16},{64,96},{80,112},{96,64},{112,80},{1... | collective-permute-start | bytes 393224 | tf_op jit(solution)/shard_map/ppermute | solution.py:20
  332.1 13.6 %collective-permute-start.44 = (f32[2,128,128]{2,1,0:T(8,128)S(1)}, f32[2,128,128]{2,1,0:T(8,128)S(1)}, u32[]{:S(2)}, u32[]{:S(2)}) collective-permute-start(f32[2,128,128]{2,1,0:T(8,128)S(1)} %add.241), channel_id=1, source_target_pairs={{0,64},{16,80},{32,96},{48,112},{64,0},{80,16},{96,32},{112,48},{1... | collective-permute-start | bytes 393224 | tf_op jit(solution)/shard_map/ppermute | solution.py:20
  366.1 10.2 %collective-permute-start.48 = (f32[2,256,128]{2,1,0:T(8,128)S(1)}, f32[2,256,128]{2,1,0:T(8,128)S(1)}, u32[]{:S(2)}, u32[]{:S(2)}) collective-permute-start(f32[2,256,128]{2,1,0:T(8,128)S(1)} %add.249), channel_id=1, source_target_pairs={{0,2},{1,3},{2,0},{3,1},{4,6},{5,7},{6,4},{7,5},{8,10},{9,11},{10,... | collective-permute-start | bytes 786440 | tf_op jit(solution)/shard_map/ppermute | solution.py:20
  376.4 16.8 %collective-permute-start.49 = (f32[2,256,128]{2,1,0:T(8,128)S(1)}, f32[2,256,128]{2,1,0:T(8,128)S(1)}, u32[]{:S(2)}, u32[]{:S(2)}) collective-permute-start(f32[2,256,128]{2,1,0:T(8,128)S(1)} %add.250), channel_id=1, source_target_pairs={{0,4},{1,5},{2,6},{3,7},{4,0},{5,1},{6,2},{7,3},{8,12},{9,13},{10,... | collective-permute-start | bytes 786440 | tf_op jit(solution)/shard_map/ppermute | solution.py:20
  393.2 18.4 %collective-permute-start.50 = (f32[2,256,128]{2,1,0:T(8,128)S(1)}, f32[2,256,128]{2,1,0:T(8,128)S(1)}, u32[]{:S(2)}, u32[]{:S(2)}) collective-permute-start(f32[2,256,128]{2,1,0:T(8,128)S(1)} %add.251), channel_id=1, source_target_pairs={{0,8},{1,9},{2,10},{3,11},{4,12},{5,13},{6,14},{7,15},{8,0},{9,1},... | collective-permute-start | bytes 786440 | tf_op jit(solution)/shard_map/ppermute | solution.py:20
  429.5 13.4 %collective-permute-start.53 = (f32[2,128,128]{2,1,0:T(8,128)S(1)}, f32[2,128,128]{2,1,0:T(8,128)S(1)}, u32[]{:S(2)}, u32[]{:S(2)}) collective-permute-start(f32[2,128,128]{2,1,0:T(8,128)S(1)} %add.255), channel_id=1, source_target_pairs={{0,64},{16,80},{32,96},{48,112},{64,0},{80,16},{96,32},{112,48},{1... | collective-permute-start | bytes 393224 | tf_op jit(solution)/shard_map/ppermute | solution.py:20
  (29 other events, 245.4 us)

commit v2 on v1

--- a/solution.py
+++ b/solution.py
@@ -14,41 +14,53 @@
 BF16 = jnp.bfloat16
 
 
-def exchange(tree, axis, bit):
-    size = lax.axis_size(axis)
-    pairs = [(s, s ^ bit) for s in range(size)]
-    return jax.tree.map(lambda a: lax.ppermute(a, axis, pairs), tree)
+def digit_groups(size):
+    groups = []
+    bit = 1
+    while bit < size:
+        radix = 4 if bit * 4 <= size else 2
+        groups.append((bit, radix))
+        bit *= radix
+    return groups
 
 
-def butterfly_sum(value, axis):
-    bit = 1
-    while bit < lax.axis_size(axis):
-        value = value + exchange(value, axis, bit)
-        bit *= 2
+def gather_group(value, axis, stride, radix):
+    size = lax.axis_size(axis)
+    me = lax.axis_index(axis)
+    digit = (me // stride) % radix
+    got = [value]
+    for k in range(1, radix):
+        pairs = [(s, s ^ (k * stride)) for s in range(size)]
+        got.append(jax.tree.map(lambda a: lax.ppermute(a, axis, pairs), value))
+    stacked = jax.tree.map(lambda *a: jnp.stack(a), *got)
+    return [
+        jax.tree.map(lambda a: lax.dynamic_index_in_dim(a, digit ^ g, 0, False), stacked)
+        for g in range(radix)
+    ]
+
+
+def group_sum(value, axis):
+    for stride, radix in digit_groups(lax.axis_size(axis)):
+        members = gather_group(value, axis, stride, radix)
+        value = members[0]
+        for other in members[1:]:
+            value = value + other
     return value
 
 
-def butterfly(tree, axis, combine):
-    bit = 1
-    while bit < lax.axis_size(axis):
-        tree = combine(tree, exchange(tree, axis, bit))
-        bit *= 2
-    return tree
-
-
-def scatter_halving(blocks, axis):
+def scatter_groups(blocks, axis):
+    size = lax.axis_size(axis)
     me = lax.axis_index(axis)
-    bit = 1
-    level = 0
-    while bit < lax.axis_size(axis):
-        rest = blocks.shape[0] // 2
-        pair = blocks.reshape((rest, 2) + blocks.shape[1:])
-        mine = (me >> level) & 1
-        keep = jnp.where(mine == 0, pair[:, 0], pair[:, 1])
-        give = jnp.where(mine == 0, pair[:, 1], pair[:, 0])
-        blocks = keep + exchange(give, axis, bit)
-        bit *= 2
-        level += 1
+    for stride, radix in digit_groups(size):
+        digit = (me // stride) % radix
+        rest = blocks.shape[0] // radix
+        split = blocks.reshape((rest, radix) + blocks.shape[1:])
+        total = lax.dynamic_index_in_dim(split, digit, 1, False)
+        for k in range(1, radix):
+            pairs = [(s, s ^ (k * stride)) for s in range(size)]
+            give = lax.dynamic_index_in_dim(split, digit ^ k, 1, False)
+            total = total + lax.ppermute(give, axis, pairs)
+        blocks = total
     return blocks[0]
 
 
@@ -60,22 +72,32 @@
     )
 
 
-def combine_stats(first, second):
-    peak_a, denom_a, numer_a, cpeak_a, cdenom_a = first
-    peak_b, denom_b, numer_b, cpeak_b, cdenom_b = second
-    peak = jnp.maximum(peak_a, peak_b)
-    fa = jnp.exp(peak_a - peak)
-    fb = jnp.exp(peak_b - peak)
-    cpeak = jnp.maximum(cpeak_a, cpeak_b)
-    ga = jnp.exp(cpeak_a - cpeak)
-    gb = jnp.exp(cpeak_b - cpeak)
-    return (
-        peak,
-        denom_a * fa + denom_b * fb,
-        numer_a * fa[..., None] + numer_b * fb[..., None],
-        cpeak,
-        cdenom_a * ga + cdenom_b * gb,
-    )
+def combine_members(members, rows):
+    def unpack(a):
+        stats = a[:, rows:, :].reshape(a.shape[0], 4, rows)
+        return a[:, :rows, :], stats[:, 0], stats[:, 1], stats[:, 2], stats[:, 3]
+
+    parts = [unpack(a) for a in members]
+    peak = parts[0][1]
+    cpeak = parts[0][3]
+    for p in parts[1:]:
+        peak = jnp.maximum(peak, p[1])
+        cpeak = jnp.maximum(cpeak, p[3])
+    numer = denom = cdenom = None
+    for p in parts:
+        f = jnp.exp(p[1] - peak)
+        g = jnp.exp(p[3] - cpeak)
+        n_term = p[0] * f[..., None]
+        numer = n_term if numer is None else numer + n_term
+        denom = p[2] * f if denom is None else denom + p[2] * f
+        cdenom = p[4] * g if cdenom is None else cdenom + p[4] * g
+    return numer, peak, denom, cpeak, cdenom
+
+
+def pack(numer, peak, denom, cpeak, cdenom):
+    heads, rows, width = numer.shape
+    stats = jnp.stack([peak, denom, cpeak, cdenom], axis=1).reshape(heads, 4 * rows // width, width)
+    return jnp.concatenate([numer, stats], axis=1)
 
 
 def per_device(queries, cache_keys, cache_values, selected):
@@ -95,7 +117,7 @@
     ).astype(BF16)
     kept_mask = jnp.any(owned, axis=1)
     blocks = picked.reshape(head_count, col_devices, col_len, head_width).transpose(1, 0, 2, 3)
-    chosen_block = scatter_halving(blocks, "kv")
+    chosen_block = scatter_groups(blocks, "kv")
 
     scores = (
         jnp.einsum("hqd,hkd->hqk", queries, cache_keys, preferred_element_type=F32) * score_scale
@@ -114,9 +136,11 @@
     cweights = jnp.where(kept_mask[:, None, :], jnp.exp(kept_scores - cpeak[..., None]), 0.0)
     cdenom = jnp.sum(cweights, axis=-1)
 
-    peak, denom, numer, cpeak, cdenom = butterfly(
-        (peak, denom, numer, cpeak, cdenom), "kv", combine_stats
-    )
+    packed = pack(numer, peak, denom, cpeak, cdenom)
+    for stride, radix in digit_groups(col_devices):
+        members = gather_group(packed, "kv", stride, radix)
+        numer, peak, denom, cpeak, cdenom = combine_members(members, query_rows)
+        packed = pack(numer, peak, denom, cpeak, cdenom)
     attended = (numer / denom[..., None]).astype(BF16)
 
     compact = (
@@ -127,11 +151,11 @@
 
     weighting = order_size / (query_rows * row_devices)
     rhs_part = jnp.einsum("hqa,hqd->had", probs, attended, preferred_element_type=F32)
-    rhs = butterfly_sum(rhs_part, "pb") * weighting
+    rhs = group_sum(rhs_part, "pb") * weighting
 
     def gram_times(vec):
-        across = butterfly_sum(split_dot("hqa,had->hqd", probs, vec), "kv")
-        back = butterfly_sum(split_dot("hqa,hqd->had", probs, across), "pb")
+        across = group_sum(split_dot("hqa,had->hqd", probs, vec), "kv")
+        back = group_sum(split_dot("hqa,hqd->had", probs, across), "pb")
         return back * weighting + ridge_weight * vec
 
     sigma = theta_mid / delta_half

time: 461 us -> 431 us (0.935)
  waiting for transfers between devices: 239 us -> 178 us
  starting transfers between devices: 201 us -> 223 us
    ppermute x56 -> x58, waiting for transfers between devices: 239 us -> 178 us  [the longest x52 176 us: gather_group(): got.append(jax.tree.map(lambda a: lax.ppermute(a, axis, pairs), value))]
    ppermute x56 -> x58, starting transfers between devices: 201 us -> 223 us  [the longest x52 200 us: gather_group(): got.append(jax.tree.map(lambda a: lax.ppermute(a, axis, pairs), value))]
  transfers between devices with their start and end apart: 56 -> 58, of which waited for: 37 -> 29; matrix products, arithmetic and copies ran while one was open for 2% -> 2% of each run, Pallas kernels for 0% -> 0%
where the time goes in v2:
time: 431 us; the launch traced here: 426 us
  starting transfers between devices  223 us (52%)
  waiting for transfers between devices  178 us (41%)
  other arithmetic  10.4 us (2%)
  matrix products  9.49 us (2%)
    ppermute x52, starting transfers between devices, gather_group(): got.append(jax.tree.map(lambda a: lax.ppermute(a, axis, pairs), value))  200 us
    ppermute x52, waiting for transfers between devices, gather_group(): got.append(jax.tree.map(lambda a: lax.ppermute(a, axis, pairs), value))  176 us
    ppermute x6, starting transfers between devices, scatter_groups(): total = total + lax.ppermute(give, axis, pairs)  23 us
  transfers between devices with their start and end apart: 58, of which 29 were waited for; matrix products, arithmetic and copies ran while one was open for 2% of the time, Pallas kernels for 0%

profile of v2, /device:TPU:6, one launch (start us, length us, event | category | flops | bytes accessed | tf_op | source)
XLA Modules:
  0.0 425.7 jit_solution(13287747320571568131)
XLA Ops:
  31.5 6.1 %collective-permute-start.9 = (f32[2,264,128]{2,1,0:T(8,128)S(1)}, f32[2,264,128]{2,1,0:T(8,128)S(1)}, u32[]{:S(2)}, u32[]{:S(2)}) collective-permute-start(f32[2,264,128]{2,1,0:T(8,128)S(1)} %get-tuple-element.30), channel_id=1, source_target_pairs={{0,4},{1,5},{2,6},{3,7},{4,0},{5,1},{6,2},{7,3},{8,12},{9,13},{10,... | collective-permute-start | bytes 811016 | tf_op jit(solution)/shard_map/ppermute | solution.py:34
  37.6 8.3 %collective-permute-start.10 = (f32[2,264,128]{2,1,0:T(8,128)S(1)}, f32[2,264,128]{2,1,0:T(8,128)S(1)}, u32[]{:S(2)}, u32[]{:S(2)}) collective-permute-start(f32[2,264,128]{2,1,0:T(8,128)S(1)} %get-tuple-element.30), channel_id=1, source_target_pairs={{0,8},{1,9},{2,10},{3,11},{4,12},{5,13},{6,14},{7,15},{8,0},{9,1},... | collective-permute-start | bytes 811016 | tf_op jit(solution)/shard_map/ppermute | solution.py:34
  50.5 7.8 %collective-permute-start.4 = (bf16[1,2,128,128]{3,2,1,0:T(8,128)(2,1)S(1)}, bf16[1,2,128,128]{3,2,1,0:T(8,128)(2,1)S(1)}, u32[]{:S(2)}, u32[]{:S(2)}) collective-permute-start(bf16[1,2,128,128]{3,2,1,0:T(8,128)(2,1)S(1)} %get-tuple-element.35), channel_id=1, source_target_pairs={{0,8},{1,9},{2,10},{3,11},{4,12},{5,13},{6,14},{7,15},{8,0},{9,1},... | collective-permute-start | bytes 196616 | tf_op jit(solution)/shard_map/ppermute | solution.py:62
  58.3 7.1 %collective-permute-done.9 = f32[2,264,128]{2,1,0:T(8,128)S(1)} collective-permute-done((f32[2,264,128]{2,1,0:T(8,128)S(1)}, f32[2,264,128]{2,1,0:T(8,128)S(1)}, u32[]{:S(2)}, u32[]{:S(2)}) %collective-permute-start.9) | collective-permute-done | bytes 270368 | tf_op jit(solution)/shard_map/ppermute | solution.py:34
  65.4 4.9 %collective-permute-start.5 = (bf16[1,2,128,128]{3,2,1,0:T(8,128)(2,1)S(1)}, bf16[1,2,128,128]{3,2,1,0:T(8,128)(2,1)S(1)}, u32[]{:S(2)}, u32[]{:S(2)}) collective-permute-start(bf16[1,2,128,128]{3,2,1,0:T(8,128)(2,1)S(1)} %get-tuple-element.34), channel_id=1, source_target_pairs={{0,12},{1,13},{2,14},{3,15},{4,8},{5,9},{6,10},{7,11},{8,4},{9,5},... | collective-permute-start | bytes 196616 | tf_op jit(solution)/shard_map/ppermute | solution.py:62
  87.3 7.2 %collective-permute-done.13 = f32[2,128,128]{2,1,0:T(8,128)S(1)} collective-permute-done((f32[2,128,128]{2,1,0:T(8,128)S(1)}, f32[2,128,128]{2,1,0:T(8,128)S(1)}, u32[]{:S(2)}, u32[]{:S(2)}) %collective-permute-start.13) | collective-permute-done | bytes 131104 | tf_op jit(solution)/shard_map/ppermute | solution.py:34
  94.6 6.9 %collective-permute-start.15 = (f32[2,128,128]{2,1,0:T(8,128)S(1)}, f32[2,128,128]{2,1,0:T(8,128)S(1)}, u32[]{:S(2)}, u32[]{:S(2)}) collective-permute-start(f32[2,128,128]{2,1,0:T(8,128)S(1)} %fusion.169), channel_id=1, source_target_pairs={{0,64},{16,80},{32,96},{48,112},{64,0},{80,16},{96,32},{112,48},{1... | collective-permute-start | bytes 393224 | tf_op jit(solution)/shard_map/ppermute | solution.py:34
  108.3 8.2 %collective-permute-done.17 = f32[2,128,128]{2,1,0:T(8,128)S(1)} collective-permute-done((f32[2,128,128]{2,1,0:T(8,128)S(1)}, f32[2,128,128]{2,1,0:T(8,128)S(1)}, u32[]{:S(2)}, u32[]{:S(2)}) %collective-permute-start.17) | collective-permute-done | bytes 131104 | tf_op jit(solution)/shard_map/ppermute | solution.py:34
  119.6 5.3 %collective-permute-done.18 = f32[2,128,128]{2,1,0:T(8,128)S(1)} collective-permute-done((f32[2,128,128]{2,1,0:T(8,128)S(1)}, f32[2,128,128]{2,1,0:T(8,128)S(1)}, u32[]{:S(2)}, u32[]{:S(2)}) %collective-permute-start.18) | collective-permute-done | bytes 131104 | tf_op jit(solution)/shard_map/ppermute | solution.py:34
  127.4 5.8 %collective-permute-start.20 = (f32[2,256,128]{2,1,0:T(8,128)S(1)}, f32[2,256,128]{2,1,0:T(8,128)S(1)}, u32[]{:S(2)}, u32[]{:S(2)}) collective-permute-start(f32[2,256,128]{2,1,0:T(8,128)S(1)} %convolution_add_fusion.2), channel_id=1, source_target_pairs={{0,2},{1,3},{2,0},{3,1},{4,6},{5,7},{6,4},{7,5},{8,10},{9,11},{10,... | collective-permute-start | bytes 786440 | tf_op jit(solution)/shard_map/ppermute | solution.py:34
  135.3 5.1 %collective-permute-done.20 = f32[2,256,128]{2,1,0:T(8,128)S(1)} collective-permute-done((f32[2,256,128]{2,1,0:T(8,128)S(1)}, f32[2,256,128]{2,1,0:T(8,128)S(1)}, u32[]{:S(2)}, u32[]{:S(2)}) %collective-permute-start.20) | collective-permute-done | bytes 262176 | tf_op jit(solution)/shard_map/ppermute | solution.py:34
  140.4 5.2 %collective-permute-done.21 = f32[2,256,128]{2,1,0:T(8,128)S(1)} collective-permute-done((f32[2,256,128]{2,1,0:T(8,128)S(1)}, f32[2,256,128]{2,1,0:T(8,128)S(1)}, u32[]{:S(2)}, u32[]{:S(2)}) %collective-permute-start.21) | collective-permute-done | bytes 262176 | tf_op jit(solution)/shard_map/ppermute | solution.py:34
  158.0 15.7 %collective-permute-done.22 = f32[2,256,128]{2,1,0:T(8,128)S(1)} collective-permute-done((f32[2,256,128]{2,1,0:T(8,128)S(1)}, f32[2,256,128]{2,1,0:T(8,128)S(1)}, u32[]{:S(2)}, u32[]{:S(2)}) %collective-permute-start.22) | collective-permute-done | bytes 262176 | tf_op jit(solution)/shard_map/ppermute | solution.py:34
  178.4 5.4 %collective-permute-start.25 = (f32[2,128,128]{2,1,0:T(8,128)S(1)}, f32[2,128,128]{2,1,0:T(8,128)S(1)}, u32[]{:S(2)}, u32[]{:S(2)}) collective-permute-start(f32[2,128,128]{2,1,0:T(8,128)S(1)} %convolution_add_fusion.5), channel_id=1, source_target_pairs={{0,16},{16,0},{32,48},{48,32},{64,80},{80,64},{96,112},{112,96},{1... | collective-permute-start | bytes 393224 | tf_op jit(solution)/shard_map/ppermute | solution.py:34
  190.0 6.9 %collective-permute-done.26 = f32[2,128,128]{2,1,0:T(8,128)S(1)} collective-permute-done((f32[2,128,128]{2,1,0:T(8,128)S(1)}, f32[2,128,128]{2,1,0:T(8,128)S(1)}, u32[]{:S(2)}, u32[]{:S(2)}) %collective-permute-start.26) | collective-permute-done | bytes 131104 | tf_op jit(solution)/shard_map/ppermute | solution.py:34
  203.2 6.9 %collective-permute-start.30 = (f32[2,128,128]{2,1,0:T(8,128)S(1)}, f32[2,128,128]{2,1,0:T(8,128)S(1)}, u32[]{:S(2)}, u32[]{:S(2)}) collective-permute-start(f32[2,128,128]{2,1,0:T(8,128)S(1)} %fusion.165), channel_id=1, source_target_pairs={{0,192},{16,208},{32,224},{48,240},{64,128},{80,144},{96,160},{112... | collective-permute-start | bytes 393224 | tf_op jit(solution)/shard_map/ppermute | solution.py:34
  218.3 5.1 %collective-permute-done.31 = f32[2,128,128]{2,1,0:T(8,128)S(1)} collective-permute-done((f32[2,128,128]{2,1,0:T(8,128)S(1)}, f32[2,128,128]{2,1,0:T(8,128)S(1)}, u32[]{:S(2)}, u32[]{:S(2)}) %collective-permute-start.31) | collective-permute-done | bytes 131104 | tf_op jit(solution)/shard_map/ppermute | solution.py:34
  232.7 5.1 %collective-permute-done.33 = f32[2,256,128]{2,1,0:T(8,128)S(1)} collective-permute-done((f32[2,256,128]{2,1,0:T(8,128)S(1)}, f32[2,256,128]{2,1,0:T(8,128)S(1)}, u32[]{:S(2)}, u32[]{:S(2)}) %collective-permute-start.33) | collective-permute-done | bytes 262176 | tf_op jit(solution)/shard_map/ppermute | solution.py:34
  237.8 5.2 %collective-permute-done.34 = f32[2,256,128]{2,1,0:T(8,128)S(1)} collective-permute-done((f32[2,256,128]{2,1,0:T(8,128)S(1)}, f32[2,256,128]{2,1,0:T(8,128)S(1)}, u32[]{:S(2)}, u32[]{:S(2)}) %collective-permute-start.34) | collective-permute-done | bytes 262176 | tf_op jit(solution)/shard_map/ppermute | solution.py:34
  255.5 15.7 %collective-permute-done.35 = f32[2,256,128]{2,1,0:T(8,128)S(1)} collective-permute-done((f32[2,256,128]{2,1,0:T(8,128)S(1)}, f32[2,256,128]{2,1,0:T(8,128)S(1)}, u32[]{:S(2)}, u32[]{:S(2)}) %collective-permute-start.35) | collective-permute-done | bytes 262176 | tf_op jit(solution)/shard_map/ppermute | solution.py:34
  275.9 6.7 %collective-permute-start.38 = (f32[2,128,128]{2,1,0:T(8,128)S(1)}, f32[2,128,128]{2,1,0:T(8,128)S(1)}, u32[]{:S(2)}, u32[]{:S(2)}) collective-permute-start(f32[2,128,128]{2,1,0:T(8,128)S(1)} %convolution_add_fusion.4), channel_id=1, source_target_pairs={{0,16},{16,0},{32,48},{48,32},{64,80},{80,64},{96,112},{112,96},{1... | collective-permute-start | bytes 393224 | tf_op jit(solution)/shard_map/ppermute | solution.py:34
  288.7 7.2 %collective-permute-done.39 = f32[2,128,128]{2,1,0:T(8,128)S(1)} collective-permute-done((f32[2,128,128]{2,1,0:T(8,128)S(1)}, f32[2,128,128]{2,1,0:T(8,128)S(1)}, u32[]{:S(2)}, u32[]{:S(2)}) %collective-permute-start.39) | collective-permute-done | bytes 131104 | tf_op jit(solution)/shard_map/ppermute | solution.py:34
  296.1 6.8 %collective-permute-start.41 = (f32[2,128,128]{2,1,0:T(8,128)S(1)}, f32[2,128,128]{2,1,0:T(8,128)S(1)}, u32[]{:S(2)}, u32[]{:S(2)}) collective-permute-start(f32[2,128,128]{2,1,0:T(8,128)S(1)} %fusion.161), channel_id=1, source_target_pairs={{0,64},{16,80},{32,96},{48,112},{64,0},{80,16},{96,32},{112,48},{1... | collective-permute-start | bytes 393224 | tf_op jit(solution)/shard_map/ppermute | solution.py:34
  309.8 7.9 %collective-permute-done.43 = f32[2,128,128]{2,1,0:T(8,128)S(1)} collective-permute-done((f32[2,128,128]{2,1,0:T(8,128)S(1)}, f32[2,128,128]{2,1,0:T(8,128)S(1)}, u32[]{:S(2)}, u32[]{:S(2)}) %collective-permute-start.43) | collective-permute-done | bytes 131104 | tf_op jit(solution)/shard_map/ppermute | solution.py:34
  320.7 5.4 %collective-permute-done.44 = f32[2,128,128]{2,1,0:T(8,128)S(1)} collective-permute-done((f32[2,128,128]{2,1,0:T(8,128)S(1)}, f32[2,128,128]{2,1,0:T(8,128)S(1)}, u32[]{:S(2)}, u32[]{:S(2)}) %collective-permute-start.44) | collective-permute-done | bytes 131104 | tf_op jit(solution)/shard_map/ppermute | solution.py:34
  329.3 5.4 %collective-permute-start.46 = (f32[2,256,128]{2,1,0:T(8,128)S(1)}, f32[2,256,128]{2,1,0:T(8,128)S(1)}, u32[]{:S(2)}, u32[]{:S(2)}) collective-permute-start(f32[2,256,128]{2,1,0:T(8,128)S(1)} %convolution_add_fusion), channel_id=1, source_target_pairs={{0,2},{1,3},{2,0},{3,1},{4,6},{5,7},{6,4},{7,5},{8,10},{9,11},{10,... | collective-permute-start | bytes 786440 | tf_op jit(solution)/shard_map/ppermute | solution.py:34
  336.7 5.1 %collective-permute-done.46 = f32[2,256,128]{2,1,0:T(8,128)S(1)} collective-permute-done((f32[2,256,128]{2,1,0:T(8,128)S(1)}, f32[2,256,128]{2,1,0:T(8,128)S(1)}, u32[]{:S(2)}, u32[]{:S(2)}) %collective-permute-start.46) | collective-permute-done | bytes 262176 | tf_op jit(solution)/shard_map/ppermute | solution.py:34
  341.8 5.2 %collective-permute-done.47 = f32[2,256,128]{2,1,0:T(8,128)S(1)} collective-permute-done((f32[2,256,128]{2,1,0:T(8,128)S(1)}, f32[2,256,128]{2,1,0:T(8,128)S(1)}, u32[]{:S(2)}, u32[]{:S(2)}) %collective-permute-start.47) | collective-permute-done | bytes 262176 | tf_op jit(solution)/shard_map/ppermute | solution.py:34
  359.5 15.7 %collective-permute-done.48 = f32[2,256,128]{2,1,0:T(8,128)S(1)} collective-permute-done((f32[2,256,128]{2,1,0:T(8,128)S(1)}, f32[2,256,128]{2,1,0:T(8,128)S(1)}, u32[]{:S(2)}, u32[]{:S(2)}) %collective-permute-start.48) | collective-permute-done | bytes 262176 | tf_op jit(solution)/shard_map/ppermute | solution.py:34
  379.8 5.6 %collective-permute-start.51 = (f32[2,128,128]{2,1,0:T(8,128)S(1)}, f32[2,128,128]{2,1,0:T(8,128)S(1)}, u32[]{:S(2)}, u32[]{:S(2)}) collective-permute-start(f32[2,128,128]{2,1,0:T(8,128)S(1)} %convolution_add_fusion.3), channel_id=1, source_target_pairs={{0,16},{16,0},{32,48},{48,32},{64,80},{80,64},{96,112},{112,96},{1... | collective-permute-start | bytes 393224 | tf_op jit(solution)/shard_map/ppermute | solution.py:34
  391.7 7.0 %collective-permute-done.52 = f32[2,128,128]{2,1,0:T(8,128)S(1)} collective-permute-done((f32[2,128,128]{2,1,0:T(8,128)S(1)}, f32[2,128,128]{2,1,0:T(8,128)S(1)}, u32[]{:S(2)}, u32[]{:S(2)}) %collective-permute-start.52) | collective-permute-done | bytes 131104 | tf_op jit(solution)/shard_map/ppermute | solution.py:34
  404.8 7.1 %collective-permute-start.56 = (f32[2,128,128]{2,1,0:T(8,128)S(1)}, f32[2,128,128]{2,1,0:T(8,128)S(1)}, u32[]{:S(2)}, u32[]{:S(2)}) collective-permute-start(f32[2,128,128]{2,1,0:T(8,128)S(1)} %fusion.157), channel_id=1, source_target_pairs={{0,192},{16,208},{32,224},{48,240},{64,128},{80,144},{96,160},{112... | collective-permute-start | bytes 393224 | tf_op jit(solution)/shard_map/ppermute | solution.py:34
  (197 shorter events, 194.6 us)
Async XLA Ops:
  8.9 18.9 %collective-permute-start.6 = (f32[2,264,128]{2,1,0:T(8,128)}, f32[2,264,128]{2,1,0:T(8,128)S(1)}, u32[]{:S(2)}, u32[]{:S(2)}) collective-permute-start(f32[2,264,128]{2,1,0:T(8,128)} %get-tuple-element.32), channel_id=1, source_target_pairs={{0,1},{1,0},{2,3},{3,2},{4,5},{5,4},{6,7},{7,6},{8,9},{9,8},{10,11... | collective-permute-start | bytes 811016 | tf_op jit(solution)/shard_map/ppermute | solution.py:34
  10.8 18.9 %collective-permute-start.7 = (f32[2,264,128]{2,1,0:T(8,128)}, f32[2,264,128]{2,1,0:T(8,128)S(1)}, u32[]{:S(2)}, u32[]{:S(2)}) collective-permute-start(f32[2,264,128]{2,1,0:T(8,128)} %get-tuple-element.32), channel_id=1, source_target_pairs={{0,2},{1,3},{2,0},{3,1},{4,6},{5,7},{6,4},{7,5},{8,10},{9,11},{10,... | collective-permute-start | bytes 811016 | tf_op jit(solution)/shard_map/ppermute | solution.py:34
  15.1 14.7 %collective-permute-start.8 = (f32[2,264,128]{2,1,0:T(8,128)}, f32[2,264,128]{2,1,0:T(8,128)}, u32[]{:S(2)}, u32[]{:S(2)}) collective-permute-start(f32[2,264,128]{2,1,0:T(8,128)} %get-tuple-element.32), channel_id=1, source_target_pairs={{0,3},{1,2},{2,1},{3,0},{4,7},{5,6},{6,5},{7,4},{8,11},{9,10},{10,... | collective-permute-start | bytes 811016 | tf_op jit(solution)/shard_map/ppermute | solution.py:34
  21.2 24.8 %collective-permute-start = (bf16[4,2,128,128]{3,2,1,0:T(8,128)(2,1)}, bf16[4,2,128,128]{3,2,1,0:T(8,128)(2,1)S(1)}, u32[]{:S(2)}, u32[]{:S(2)}) collective-permute-start(bf16[4,2,128,128]{3,2,1,0:T(8,128)(2,1)} %bitcast.380), channel_id=1, source_target_pairs={{0,1},{1,0},{2,3},{3,2},{4,5},{5,4},{6,7},{7,6},{8,9},{9,8},{10,11... | collective-permute-start | bytes 786440 | tf_op jit(solution)/shard_map/ppermute | solution.py:62
  23.2 24.6 %collective-permute-start.1 = (bf16[4,2,128,128]{3,2,1,0:T(8,128)(2,1)S(1)}, bf16[4,2,128,128]{3,2,1,0:T(8,128)(2,1)S(1)}, u32[]{:S(2)}, u32[]{:S(2)}) collective-permute-start(bf16[4,2,128,128]{3,2,1,0:T(8,128)(2,1)S(1)} %bitcast.393), channel_id=1, source_target_pairs={{0,2},{1,3},{2,0},{3,1},{4,6},{5,7},{6,4},{7,5},{8,10},{9,11},{10,... | collective-permute-start | bytes 786440 | tf_op jit(solution)/shard_map/ppermute | solution.py:62
  27.8 20.1 %collective-permute-start.2 = (bf16[4,2,128,128]{3,2,1,0:T(8,128)(2,1)}, bf16[4,2,128,128]{3,2,1,0:T(8,128)(2,1)S(1)}, u32[]{:S(2)}, u32[]{:S(2)}) collective-permute-start(bf16[4,2,128,128]{3,2,1,0:T(8,128)(2,1)} %bitcast.378), channel_id=1, source_target_pairs={{0,3},{1,2},{2,1},{3,0},{4,7},{5,6},{6,5},{7,4},{8,11},{9,10},{10,... | collective-permute-start | bytes 786440 | tf_op jit(solution)/shard_map/ppermute | solution.py:62
  31.5 33.8 %collective-permute-start.9 = (f32[2,264,128]{2,1,0:T(8,128)S(1)}, f32[2,264,128]{2,1,0:T(8,128)S(1)}, u32[]{:S(2)}, u32[]{:S(2)}) collective-permute-start(f32[2,264,128]{2,1,0:T(8,128)S(1)} %get-tuple-element.30), channel_id=1, source_target_pairs={{0,4},{1,5},{2,6},{3,7},{4,0},{5,1},{6,2},{7,3},{8,12},{9,13},{10,... | collective-permute-start | bytes 811016 | tf_op jit(solution)/shard_map/ppermute | solution.py:34
  37.6 32.7 %collective-permute-start.10 = (f32[2,264,128]{2,1,0:T(8,128)S(1)}, f32[2,264,128]{2,1,0:T(8,128)S(1)}, u32[]{:S(2)}, u32[]{:S(2)}) collective-permute-start(f32[2,264,128]{2,1,0:T(8,128)S(1)} %get-tuple-element.30), channel_id=1, source_target_pairs={{0,8},{1,9},{2,10},{3,11},{4,12},{5,13},{6,14},{7,15},{8,0},{9,1},... | collective-permute-start | bytes 811016 | tf_op jit(solution)/shard_map/ppermute | solution.py:34
  45.9 28.0 %collective-permute-start.11 = (f32[2,264,128]{2,1,0:T(8,128)S(1)}, f32[2,264,128]{2,1,0:T(8,128)S(1)}, u32[]{:S(2)}, u32[]{:S(2)}) collective-permute-start(f32[2,264,128]{2,1,0:T(8,128)S(1)} %get-tuple-element.30), channel_id=1, source_target_pairs={{0,12},{1,13},{2,14},{3,15},{4,8},{5,9},{6,10},{7,11},{8,4},{9,5},... | collective-permute-start | bytes 811016 | tf_op jit(solution)/shard_map/ppermute | solution.py:34
  48.0 26.3 %collective-permute-start.3 = (bf16[1,2,128,128]{3,2,1,0:T(8,128)(2,1)S(1)}, bf16[1,2,128,128]{3,2,1,0:T(8,128)(2,1)S(1)}, u32[]{:S(2)}, u32[]{:S(2)}) collective-permute-start(bf16[1,2,128,128]{3,2,1,0:T(8,128)(2,1)S(1)} %get-tuple-element.33), channel_id=1, source_target_pairs={{0,4},{1,5},{2,6},{3,7},{4,0},{5,1},{6,2},{7,3},{8,12},{9,13},{10,... | collective-permute-start | bytes 196616 | tf_op jit(solution)/shard_map/ppermute | solution.py:62
  50.5 23.9 %collective-permute-start.4 = (bf16[1,2,128,128]{3,2,1,0:T(8,128)(2,1)S(1)}, bf16[1,2,128,128]{3,2,1,0:T(8,128)(2,1)S(1)}, u32[]{:S(2)}, u32[]{:S(2)}) collective-permute-start(bf16[1,2,128,128]{3,2,1,0:T(8,128)(2,1)S(1)} %get-tuple-element.35), channel_id=1, source_target_pairs={{0,8},{1,9},{2,10},{3,11},{4,12},{5,13},{6,14},{7,15},{8,0},{9,1},... | collective-permute-start | bytes 196616 | tf_op jit(solution)/shard_map/ppermute | solution.py:62
  80.6 13.8 %collective-permute-start.13 = (f32[2,128,128]{2,1,0:T(8,128)S(1)}, f32[2,128,128]{2,1,0:T(8,128)S(1)}, u32[]{:S(2)}, u32[]{:S(2)}) collective-permute-start(f32[2,128,128]{2,1,0:T(8,128)S(1)} %fusion.64), channel_id=1, source_target_pairs={{0,32},{16,48},{32,0},{48,16},{64,96},{80,112},{96,64},{112,80},{1... | collective-permute-start | bytes 393224 | tf_op jit(solution)/shard_map/ppermute | solution.py:34
  94.6 13.2 %collective-permute-start.15 = (f32[2,128,128]{2,1,0:T(8,128)S(1)}, f32[2,128,128]{2,1,0:T(8,128)S(1)}, u32[]{:S(2)}, u32[]{:S(2)}) collective-permute-start(f32[2,128,128]{2,1,0:T(8,128)S(1)} %fusion.169), channel_id=1, source_target_pairs={{0,64},{16,80},{32,96},{48,112},{64,0},{80,16},{96,32},{112,48},{1... | collective-permute-start | bytes 393224 | tf_op jit(solution)/shard_map/ppermute | solution.py:34
  127.4 13.0 %collective-permute-start.20 = (f32[2,256,128]{2,1,0:T(8,128)S(1)}, f32[2,256,128]{2,1,0:T(8,128)S(1)}, u32[]{:S(2)}, u32[]{:S(2)}) collective-permute-start(f32[2,256,128]{2,1,0:T(8,128)S(1)} %convolution_add_fusion.2), channel_id=1, source_target_pairs={{0,2},{1,3},{2,0},{3,1},{4,6},{5,7},{6,4},{7,5},{8,10},{9,11},{10,... | collective-permute-start | bytes 786440 | tf_op jit(solution)/shard_map/ppermute | solution.py:34
  133.2 12.4 %collective-permute-start.21 = (f32[2,256,128]{2,1,0:T(8,128)S(1)}, f32[2,256,128]{2,1,0:T(8,128)S(1)}, u32[]{:S(2)}, u32[]{:S(2)}) collective-permute-start(f32[2,256,128]{2,1,0:T(8,128)S(1)} %convolution_add_fusion.2), channel_id=1, source_target_pairs={{0,3},{1,2},{2,1},{3,0},{4,7},{5,6},{6,5},{7,4},{8,11},{9,10},{10,... | collective-permute-start | bytes 786440 | tf_op jit(solution)/shard_map/ppermute | solution.py:34
  145.7 28.0 %collective-permute-start.22 = (f32[2,256,128]{2,1,0:T(8,128)S(1)}, f32[2,256,128]{2,1,0:T(8,128)S(1)}, u32[]{:S(2)}, u32[]{:S(2)}) collective-permute-start(f32[2,256,128]{2,1,0:T(8,128)S(1)} %fusion.167), channel_id=1, source_target_pairs={{0,4},{1,5},{2,6},{3,7},{4,0},{5,1},{6,2},{7,3},{8,12},{9,13},{10,... | collective-permute-start | bytes 786440 | tf_op jit(solution)/shard_map/ppermute | solution.py:34
  150.0 23.7 %collective-permute-start.23 = (f32[2,256,128]{2,1,0:T(8,128)S(1)}, f32[2,256,128]{2,1,0:T(8,128)S(1)}, u32[]{:S(2)}, u32[]{:S(2)}) collective-permute-start(f32[2,256,128]{2,1,0:T(8,128)S(1)} %fusion.167), channel_id=1, source_target_pairs={{0,8},{1,9},{2,10},{3,11},{4,12},{5,13},{6,14},{7,15},{8,0},{9,1},... | collective-permute-start | bytes 786440 | tf_op jit(solution)/shard_map/ppermute | solution.py:34
  154.2 23.6 %collective-permute-start.24 = (f32[2,256,128]{2,1,0:T(8,128)S(1)}, f32[2,256,128]{2,1,0:T(8,128)S(1)}, u32[]{:S(2)}, u32[]{:S(2)}) collective-permute-start(f32[2,256,128]{2,1,0:T(8,128)S(1)} %fusion.167), channel_id=1, source_target_pairs={{0,12},{1,13},{2,14},{3,15},{4,8},{5,9},{6,10},{7,11},{8,4},{9,5},... | collective-permute-start | bytes 786440 | tf_op jit(solution)/shard_map/ppermute | solution.py:34
  183.8 13.1 %collective-permute-start.26 = (f32[2,128,128]{2,1,0:T(8,128)S(1)}, f32[2,128,128]{2,1,0:T(8,128)S(1)}, u32[]{:S(2)}, u32[]{:S(2)}) collective-permute-start(f32[2,128,128]{2,1,0:T(8,128)S(1)} %convolution_add_fusion.5), channel_id=1, source_target_pairs={{0,32},{16,48},{32,0},{48,16},{64,96},{80,112},{96,64},{112,80},{1... | collective-permute-start | bytes 393224 | tf_op jit(solution)/shard_map/ppermute | solution.py:34
  197.0 13.2 %collective-permute-start.28 = (f32[2,128,128]{2,1,0:T(8,128)S(1)}, f32[2,128,128]{2,1,0:T(8,128)S(1)}, u32[]{:S(2)}, u32[]{:S(2)}) collective-permute-start(f32[2,128,128]{2,1,0:T(8,128)S(1)} %fusion.165), channel_id=1, source_target_pairs={{0,64},{16,80},{32,96},{48,112},{64,0},{80,16},{96,32},{112,48},{1... | collective-permute-start | bytes 393224 | tf_op jit(solution)/shard_map/ppermute | solution.py:34
  243.2 28.0 %collective-permute-start.35 = (f32[2,256,128]{2,1,0:T(8,128)S(1)}, f32[2,256,128]{2,1,0:T(8,128)S(1)}, u32[]{:S(2)}, u32[]{:S(2)}) collective-permute-start(f32[2,256,128]{2,1,0:T(8,128)S(1)} %fusion.163), channel_id=1, source_target_pairs={{0,4},{1,5},{2,6},{3,7},{4,0},{5,1},{6,2},{7,3},{8,12},{9,13},{10,... | collective-permute-start | bytes 786440 | tf_op jit(solution)/shard_map/ppermute | solution.py:34
  247.3 23.8 %collective-permute-start.36 = (f32[2,256,128]{2,1,0:T(8,128)S(1)}, f32[2,256,128]{2,1,0:T(8,128)S(1)}, u32[]{:S(2)}, u32[]{:S(2)}) collective-permute-start(f32[2,256,128]{2,1,0:T(8,128)S(1)} %fusion.163), channel_id=1, source_target_pairs={{0,8},{1,9},{2,10},{3,11},{4,12},{5,13},{6,14},{7,15},{8,0},{9,1},... | collective-permute-start | bytes 786440 | tf_op jit(solution)/shard_map/ppermute | solution.py:34
  251.7 23.7 %collective-permute-start.37 = (f32[2,256,128]{2,1,0:T(8,128)S(1)}, f32[2,256,128]{2,1,0:T(8,128)S(1)}, u32[]{:S(2)}, u32[]{:S(2)}) collective-permute-start(f32[2,256,128]{2,1,0:T(8,128)S(1)} %fusion.163), channel_id=1, source_target_pairs={{0,12},{1,13},{2,14},{3,15},{4,8},{5,9},{6,10},{7,11},{8,4},{9,5},... | collective-permute-start | bytes 786440 | tf_op jit(solution)/shard_map/ppermute | solution.py:34
  275.9 12.9 %collective-permute-start.38 = (f32[2,128,128]{2,1,0:T(8,128)S(1)}, f32[2,128,128]{2,1,0:T(8,128)S(1)}, u32[]{:S(2)}, u32[]{:S(2)}) collective-permute-start(f32[2,128,128]{2,1,0:T(8,128)S(1)} %convolution_add_fusion.4), channel_id=1, source_target_pairs={{0,16},{16,0},{32,48},{48,32},{64,80},{80,64},{96,112},{112,96},{1... | collective-permute-start | bytes 393224 | tf_op jit(solution)/shard_map/ppermute | solution.py:34
  282.5 13.5 %collective-permute-start.39 = (f32[2,128,128]{2,1,0:T(8,128)S(1)}, f32[2,128,128]{2,1,0:T(8,128)S(1)}, u32[]{:S(2)}, u32[]{:S(2)}) collective-permute-start(f32[2,128,128]{2,1,0:T(8,128)S(1)} %convolution_add_fusion.4), channel_id=1, source_target_pairs={{0,32},{16,48},{32,0},{48,16},{64,96},{80,112},{96,64},{112,80},{1... | collective-permute-start | bytes 393224 | tf_op jit(solution)/shard_map/ppermute | solution.py:34
  296.1 13.4 %collective-permute-start.41 = (f32[2,128,128]{2,1,0:T(8,128)S(1)}, f32[2,128,128]{2,1,0:T(8,128)S(1)}, u32[]{:S(2)}, u32[]{:S(2)}) collective-permute-start(f32[2,128,128]{2,1,0:T(8,128)S(1)} %fusion.161), channel_id=1, source_target_pairs={{0,64},{16,80},{32,96},{48,112},{64,0},{80,16},{96,32},{112,48},{1... | collective-permute-start | bytes 393224 | tf_op jit(solution)/shard_map/ppermute | solution.py:34
  329.3 12.5 %collective-permute-start.46 = (f32[2,256,128]{2,1,0:T(8,128)S(1)}, f32[2,256,128]{2,1,0:T(8,128)S(1)}, u32[]{:S(2)}, u32[]{:S(2)}) collective-permute-start(f32[2,256,128]{2,1,0:T(8,128)S(1)} %convolution_add_fusion), channel_id=1, source_target_pairs={{0,2},{1,3},{2,0},{3,1},{4,6},{5,7},{6,4},{7,5},{8,10},{9,11},{10,... | collective-permute-start | bytes 786440 | tf_op jit(solution)/shard_map/ppermute | solution.py:34
  347.1 28.0 %collective-permute-start.48 = (f32[2,256,128]{2,1,0:T(8,128)S(1)}, f32[2,256,128]{2,1,0:T(8,128)S(1)}, u32[]{:S(2)}, u32[]{:S(2)}) collective-permute-start(f32[2,256,128]{2,1,0:T(8,128)S(1)} %fusion.159), channel_id=1, source_target_pairs={{0,4},{1,5},{2,6},{3,7},{4,0},{5,1},{6,2},{7,3},{8,12},{9,13},{10,... | collective-permute-start | bytes 786440 | tf_op jit(solution)/shard_map/ppermute | solution.py:34
  351.4 23.7 %collective-permute-start.49 = (f32[2,256,128]{2,1,0:T(8,128)S(1)}, f32[2,256,128]{2,1,0:T(8,128)S(1)}, u32[]{:S(2)}, u32[]{:S(2)}) collective-permute-start(f32[2,256,128]{2,1,0:T(8,128)S(1)} %fusion.159), channel_id=1, source_target_pairs={{0,8},{1,9},{2,10},{3,11},{4,12},{5,13},{6,14},{7,15},{8,0},{9,1},... | collective-permute-start | bytes 786440 | tf_op jit(solution)/shard_map/ppermute | solution.py:34
  355.7 23.6 %collective-permute-start.50 = (f32[2,256,128]{2,1,0:T(8,128)S(1)}, f32[2,256,128]{2,1,0:T(8,128)S(1)}, u32[]{:S(2)}, u32[]{:S(2)}) collective-permute-start(f32[2,256,128]{2,1,0:T(8,128)S(1)} %fusion.159), channel_id=1, source_target_pairs={{0,12},{1,13},{2,14},{3,15},{4,8},{5,9},{6,10},{7,11},{8,4},{9,5},... | collective-permute-start | bytes 786440 | tf_op jit(solution)/shard_map/ppermute | solution.py:34
  385.4 13.3 %collective-permute-start.52 = (f32[2,128,128]{2,1,0:T(8,128)S(1)}, f32[2,128,128]{2,1,0:T(8,128)S(1)}, u32[]{:S(2)}, u32[]{:S(2)}) collective-permute-start(f32[2,128,128]{2,1,0:T(8,128)S(1)} %convolution_add_fusion.3), channel_id=1, source_target_pairs={{0,32},{16,48},{32,0},{48,16},{64,96},{80,112},{96,64},{112,80},{1... | collective-permute-start | bytes 393224 | tf_op jit(solution)/shard_map/ppermute | solution.py:34
  398.8 13.2 %collective-permute-start.54 = (f32[2,128,128]{2,1,0:T(8,128)S(1)}, f32[2,128,128]{2,1,0:T(8,128)S(1)}, u32[]{:S(2)}, u32[]{:S(2)}) collective-permute-start(f32[2,128,128]{2,1,0:T(8,128)S(1)} %fusion.157), channel_id=1, source_target_pairs={{0,64},{16,80},{32,96},{48,112},{64,0},{80,16},{96,32},{112,48},{1... | collective-permute-start | bytes 393224 | tf_op jit(solution)/shard_map/ppermute | solution.py:34
  (30 other events, 283.2 us)

commit v3 on v2

--- a/solution.py
+++ b/solution.py
@@ -151,24 +151,30 @@
 
     weighting = order_size / (query_rows * row_devices)
     rhs_part = jnp.einsum("hqa,hqd->had", probs, attended, preferred_element_type=F32)
-    rhs = group_sum(rhs_part, "pb") * weighting
+    sigma = theta_mid / delta_half
+    outputs = []
+    for head in range(head_count):
+        head_probs = probs[head : head + 1]
 
-    def gram_times(vec):
-        across = group_sum(split_dot("hqa,had->hqd", probs, vec), "kv")
-        back = group_sum(split_dot("hqa,hqd->had", probs, across), "pb")
-        return back * weighting + ridge_weight * vec
+        def gram_times(vec):
+            across = group_sum(split_dot("hqa,had->hqd", head_probs, vec), "kv")
+            back = group_sum(split_dot("hqa,hqd->had", head_probs, across), "pb")
+            return back * weighting + ridge_weight * vec
 
-    sigma = theta_mid / delta_half
-    solution = jnp.zeros_like(rhs)
-    resid = rhs
-    direction = rhs / theta_mid
-    recur_now = 1.0 / sigma
-    for iteration in range(STEPS):
-        solution = solution + direction
-        resid = resid - gram_times(direction)
-        recur_next = 1.0 / (2.0 * sigma - recur_now)
-        direction = recur_next * recur_now * direction + 2.0 * recur_next / delta_half * resid
-        recur_now = recur_next
+        rhs = group_sum(rhs_part[head : head + 1], "pb") * weighting
+        solution = jnp.zeros_like(rhs)
+        resid = rhs
+        direction = rhs / theta_mid
+        recur_now = 1.0 / sigma
+        for iteration in range(STEPS):
+            solution = solution + direction
+            resid = resid - gram_times(direction)
+            recur_next = 1.0 / (2.0 * sigma - recur_now)
+            direction = recur_next * recur_now * direction + 2.0 * recur_next / delta_half * resid
+            recur_now = recur_next
+        outputs.append((solution, resid))
+    solution = jnp.concatenate([o[0] for o in outputs], axis=0)
+    resid = jnp.concatenate([o[1] for o in outputs], axis=0)
     return (solution, resid)
 
 

time: 431 us -> 453 us (1.051)
  starting transfers between devices: 223 us -> 382 us
  waiting for transfers between devices: 178 us -> 38.5 us
    ppermute x52 -> x98, starting transfers between devices: 200 us -> 362 us  [gather_group(): got.append(jax.tree.map(lambda a: lax.ppermute(a, axis, pairs), value))]
    ppermute x52 -> x98, waiting for transfers between devices: 176 us -> 37.6 us  [gather_group(): got.append(jax.tree.map(lambda a: lax.ppermute(a, axis, pairs), value))]
  transfers between devices with their start and end apart: 58 -> 104, of which waited for: 29 -> 13; matrix products, arithmetic and copies ran while one was open for 2% -> 3% of each run, Pallas kernels for 0% -> 0%
where the time goes in v3:
time: 453 us; the launch traced here: 448 us
  starting transfers between devices  382 us (84%)
  waiting for transfers between devices  38.5 us (8%)
  other arithmetic  11.1 us (2%)
  matrix products  10.9 us (2%)
    ppermute x98, starting transfers between devices, gather_group(): got.append(jax.tree.map(lambda a: lax.ppermute(a, axis, pairs), value))  362 us
    ppermute x98, waiting for transfers between devices, gather_group(): got.append(jax.tree.map(lambda a: lax.ppermute(a, axis, pairs), value))  37.6 us
    ppermute x6, starting transfers between devices, scatter_groups(): total = total + lax.ppermute(give, axis, pairs)  20.1 us
  transfers between devices with their start and end apart: 104, of which 13 were waited for; matrix products, arithmetic and copies ran while one was open for 3% of the time, Pallas kernels for 0%

profile of v3, /device:TPU:6, one launch (start us, length us, event | category | flops | bytes accessed | tf_op | source)
XLA Modules:
  0.0 448.0 jit_solution(294029772467681834)
XLA Ops:
  31.6 10.6 %collective-permute-start.10 = (f32[2,264,128]{2,1,0:T(8,128)S(1)}, f32[2,264,128]{2,1,0:T(8,128)S(1)}, u32[]{:S(2)}, u32[]{:S(2)}) collective-permute-start(f32[2,264,128]{2,1,0:T(8,128)S(1)} %get-tuple-element.30), channel_id=1, source_target_pairs={{0,8},{1,9},{2,10},{3,11},{4,12},{5,13},{6,14},{7,15},{8,0},{9,1},... | collective-permute-start | bytes 811016 | tf_op jit(solution)/shard_map/ppermute | solution.py:34
  42.1 4.3 collective-permute-start.9
  51.0 6.0 %collective-permute-start.5 = (bf16[1,2,128,128]{3,2,1,0:T(8,128)(2,1)S(1)}, bf16[1,2,128,128]{3,2,1,0:T(8,128)(2,1)S(1)}, u32[]{:S(2)}, u32[]{:S(2)}) collective-permute-start(bf16[1,2,128,128]{3,2,1,0:T(8,128)(2,1)S(1)} %get-tuple-element.34), channel_id=1, source_target_pairs={{0,12},{1,13},{2,14},{3,15},{4,8},{5,9},{6,10},{7,11},{8,4},{9,5},... | collective-permute-start | bytes 196616 | tf_op jit(solution)/shard_map/ppermute | solution.py:62
  60.7 11.5 %collective-permute-done.9 = f32[2,264,128]{2,1,0:T(8,128)S(1)} collective-permute-done((f32[2,264,128]{2,1,0:T(8,128)S(1)}, f32[2,264,128]{2,1,0:T(8,128)S(1)}, u32[]{:S(2)}, u32[]{:S(2)}) %collective-permute-start.9) | collective-permute-done | bytes 270368 | tf_op jit(solution)/shard_map/ppermute | solution.py:34
  74.6 4.5 %collective-permute-start.46 = (f32[1,128,128]{2,1,0:T(8,128)S(1)}, f32[1,128,128]{2,1,0:T(8,128)S(1)}, u32[]{:S(2)}, u32[]{:S(2)}) collective-permute-start(f32[1,128,128]{2,1,0:T(8,128)S(1)} %get-tuple-element.38), channel_id=1, source_target_pairs={{0,32},{16,48},{32,0},{48,16},{64,96},{80,112},{96,64},{112,80},{1... | collective-permute-start | bytes 196616 | tf_op jit(solution)/shard_map/ppermute | solution.py:34
  88.4 4.4 collective-permute-start.12
  95.0 8.0 %collective-permute-start.50 = (f32[1,128,128]{2,1,0:T(8,128)S(1)}, f32[1,128,128]{2,1,0:T(8,128)S(1)}, u32[]{:S(2)}, u32[]{:S(2)}) collective-permute-start(f32[1,128,128]{2,1,0:T(8,128)S(1)} %fusion.235), channel_id=1, source_target_pairs={{0,192},{16,208},{32,224},{48,240},{64,128},{80,144},{96,160},{112... | collective-permute-start | bytes 196616 | tf_op jit(solution)/shard_map/ppermute | solution.py:34
  108.3 8.0 %collective-permute-start.17 = (f32[1,128,128]{2,1,0:T(8,128)S(1)}, f32[1,128,128]{2,1,0:T(8,128)S(1)}, u32[]{:S(2)}, u32[]{:S(2)}) collective-permute-start(f32[1,128,128]{2,1,0:T(8,128)S(1)} %fusion.227), channel_id=1, source_target_pairs={{0,192},{16,208},{32,224},{48,240},{64,128},{80,144},{96,160},{112... | collective-permute-start | bytes 196616 | tf_op jit(solution)/shard_map/ppermute | solution.py:34
  125.0 4.6 %collective-permute-done.15 = f32[1,128,128]{2,1,0:T(8,128)S(1)} collective-permute-done((f32[1,128,128]{2,1,0:T(8,128)S(1)}, f32[1,128,128]{2,1,0:T(8,128)S(1)}, u32[]{:S(2)}, u32[]{:S(2)}) %collective-permute-start.15) | collective-permute-done | bytes 65568 | tf_op jit(solution)/shard_map/ppermute | solution.py:34
  135.3 4.4 collective-permute-start.53
  150.1 4.6 %collective-permute-start.57 = (f32[1,256,128]{2,1,0:T(8,128)S(1)}, f32[1,256,128]{2,1,0:T(8,128)S(1)}, u32[]{:S(2)}, u32[]{:S(2)}) collective-permute-start(f32[1,256,128]{2,1,0:T(8,128)S(1)} %fusion.233), channel_id=1, source_target_pairs={{0,12},{1,13},{2,14},{3,15},{4,8},{5,9},{6,10},{7,11},{8,4},{9,5},... | collective-permute-start | bytes 393224 | tf_op jit(solution)/shard_map/ppermute | solution.py:34
  154.7 5.2 %collective-permute-start.56 = (f32[1,256,128]{2,1,0:T(8,128)S(1)}, f32[1,256,128]{2,1,0:T(8,128)S(1)}, u32[]{:S(2)}, u32[]{:S(2)}) collective-permute-start(f32[1,256,128]{2,1,0:T(8,128)S(1)} %fusion.233), channel_id=1, source_target_pairs={{0,8},{1,9},{2,10},{3,11},{4,12},{5,13},{6,14},{7,15},{8,0},{9,1},... | collective-permute-start | bytes 393224 | tf_op jit(solution)/shard_map/ppermute | solution.py:34
  162.5 4.6 %collective-permute-start.24 = (f32[1,256,128]{2,1,0:T(8,128)S(1)}, f32[1,256,128]{2,1,0:T(8,128)S(1)}, u32[]{:S(2)}, u32[]{:S(2)}) collective-permute-start(f32[1,256,128]{2,1,0:T(8,128)S(1)} %fusion.225), channel_id=1, source_target_pairs={{0,12},{1,13},{2,14},{3,15},{4,8},{5,9},{6,10},{7,11},{8,4},{9,5},... | collective-permute-start | bytes 393224 | tf_op jit(solution)/shard_map/ppermute | solution.py:34
  167.1 5.2 %collective-permute-start.23 = (f32[1,256,128]{2,1,0:T(8,128)S(1)}, f32[1,256,128]{2,1,0:T(8,128)S(1)}, u32[]{:S(2)}, u32[]{:S(2)}) collective-permute-start(f32[1,256,128]{2,1,0:T(8,128)S(1)} %fusion.225), channel_id=1, source_target_pairs={{0,8},{1,9},{2,10},{3,11},{4,12},{5,13},{6,14},{7,15},{8,0},{9,1},... | collective-permute-start | bytes 393224 | tf_op jit(solution)/shard_map/ppermute | solution.py:34
  181.4 5.4 %collective-permute-start.58 = (f32[1,128,128]{2,1,0:T(8,128)S(1)}, f32[1,128,128]{2,1,0:T(8,128)S(1)}, u32[]{:S(2)}, u32[]{:S(2)}) collective-permute-start(f32[1,128,128]{2,1,0:T(8,128)S(1)} %bitcast.603), channel_id=1, source_target_pairs={{0,16},{16,0},{32,48},{48,32},{64,80},{80,64},{96,112},{112,96},{1... | collective-permute-start | bytes 196616 | tf_op jit(solution)/shard_map/ppermute | solution.py:34
  192.6 4.8 %collective-permute-start.25 = (f32[1,128,128]{2,1,0:T(8,128)S(1)}, f32[1,128,128]{2,1,0:T(8,128)S(1)}, u32[]{:S(2)}, u32[]{:S(2)}) collective-permute-start(f32[1,128,128]{2,1,0:T(8,128)S(1)} %bitcast.615), channel_id=1, source_target_pairs={{0,16},{16,0},{32,48},{48,32},{64,80},{80,64},{96,112},{112,96},{1... | collective-permute-start | bytes 196616 | tf_op jit(solution)/shard_map/ppermute | solution.py:34
  204.9 5.8 %collective-permute-start.61 = (f32[1,128,128]{2,1,0:T(8,128)S(1)}, f32[1,128,128]{2,1,0:T(8,128)S(1)}, u32[]{:S(2)}, u32[]{:S(2)}) collective-permute-start(f32[1,128,128]{2,1,0:T(8,128)S(1)} %fusion.232), channel_id=1, source_target_pairs={{0,64},{16,80},{32,96},{48,112},{64,0},{80,16},{96,32},{112,48},{1... | collective-permute-start | bytes 196616 | tf_op jit(solution)/shard_map/ppermute | solution.py:34
  218.2 5.8 %collective-permute-start.28 = (f32[1,128,128]{2,1,0:T(8,128)S(1)}, f32[1,128,128]{2,1,0:T(8,128)S(1)}, u32[]{:S(2)}, u32[]{:S(2)}) collective-permute-start(f32[1,128,128]{2,1,0:T(8,128)S(1)} %fusion.224), channel_id=1, source_target_pairs={{0,64},{16,80},{32,96},{48,112},{64,0},{80,16},{96,32},{112,48},{1... | collective-permute-start | bytes 196616 | tf_op jit(solution)/shard_map/ppermute | solution.py:34
  234.4 5.4 %collective-permute-start.66 = (f32[1,256,128]{2,1,0:T(8,128)S(1)}, f32[1,256,128]{2,1,0:T(8,128)S(1)}, u32[]{:S(2)}, u32[]{:S(2)}) collective-permute-start(f32[1,256,128]{2,1,0:T(8,128)S(1)} %bitcast.584), channel_id=1, source_target_pairs={{0,2},{1,3},{2,0},{3,1},{4,6},{5,7},{6,4},{7,5},{8,10},{9,11},{10,... | collective-permute-start | bytes 393224 | tf_op jit(solution)/shard_map/ppermute | solution.py:34
  252.2 9.0 %collective-permute-start.69 = (f32[1,256,128]{2,1,0:T(8,128)S(1)}, f32[1,256,128]{2,1,0:T(8,128)S(1)}, u32[]{:S(2)}, u32[]{:S(2)}) collective-permute-start(f32[1,256,128]{2,1,0:T(8,128)S(1)} %fusion.230), channel_id=1, source_target_pairs={{0,8},{1,9},{2,10},{3,11},{4,12},{5,13},{6,14},{7,15},{8,0},{9,1},... | collective-permute-start | bytes 393224 | tf_op jit(solution)/shard_map/ppermute | solution.py:34
  265.8 7.8 %collective-permute-start.36 = (f32[1,256,128]{2,1,0:T(8,128)S(1)}, f32[1,256,128]{2,1,0:T(8,128)S(1)}, u32[]{:S(2)}, u32[]{:S(2)}) collective-permute-start(f32[1,256,128]{2,1,0:T(8,128)S(1)} %fusion.222), channel_id=1, source_target_pairs={{0,8},{1,9},{2,10},{3,11},{4,12},{5,13},{6,14},{7,15},{8,0},{9,1},... | collective-permute-start | bytes 393224 | tf_op jit(solution)/shard_map/ppermute | solution.py:34
  298.6 6.9 %collective-permute-start.76 = (f32[1,128,128]{2,1,0:T(8,128)S(1)}, f32[1,128,128]{2,1,0:T(8,128)S(1)}, u32[]{:S(2)}, u32[]{:S(2)}) collective-permute-start(f32[1,128,128]{2,1,0:T(8,128)S(1)} %fusion.229), channel_id=1, source_target_pairs={{0,192},{16,208},{32,224},{48,240},{64,128},{80,144},{96,160},{112... | collective-permute-start | bytes 196616 | tf_op jit(solution)/shard_map/ppermute | solution.py:34
  311.9 6.9 %collective-permute-start.43 = (f32[1,128,128]{2,1,0:T(8,128)S(1)}, f32[1,128,128]{2,1,0:T(8,128)S(1)}, u32[]{:S(2)}, u32[]{:S(2)}) collective-permute-start(f32[1,128,128]{2,1,0:T(8,128)S(1)} %fusion.221), channel_id=1, source_target_pairs={{0,192},{16,208},{32,224},{48,240},{64,128},{80,144},{96,160},{112... | collective-permute-start | bytes 196616 | tf_op jit(solution)/shard_map/ppermute | solution.py:34
  354.8 5.9 %collective-permute-start.95 = (f32[1,256,128]{2,1,0:T(8,128)S(1)}, f32[1,256,128]{2,1,0:T(8,128)S(1)}, u32[]{:S(2)}, u32[]{:S(2)}) collective-permute-start(f32[1,256,128]{2,1,0:T(8,128)S(1)} %fusion.219), channel_id=1, source_target_pairs={{0,8},{1,9},{2,10},{3,11},{4,12},{5,13},{6,14},{7,15},{8,0},{9,1},... | collective-permute-start | bytes 393224 | tf_op jit(solution)/shard_map/ppermute | solution.py:34
  367.2 5.9 %collective-permute-start.82 = (f32[1,256,128]{2,1,0:T(8,128)S(1)}, f32[1,256,128]{2,1,0:T(8,128)S(1)}, u32[]{:S(2)}, u32[]{:S(2)}) collective-permute-start(f32[1,256,128]{2,1,0:T(8,128)S(1)} %fusion.218), channel_id=1, source_target_pairs={{0,8},{1,9},{2,10},{3,11},{4,12},{5,13},{6,14},{7,15},{8,0},{9,1},... | collective-permute-start | bytes 393224 | tf_op jit(solution)/shard_map/ppermute | solution.py:34
  381.1 6.4 %collective-permute-done.81 = f32[1,256,128]{2,1,0:T(8,128)S(1)} collective-permute-done((f32[1,256,128]{2,1,0:T(8,128)S(1)}, f32[1,256,128]{2,1,0:T(8,128)S(1)}, u32[]{:S(2)}, u32[]{:S(2)}) %collective-permute-start.81) | collective-permute-done | bytes 131104 | tf_op jit(solution)/shard_map/ppermute | solution.py:34
  393.2 4.9 %collective-permute-start.84 = (f32[1,128,128]{2,1,0:T(8,128)S(1)}, f32[1,128,128]{2,1,0:T(8,128)S(1)}, u32[]{:S(2)}, u32[]{:S(2)}) collective-permute-start(f32[1,128,128]{2,1,0:T(8,128)S(1)} %bitcast.623), channel_id=1, source_target_pairs={{0,16},{16,0},{32,48},{48,32},{64,80},{80,64},{96,112},{112,96},{1... | collective-permute-start | bytes 196616 | tf_op jit(solution)/shard_map/ppermute | solution.py:34
  403.7 4.8 %collective-permute-start.97 = (f32[1,128,128]{2,1,0:T(8,128)S(1)}, f32[1,128,128]{2,1,0:T(8,128)S(1)}, u32[]{:S(2)}, u32[]{:S(2)}) collective-permute-start(f32[1,128,128]{2,1,0:T(8,128)S(1)} %bitcast.611), channel_id=1, source_target_pairs={{0,16},{16,0},{32,48},{48,32},{64,80},{80,64},{96,112},{112,96},{1... | collective-permute-start | bytes 196616 | tf_op jit(solution)/shard_map/ppermute | solution.py:34
  408.6 5.6 %collective-permute-start.89 = (f32[1,128,128]{2,1,0:T(8,128)S(1)}, f32[1,128,128]{2,1,0:T(8,128)S(1)}, u32[]{:S(2)}, u32[]{:S(2)}) collective-permute-start(f32[1,128,128]{2,1,0:T(8,128)S(1)} %fusion.215), channel_id=1, source_target_pairs={{0,192},{16,208},{32,224},{48,240},{64,128},{80,144},{96,160},{112... | collective-permute-start | bytes 196616 | tf_op jit(solution)/shard_map/ppermute | solution.py:34
  416.2 5.6 %collective-permute-start.87 = (f32[1,128,128]{2,1,0:T(8,128)S(1)}, f32[1,128,128]{2,1,0:T(8,128)S(1)}, u32[]{:S(2)}, u32[]{:S(2)}) collective-permute-start(f32[1,128,128]{2,1,0:T(8,128)S(1)} %fusion.215), channel_id=1, source_target_pairs={{0,64},{16,80},{32,96},{48,112},{64,0},{80,16},{96,32},{112,48},{1... | collective-permute-start | bytes 196616 | tf_op jit(solution)/shard_map/ppermute | solution.py:34
  421.9 5.6 %collective-permute-start.102 = (f32[1,128,128]{2,1,0:T(8,128)S(1)}, f32[1,128,128]{2,1,0:T(8,128)S(1)}, u32[]{:S(2)}, u32[]{:S(2)}) collective-permute-start(f32[1,128,128]{2,1,0:T(8,128)S(1)} %fusion.217), channel_id=1, source_target_pairs={{0,192},{16,208},{32,224},{48,240},{64,128},{80,144},{96,160},{112... | collective-permute-start | bytes 196616 | tf_op jit(solution)/shard_map/ppermute | solution.py:34
  429.5 5.6 %collective-permute-start.100 = (f32[1,128,128]{2,1,0:T(8,128)S(1)}, f32[1,128,128]{2,1,0:T(8,128)S(1)}, u32[]{:S(2)}, u32[]{:S(2)}) collective-permute-start(f32[1,128,128]{2,1,0:T(8,128)S(1)} %fusion.217), channel_id=1, source_target_pairs={{0,64},{16,80},{32,96},{48,112},{64,0},{80,16},{96,32},{112,48},{1... | collective-permute-start | bytes 196616 | tf_op jit(solution)/shard_map/ppermute | solution.py:34
  (350 shorter events, 250.8 us)
Async XLA Ops:
  8.9 19.0 %collective-permute-start.7 = (f32[2,264,128]{2,1,0:T(8,128)}, f32[2,264,128]{2,1,0:T(8,128)S(1)}, u32[]{:S(2)}, u32[]{:S(2)}) collective-permute-start(f32[2,264,128]{2,1,0:T(8,128)} %get-tuple-element.32), channel_id=1, source_target_pairs={{0,2},{1,3},{2,0},{3,1},{4,6},{5,7},{6,4},{7,5},{8,10},{9,11},{10,... | collective-permute-start | bytes 811016 | tf_op jit(solution)/shard_map/ppermute | solution.py:34
  21.1 25.3 %collective-permute-start.2 = (bf16[4,2,128,128]{3,2,1,0:T(8,128)(2,1)}, bf16[4,2,128,128]{3,2,1,0:T(8,128)(2,1)S(1)}, u32[]{:S(2)}, u32[]{:S(2)}) collective-permute-start(bf16[4,2,128,128]{3,2,1,0:T(8,128)(2,1)} %bitcast.543), channel_id=1, source_target_pairs={{0,3},{1,2},{2,1},{3,0},{4,7},{5,6},{6,5},{7,4},{8,11},{9,10},{10,... | collective-permute-start | bytes 786440 | tf_op jit(solution)/shard_map/ppermute | solution.py:62
  24.7 23.7 %collective-permute-start = (bf16[4,2,128,128]{3,2,1,0:T(8,128)(2,1)S(1)}, bf16[4,2,128,128]{3,2,1,0:T(8,128)(2,1)S(1)}, u32[]{:S(2)}, u32[]{:S(2)}) collective-permute-start(bf16[4,2,128,128]{3,2,1,0:T(8,128)(2,1)S(1)} %bitcast.600), channel_id=1, source_target_pairs={{0,1},{1,0},{2,3},{3,2},{4,5},{5,4},{6,7},{7,6},{8,9},{9,8},{10,11... | collective-permute-start | bytes 786440 | tf_op jit(solution)/shard_map/ppermute | solution.py:62
  27.9 20.5 %collective-permute-start.1 = (bf16[4,2,128,128]{3,2,1,0:T(8,128)(2,1)}, bf16[4,2,128,128]{3,2,1,0:T(8,128)(2,1)S(1)}, u32[]{:S(2)}, u32[]{:S(2)}) collective-permute-start(bf16[4,2,128,128]{3,2,1,0:T(8,128)(2,1)} %bitcast.544), channel_id=1, source_target_pairs={{0,2},{1,3},{2,0},{3,1},{4,6},{5,7},{6,4},{7,5},{8,10},{9,11},{10,... | collective-permute-start | bytes 786440 | tf_op jit(solution)/shard_map/ppermute | solution.py:62
  31.6 25.4 %collective-permute-start.10 = (f32[2,264,128]{2,1,0:T(8,128)S(1)}, f32[2,264,128]{2,1,0:T(8,128)S(1)}, u32[]{:S(2)}, u32[]{:S(2)}) collective-permute-start(f32[2,264,128]{2,1,0:T(8,128)S(1)} %get-tuple-element.30), channel_id=1, source_target_pairs={{0,8},{1,9},{2,10},{3,11},{4,12},{5,13},{6,14},{7,15},{8,0},{9,1},... | collective-permute-start | bytes 811016 | tf_op jit(solution)/shard_map/ppermute | solution.py:34
  42.1 30.1 %collective-permute-start.9 = (f32[2,264,128]{2,1,0:T(8,128)S(1)}, f32[2,264,128]{2,1,0:T(8,128)S(1)}, u32[]{:S(2)}, u32[]{:S(2)}) collective-permute-start(f32[2,264,128]{2,1,0:T(8,128)S(1)} %get-tuple-element.30), channel_id=1, source_target_pairs={{0,4},{1,5},{2,6},{3,7},{4,0},{5,1},{6,2},{7,3},{8,12},{9,13},{10,... | collective-permute-start | bytes 811016 | tf_op jit(solution)/shard_map/ppermute | solution.py:34
  46.4 25.8 %collective-permute-start.11 = (f32[2,264,128]{2,1,0:T(8,128)S(1)}, f32[2,264,128]{2,1,0:T(8,128)S(1)}, u32[]{:S(2)}, u32[]{:S(2)}) collective-permute-start(f32[2,264,128]{2,1,0:T(8,128)S(1)} %get-tuple-element.30), channel_id=1, source_target_pairs={{0,12},{1,13},{2,14},{3,15},{4,8},{5,9},{6,10},{7,11},{8,4},{9,5},... | collective-permute-start | bytes 811016 | tf_op jit(solution)/shard_map/ppermute | solution.py:34
  48.5 25.0 %collective-permute-start.3 = (bf16[1,2,128,128]{3,2,1,0:T(8,128)(2,1)S(1)}, bf16[1,2,128,128]{3,2,1,0:T(8,128)(2,1)S(1)}, u32[]{:S(2)}, u32[]{:S(2)}) collective-permute-start(bf16[1,2,128,128]{3,2,1,0:T(8,128)(2,1)S(1)} %get-tuple-element.33), channel_id=1, source_target_pairs={{0,4},{1,5},{2,6},{3,7},{4,0},{5,1},{6,2},{7,3},{8,12},{9,13},{10,... | collective-permute-start | bytes 196616 | tf_op jit(solution)/shard_map/ppermute | solution.py:62
  51.0 22.6 %collective-permute-start.5 = (bf16[1,2,128,128]{3,2,1,0:T(8,128)(2,1)S(1)}, bf16[1,2,128,128]{3,2,1,0:T(8,128)(2,1)S(1)}, u32[]{:S(2)}, u32[]{:S(2)}) collective-permute-start(bf16[1,2,128,128]{3,2,1,0:T(8,128)(2,1)S(1)} %get-tuple-element.34), channel_id=1, source_target_pairs={{0,12},{1,13},{2,14},{3,15},{4,8},{5,9},{6,10},{7,11},{8,4},{9,5},... | collective-permute-start | bytes 196616 | tf_op jit(solution)/shard_map/ppermute | solution.py:62
  84.8 21.4 %collective-permute-start.13 = (f32[1,128,128]{2,1,0:T(8,128)S(1)}, f32[1,128,128]{2,1,0:T(8,128)S(1)}, u32[]{:S(2)}, u32[]{:S(2)}) collective-permute-start(f32[1,128,128]{2,1,0:T(8,128)S(1)} %get-tuple-element.39), channel_id=1, source_target_pairs={{0,32},{16,48},{32,0},{48,16},{64,96},{80,112},{96,64},{112,80},{1... | collective-permute-start | bytes 196616 | tf_op jit(solution)/shard_map/ppermute | solution.py:34
  88.4 19.8 %collective-permute-start.12 = (f32[1,128,128]{2,1,0:T(8,128)S(1)}, f32[1,128,128]{2,1,0:T(8,128)S(1)}, u32[]{:S(2)}, u32[]{:S(2)}) collective-permute-start(f32[1,128,128]{2,1,0:T(8,128)S(1)} %get-tuple-element.39), channel_id=1, source_target_pairs={{0,16},{16,0},{32,48},{48,32},{64,80},{80,64},{96,112},{112,96},{1... | collective-permute-start | bytes 196616 | tf_op jit(solution)/shard_map/ppermute | solution.py:34
  95.0 24.4 %collective-permute-start.50 = (f32[1,128,128]{2,1,0:T(8,128)S(1)}, f32[1,128,128]{2,1,0:T(8,128)S(1)}, u32[]{:S(2)}, u32[]{:S(2)}) collective-permute-start(f32[1,128,128]{2,1,0:T(8,128)S(1)} %fusion.235), channel_id=1, source_target_pairs={{0,192},{16,208},{32,224},{48,240},{64,128},{80,144},{96,160},{112... | collective-permute-start | bytes 196616 | tf_op jit(solution)/shard_map/ppermute | solution.py:34
  150.1 22.2 %collective-permute-start.57 = (f32[1,256,128]{2,1,0:T(8,128)S(1)}, f32[1,256,128]{2,1,0:T(8,128)S(1)}, u32[]{:S(2)}, u32[]{:S(2)}) collective-permute-start(f32[1,256,128]{2,1,0:T(8,128)S(1)} %fusion.233), channel_id=1, source_target_pairs={{0,12},{1,13},{2,14},{3,15},{4,8},{5,9},{6,10},{7,11},{8,4},{9,5},... | collective-permute-start | bytes 393224 | tf_op jit(solution)/shard_map/ppermute | solution.py:34
  154.7 20.1 %collective-permute-start.56 = (f32[1,256,128]{2,1,0:T(8,128)S(1)}, f32[1,256,128]{2,1,0:T(8,128)S(1)}, u32[]{:S(2)}, u32[]{:S(2)}) collective-permute-start(f32[1,256,128]{2,1,0:T(8,128)S(1)} %fusion.233), channel_id=1, source_target_pairs={{0,8},{1,9},{2,10},{3,11},{4,12},{5,13},{6,14},{7,15},{8,0},{9,1},... | collective-permute-start | bytes 393224 | tf_op jit(solution)/shard_map/ppermute | solution.py:34
  167.1 19.7 %collective-permute-start.23 = (f32[1,256,128]{2,1,0:T(8,128)S(1)}, f32[1,256,128]{2,1,0:T(8,128)S(1)}, u32[]{:S(2)}, u32[]{:S(2)}) collective-permute-start(f32[1,256,128]{2,1,0:T(8,128)S(1)} %fusion.225), channel_id=1, source_target_pairs={{0,8},{1,9},{2,10},{3,11},{4,12},{5,13},{6,14},{7,15},{8,0},{9,1},... | collective-permute-start | bytes 393224 | tf_op jit(solution)/shard_map/ppermute | solution.py:34
  190.1 20.6 %collective-permute-start.26 = (f32[1,128,128]{2,1,0:T(8,128)S(1)}, f32[1,128,128]{2,1,0:T(8,128)S(1)}, u32[]{:S(2)}, u32[]{:S(2)}) collective-permute-start(f32[1,128,128]{2,1,0:T(8,128)S(1)} %bitcast.614), channel_id=1, source_target_pairs={{0,32},{16,48},{32,0},{48,16},{64,96},{80,112},{96,64},{112,80},{1... | collective-permute-start | bytes 196616 | tf_op jit(solution)/shard_map/ppermute | solution.py:34
  197.5 20.7 %collective-permute-start.63 = (f32[1,128,128]{2,1,0:T(8,128)S(1)}, f32[1,128,128]{2,1,0:T(8,128)S(1)}, u32[]{:S(2)}, u32[]{:S(2)}) collective-permute-start(f32[1,128,128]{2,1,0:T(8,128)S(1)} %fusion.232), channel_id=1, source_target_pairs={{0,192},{16,208},{32,224},{48,240},{64,128},{80,144},{96,160},{112... | collective-permute-start | bytes 196616 | tf_op jit(solution)/shard_map/ppermute | solution.py:34
  201.7 22.2 %collective-permute-start.62 = (f32[1,128,128]{2,1,0:T(8,128)S(1)}, f32[1,128,128]{2,1,0:T(8,128)S(1)}, u32[]{:S(2)}, u32[]{:S(2)}) collective-permute-start(f32[1,128,128]{2,1,0:T(8,128)S(1)} %fusion.232), channel_id=1, source_target_pairs={{0,128},{16,144},{32,160},{48,176},{64,192},{80,208},{96,224},{112... | collective-permute-start | bytes 196616 | tf_op jit(solution)/shard_map/ppermute | solution.py:34
  204.9 19.1 %collective-permute-start.61 = (f32[1,128,128]{2,1,0:T(8,128)S(1)}, f32[1,128,128]{2,1,0:T(8,128)S(1)}, u32[]{:S(2)}, u32[]{:S(2)}) collective-permute-start(f32[1,128,128]{2,1,0:T(8,128)S(1)} %fusion.232), channel_id=1, source_target_pairs={{0,64},{16,80},{32,96},{48,112},{64,0},{80,16},{96,32},{112,48},{1... | collective-permute-start | bytes 196616 | tf_op jit(solution)/shard_map/ppermute | solution.py:34
  250.3 23.4 %collective-permute-start.70 = (f32[1,256,128]{2,1,0:T(8,128)S(1)}, f32[1,256,128]{2,1,0:T(8,128)S(1)}, u32[]{:S(2)}, u32[]{:S(2)}) collective-permute-start(f32[1,256,128]{2,1,0:T(8,128)S(1)} %fusion.230), channel_id=1, source_target_pairs={{0,12},{1,13},{2,14},{3,15},{4,8},{5,9},{6,10},{7,11},{8,4},{9,5},... | collective-permute-start | bytes 393224 | tf_op jit(solution)/shard_map/ppermute | solution.py:34
  252.2 23.4 %collective-permute-start.69 = (f32[1,256,128]{2,1,0:T(8,128)S(1)}, f32[1,256,128]{2,1,0:T(8,128)S(1)}, u32[]{:S(2)}, u32[]{:S(2)}) collective-permute-start(f32[1,256,128]{2,1,0:T(8,128)S(1)} %fusion.230), channel_id=1, source_target_pairs={{0,8},{1,9},{2,10},{3,11},{4,12},{5,13},{6,14},{7,15},{8,0},{9,1},... | collective-permute-start | bytes 393224 | tf_op jit(solution)/shard_map/ppermute | solution.py:34
  265.8 20.4 %collective-permute-start.36 = (f32[1,256,128]{2,1,0:T(8,128)S(1)}, f32[1,256,128]{2,1,0:T(8,128)S(1)}, u32[]{:S(2)}, u32[]{:S(2)}) collective-permute-start(f32[1,256,128]{2,1,0:T(8,128)S(1)} %fusion.222), channel_id=1, source_target_pairs={{0,8},{1,9},{2,10},{3,11},{4,12},{5,13},{6,14},{7,15},{8,0},{9,1},... | collective-permute-start | bytes 393224 | tf_op jit(solution)/shard_map/ppermute | solution.py:34
  288.4 20.1 %collective-permute-start.40 = (f32[1,128,128]{2,1,0:T(8,128)S(1)}, f32[1,128,128]{2,1,0:T(8,128)S(1)}, u32[]{:S(2)}, u32[]{:S(2)}) collective-permute-start(f32[1,128,128]{2,1,0:T(8,128)S(1)} %bitcast.617), channel_id=1, source_target_pairs={{0,48},{16,32},{32,16},{48,0},{64,112},{80,96},{96,80},{112,64},{1... | collective-permute-start | bytes 196616 | tf_op jit(solution)/shard_map/ppermute | solution.py:34
  292.5 19.3 %collective-permute-start.39 = (f32[1,128,128]{2,1,0:T(8,128)S(1)}, f32[1,128,128]{2,1,0:T(8,128)S(1)}, u32[]{:S(2)}, u32[]{:S(2)}) collective-permute-start(f32[1,128,128]{2,1,0:T(8,128)S(1)} %bitcast.618), channel_id=1, source_target_pairs={{0,32},{16,48},{32,0},{48,16},{64,96},{80,112},{96,64},{112,80},{1... | collective-permute-start | bytes 196616 | tf_op jit(solution)/shard_map/ppermute | solution.py:34
  298.6 23.1 %collective-permute-start.76 = (f32[1,128,128]{2,1,0:T(8,128)S(1)}, f32[1,128,128]{2,1,0:T(8,128)S(1)}, u32[]{:S(2)}, u32[]{:S(2)}) collective-permute-start(f32[1,128,128]{2,1,0:T(8,128)S(1)} %fusion.229), channel_id=1, source_target_pairs={{0,192},{16,208},{32,224},{48,240},{64,128},{80,144},{96,160},{112... | collective-permute-start | bytes 196616 | tf_op jit(solution)/shard_map/ppermute | solution.py:34
  305.6 19.5 %collective-permute-start.75 = (f32[1,128,128]{2,1,0:T(8,128)S(1)}, f32[1,128,128]{2,1,0:T(8,128)S(1)}, u32[]{:S(2)}, u32[]{:S(2)}) collective-permute-start(f32[1,128,128]{2,1,0:T(8,128)S(1)} %fusion.229), channel_id=1, source_target_pairs={{0,128},{16,144},{32,160},{48,176},{64,192},{80,208},{96,224},{112... | collective-permute-start | bytes 196616 | tf_op jit(solution)/shard_map/ppermute | solution.py:34
  352.2 20.9 %collective-permute-start.96 = (f32[1,256,128]{2,1,0:T(8,128)S(1)}, f32[1,256,128]{2,1,0:T(8,128)S(1)}, u32[]{:S(2)}, u32[]{:S(2)}) collective-permute-start(f32[1,256,128]{2,1,0:T(8,128)S(1)} %fusion.219), channel_id=1, source_target_pairs={{0,12},{1,13},{2,14},{3,15},{4,8},{5,9},{6,10},{7,11},{8,4},{9,5},... | collective-permute-start | bytes 393224 | tf_op jit(solution)/shard_map/ppermute | solution.py:34
  354.8 22.1 %collective-permute-start.95 = (f32[1,256,128]{2,1,0:T(8,128)S(1)}, f32[1,256,128]{2,1,0:T(8,128)S(1)}, u32[]{:S(2)}, u32[]{:S(2)}) collective-permute-start(f32[1,256,128]{2,1,0:T(8,128)S(1)} %fusion.219), channel_id=1, source_target_pairs={{0,8},{1,9},{2,10},{3,11},{4,12},{5,13},{6,14},{7,15},{8,0},{9,1},... | collective-permute-start | bytes 393224 | tf_op jit(solution)/shard_map/ppermute | solution.py:34
  401.2 20.7 %collective-permute-start.98 = (f32[1,128,128]{2,1,0:T(8,128)S(1)}, f32[1,128,128]{2,1,0:T(8,128)S(1)}, u32[]{:S(2)}, u32[]{:S(2)}) collective-permute-start(f32[1,128,128]{2,1,0:T(8,128)S(1)} %bitcast.610), channel_id=1, source_target_pairs={{0,32},{16,48},{32,0},{48,16},{64,96},{80,112},{96,64},{112,80},{1... | collective-permute-start | bytes 196616 | tf_op jit(solution)/shard_map/ppermute | solution.py:34
  408.6 20.8 %collective-permute-start.89 = (f32[1,128,128]{2,1,0:T(8,128)S(1)}, f32[1,128,128]{2,1,0:T(8,128)S(1)}, u32[]{:S(2)}, u32[]{:S(2)}) collective-permute-start(f32[1,128,128]{2,1,0:T(8,128)S(1)} %fusion.215), channel_id=1, source_target_pairs={{0,192},{16,208},{32,224},{48,240},{64,128},{80,144},{96,160},{112... | collective-permute-start | bytes 196616 | tf_op jit(solution)/shard_map/ppermute | solution.py:34
  414.2 20.9 %collective-permute-start.88 = (f32[1,128,128]{2,1,0:T(8,128)S(1)}, f32[1,128,128]{2,1,0:T(8,128)S(1)}, u32[]{:S(2)}, u32[]{:S(2)}) collective-permute-start(f32[1,128,128]{2,1,0:T(8,128)S(1)} %fusion.215), channel_id=1, source_target_pairs={{0,128},{16,144},{32,160},{48,176},{64,192},{80,208},{96,224},{112... | collective-permute-start | bytes 196616 | tf_op jit(solution)/shard_map/ppermute | solution.py:34
  416.2 18.9 %collective-permute-start.87 = (f32[1,128,128]{2,1,0:T(8,128)S(1)}, f32[1,128,128]{2,1,0:T(8,128)S(1)}, u32[]{:S(2)}, u32[]{:S(2)}) collective-permute-start(f32[1,128,128]{2,1,0:T(8,128)S(1)} %fusion.215), channel_id=1, source_target_pairs={{0,64},{16,80},{32,96},{48,112},{64,0},{80,16},{96,32},{112,48},{1... | collective-permute-start | bytes 196616 | tf_op jit(solution)/shard_map/ppermute | solution.py:34
  (76 other events, 1080.4 us)

commit v4 on v2

--- a/solution.py
+++ b/solution.py
@@ -39,9 +39,30 @@
     ]
 
 
+def gather_bits(value, axis, bits):
+    size = lax.axis_size(axis)
+    me = lax.axis_index(axis)
+    digit = sum(((me >> b) & 1) << t for t, b in enumerate(bits))
+    radix = 1 << len(bits)
+    got = [value]
+    for k in range(1, radix):
+        mask = sum(((k >> t) & 1) << b for t, b in enumerate(bits))
+        pairs = [(s, s ^ mask) for s in range(size)]
+        got.append(lax.ppermute(value, axis, pairs))
+    stacked = jnp.stack(got)
+    return [lax.dynamic_index_in_dim(stacked, digit ^ g, 0, False) for g in range(radix)]
+
+
+def bit_stages(size):
+    count = size.bit_length() - 1
+    if count == 5:
+        return [[0, 1], [3, 4], [2]]
+    return [[b, b + 1] if b + 1 < count else [b] for b in range(0, count, 2)]
+
+
 def group_sum(value, axis):
-    for stride, radix in digit_groups(lax.axis_size(axis)):
-        members = gather_group(value, axis, stride, radix)
+    for bits in bit_stages(lax.axis_size(axis)):
+        members = gather_bits(value, axis, bits)
         value = members[0]
         for other in members[1:]:
             value = value + other
@@ -117,7 +138,6 @@
     ).astype(BF16)
     kept_mask = jnp.any(owned, axis=1)
     blocks = picked.reshape(head_count, col_devices, col_len, head_width).transpose(1, 0, 2, 3)
-    chosen_block = scatter_groups(blocks, "kv")
 
     scores = (
         jnp.einsum("hqd,hkd->hqk", queries, cache_keys, preferred_element_type=F32) * score_scale
@@ -138,9 +158,26 @@
 
     packed = pack(numer, peak, denom, cpeak, cdenom)
     for stride, radix in digit_groups(col_devices):
-        members = gather_group(packed, "kv", stride, radix)
+        digit = (me_kv // stride) % radix
+        split = blocks.reshape((blocks.shape[0] // radix, radix) + blocks.shape[1:])
+        total = lax.dynamic_index_in_dim(split, digit, 1, False)
+        got = [packed]
+        for k in range(1, radix):
+            pairs = [(s, s ^ (k * stride)) for s in range(col_devices)]
+            give = lax.dynamic_index_in_dim(split, digit ^ k, 1, False)
+            key_rows_sent = give.size // head_width
+            payload = jnp.concatenate(
+                [give.astype(F32).reshape(key_rows_sent, head_width), packed.reshape(-1, head_width)]
+            )
+            arrived = lax.ppermute(payload, "kv", pairs)
+            total = total + arrived[:key_rows_sent].reshape(give.shape).astype(BF16)
+            got.append(arrived[key_rows_sent:].reshape(packed.shape))
+        blocks = total
+        stacked = jnp.stack(got)
+        members = [lax.dynamic_index_in_dim(stacked, digit ^ g, 0, False) for g in range(radix)]
         numer, peak, denom, cpeak, cdenom = combine_members(members, query_rows)
         packed = pack(numer, peak, denom, cpeak, cdenom)
+    chosen_block = blocks[0]
     attended = (numer / denom[..., None]).astype(BF16)
 
     compact = (

time: 431 us -> 458 us (1.063)
  waiting for transfers between devices: 178 us -> 219 us
  starting transfers between devices: 223 us -> 202 us
  local copies, waits for them, and re-layouts: 1.93 us -> 8.72 us
    ppermute x58 -> x52, waiting for transfers between devices: 178 us -> 219 us  [the longest x46 153 us: gather_bits(): got.append(lax.ppermute(value, axis, pairs))]
    ppermute x58 -> x52, starting transfers between devices: 223 us -> 202 us  [the longest x46 177 us: gather_bits(): got.append(lax.ppermute(value, axis, pairs))]
    slice x0 -> x12, local copies, waits for them, and re-layouts: none -> 6.07 us  [the longest x6 3.1 us: per_device(): total = total + arrived[:key_rows_sent].reshape(give.shape).astype(BF16)]
  transfers between devices with their start and end apart: 58 -> 52, of which waited for: 29 -> 34; matrix products, arithmetic and copies ran while one was open for 2% -> 0% of each run, Pallas kernels for 0% -> 0%
where the time goes in v4:
time: 458 us; the launch traced here: 452 us
  waiting for transfers between devices  219 us (48%)
  starting transfers between devices  202 us (44%)
  other arithmetic  10.4 us (2%)
  matrix products  10.4 us (2%)
  local copies, waits for them, and re-layouts  8.72 us (2%)
    ppermute x46, starting transfers between devices, gather_bits(): got.append(lax.ppermute(value, axis, pairs))  177 us
    ppermute x46, waiting for transfers between devices, gather_bits(): got.append(lax.ppermute(value, axis, pairs))  153 us
    ppermute x6, waiting for transfers between devices, per_device(): arrived = lax.ppermute(payload, 'kv', pairs)  66 us
    ppermute x6, starting transfers between devices, per_device(): arrived = lax.ppermute(payload, 'kv', pairs)  24.4 us
  transfers between devices with their start and end apart: 52, of which 34 were waited for; matrix products, arithmetic and copies ran while one was open for 0% of the time, Pallas kernels for 0%

profile of v4, /device:TPU:6, one launch (start us, length us, event | category | flops | bytes accessed | tf_op | source)
XLA Modules:
  0.0 452.2 jit_solution(3971254394464274124)
XLA Ops:
  24.5 16.8 %collective-permute-done.1 = f32[1552,128]{1,0:T(8,128)} collective-permute-done((f32[1552,128]{1,0:T(8,128)}, f32[1552,128]{1,0:T(8,128)}, u32[]{:S(2)}, u32[]{:S(2)}) %collective-permute-start.1) | collective-permute-done | bytes 794656 | tf_op jit(solution)/shard_map/ppermute | solution.py:172
  42.3 15.7 %collective-permute-done.2 = f32[1552,128]{1,0:T(8,128)} collective-permute-done((f32[1552,128]{1,0:T(8,128)S(1)}, f32[1552,128]{1,0:T(8,128)}, u32[]{:S(2)}, u32[]{:S(2)}) %collective-permute-start.2) | collective-permute-done | bytes 794656 | tf_op jit(solution)/shard_map/ppermute | solution.py:172
  62.1 6.1 %collective-permute-start.3 = (f32[784,128]{1,0:T(8,128)S(1)}, f32[784,128]{1,0:T(8,128)S(1)}, u32[]{:S(2)}, u32[]{:S(2)}) collective-permute-start(f32[784,128]{1,0:T(8,128)S(1)} %get-tuple-element.31), channel_id=1, source_target_pairs={{0,4},{1,5},{2,6},{3,7},{4,0},{5,1},{6,2},{7,3},{8,12},{9,13},{10,... | collective-permute-start | bytes 1204232 | tf_op jit(solution)/shard_map/ppermute | solution.py:172
  68.2 8.2 %collective-permute-start.4 = (f32[784,128]{1,0:T(8,128)S(1)}, f32[784,128]{1,0:T(8,128)S(1)}, u32[]{:S(2)}, u32[]{:S(2)}) collective-permute-start(f32[784,128]{1,0:T(8,128)S(1)} %get-tuple-element.32), channel_id=1, source_target_pairs={{0,8},{1,9},{2,10},{3,11},{4,12},{5,13},{6,14},{7,15},{8,0},{9,1},... | collective-permute-start | bytes 1204232 | tf_op jit(solution)/shard_map/ppermute | solution.py:172
  78.4 25.3 %collective-permute-done.3 = f32[784,128]{1,0:T(8,128)S(1)} collective-permute-done((f32[784,128]{1,0:T(8,128)S(1)}, f32[784,128]{1,0:T(8,128)S(1)}, u32[]{:S(2)}, u32[]{:S(2)}) %collective-permute-start.3) | collective-permute-done | bytes 401440 | tf_op jit(solution)/shard_map/ppermute | solution.py:172
  103.7 6.3 %collective-permute-done.4 = f32[784,128]{1,0:T(8,128)S(1)} collective-permute-done((f32[784,128]{1,0:T(8,128)S(1)}, f32[784,128]{1,0:T(8,128)S(1)}, u32[]{:S(2)}, u32[]{:S(2)}) %collective-permute-start.4) | collective-permute-done | bytes 401440 | tf_op jit(solution)/shard_map/ppermute | solution.py:172
  125.5 7.3 %collective-permute-done.7 = f32[2,128,128]{2,1,0:T(8,128)S(1)} collective-permute-done((f32[2,128,128]{2,1,0:T(8,128)S(1)}, f32[2,128,128]{2,1,0:T(8,128)S(1)}, u32[]{:S(2)}, u32[]{:S(2)}) %collective-permute-start.7) | collective-permute-done | bytes 131104 | tf_op jit(solution)/shard_map/ppermute | solution.py:51
  138.7 4.7 %collective-permute-start.11 = (f32[2,128,128]{2,1,0:T(8,128)S(1)}, f32[2,128,128]{2,1,0:T(8,128)S(1)}, u32[]{:S(2)}, u32[]{:S(2)}) collective-permute-start(f32[2,128,128]{2,1,0:T(8,128)S(1)} %fusion.169), channel_id=1, source_target_pairs={{0,384},{16,400},{32,416},{48,432},{64,448},{80,464},{96,480},{112... | collective-permute-start | bytes 393224 | tf_op jit(solution)/shard_map/ppermute | solution.py:51
  146.9 7.1 %collective-permute-start.12 = (f32[2,128,128]{2,1,0:T(8,128)S(1)}, f32[2,128,128]{2,1,0:T(8,128)S(1)}, u32[]{:S(2)}, u32[]{:S(2)}) collective-permute-start(f32[2,128,128]{2,1,0:T(8,128)S(1)} %fusion.168), channel_id=1, source_target_pairs={{0,64},{16,80},{32,96},{48,112},{64,0},{80,16},{96,32},{112,48},{1... | collective-permute-start | bytes 393224 | tf_op jit(solution)/shard_map/ppermute | solution.py:51
  165.9 5.4 %collective-permute-done.14 = f32[2,256,128]{2,1,0:T(8,128)S(1)} collective-permute-done((f32[2,256,128]{2,1,0:T(8,128)S(1)}, f32[2,256,128]{2,1,0:T(8,128)S(1)}, u32[]{:S(2)}, u32[]{:S(2)}) %collective-permute-start.14) | collective-permute-done | bytes 262176 | tf_op jit(solution)/shard_map/ppermute | solution.py:51
  179.4 7.6 %collective-permute-start.17 = (f32[2,256,128]{2,1,0:T(8,128)S(1)}, f32[2,256,128]{2,1,0:T(8,128)S(1)}, u32[]{:S(2)}, u32[]{:S(2)}) collective-permute-start(f32[2,256,128]{2,1,0:T(8,128)S(1)} %fusion.167), channel_id=1, source_target_pairs={{0,8},{1,9},{2,10},{3,11},{4,12},{5,13},{6,14},{7,15},{8,0},{9,1},... | collective-permute-start | bytes 786440 | tf_op jit(solution)/shard_map/ppermute | solution.py:51
  189.0 15.0 %collective-permute-done.16 = f32[2,256,128]{2,1,0:T(8,128)S(1)} collective-permute-done((f32[2,256,128]{2,1,0:T(8,128)S(1)}, f32[2,256,128]{2,1,0:T(8,128)S(1)}, u32[]{:S(2)}, u32[]{:S(2)}) %collective-permute-start.16) | collective-permute-done | bytes 262176 | tf_op jit(solution)/shard_map/ppermute | solution.py:51
  204.1 5.3 %collective-permute-done.18 = f32[2,256,128]{2,1,0:T(8,128)S(1)} collective-permute-done((f32[2,256,128]{2,1,0:T(8,128)S(1)}, f32[2,256,128]{2,1,0:T(8,128)S(1)}, u32[]{:S(2)}, u32[]{:S(2)}) %collective-permute-start.18) | collective-permute-done | bytes 262176 | tf_op jit(solution)/shard_map/ppermute | solution.py:51
  210.0 6.1 %collective-permute-start.19 = (f32[2,128,128]{2,1,0:T(8,128)S(1)}, f32[2,128,128]{2,1,0:T(8,128)S(1)}, u32[]{:S(2)}, u32[]{:S(2)}) collective-permute-start(f32[2,128,128]{2,1,0:T(8,128)S(1)} %convolution_add_fusion.5), channel_id=1, source_target_pairs={{0,16},{16,0},{32,48},{48,32},{64,80},{80,64},{96,112},{112,96},{1... | collective-permute-start | bytes 393224 | tf_op jit(solution)/shard_map/ppermute | solution.py:51
  222.2 7.0 %collective-permute-done.20 = f32[2,128,128]{2,1,0:T(8,128)S(1)} collective-permute-done((f32[2,128,128]{2,1,0:T(8,128)S(1)}, f32[2,128,128]{2,1,0:T(8,128)S(1)}, u32[]{:S(2)}, u32[]{:S(2)}) %collective-permute-start.20) | collective-permute-done | bytes 131104 | tf_op jit(solution)/shard_map/ppermute | solution.py:51
  245.1 7.1 %collective-permute-start.25 = (f32[2,128,128]{2,1,0:T(8,128)S(1)}, f32[2,128,128]{2,1,0:T(8,128)S(1)}, u32[]{:S(2)}, u32[]{:S(2)}) collective-permute-start(f32[2,128,128]{2,1,0:T(8,128)S(1)} %fusion.164), channel_id=1, source_target_pairs={{0,64},{16,80},{32,96},{48,112},{64,0},{80,16},{96,32},{112,48},{1... | collective-permute-start | bytes 393224 | tf_op jit(solution)/shard_map/ppermute | solution.py:51
  264.3 5.1 %collective-permute-done.27 = f32[2,256,128]{2,1,0:T(8,128)S(1)} collective-permute-done((f32[2,256,128]{2,1,0:T(8,128)S(1)}, f32[2,256,128]{2,1,0:T(8,128)S(1)}, u32[]{:S(2)}, u32[]{:S(2)}) %collective-permute-start.27) | collective-permute-done | bytes 262176 | tf_op jit(solution)/shard_map/ppermute | solution.py:51
  269.5 5.2 %collective-permute-done.28 = f32[2,256,128]{2,1,0:T(8,128)S(1)} collective-permute-done((f32[2,256,128]{2,1,0:T(8,128)S(1)}, f32[2,256,128]{2,1,0:T(8,128)S(1)}, u32[]{:S(2)}, u32[]{:S(2)}) %collective-permute-start.28) | collective-permute-done | bytes 262176 | tf_op jit(solution)/shard_map/ppermute | solution.py:51
  277.0 8.1 %collective-permute-start.30 = (f32[2,256,128]{2,1,0:T(8,128)S(1)}, f32[2,256,128]{2,1,0:T(8,128)S(1)}, u32[]{:S(2)}, u32[]{:S(2)}) collective-permute-start(f32[2,256,128]{2,1,0:T(8,128)S(1)} %fusion.163), channel_id=1, source_target_pairs={{0,8},{1,9},{2,10},{3,11},{4,12},{5,13},{6,14},{7,15},{8,0},{9,1},... | collective-permute-start | bytes 786440 | tf_op jit(solution)/shard_map/ppermute | solution.py:51
  287.2 15.5 %collective-permute-done.29 = f32[2,256,128]{2,1,0:T(8,128)S(1)} collective-permute-done((f32[2,256,128]{2,1,0:T(8,128)S(1)}, f32[2,256,128]{2,1,0:T(8,128)S(1)}, u32[]{:S(2)}, u32[]{:S(2)}) %collective-permute-start.29) | collective-permute-done | bytes 262176 | tf_op jit(solution)/shard_map/ppermute | solution.py:51
  302.7 4.9 %collective-permute-done.31 = f32[2,256,128]{2,1,0:T(8,128)S(1)} collective-permute-done((f32[2,256,128]{2,1,0:T(8,128)S(1)}, f32[2,256,128]{2,1,0:T(8,128)S(1)}, u32[]{:S(2)}, u32[]{:S(2)}) %collective-permute-start.31) | collective-permute-done | bytes 262176 | tf_op jit(solution)/shard_map/ppermute | solution.py:51
  308.2 5.9 %collective-permute-start.32 = (f32[2,128,128]{2,1,0:T(8,128)S(1)}, f32[2,128,128]{2,1,0:T(8,128)S(1)}, u32[]{:S(2)}, u32[]{:S(2)}) collective-permute-start(f32[2,128,128]{2,1,0:T(8,128)S(1)} %convolution_add_fusion.4), channel_id=1, source_target_pairs={{0,16},{16,0},{32,48},{48,32},{64,80},{80,64},{96,112},{112,96},{1... | collective-permute-start | bytes 393224 | tf_op jit(solution)/shard_map/ppermute | solution.py:51
  320.5 7.0 %collective-permute-done.33 = f32[2,128,128]{2,1,0:T(8,128)S(1)} collective-permute-done((f32[2,128,128]{2,1,0:T(8,128)S(1)}, f32[2,128,128]{2,1,0:T(8,128)S(1)}, u32[]{:S(2)}, u32[]{:S(2)}) %collective-permute-start.33) | collective-permute-done | bytes 131104 | tf_op jit(solution)/shard_map/ppermute | solution.py:51
  342.0 7.0 %collective-permute-start.38 = (f32[2,128,128]{2,1,0:T(8,128)S(1)}, f32[2,128,128]{2,1,0:T(8,128)S(1)}, u32[]{:S(2)}, u32[]{:S(2)}) collective-permute-start(f32[2,128,128]{2,1,0:T(8,128)S(1)} %fusion.160), channel_id=1, source_target_pairs={{0,64},{16,80},{32,96},{48,112},{64,0},{80,16},{96,32},{112,48},{1... | collective-permute-start | bytes 393224 | tf_op jit(solution)/shard_map/ppermute | solution.py:51
  361.7 5.4 %collective-permute-done.40 = f32[2,256,128]{2,1,0:T(8,128)S(1)} collective-permute-done((f32[2,256,128]{2,1,0:T(8,128)S(1)}, f32[2,256,128]{2,1,0:T(8,128)S(1)}, u32[]{:S(2)}, u32[]{:S(2)}) %collective-permute-start.40) | collective-permute-done | bytes 262176 | tf_op jit(solution)/shard_map/ppermute | solution.py:51
  367.1 4.7 %collective-permute-done.41 = f32[2,256,128]{2,1,0:T(8,128)S(1)} collective-permute-done((f32[2,256,128]{2,1,0:T(8,128)S(1)}, f32[2,256,128]{2,1,0:T(8,128)S(1)}, u32[]{:S(2)}, u32[]{:S(2)}) %collective-permute-start.41) | collective-permute-done | bytes 262176 | tf_op jit(solution)/shard_map/ppermute | solution.py:51
  375.4 7.4 %collective-permute-start.43 = (f32[2,256,128]{2,1,0:T(8,128)S(1)}, f32[2,256,128]{2,1,0:T(8,128)S(1)}, u32[]{:S(2)}, u32[]{:S(2)}) collective-permute-start(f32[2,256,128]{2,1,0:T(8,128)S(1)} %fusion.159), channel_id=1, source_target_pairs={{0,8},{1,9},{2,10},{3,11},{4,12},{5,13},{6,14},{7,15},{8,0},{9,1},... | collective-permute-start | bytes 786440 | tf_op jit(solution)/shard_map/ppermute | solution.py:51
  384.8 15.3 %collective-permute-done.42 = f32[2,256,128]{2,1,0:T(8,128)S(1)} collective-permute-done((f32[2,256,128]{2,1,0:T(8,128)S(1)}, f32[2,256,128]{2,1,0:T(8,128)S(1)}, u32[]{:S(2)}, u32[]{:S(2)}) %collective-permute-start.42) | collective-permute-done | bytes 262176 | tf_op jit(solution)/shard_map/ppermute | solution.py:51
  400.2 5.4 %collective-permute-done.44 = f32[2,256,128]{2,1,0:T(8,128)S(1)} collective-permute-done((f32[2,256,128]{2,1,0:T(8,128)S(1)}, f32[2,256,128]{2,1,0:T(8,128)S(1)}, u32[]{:S(2)}, u32[]{:S(2)}) %collective-permute-start.44) | collective-permute-done | bytes 262176 | tf_op jit(solution)/shard_map/ppermute | solution.py:51
  406.1 5.4 %collective-permute-start.45 = (f32[2,128,128]{2,1,0:T(8,128)S(1)}, f32[2,128,128]{2,1,0:T(8,128)S(1)}, u32[]{:S(2)}, u32[]{:S(2)}) collective-permute-start(f32[2,128,128]{2,1,0:T(8,128)S(1)} %convolution_add_fusion.3), channel_id=1, source_target_pairs={{0,16},{16,0},{32,48},{48,32},{64,80},{80,64},{96,112},{112,96},{1... | collective-permute-start | bytes 393224 | tf_op jit(solution)/shard_map/ppermute | solution.py:51
  417.7 7.7 %collective-permute-done.46 = f32[2,128,128]{2,1,0:T(8,128)S(1)} collective-permute-done((f32[2,128,128]{2,1,0:T(8,128)S(1)}, f32[2,128,128]{2,1,0:T(8,128)S(1)}, u32[]{:S(2)}, u32[]{:S(2)}) %collective-permute-start.46) | collective-permute-done | bytes 131104 | tf_op jit(solution)/shard_map/ppermute | solution.py:51
  440.6 7.3 %collective-permute-start.51 = (f32[2,128,128]{2,1,0:T(8,128)S(1)}, f32[2,128,128]{2,1,0:T(8,128)S(1)}, u32[]{:S(2)}, u32[]{:S(2)}) collective-permute-start(f32[2,128,128]{2,1,0:T(8,128)S(1)} %fusion.156), channel_id=1, source_target_pairs={{0,64},{16,80},{32,96},{48,112},{64,0},{80,16},{96,32},{112,48},{1... | collective-permute-start | bytes 393224 | tf_op jit(solution)/shard_map/ppermute | solution.py:51
  (206 shorter events, 181.9 us)
Async XLA Ops:
  18.1 23.2 %collective-permute-start.1 = (f32[1552,128]{1,0:T(8,128)}, f32[1552,128]{1,0:T(8,128)}, u32[]{:S(2)}, u32[]{:S(2)}) collective-permute-start(f32[1552,128]{1,0:T(8,128)} %get-tuple-element.37), channel_id=1, source_target_pairs={{0,2},{1,3},{2,0},{3,1},{4,6},{5,7},{6,4},{7,5},{8,10},{9,11},{10,... | collective-permute-start | bytes 2383880 | tf_op jit(solution)/shard_map/ppermute | solution.py:172
  22.4 35.5 %collective-permute-start.2 = (f32[1552,128]{1,0:T(8,128)S(1)}, f32[1552,128]{1,0:T(8,128)}, u32[]{:S(2)}, u32[]{:S(2)}) collective-permute-start(f32[1552,128]{1,0:T(8,128)S(1)} %get-tuple-element.38), channel_id=1, source_target_pairs={{0,3},{1,2},{2,1},{3,0},{4,7},{5,6},{6,5},{7,4},{8,11},{9,10},{10,... | collective-permute-start | bytes 2383880 | tf_op jit(solution)/shard_map/ppermute | solution.py:172
  62.1 41.6 %collective-permute-start.3 = (f32[784,128]{1,0:T(8,128)S(1)}, f32[784,128]{1,0:T(8,128)S(1)}, u32[]{:S(2)}, u32[]{:S(2)}) collective-permute-start(f32[784,128]{1,0:T(8,128)S(1)} %get-tuple-element.31), channel_id=1, source_target_pairs={{0,4},{1,5},{2,6},{3,7},{4,0},{5,1},{6,2},{7,3},{8,12},{9,13},{10,... | collective-permute-start | bytes 1204232 | tf_op jit(solution)/shard_map/ppermute | solution.py:172
  68.2 41.7 %collective-permute-start.4 = (f32[784,128]{1,0:T(8,128)S(1)}, f32[784,128]{1,0:T(8,128)S(1)}, u32[]{:S(2)}, u32[]{:S(2)}) collective-permute-start(f32[784,128]{1,0:T(8,128)S(1)} %get-tuple-element.32), channel_id=1, source_target_pairs={{0,8},{1,9},{2,10},{3,11},{4,12},{5,13},{6,14},{7,15},{8,0},{9,1},... | collective-permute-start | bytes 1204232 | tf_op jit(solution)/shard_map/ppermute | solution.py:172
  76.4 35.5 %collective-permute-start.5 = (f32[784,128]{1,0:T(8,128)S(1)}, f32[784,128]{1,0:T(8,128)}, u32[]{:S(2)}, u32[]{:S(2)}) collective-permute-start(f32[784,128]{1,0:T(8,128)S(1)} %get-tuple-element.33), channel_id=1, source_target_pairs={{0,12},{1,13},{2,14},{3,15},{4,8},{5,9},{6,10},{7,11},{8,4},{9,5},... | collective-permute-start | bytes 1204232 | tf_op jit(solution)/shard_map/ppermute | solution.py:172
  118.8 14.0 %collective-permute-start.7 = (f32[2,128,128]{2,1,0:T(8,128)S(1)}, f32[2,128,128]{2,1,0:T(8,128)S(1)}, u32[]{:S(2)}, u32[]{:S(2)}) collective-permute-start(f32[2,128,128]{2,1,0:T(8,128)S(1)} %fusion.64), channel_id=1, source_target_pairs={{0,32},{16,48},{32,0},{48,16},{64,96},{80,112},{96,64},{112,80},{1... | collective-permute-start | bytes 393224 | tf_op jit(solution)/shard_map/ppermute | solution.py:51
  146.9 10.9 %collective-permute-start.12 = (f32[2,128,128]{2,1,0:T(8,128)S(1)}, f32[2,128,128]{2,1,0:T(8,128)S(1)}, u32[]{:S(2)}, u32[]{:S(2)}) collective-permute-start(f32[2,128,128]{2,1,0:T(8,128)S(1)} %fusion.168), channel_id=1, source_target_pairs={{0,64},{16,80},{32,96},{48,112},{64,0},{80,16},{96,32},{112,48},{1... | collective-permute-start | bytes 393224 | tf_op jit(solution)/shard_map/ppermute | solution.py:51
  160.2 11.1 %collective-permute-start.14 = (f32[2,256,128]{2,1,0:T(8,128)S(1)}, f32[2,256,128]{2,1,0:T(8,128)S(1)}, u32[]{:S(2)}, u32[]{:S(2)}) collective-permute-start(f32[2,256,128]{2,1,0:T(8,128)S(1)} %convolution_add_fusion.2), channel_id=1, source_target_pairs={{0,2},{1,3},{2,0},{3,1},{4,6},{5,7},{6,4},{7,5},{8,10},{9,11},{10,... | collective-permute-start | bytes 786440 | tf_op jit(solution)/shard_map/ppermute | solution.py:51
  162.1 13.8 %collective-permute-start.15 = (f32[2,256,128]{2,1,0:T(8,128)S(1)}, f32[2,256,128]{2,1,0:T(8,128)S(1)}, u32[]{:S(2)}, u32[]{:S(2)}) collective-permute-start(f32[2,256,128]{2,1,0:T(8,128)S(1)} %convolution_add_fusion.2), channel_id=1, source_target_pairs={{0,3},{1,2},{2,1},{3,0},{4,7},{5,6},{6,5},{7,4},{8,11},{9,10},{10,... | collective-permute-start | bytes 786440 | tf_op jit(solution)/shard_map/ppermute | solution.py:51
  176.1 28.0 %collective-permute-start.16 = (f32[2,256,128]{2,1,0:T(8,128)S(1)}, f32[2,256,128]{2,1,0:T(8,128)S(1)}, u32[]{:S(2)}, u32[]{:S(2)}) collective-permute-start(f32[2,256,128]{2,1,0:T(8,128)S(1)} %fusion.167), channel_id=1, source_target_pairs={{0,4},{1,5},{2,6},{3,7},{4,0},{5,1},{6,2},{7,3},{8,12},{9,13},{10,... | collective-permute-start | bytes 786440 | tf_op jit(solution)/shard_map/ppermute | solution.py:51
  179.4 24.7 %collective-permute-start.17 = (f32[2,256,128]{2,1,0:T(8,128)S(1)}, f32[2,256,128]{2,1,0:T(8,128)S(1)}, u32[]{:S(2)}, u32[]{:S(2)}) collective-permute-start(f32[2,256,128]{2,1,0:T(8,128)S(1)} %fusion.167), channel_id=1, source_target_pairs={{0,8},{1,9},{2,10},{3,11},{4,12},{5,13},{6,14},{7,15},{8,0},{9,1},... | collective-permute-start | bytes 786440 | tf_op jit(solution)/shard_map/ppermute | solution.py:51
  187.0 22.4 %collective-permute-start.18 = (f32[2,256,128]{2,1,0:T(8,128)S(1)}, f32[2,256,128]{2,1,0:T(8,128)S(1)}, u32[]{:S(2)}, u32[]{:S(2)}) collective-permute-start(f32[2,256,128]{2,1,0:T(8,128)S(1)} %fusion.167), channel_id=1, source_target_pairs={{0,12},{1,13},{2,14},{3,15},{4,8},{5,9},{6,10},{7,11},{8,4},{9,5},... | collective-permute-start | bytes 786440 | tf_op jit(solution)/shard_map/ppermute | solution.py:51
  210.0 12.3 %collective-permute-start.19 = (f32[2,128,128]{2,1,0:T(8,128)S(1)}, f32[2,128,128]{2,1,0:T(8,128)S(1)}, u32[]{:S(2)}, u32[]{:S(2)}) collective-permute-start(f32[2,128,128]{2,1,0:T(8,128)S(1)} %convolution_add_fusion.5), channel_id=1, source_target_pairs={{0,16},{16,0},{32,48},{48,32},{64,80},{80,64},{96,112},{112,96},{1... | collective-permute-start | bytes 393224 | tf_op jit(solution)/shard_map/ppermute | solution.py:51
  216.0 13.2 %collective-permute-start.20 = (f32[2,128,128]{2,1,0:T(8,128)S(1)}, f32[2,128,128]{2,1,0:T(8,128)S(1)}, u32[]{:S(2)}, u32[]{:S(2)}) collective-permute-start(f32[2,128,128]{2,1,0:T(8,128)S(1)} %convolution_add_fusion.5), channel_id=1, source_target_pairs={{0,32},{16,48},{32,0},{48,16},{64,96},{80,112},{96,64},{112,80},{1... | collective-permute-start | bytes 393224 | tf_op jit(solution)/shard_map/ppermute | solution.py:51
  218.2 11.0 %collective-permute-start.21 = (f32[2,128,128]{2,1,0:T(8,128)S(1)}, f32[2,128,128]{2,1,0:T(8,128)S(1)}, u32[]{:S(2)}, u32[]{:S(2)}) collective-permute-start(f32[2,128,128]{2,1,0:T(8,128)S(1)} %convolution_add_fusion.5), channel_id=1, source_target_pairs={{0,48},{16,32},{32,16},{48,0},{64,112},{80,96},{96,80},{112,64},{1... | collective-permute-start | bytes 393224 | tf_op jit(solution)/shard_map/ppermute | solution.py:51
  258.4 11.1 %collective-permute-start.27 = (f32[2,256,128]{2,1,0:T(8,128)S(1)}, f32[2,256,128]{2,1,0:T(8,128)S(1)}, u32[]{:S(2)}, u32[]{:S(2)}) collective-permute-start(f32[2,256,128]{2,1,0:T(8,128)S(1)} %convolution_add_fusion.1), channel_id=1, source_target_pairs={{0,2},{1,3},{2,0},{3,1},{4,6},{5,7},{6,4},{7,5},{8,10},{9,11},{10,... | collective-permute-start | bytes 786440 | tf_op jit(solution)/shard_map/ppermute | solution.py:51
  262.3 12.3 %collective-permute-start.28 = (f32[2,256,128]{2,1,0:T(8,128)S(1)}, f32[2,256,128]{2,1,0:T(8,128)S(1)}, u32[]{:S(2)}, u32[]{:S(2)}) collective-permute-start(f32[2,256,128]{2,1,0:T(8,128)S(1)} %convolution_add_fusion.1), channel_id=1, source_target_pairs={{0,3},{1,2},{2,1},{3,0},{4,7},{5,6},{6,5},{7,4},{8,11},{9,10},{10,... | collective-permute-start | bytes 786440 | tf_op jit(solution)/shard_map/ppermute | solution.py:51
  274.8 28.0 %collective-permute-start.29 = (f32[2,256,128]{2,1,0:T(8,128)S(1)}, f32[2,256,128]{2,1,0:T(8,128)S(1)}, u32[]{:S(2)}, u32[]{:S(2)}) collective-permute-start(f32[2,256,128]{2,1,0:T(8,128)S(1)} %fusion.163), channel_id=1, source_target_pairs={{0,4},{1,5},{2,6},{3,7},{4,0},{5,1},{6,2},{7,3},{8,12},{9,13},{10,... | collective-permute-start | bytes 786440 | tf_op jit(solution)/shard_map/ppermute | solution.py:51
  277.0 25.7 %collective-permute-start.30 = (f32[2,256,128]{2,1,0:T(8,128)S(1)}, f32[2,256,128]{2,1,0:T(8,128)S(1)}, u32[]{:S(2)}, u32[]{:S(2)}) collective-permute-start(f32[2,256,128]{2,1,0:T(8,128)S(1)} %fusion.163), channel_id=1, source_target_pairs={{0,8},{1,9},{2,10},{3,11},{4,12},{5,13},{6,14},{7,15},{8,0},{9,1},... | collective-permute-start | bytes 786440 | tf_op jit(solution)/shard_map/ppermute | solution.py:51
  285.2 22.5 %collective-permute-start.31 = (f32[2,256,128]{2,1,0:T(8,128)S(1)}, f32[2,256,128]{2,1,0:T(8,128)S(1)}, u32[]{:S(2)}, u32[]{:S(2)}) collective-permute-start(f32[2,256,128]{2,1,0:T(8,128)S(1)} %fusion.163), channel_id=1, source_target_pairs={{0,12},{1,13},{2,14},{3,15},{4,8},{5,9},{6,10},{7,11},{8,4},{9,5},... | collective-permute-start | bytes 786440 | tf_op jit(solution)/shard_map/ppermute | solution.py:51
  308.2 12.3 %collective-permute-start.32 = (f32[2,128,128]{2,1,0:T(8,128)S(1)}, f32[2,128,128]{2,1,0:T(8,128)S(1)}, u32[]{:S(2)}, u32[]{:S(2)}) collective-permute-start(f32[2,128,128]{2,1,0:T(8,128)S(1)} %convolution_add_fusion.4), channel_id=1, source_target_pairs={{0,16},{16,0},{32,48},{48,32},{64,80},{80,64},{96,112},{112,96},{1... | collective-permute-start | bytes 393224 | tf_op jit(solution)/shard_map/ppermute | solution.py:51
  314.1 13.4 %collective-permute-start.33 = (f32[2,128,128]{2,1,0:T(8,128)S(1)}, f32[2,128,128]{2,1,0:T(8,128)S(1)}, u32[]{:S(2)}, u32[]{:S(2)}) collective-permute-start(f32[2,128,128]{2,1,0:T(8,128)S(1)} %convolution_add_fusion.4), channel_id=1, source_target_pairs={{0,32},{16,48},{32,0},{48,16},{64,96},{80,112},{96,64},{112,80},{1... | collective-permute-start | bytes 393224 | tf_op jit(solution)/shard_map/ppermute | solution.py:51
  316.2 11.2 %collective-permute-start.34 = (f32[2,128,128]{2,1,0:T(8,128)S(1)}, f32[2,128,128]{2,1,0:T(8,128)S(1)}, u32[]{:S(2)}, u32[]{:S(2)}) collective-permute-start(f32[2,128,128]{2,1,0:T(8,128)S(1)} %convolution_add_fusion.4), channel_id=1, source_target_pairs={{0,48},{16,32},{32,16},{48,0},{64,112},{80,96},{96,80},{112,64},{1... | collective-permute-start | bytes 393224 | tf_op jit(solution)/shard_map/ppermute | solution.py:51
  342.0 10.9 %collective-permute-start.38 = (f32[2,128,128]{2,1,0:T(8,128)S(1)}, f32[2,128,128]{2,1,0:T(8,128)S(1)}, u32[]{:S(2)}, u32[]{:S(2)}) collective-permute-start(f32[2,128,128]{2,1,0:T(8,128)S(1)} %fusion.160), channel_id=1, source_target_pairs={{0,64},{16,80},{32,96},{48,112},{64,0},{80,16},{96,32},{112,48},{1... | collective-permute-start | bytes 393224 | tf_op jit(solution)/shard_map/ppermute | solution.py:51
  356.0 11.1 %collective-permute-start.40 = (f32[2,256,128]{2,1,0:T(8,128)S(1)}, f32[2,256,128]{2,1,0:T(8,128)S(1)}, u32[]{:S(2)}, u32[]{:S(2)}) collective-permute-start(f32[2,256,128]{2,1,0:T(8,128)S(1)} %convolution_add_fusion), channel_id=1, source_target_pairs={{0,2},{1,3},{2,0},{3,1},{4,6},{5,7},{6,4},{7,5},{8,10},{9,11},{10,... | collective-permute-start | bytes 786440 | tf_op jit(solution)/shard_map/ppermute | solution.py:51
  359.1 12.7 %collective-permute-start.41 = (f32[2,256,128]{2,1,0:T(8,128)S(1)}, f32[2,256,128]{2,1,0:T(8,128)S(1)}, u32[]{:S(2)}, u32[]{:S(2)}) collective-permute-start(f32[2,256,128]{2,1,0:T(8,128)S(1)} %convolution_add_fusion), channel_id=1, source_target_pairs={{0,3},{1,2},{2,1},{3,0},{4,7},{5,6},{6,5},{7,4},{8,11},{9,10},{10,... | collective-permute-start | bytes 786440 | tf_op jit(solution)/shard_map/ppermute | solution.py:51
  371.9 28.3 %collective-permute-start.42 = (f32[2,256,128]{2,1,0:T(8,128)S(1)}, f32[2,256,128]{2,1,0:T(8,128)S(1)}, u32[]{:S(2)}, u32[]{:S(2)}) collective-permute-start(f32[2,256,128]{2,1,0:T(8,128)S(1)} %fusion.159), channel_id=1, source_target_pairs={{0,4},{1,5},{2,6},{3,7},{4,0},{5,1},{6,2},{7,3},{8,12},{9,13},{10,... | collective-permute-start | bytes 786440 | tf_op jit(solution)/shard_map/ppermute | solution.py:51
  375.4 24.7 %collective-permute-start.43 = (f32[2,256,128]{2,1,0:T(8,128)S(1)}, f32[2,256,128]{2,1,0:T(8,128)S(1)}, u32[]{:S(2)}, u32[]{:S(2)}) collective-permute-start(f32[2,256,128]{2,1,0:T(8,128)S(1)} %fusion.159), channel_id=1, source_target_pairs={{0,8},{1,9},{2,10},{3,11},{4,12},{5,13},{6,14},{7,15},{8,0},{9,1},... | collective-permute-start | bytes 786440 | tf_op jit(solution)/shard_map/ppermute | solution.py:51
  382.8 22.7 %collective-permute-start.44 = (f32[2,256,128]{2,1,0:T(8,128)S(1)}, f32[2,256,128]{2,1,0:T(8,128)S(1)}, u32[]{:S(2)}, u32[]{:S(2)}) collective-permute-start(f32[2,256,128]{2,1,0:T(8,128)S(1)} %fusion.159), channel_id=1, source_target_pairs={{0,12},{1,13},{2,14},{3,15},{4,8},{5,9},{6,10},{7,11},{8,4},{9,5},... | collective-permute-start | bytes 786440 | tf_op jit(solution)/shard_map/ppermute | solution.py:51
  406.1 11.6 %collective-permute-start.45 = (f32[2,128,128]{2,1,0:T(8,128)S(1)}, f32[2,128,128]{2,1,0:T(8,128)S(1)}, u32[]{:S(2)}, u32[]{:S(2)}) collective-permute-start(f32[2,128,128]{2,1,0:T(8,128)S(1)} %convolution_add_fusion.3), channel_id=1, source_target_pairs={{0,16},{16,0},{32,48},{48,32},{64,80},{80,64},{96,112},{112,96},{1... | collective-permute-start | bytes 393224 | tf_op jit(solution)/shard_map/ppermute | solution.py:51
  411.5 14.0 %collective-permute-start.46 = (f32[2,128,128]{2,1,0:T(8,128)S(1)}, f32[2,128,128]{2,1,0:T(8,128)S(1)}, u32[]{:S(2)}, u32[]{:S(2)}) collective-permute-start(f32[2,128,128]{2,1,0:T(8,128)S(1)} %convolution_add_fusion.3), channel_id=1, source_target_pairs={{0,32},{16,48},{32,0},{48,16},{64,96},{80,112},{96,64},{112,80},{1... | collective-permute-start | bytes 393224 | tf_op jit(solution)/shard_map/ppermute | solution.py:51
  414.3 11.1 %collective-permute-start.47 = (f32[2,128,128]{2,1,0:T(8,128)S(1)}, f32[2,128,128]{2,1,0:T(8,128)S(1)}, u32[]{:S(2)}, u32[]{:S(2)}) collective-permute-start(f32[2,128,128]{2,1,0:T(8,128)S(1)} %convolution_add_fusion.3), channel_id=1, source_target_pairs={{0,48},{16,32},{32,16},{48,0},{64,112},{80,96},{96,80},{112,64},{1... | collective-permute-start | bytes 393224 | tf_op jit(solution)/shard_map/ppermute | solution.py:51
  (26 other events, 191.1 us)

commit v5 on v2

--- a/solution.py
+++ b/solution.py
@@ -39,13 +39,55 @@
     ]
 
 
-def group_sum(value, axis):
-    for stride, radix in digit_groups(lax.axis_size(axis)):
-        members = gather_group(value, axis, stride, radix)
+def gather_bits(value, axis, bits):
+    size = lax.axis_size(axis)
+    me = lax.axis_index(axis)
+    digit = sum(((me >> b) & 1) << t for t, b in enumerate(bits))
+    radix = 1 << len(bits)
+    got = [value]
+    for k in range(1, radix):
+        mask = sum(((k >> t) & 1) << b for t, b in enumerate(bits))
+        pairs = [(s, s ^ mask) for s in range(size)]
+        got.append(lax.ppermute(value, axis, pairs))
+    stacked = jnp.stack(got)
+    return [lax.dynamic_index_in_dim(stacked, digit ^ g, 0, False) for g in range(radix)]
+
+
+def sum_over_bits(value, axis, stages):
+    for bits in stages:
+        members = gather_bits(value, axis, bits)
         value = members[0]
         for other in members[1:]:
             value = value + other
     return value
+
+
+def bit_stages(bits):
+    return [bits[b : b + 2] for b in range(0, len(bits), 2)]
+
+
+def group_sum(value, axis):
+    count = lax.axis_size(axis).bit_length() - 1
+    if count == 5:
+        return sum_over_bits(value, axis, [[0, 1], [3, 4], [2]])
+    return sum_over_bits(value, axis, bit_stages(list(range(count))))
+
+
+def pair_split_sum(value, axis, split_axis):
+    count = lax.axis_size(axis).bit_length() - 1
+    value = sum_over_bits(value, axis, [[0]])
+    half = value.shape[split_axis] // 2
+    low = (lax.axis_index(axis) & 1) == 0
+    first = lax.slice_in_dim(value, 0, half, axis=split_axis)
+    second = lax.slice_in_dim(value, half, 2 * half, axis=split_axis)
+    mine = jnp.where(low, first, second)
+    mine = sum_over_bits(mine, axis, bit_stages(list(range(1, count))))
+    other = lax.ppermute(
+        mine, axis, [(s, s ^ 1) for s in range(lax.axis_size(axis))]
+    )
+    return jnp.concatenate(
+        [jnp.where(low, mine, other), jnp.where(low, other, mine)], axis=split_axis
+    )
 
 
 def scatter_groups(blocks, axis):
@@ -154,7 +196,7 @@
     rhs = group_sum(rhs_part, "pb") * weighting
 
     def gram_times(vec):
-        across = group_sum(split_dot("hqa,had->hqd", probs, vec), "kv")
+        across = pair_split_sum(split_dot("hqa,had->hqd", probs, vec), "kv", 1)
         back = group_sum(split_dot("hqa,hqd->had", probs, across), "pb")
         return back * weighting + ridge_weight * vec
 

time: 431 us -> 382 us (0.89)
  the two profiles are of different devices: /device:TPU:6 before, /device:TPU:107 now
where the time goes in v5:
time: 382 us; the launch traced here: 380 us
  starting transfers between devices  184 us (48%)
  waiting for transfers between devices  172 us (45%)
  other arithmetic  10.6 us (3%)
  matrix products  9.26 us (2%)
    ppermute x43, waiting for transfers between devices, gather_bits(): got.append(lax.ppermute(value, axis, pairs))  157 us
    ppermute x43, starting transfers between devices, gather_bits(): got.append(lax.ppermute(value, axis, pairs))  128 us
    ppermute x6, starting transfers between devices, scatter_groups(): total = total + lax.ppermute(give, axis, pairs)  25.3 us
    ppermute x6, starting transfers between devices, gather_group(): got.append(jax.tree.map(lambda a: lax.ppermute(a, axis, pairs), value))  23.7 us
    ppermute x6, waiting for transfers between devices, gather_group(): got.append(jax.tree.map(lambda a: lax.ppermute(a, axis, pairs), value))  11.5 us
  transfers between devices with their start and end apart: 58, of which 38 were waited for; matrix products, arithmetic and copies ran while one was open for 2% of the time, Pallas kernels for 0%

profile of v5, /device:TPU:107, one launch (start us, length us, event | category | flops | bytes accessed | tf_op | source)
XLA Modules:
  0.0 380.3 jit_solution(12132321493691000977)
XLA Ops:
  31.4 5.8 %collective-permute-start.9 = (f32[2,264,128]{2,1,0:T(8,128)S(1)}, f32[2,264,128]{2,1,0:T(8,128)S(1)}, u32[]{:S(2)}, u32[]{:S(2)}) collective-permute-start(f32[2,264,128]{2,1,0:T(8,128)S(1)} %get-tuple-element.30), channel_id=1, source_target_pairs={{0,4},{1,5},{2,6},{3,7},{4,0},{5,1},{6,2},{7,3},{8,12},{9,13},{10,... | collective-permute-start | bytes 811016 | tf_op jit(solution)/shard_map/ppermute | solution.py:34
  37.2 7.9 %collective-permute-start.10 = (f32[2,264,128]{2,1,0:T(8,128)S(1)}, f32[2,264,128]{2,1,0:T(8,128)S(1)}, u32[]{:S(2)}, u32[]{:S(2)}) collective-permute-start(f32[2,264,128]{2,1,0:T(8,128)S(1)} %get-tuple-element.30), channel_id=1, source_target_pairs={{0,8},{1,9},{2,10},{3,11},{4,12},{5,13},{6,14},{7,15},{8,0},{9,1},... | collective-permute-start | bytes 811016 | tf_op jit(solution)/shard_map/ppermute | solution.py:34
  49.4 7.3 %collective-permute-start.4 = (bf16[1,2,128,128]{3,2,1,0:T(8,128)(2,1)S(1)}, bf16[1,2,128,128]{3,2,1,0:T(8,128)(2,1)S(1)}, u32[]{:S(2)}, u32[]{:S(2)}) collective-permute-start(bf16[1,2,128,128]{3,2,1,0:T(8,128)(2,1)S(1)} %get-tuple-element.41), channel_id=1, source_target_pairs={{0,8},{1,9},{2,10},{3,11},{4,12},{5,13},{6,14},{7,15},{8,0},{9,1},... | collective-permute-start | bytes 196616 | tf_op jit(solution)/shard_map/ppermute | solution.py:104
  56.7 6.8 %collective-permute-done.9 = f32[2,264,128]{2,1,0:T(8,128)S(1)} collective-permute-done((f32[2,264,128]{2,1,0:T(8,128)S(1)}, f32[2,264,128]{2,1,0:T(8,128)S(1)}, u32[]{:S(2)}, u32[]{:S(2)}) %collective-permute-start.9) | collective-permute-done | bytes 270368 | tf_op jit(solution)/shard_map/ppermute | solution.py:34
  63.4 8.0 %collective-permute-start.5 = (bf16[1,2,128,128]{3,2,1,0:T(8,128)(2,1)S(1)}, bf16[1,2,128,128]{3,2,1,0:T(8,128)(2,1)S(1)}, u32[]{:S(2)}, u32[]{:S(2)}) collective-permute-start(bf16[1,2,128,128]{3,2,1,0:T(8,128)(2,1)S(1)} %get-tuple-element.40), channel_id=1, source_target_pairs={{0,12},{1,13},{2,14},{3,15},{4,8},{5,9},{6,10},{7,11},{8,4},{9,5},... | collective-permute-start | bytes 196616 | tf_op jit(solution)/shard_map/ppermute | solution.py:104
  71.5 4.7 %collective-permute-done.11 = f32[2,264,128]{2,1,0:T(8,128)S(1)} collective-permute-done((f32[2,264,128]{2,1,0:T(8,128)S(1)}, f32[2,264,128]{2,1,0:T(8,128)S(1)}, u32[]{:S(2)}, u32[]{:S(2)}) %collective-permute-start.11) | collective-permute-done | bytes 270368 | tf_op jit(solution)/shard_map/ppermute | solution.py:34
  89.4 7.3 %collective-permute-done.14 = f32[2,128,128]{2,1,0:T(8,128)S(1)} collective-permute-done((f32[2,128,128]{2,1,0:T(8,128)S(1)}, f32[2,128,128]{2,1,0:T(8,128)S(1)}, u32[]{:S(2)}, u32[]{:S(2)}) %collective-permute-start.14) | collective-permute-done | bytes 131104 | tf_op jit(solution)/shard_map/ppermute | solution.py:51
  112.9 6.5 %collective-permute-done.18 = f32[2,128,128]{2,1,0:T(8,128)S(1)} collective-permute-done((f32[2,128,128]{2,1,0:T(8,128)S(1)}, f32[2,128,128]{2,1,0:T(8,128)S(1)}, u32[]{:S(2)}, u32[]{:S(2)}) %collective-permute-start.18) | collective-permute-done | bytes 131104 | tf_op jit(solution)/shard_map/ppermute | solution.py:51
  120.0 6.2 %collective-permute-start.19 = (f32[2,256,128]{2,1,0:T(8,128)S(1)}, f32[2,256,128]{2,1,0:T(8,128)S(1)}, u32[]{:S(2)}, u32[]{:S(2)}) collective-permute-start(f32[2,256,128]{2,1,0:T(8,128)S(1)} %convolution_add_fusion.2), channel_id=1, source_target_pairs={{0,1},{1,0},{2,3},{3,2},{4,5},{5,4},{6,7},{7,6},{8,9},{9,8},{10,11... | collective-permute-start | bytes 786440 | tf_op jit(solution)/shard_map/ppermute | solution.py:51
  129.5 4.2 %collective-permute-start.21 = (f32[2,128,128]{2,1,0:T(8,128)S(1)}, f32[2,128,128]{2,1,0:T(8,128)S(1)}, u32[]{:S(2)}, u32[]{:S(2)}) collective-permute-start(f32[2,128,128]{2,1,0:T(8,128)S(1)} %slice_select_fusion.2), channel_id=1, source_target_pairs={{0,4},{1,5},{2,6},{3,7},{4,0},{5,1},{6,2},{7,3},{8,12},{9,13},{10,... | collective-permute-start | bytes 393224 | tf_op jit(solution)/shard_map/ppermute | solution.py:51
  136.0 6.3 %collective-permute-done.21 = f32[2,128,128]{2,1,0:T(8,128)S(1)} collective-permute-done((f32[2,128,128]{2,1,0:T(8,128)S(1)}, f32[2,128,128]{2,1,0:T(8,128)S(1)}, u32[]{:S(2)}, u32[]{:S(2)}) %collective-permute-start.21) | collective-permute-done | bytes 131104 | tf_op jit(solution)/shard_map/ppermute | solution.py:51
  145.9 5.1 %collective-permute-start.23 = (f32[2,128,128]{2,1,0:T(8,128)S(1)}, f32[2,128,128]{2,1,0:T(8,128)S(1)}, u32[]{:S(2)}, u32[]{:S(2)}) collective-permute-start(f32[2,128,128]{2,1,0:T(8,128)S(1)} %fusion.181), channel_id=1, source_target_pairs={{0,8},{1,9},{2,10},{3,11},{4,12},{5,13},{6,14},{7,15},{8,0},{9,1},... | collective-permute-start | bytes 393224 | tf_op jit(solution)/shard_map/ppermute | solution.py:51
  151.0 8.1 %collective-permute-done.23 = f32[2,128,128]{2,1,0:T(8,128)S(1)} collective-permute-done((f32[2,128,128]{2,1,0:T(8,128)S(1)}, f32[2,128,128]{2,1,0:T(8,128)S(1)}, u32[]{:S(2)}, u32[]{:S(2)}) %collective-permute-start.23) | collective-permute-done | bytes 131104 | tf_op jit(solution)/shard_map/ppermute | solution.py:51
  171.4 5.3 %collective-permute-done.26 = f32[2,128,128]{2,1,0:T(8,128)S(1)} collective-permute-done((f32[2,128,128]{2,1,0:T(8,128)S(1)}, f32[2,128,128]{2,1,0:T(8,128)S(1)}, u32[]{:S(2)}, u32[]{:S(2)}) %collective-permute-start.26) | collective-permute-done | bytes 131104 | tf_op jit(solution)/shard_map/ppermute | solution.py:51
  176.7 5.0 %collective-permute-done.27 = f32[2,128,128]{2,1,0:T(8,128)S(1)} collective-permute-done((f32[2,128,128]{2,1,0:T(8,128)S(1)}, f32[2,128,128]{2,1,0:T(8,128)S(1)}, u32[]{:S(2)}, u32[]{:S(2)}) %collective-permute-start.27) | collective-permute-done | bytes 131104 | tf_op jit(solution)/shard_map/ppermute | solution.py:51
  192.9 4.3 %collective-permute-done.30 = f32[2,128,128]{2,1,0:T(8,128)S(1)} collective-permute-done((f32[2,128,128]{2,1,0:T(8,128)S(1)}, f32[2,128,128]{2,1,0:T(8,128)S(1)}, u32[]{:S(2)}, u32[]{:S(2)}) %collective-permute-start.30) | collective-permute-done | bytes 131104 | tf_op jit(solution)/shard_map/ppermute | solution.py:51
  200.2 9.4 %collective-permute-done.31 = f32[2,128,128]{2,1,0:T(8,128)S(1)} collective-permute-done((f32[2,128,128]{2,1,0:T(8,128)S(1)}, f32[2,128,128]{2,1,0:T(8,128)S(1)}, u32[]{:S(2)}, u32[]{:S(2)}) %collective-permute-start.31) | collective-permute-done | bytes 131104 | tf_op jit(solution)/shard_map/ppermute | solution.py:51
  222.3 5.3 %collective-permute-done.34 = f32[2,128,128]{2,1,0:T(8,128)S(1)} collective-permute-done((f32[2,128,128]{2,1,0:T(8,128)S(1)}, f32[2,128,128]{2,1,0:T(8,128)S(1)}, u32[]{:S(2)}, u32[]{:S(2)}) %collective-permute-start.34) | collective-permute-done | bytes 131104 | tf_op jit(solution)/shard_map/ppermute | solution.py:51
  227.6 4.9 %collective-permute-done.35 = f32[2,128,128]{2,1,0:T(8,128)S(1)} collective-permute-done((f32[2,128,128]{2,1,0:T(8,128)S(1)}, f32[2,128,128]{2,1,0:T(8,128)S(1)}, u32[]{:S(2)}, u32[]{:S(2)}) %collective-permute-start.35) | collective-permute-done | bytes 131104 | tf_op jit(solution)/shard_map/ppermute | solution.py:51
  236.4 8.8 %collective-permute-done.36 = f32[2,128,128]{2,1,0:T(8,128)S(1)} collective-permute-done((f32[2,128,128]{2,1,0:T(8,128)S(1)}, f32[2,128,128]{2,1,0:T(8,128)S(1)}, u32[]{:S(2)}, u32[]{:S(2)}) %collective-permute-start.36) | collective-permute-done | bytes 131104 | tf_op jit(solution)/shard_map/ppermute | solution.py:51
  257.4 5.4 %collective-permute-done.39 = f32[2,128,128]{2,1,0:T(8,128)S(1)} collective-permute-done((f32[2,128,128]{2,1,0:T(8,128)S(1)}, f32[2,128,128]{2,1,0:T(8,128)S(1)}, u32[]{:S(2)}, u32[]{:S(2)}) %collective-permute-start.39) | collective-permute-done | bytes 131104 | tf_op jit(solution)/shard_map/ppermute | solution.py:51
  262.8 4.8 %collective-permute-done.40 = f32[2,128,128]{2,1,0:T(8,128)S(1)} collective-permute-done((f32[2,128,128]{2,1,0:T(8,128)S(1)}, f32[2,128,128]{2,1,0:T(8,128)S(1)}, u32[]{:S(2)}, u32[]{:S(2)}) %collective-permute-start.40) | collective-permute-done | bytes 131104 | tf_op jit(solution)/shard_map/ppermute | solution.py:51
  276.8 4.1 %collective-permute-done.43 = f32[2,128,128]{2,1,0:T(8,128)S(1)} collective-permute-done((f32[2,128,128]{2,1,0:T(8,128)S(1)}, f32[2,128,128]{2,1,0:T(8,128)S(1)}, u32[]{:S(2)}, u32[]{:S(2)}) %collective-permute-start.43) | collective-permute-done | bytes 131104 | tf_op jit(solution)/shard_map/ppermute | solution.py:51
  283.8 10.1 %collective-permute-done.44 = f32[2,128,128]{2,1,0:T(8,128)S(1)} collective-permute-done((f32[2,128,128]{2,1,0:T(8,128)S(1)}, f32[2,128,128]{2,1,0:T(8,128)S(1)}, u32[]{:S(2)}, u32[]{:S(2)}) %collective-permute-start.44) | collective-permute-done | bytes 131104 | tf_op jit(solution)/shard_map/ppermute | solution.py:51
  307.3 5.6 %collective-permute-done.47 = f32[2,128,128]{2,1,0:T(8,128)S(1)} collective-permute-done((f32[2,128,128]{2,1,0:T(8,128)S(1)}, f32[2,128,128]{2,1,0:T(8,128)S(1)}, u32[]{:S(2)}, u32[]{:S(2)}) %collective-permute-start.47) | collective-permute-done | bytes 131104 | tf_op jit(solution)/shard_map/ppermute | solution.py:51
  312.9 4.4 %collective-permute-done.48 = f32[2,128,128]{2,1,0:T(8,128)S(1)} collective-permute-done((f32[2,128,128]{2,1,0:T(8,128)S(1)}, f32[2,128,128]{2,1,0:T(8,128)S(1)}, u32[]{:S(2)}, u32[]{:S(2)}) %collective-permute-start.48) | collective-permute-done | bytes 131104 | tf_op jit(solution)/shard_map/ppermute | solution.py:51
  317.4 4.5 %collective-permute-start.49 = (f32[2,128,128]{2,1,0:T(8,128)S(1)}, f32[2,128,128]{2,1,0:T(8,128)S(1)}, u32[]{:S(2)}, u32[]{:S(2)}) collective-permute-start(f32[2,128,128]{2,1,0:T(8,128)S(1)} %fusion.173), channel_id=1, source_target_pairs={{0,8},{1,9},{2,10},{3,11},{4,12},{5,13},{6,14},{7,15},{8,0},{9,1},... | collective-permute-start | bytes 393224 | tf_op jit(solution)/shard_map/ppermute | solution.py:51
  322.0 7.9 %collective-permute-done.49 = f32[2,128,128]{2,1,0:T(8,128)S(1)} collective-permute-done((f32[2,128,128]{2,1,0:T(8,128)S(1)}, f32[2,128,128]{2,1,0:T(8,128)S(1)}, u32[]{:S(2)}, u32[]{:S(2)}) %collective-permute-start.49) | collective-permute-done | bytes 131104 | tf_op jit(solution)/shard_map/ppermute | solution.py:51
  342.2 4.9 %collective-permute-done.52 = f32[2,128,128]{2,1,0:T(8,128)S(1)} collective-permute-done((f32[2,128,128]{2,1,0:T(8,128)S(1)}, f32[2,128,128]{2,1,0:T(8,128)S(1)}, u32[]{:S(2)}, u32[]{:S(2)}) %collective-permute-start.52) | collective-permute-done | bytes 131104 | tf_op jit(solution)/shard_map/ppermute | solution.py:51
  347.2 5.2 %collective-permute-done.53 = f32[2,128,128]{2,1,0:T(8,128)S(1)} collective-permute-done((f32[2,128,128]{2,1,0:T(8,128)S(1)}, f32[2,128,128]{2,1,0:T(8,128)S(1)}, u32[]{:S(2)}, u32[]{:S(2)}) %collective-permute-start.53) | collective-permute-done | bytes 131104 | tf_op jit(solution)/shard_map/ppermute | solution.py:51
  362.4 4.1 %collective-permute-done.56 = f32[2,128,128]{2,1,0:T(8,128)S(1)} collective-permute-done((f32[2,128,128]{2,1,0:T(8,128)S(1)}, f32[2,128,128]{2,1,0:T(8,128)S(1)}, u32[]{:S(2)}, u32[]{:S(2)}) %collective-permute-start.56) | collective-permute-done | bytes 131104 | tf_op jit(solution)/shard_map/ppermute | solution.py:51
  368.6 10.9 %collective-permute-done.57 = f32[2,128,128]{2,1,0:T(8,128)S(1)} collective-permute-done((f32[2,128,128]{2,1,0:T(8,128)S(1)}, f32[2,128,128]{2,1,0:T(8,128)S(1)}, u32[]{:S(2)}, u32[]{:S(2)}) %collective-permute-start.57) | collective-permute-done | bytes 131104 | tf_op jit(solution)/shard_map/ppermute | solution.py:51
  (209 shorter events, 178.9 us)
Async XLA Ops:
  8.9 16.9 %collective-permute-start.6 = (f32[2,264,128]{2,1,0:T(8,128)}, f32[2,264,128]{2,1,0:T(8,128)S(1)}, u32[]{:S(2)}, u32[]{:S(2)}) collective-permute-start(f32[2,264,128]{2,1,0:T(8,128)} %get-tuple-element.32), channel_id=1, source_target_pairs={{0,1},{1,0},{2,3},{3,2},{4,5},{5,4},{6,7},{7,6},{8,9},{9,8},{10,11... | collective-permute-start | bytes 811016 | tf_op jit(solution)/shard_map/ppermute | solution.py:34
  11.4 18.2 %collective-permute-start.7 = (f32[2,264,128]{2,1,0:T(8,128)}, f32[2,264,128]{2,1,0:T(8,128)S(1)}, u32[]{:S(2)}, u32[]{:S(2)}) collective-permute-start(f32[2,264,128]{2,1,0:T(8,128)} %get-tuple-element.32), channel_id=1, source_target_pairs={{0,2},{1,3},{2,0},{3,1},{4,6},{5,7},{6,4},{7,5},{8,10},{9,11},{10,... | collective-permute-start | bytes 811016 | tf_op jit(solution)/shard_map/ppermute | solution.py:34
  13.4 16.3 %collective-permute-start.8 = (f32[2,264,128]{2,1,0:T(8,128)}, f32[2,264,128]{2,1,0:T(8,128)}, u32[]{:S(2)}, u32[]{:S(2)}) collective-permute-start(f32[2,264,128]{2,1,0:T(8,128)} %get-tuple-element.32), channel_id=1, source_target_pairs={{0,3},{1,2},{2,1},{3,0},{4,7},{5,6},{6,5},{7,4},{8,11},{9,10},{10,... | collective-permute-start | bytes 811016 | tf_op jit(solution)/shard_map/ppermute | solution.py:34
  21.0 24.2 %collective-permute-start = (bf16[4,2,128,128]{3,2,1,0:T(8,128)(2,1)}, bf16[4,2,128,128]{3,2,1,0:T(8,128)(2,1)S(1)}, u32[]{:S(2)}, u32[]{:S(2)}) collective-permute-start(bf16[4,2,128,128]{3,2,1,0:T(8,128)(2,1)} %bitcast.338), channel_id=1, source_target_pairs={{0,1},{1,0},{2,3},{3,2},{4,5},{5,4},{6,7},{7,6},{8,9},{9,8},{10,11... | collective-permute-start | bytes 786440 | tf_op jit(solution)/shard_map/ppermute | solution.py:104
  23.1 24.0 %collective-permute-start.1 = (bf16[4,2,128,128]{3,2,1,0:T(8,128)(2,1)S(1)}, bf16[4,2,128,128]{3,2,1,0:T(8,128)(2,1)S(1)}, u32[]{:S(2)}, u32[]{:S(2)}) collective-permute-start(bf16[4,2,128,128]{3,2,1,0:T(8,128)(2,1)S(1)} %bitcast.351), channel_id=1, source_target_pairs={{0,2},{1,3},{2,0},{3,1},{4,6},{5,7},{6,4},{7,5},{8,10},{9,11},{10,... | collective-permute-start | bytes 786440 | tf_op jit(solution)/shard_map/ppermute | solution.py:104
  25.8 21.3 %collective-permute-start.2 = (bf16[4,2,128,128]{3,2,1,0:T(8,128)(2,1)}, bf16[4,2,128,128]{3,2,1,0:T(8,128)(2,1)S(1)}, u32[]{:S(2)}, u32[]{:S(2)}) collective-permute-start(bf16[4,2,128,128]{3,2,1,0:T(8,128)(2,1)} %bitcast.336), channel_id=1, source_target_pairs={{0,3},{1,2},{2,1},{3,0},{4,7},{5,6},{6,5},{7,4},{8,11},{9,10},{10,... | collective-permute-start | bytes 786440 | tf_op jit(solution)/shard_map/ppermute | solution.py:104
  31.4 32.0 %collective-permute-start.9 = (f32[2,264,128]{2,1,0:T(8,128)S(1)}, f32[2,264,128]{2,1,0:T(8,128)S(1)}, u32[]{:S(2)}, u32[]{:S(2)}) collective-permute-start(f32[2,264,128]{2,1,0:T(8,128)S(1)} %get-tuple-element.30), channel_id=1, source_target_pairs={{0,4},{1,5},{2,6},{3,7},{4,0},{5,1},{6,2},{7,3},{8,12},{9,13},{10,... | collective-permute-start | bytes 811016 | tf_op jit(solution)/shard_map/ppermute | solution.py:34
  37.2 34.2 %collective-permute-start.10 = (f32[2,264,128]{2,1,0:T(8,128)S(1)}, f32[2,264,128]{2,1,0:T(8,128)S(1)}, u32[]{:S(2)}, u32[]{:S(2)}) collective-permute-start(f32[2,264,128]{2,1,0:T(8,128)S(1)} %get-tuple-element.30), channel_id=1, source_target_pairs={{0,8},{1,9},{2,10},{3,11},{4,12},{5,13},{6,14},{7,15},{8,0},{9,1},... | collective-permute-start | bytes 811016 | tf_op jit(solution)/shard_map/ppermute | solution.py:34
  45.2 31.0 %collective-permute-start.11 = (f32[2,264,128]{2,1,0:T(8,128)S(1)}, f32[2,264,128]{2,1,0:T(8,128)S(1)}, u32[]{:S(2)}, u32[]{:S(2)}) collective-permute-start(f32[2,264,128]{2,1,0:T(8,128)S(1)} %get-tuple-element.30), channel_id=1, source_target_pairs={{0,12},{1,13},{2,14},{3,15},{4,8},{5,9},{6,10},{7,11},{8,4},{9,5},... | collective-permute-start | bytes 811016 | tf_op jit(solution)/shard_map/ppermute | solution.py:34
  47.2 29.4 %collective-permute-start.3 = (bf16[1,2,128,128]{3,2,1,0:T(8,128)(2,1)S(1)}, bf16[1,2,128,128]{3,2,1,0:T(8,128)(2,1)S(1)}, u32[]{:S(2)}, u32[]{:S(2)}) collective-permute-start(bf16[1,2,128,128]{3,2,1,0:T(8,128)(2,1)S(1)} %get-tuple-element.39), channel_id=1, source_target_pairs={{0,4},{1,5},{2,6},{3,7},{4,0},{5,1},{6,2},{7,3},{8,12},{9,13},{10,... | collective-permute-start | bytes 196616 | tf_op jit(solution)/shard_map/ppermute | solution.py:104
  49.4 27.2 %collective-permute-start.4 = (bf16[1,2,128,128]{3,2,1,0:T(8,128)(2,1)S(1)}, bf16[1,2,128,128]{3,2,1,0:T(8,128)(2,1)S(1)}, u32[]{:S(2)}, u32[]{:S(2)}) collective-permute-start(bf16[1,2,128,128]{3,2,1,0:T(8,128)(2,1)S(1)} %get-tuple-element.41), channel_id=1, source_target_pairs={{0,8},{1,9},{2,10},{3,11},{4,12},{5,13},{6,14},{7,15},{8,0},{9,1},... | collective-permute-start | bytes 196616 | tf_op jit(solution)/shard_map/ppermute | solution.py:104
  63.4 14.1 %collective-permute-start.5 = (bf16[1,2,128,128]{3,2,1,0:T(8,128)(2,1)S(1)}, bf16[1,2,128,128]{3,2,1,0:T(8,128)(2,1)S(1)}, u32[]{:S(2)}, u32[]{:S(2)}) collective-permute-start(bf16[1,2,128,128]{3,2,1,0:T(8,128)(2,1)S(1)} %get-tuple-element.40), channel_id=1, source_target_pairs={{0,12},{1,13},{2,14},{3,15},{4,8},{5,9},{6,10},{7,11},{8,4},{9,5},... | collective-permute-start | bytes 196616 | tf_op jit(solution)/shard_map/ppermute | solution.py:104
  84.0 12.6 %collective-permute-start.14 = (f32[2,128,128]{2,1,0:T(8,128)S(1)}, f32[2,128,128]{2,1,0:T(8,128)S(1)}, u32[]{:S(2)}, u32[]{:S(2)}) collective-permute-start(f32[2,128,128]{2,1,0:T(8,128)S(1)} %fusion.91), channel_id=1, source_target_pairs={{0,48},{16,32},{32,16},{48,0},{64,112},{80,96},{96,80},{112,64},{1... | collective-permute-start | bytes 393224 | tf_op jit(solution)/shard_map/ppermute | solution.py:51
  109.7 9.8 %collective-permute-start.18 = (f32[2,128,128]{2,1,0:T(8,128)S(1)}, f32[2,128,128]{2,1,0:T(8,128)S(1)}, u32[]{:S(2)}, u32[]{:S(2)}) collective-permute-start(f32[2,128,128]{2,1,0:T(8,128)S(1)} %fusion.183), channel_id=1, source_target_pairs={{0,64},{16,80},{32,96},{48,112},{64,0},{80,16},{96,32},{112,48},{1... | collective-permute-start | bytes 393224 | tf_op jit(solution)/shard_map/ppermute | solution.py:51
  129.5 12.8 %collective-permute-start.21 = (f32[2,128,128]{2,1,0:T(8,128)S(1)}, f32[2,128,128]{2,1,0:T(8,128)S(1)}, u32[]{:S(2)}, u32[]{:S(2)}) collective-permute-start(f32[2,128,128]{2,1,0:T(8,128)S(1)} %slice_select_fusion.2), channel_id=1, source_target_pairs={{0,4},{1,5},{2,6},{3,7},{4,0},{5,1},{6,2},{7,3},{8,12},{9,13},{10,... | collective-permute-start | bytes 393224 | tf_op jit(solution)/shard_map/ppermute | solution.py:51
  133.7 12.1 %collective-permute-start.22 = (f32[2,128,128]{2,1,0:T(8,128)S(1)}, f32[2,128,128]{2,1,0:T(8,128)S(1)}, u32[]{:S(2)}, u32[]{:S(2)}) collective-permute-start(f32[2,128,128]{2,1,0:T(8,128)S(1)} %slice_select_fusion.2), channel_id=1, source_target_pairs={{0,6},{1,7},{2,4},{3,5},{4,2},{5,3},{6,0},{7,1},{8,14},{9,15},{10,... | collective-permute-start | bytes 393224 | tf_op jit(solution)/shard_map/ppermute | solution.py:51
  145.9 13.3 %collective-permute-start.23 = (f32[2,128,128]{2,1,0:T(8,128)S(1)}, f32[2,128,128]{2,1,0:T(8,128)S(1)}, u32[]{:S(2)}, u32[]{:S(2)}) collective-permute-start(f32[2,128,128]{2,1,0:T(8,128)S(1)} %fusion.181), channel_id=1, source_target_pairs={{0,8},{1,9},{2,10},{3,11},{4,12},{5,13},{6,14},{7,15},{8,0},{9,1},... | collective-permute-start | bytes 393224 | tf_op jit(solution)/shard_map/ppermute | solution.py:51
  164.9 11.8 %collective-permute-start.26 = (f32[2,128,128]{2,1,0:T(8,128)S(1)}, f32[2,128,128]{2,1,0:T(8,128)S(1)}, u32[]{:S(2)}, u32[]{:S(2)}) collective-permute-start(f32[2,128,128]{2,1,0:T(8,128)S(1)} %convolution_add_fusion.5), channel_id=1, source_target_pairs={{0,32},{16,48},{32,0},{48,16},{64,96},{80,112},{96,64},{112,80},{1... | collective-permute-start | bytes 393224 | tf_op jit(solution)/shard_map/ppermute | solution.py:51
  168.5 13.2 %collective-permute-start.27 = (f32[2,128,128]{2,1,0:T(8,128)S(1)}, f32[2,128,128]{2,1,0:T(8,128)S(1)}, u32[]{:S(2)}, u32[]{:S(2)}) collective-permute-start(f32[2,128,128]{2,1,0:T(8,128)S(1)} %convolution_add_fusion.5), channel_id=1, source_target_pairs={{0,48},{16,32},{32,16},{48,0},{64,112},{80,96},{96,80},{112,64},{1... | collective-permute-start | bytes 393224 | tf_op jit(solution)/shard_map/ppermute | solution.py:51
  197.2 12.4 %collective-permute-start.31 = (f32[2,128,128]{2,1,0:T(8,128)S(1)}, f32[2,128,128]{2,1,0:T(8,128)S(1)}, u32[]{:S(2)}, u32[]{:S(2)}) collective-permute-start(f32[2,128,128]{2,1,0:T(8,128)S(1)} %fusion.179), channel_id=1, source_target_pairs={{0,64},{16,80},{32,96},{48,112},{64,0},{80,16},{96,32},{112,48},{1... | collective-permute-start | bytes 393224 | tf_op jit(solution)/shard_map/ppermute | solution.py:51
  215.8 11.8 %collective-permute-start.34 = (f32[2,128,128]{2,1,0:T(8,128)S(1)}, f32[2,128,128]{2,1,0:T(8,128)S(1)}, u32[]{:S(2)}, u32[]{:S(2)}) collective-permute-start(f32[2,128,128]{2,1,0:T(8,128)S(1)} %slice_select_fusion.1), channel_id=1, source_target_pairs={{0,4},{1,5},{2,6},{3,7},{4,0},{5,1},{6,2},{7,3},{8,12},{9,13},{10,... | collective-permute-start | bytes 393224 | tf_op jit(solution)/shard_map/ppermute | solution.py:51
  219.4 13.0 %collective-permute-start.35 = (f32[2,128,128]{2,1,0:T(8,128)S(1)}, f32[2,128,128]{2,1,0:T(8,128)S(1)}, u32[]{:S(2)}, u32[]{:S(2)}) collective-permute-start(f32[2,128,128]{2,1,0:T(8,128)S(1)} %slice_select_fusion.1), channel_id=1, source_target_pairs={{0,6},{1,7},{2,4},{3,5},{4,2},{5,3},{6,0},{7,1},{8,14},{9,15},{10,... | collective-permute-start | bytes 393224 | tf_op jit(solution)/shard_map/ppermute | solution.py:51
  232.5 12.6 %collective-permute-start.36 = (f32[2,128,128]{2,1,0:T(8,128)S(1)}, f32[2,128,128]{2,1,0:T(8,128)S(1)}, u32[]{:S(2)}, u32[]{:S(2)}) collective-permute-start(f32[2,128,128]{2,1,0:T(8,128)S(1)} %fusion.177), channel_id=1, source_target_pairs={{0,8},{1,9},{2,10},{3,11},{4,12},{5,13},{6,14},{7,15},{8,0},{9,1},... | collective-permute-start | bytes 393224 | tf_op jit(solution)/shard_map/ppermute | solution.py:51
  250.9 11.9 %collective-permute-start.39 = (f32[2,128,128]{2,1,0:T(8,128)S(1)}, f32[2,128,128]{2,1,0:T(8,128)S(1)}, u32[]{:S(2)}, u32[]{:S(2)}) collective-permute-start(f32[2,128,128]{2,1,0:T(8,128)S(1)} %convolution_add_fusion.4), channel_id=1, source_target_pairs={{0,32},{16,48},{32,0},{48,16},{64,96},{80,112},{96,64},{112,80},{1... | collective-permute-start | bytes 393224 | tf_op jit(solution)/shard_map/ppermute | solution.py:51
  254.5 13.0 %collective-permute-start.40 = (f32[2,128,128]{2,1,0:T(8,128)S(1)}, f32[2,128,128]{2,1,0:T(8,128)S(1)}, u32[]{:S(2)}, u32[]{:S(2)}) collective-permute-start(f32[2,128,128]{2,1,0:T(8,128)S(1)} %convolution_add_fusion.4), channel_id=1, source_target_pairs={{0,48},{16,32},{32,16},{48,0},{64,112},{80,96},{96,80},{112,64},{1... | collective-permute-start | bytes 393224 | tf_op jit(solution)/shard_map/ppermute | solution.py:51
  281.0 13.0 %collective-permute-start.44 = (f32[2,128,128]{2,1,0:T(8,128)S(1)}, f32[2,128,128]{2,1,0:T(8,128)S(1)}, u32[]{:S(2)}, u32[]{:S(2)}) collective-permute-start(f32[2,128,128]{2,1,0:T(8,128)S(1)} %fusion.175), channel_id=1, source_target_pairs={{0,64},{16,80},{32,96},{48,112},{64,0},{80,16},{96,32},{112,48},{1... | collective-permute-start | bytes 393224 | tf_op jit(solution)/shard_map/ppermute | solution.py:51
  300.8 12.1 %collective-permute-start.47 = (f32[2,128,128]{2,1,0:T(8,128)S(1)}, f32[2,128,128]{2,1,0:T(8,128)S(1)}, u32[]{:S(2)}, u32[]{:S(2)}) collective-permute-start(f32[2,128,128]{2,1,0:T(8,128)S(1)} %slice_select_fusion), channel_id=1, source_target_pairs={{0,4},{1,5},{2,6},{3,7},{4,0},{5,1},{6,2},{7,3},{8,12},{9,13},{10,... | collective-permute-start | bytes 393224 | tf_op jit(solution)/shard_map/ppermute | solution.py:51
  304.5 12.8 %collective-permute-start.48 = (f32[2,128,128]{2,1,0:T(8,128)S(1)}, f32[2,128,128]{2,1,0:T(8,128)S(1)}, u32[]{:S(2)}, u32[]{:S(2)}) collective-permute-start(f32[2,128,128]{2,1,0:T(8,128)S(1)} %slice_select_fusion), channel_id=1, source_target_pairs={{0,6},{1,7},{2,4},{3,5},{4,2},{5,3},{6,0},{7,1},{8,14},{9,15},{10,... | collective-permute-start | bytes 393224 | tf_op jit(solution)/shard_map/ppermute | solution.py:51
  317.4 12.5 %collective-permute-start.49 = (f32[2,128,128]{2,1,0:T(8,128)S(1)}, f32[2,128,128]{2,1,0:T(8,128)S(1)}, u32[]{:S(2)}, u32[]{:S(2)}) collective-permute-start(f32[2,128,128]{2,1,0:T(8,128)S(1)} %fusion.173), channel_id=1, source_target_pairs={{0,8},{1,9},{2,10},{3,11},{4,12},{5,13},{6,14},{7,15},{8,0},{9,1},... | collective-permute-start | bytes 393224 | tf_op jit(solution)/shard_map/ppermute | solution.py:51
  335.8 11.4 %collective-permute-start.52 = (f32[2,128,128]{2,1,0:T(8,128)S(1)}, f32[2,128,128]{2,1,0:T(8,128)S(1)}, u32[]{:S(2)}, u32[]{:S(2)}) collective-permute-start(f32[2,128,128]{2,1,0:T(8,128)S(1)} %convolution_add_fusion.3), channel_id=1, source_target_pairs={{0,32},{16,48},{32,0},{48,16},{64,96},{80,112},{96,64},{112,80},{1... | collective-permute-start | bytes 393224 | tf_op jit(solution)/shard_map/ppermute | solution.py:51
  338.8 13.6 %collective-permute-start.53 = (f32[2,128,128]{2,1,0:T(8,128)S(1)}, f32[2,128,128]{2,1,0:T(8,128)S(1)}, u32[]{:S(2)}, u32[]{:S(2)}) collective-permute-start(f32[2,128,128]{2,1,0:T(8,128)S(1)} %convolution_add_fusion.3), channel_id=1, source_target_pairs={{0,48},{16,32},{32,16},{48,0},{64,112},{80,96},{96,80},{112,64},{1... | collective-permute-start | bytes 393224 | tf_op jit(solution)/shard_map/ppermute | solution.py:51
  366.7 12.9 %collective-permute-start.57 = (f32[2,128,128]{2,1,0:T(8,128)S(1)}, f32[2,128,128]{2,1,0:T(8,128)S(1)}, u32[]{:S(2)}, u32[]{:S(2)}) collective-permute-start(f32[2,128,128]{2,1,0:T(8,128)S(1)} %fusion.171), channel_id=1, source_target_pairs={{0,64},{16,80},{32,96},{48,112},{64,0},{80,16},{96,32},{112,48},{1... | collective-permute-start | bytes 393224 | tf_op jit(solution)/shard_map/ppermute | solution.py:51
  (30 other events, 204.0 us)

commit v6 on v5

--- a/solution.py
+++ b/solution.py
@@ -68,9 +68,16 @@
 
 def group_sum(value, axis):
     count = lax.axis_size(axis).bit_length() - 1
-    if count == 5:
-        return sum_over_bits(value, axis, [[0, 1], [3, 4], [2]])
-    return sum_over_bits(value, axis, bit_stages(list(range(count))))
+    pairs = [(s, s ^ 1) for s in range(lax.axis_size(axis))]
+    low = (lax.axis_index(axis) & 1) == 0
+    half = value.shape[1] // 2
+    first = value[:, :half]
+    second = value[:, half:]
+    arrived = lax.ppermute(jnp.where(low, second, first), axis, pairs)
+    mine = jnp.where(low, first + arrived, arrived + second)
+    mine = sum_over_bits(mine, axis, bit_stages(list(range(1, count))))
+    other = lax.ppermute(mine, axis, pairs)
+    return jnp.concatenate([jnp.where(low, mine, other), jnp.where(low, other, mine)], axis=1)
 
 
 def pair_split_sum(value, axis, split_axis):
@@ -178,11 +185,26 @@
     cweights = jnp.where(kept_mask[:, None, :], jnp.exp(kept_scores - cpeak[..., None]), 0.0)
     cdenom = jnp.sum(cweights, axis=-1)
 
+    stat_bits = (col_devices.bit_length() - 1) if isinstance(col_devices, int) else 4
     packed = pack(numer, peak, denom, cpeak, cdenom)
-    for stride, radix in digit_groups(col_devices):
-        members = gather_group(packed, "kv", stride, radix)
-        numer, peak, denom, cpeak, cdenom = combine_members(members, query_rows)
-        packed = pack(numer, peak, denom, cpeak, cdenom)
+    members = gather_bits(packed, "kv", [0])
+    numer, peak, denom, cpeak, cdenom = combine_members(members, query_rows)
+    half = query_rows // 2
+    low = (me_kv & 1) == 0
+    halves = [
+        pack(*(a[:, :half] for a in (numer, peak, denom, cpeak, cdenom))),
+        pack(*(a[:, half:] for a in (numer, peak, denom, cpeak, cdenom))),
+    ]
+    packed = jnp.where(low, halves[0], halves[1])
+    for bits in bit_stages(list(range(1, stat_bits))):
+        members = gather_bits(packed, "kv", bits)
+        packed = pack(*combine_members(members, half))
+    other = lax.ppermute(packed, "kv", [(s, s ^ 1) for s in range(col_devices)])
+    first_half = combine_members([jnp.where(low, packed, other)], half)
+    second_half = combine_members([jnp.where(low, other, packed)], half)
+    numer, peak, denom, cpeak, cdenom = (
+        jnp.concatenate([a, b], axis=1) for a, b in zip(first_half, second_half)
+    )
     attended = (numer / denom[..., None]).astype(BF16)
 
     compact = (

time: 382 us -> 377 us (0.987)
  the two profiles are of different devices: /device:TPU:107 before, /device:TPU:6 now
where the time goes in v6:
time: 377 us; the launch traced here: 372 us
  starting transfers between devices  225 us (60%)
  waiting for transfers between devices  125 us (33%)
  other arithmetic  10.6 us (3%)
  matrix products  8.78 us (2%)
    ppermute x44, starting transfers between devices, gather_bits(): got.append(lax.ppermute(value, axis, pairs))  170 us
    ppermute x44, waiting for transfers between devices, gather_bits(): got.append(lax.ppermute(value, axis, pairs))  84.5 us
    ppermute x6, starting transfers between devices, scatter_groups(): total = total + lax.ppermute(give, axis, pairs)  21 us
    ppermute x4, starting transfers between devices, group_sum(): other = lax.ppermute(mine, axis, pairs)  13.2 us
    ppermute x4, waiting for transfers between devices, group_sum(): arrived = lax.ppermute(jnp.where(low, second, first), axis, pairs)  12.7 us
    ppermute x4, waiting for transfers between devices, group_sum(): other = lax.ppermute(mine, axis, pairs)  12.1 us
    ppermute x4, starting transfers between devices, group_sum(): arrived = lax.ppermute(jnp.where(low, second, first), axis, pairs)  12.1 us
    ppermute x6, waiting for transfers between devices, scatter_groups(): total = total + lax.ppermute(give, axis, pairs)  11.3 us
  transfers between devices with their start and end apart: 62, of which 39 were waited for; matrix products, arithmetic and copies ran while one was open for 1% of the time, Pallas kernels for 0%

profile of v6, /device:TPU:6, one launch (start us, length us, event | category | flops | bytes accessed | tf_op | source)
XLA Modules:
  0.0 372.2 jit_solution(2481975626922339898)
XLA Ops:
  15.3 4.3 %collective-permute-start.7 = (f32[2,132,128]{2,0,1:T(2,128)S(1)}, f32[2,132,128]{2,0,1:T(2,128)S(1)}, u32[]{:S(2)}, u32[]{:S(2)}) collective-permute-start(f32[2,132,128]{2,0,1:T(2,128)S(1)} %bitcast.384), channel_id=1, source_target_pairs={{0,2},{1,3},{2,0},{3,1},{4,6},{5,7},{6,4},{7,5},{8,10},{9,11},{10,... | collective-permute-start | bytes 405512 | tf_op jit(solution)/shard_map/ppermute | solution.py:51
  19.6 6.1 %collective-permute-start.8 = (f32[2,132,128]{2,0,1:T(2,128)S(1)}, f32[2,132,128]{2,0,1:T(2,128)S(1)}, u32[]{:S(2)}, u32[]{:S(2)}) collective-permute-start(f32[2,132,128]{2,0,1:T(2,128)S(1)} %bitcast.385), channel_id=1, source_target_pairs={{0,4},{1,5},{2,6},{3,7},{4,0},{5,1},{6,2},{7,3},{8,12},{9,13},{10,... | collective-permute-start | bytes 405512 | tf_op jit(solution)/shard_map/ppermute | solution.py:51
  27.7 8.2 %collective-permute-done.8 = f32[2,132,128]{2,0,1:T(2,128)S(1)} collective-permute-done((f32[2,132,128]{2,0,1:T(2,128)S(1)}, f32[2,132,128]{2,0,1:T(2,128)S(1)}, u32[]{:S(2)}, u32[]{:S(2)}) %collective-permute-start.8) | collective-permute-done | bytes 135200 | tf_op jit(solution)/shard_map/ppermute | solution.py:51
  36.6 8.5 %collective-permute-start.10 = (f32[2,132,128]{2,1,0:T(8,128)S(1)}, f32[2,132,128]{2,1,0:T(8,128)S(1)}, u32[]{:S(2)}, u32[]{:S(2)}) collective-permute-start(f32[2,132,128]{2,1,0:T(8,128)S(1)} %concatenate.101), channel_id=1, source_target_pairs={{0,8},{1,9},{2,10},{3,11},{4,12},{5,13},{6,14},{7,15},{8,0},{9,1},... | collective-permute-start | bytes 405512 | tf_op jit(solution)/shard_map/ppermute | solution.py:51
  47.2 4.9 %collective-permute-start.1 = (bf16[4,2,128,128]{3,2,1,0:T(8,128)(2,1)S(1)}, bf16[4,2,128,128]{3,2,1,0:T(8,128)(2,1)S(1)}, u32[]{:S(2)}, u32[]{:S(2)}) collective-permute-start(bf16[4,2,128,128]{3,2,1,0:T(8,128)(2,1)S(1)} %bitcast.371), channel_id=1, source_target_pairs={{0,2},{1,3},{2,0},{3,1},{4,6},{5,7},{6,4},{7,5},{8,10},{9,11},{10,... | collective-permute-start | bytes 786440 | tf_op jit(solution)/shard_map/ppermute | solution.py:111
  59.2 5.2 %collective-permute-done.2 = bf16[4,2,128,128]{3,2,1,0:T(8,128)(2,1)S(1)} collective-permute-done((bf16[4,2,128,128]{3,2,1,0:T(8,128)(2,1)S(1)}, bf16[4,2,128,128]{3,2,1,0:T(8,128)(2,1)S(1)}, u32[]{:S(2)}, u32[]{:S(2)}) %collective-permute-start.2) | collective-permute-done | bytes 262176 | tf_op jit(solution)/shard_map/ppermute | solution.py:111
  64.5 4.3 %collective-permute-start.3 = (bf16[1,2,128,128]{3,2,1,0:T(8,128)(2,1)S(1)}, bf16[1,2,128,128]{3,2,1,0:T(8,128)(2,1)S(1)}, u32[]{:S(2)}, u32[]{:S(2)}) collective-permute-start(bf16[1,2,128,128]{3,2,1,0:T(8,128)(2,1)S(1)} %get-tuple-element.36), channel_id=1, source_target_pairs={{0,4},{1,5},{2,6},{3,7},{4,0},{5,1},{6,2},{7,3},{8,12},{9,13},{10,... | collective-permute-start | bytes 196616 | tf_op jit(solution)/shard_map/ppermute | solution.py:111
  68.8 4.3 %collective-permute-start.4 = (bf16[1,2,128,128]{3,2,1,0:T(8,128)(2,1)S(1)}, bf16[1,2,128,128]{3,2,1,0:T(8,128)(2,1)S(1)}, u32[]{:S(2)}, u32[]{:S(2)}) collective-permute-start(bf16[1,2,128,128]{3,2,1,0:T(8,128)(2,1)S(1)} %get-tuple-element.38), channel_id=1, source_target_pairs={{0,8},{1,9},{2,10},{3,11},{4,12},{5,13},{6,14},{7,15},{8,0},{9,1},... | collective-permute-start | bytes 196616 | tf_op jit(solution)/shard_map/ppermute | solution.py:111
  88.1 4.5 %collective-permute-start.13 = (f32[2,64,128]{2,1,0:T(8,128)S(1)}, f32[2,64,128]{2,1,0:T(8,128)S(1)}, u32[]{:S(2)}, u32[]{:S(2)}) collective-permute-start(f32[2,64,128]{2,1,0:T(8,128)S(1)} %add_select_fusion.3), channel_id=1, source_target_pairs={{0,32},{16,48},{32,0},{48,16},{64,96},{80,112},{96,64},{112,80},{1... | collective-permute-start | bytes 196616 | tf_op jit(solution)/shard_map/ppermute | solution.py:51
  92.6 5.9 %collective-permute-start.14 = (f32[2,64,128]{2,1,0:T(8,128)S(1)}, f32[2,64,128]{2,1,0:T(8,128)S(1)}, u32[]{:S(2)}, u32[]{:S(2)}) collective-permute-start(f32[2,64,128]{2,1,0:T(8,128)S(1)} %add_select_fusion.3), channel_id=1, source_target_pairs={{0,64},{16,80},{32,96},{48,112},{64,0},{80,16},{96,32},{112,48},{1... | collective-permute-start | bytes 196616 | tf_op jit(solution)/shard_map/ppermute | solution.py:51
  112.6 4.7 %collective-permute-start.18 = (f32[2,64,128]{2,1,0:T(8,128)S(1)}, f32[2,64,128]{2,1,0:T(8,128)S(1)}, u32[]{:S(2)}, u32[]{:S(2)}) collective-permute-start(f32[2,64,128]{2,1,0:T(8,128)S(1)} %fusion.162), channel_id=1, source_target_pairs={{0,384},{16,400},{32,416},{48,432},{64,448},{80,464},{96,480},{112... | collective-permute-start | bytes 196616 | tf_op jit(solution)/shard_map/ppermute | solution.py:51
  140.5 7.5 %collective-permute-done.22 = f32[2,128,128]{2,1,0:T(8,128)S(1)} collective-permute-done((f32[2,128,128]{2,1,0:T(8,128)S(1)}, f32[2,128,128]{2,1,0:T(8,128)S(1)}, u32[]{:S(2)}, u32[]{:S(2)}) %collective-permute-start.22) | collective-permute-done | bytes 131104 | tf_op jit(solution)/shard_map/ppermute | solution.py:51
  148.0 5.0 %collective-permute-start.24 = (f32[2,128,128]{2,1,0:T(8,128)S(1)}, f32[2,128,128]{2,1,0:T(8,128)S(1)}, u32[]{:S(2)}, u32[]{:S(2)}) collective-permute-start(f32[2,128,128]{2,1,0:T(8,128)S(1)} %fusion.160), channel_id=1, source_target_pairs={{0,8},{1,9},{2,10},{3,11},{4,12},{5,13},{6,14},{7,15},{8,0},{9,1},... | collective-permute-start | bytes 393224 | tf_op jit(solution)/shard_map/ppermute | solution.py:51
  153.1 5.9 %collective-permute-done.24 = f32[2,128,128]{2,1,0:T(8,128)S(1)} collective-permute-done((f32[2,128,128]{2,1,0:T(8,128)S(1)}, f32[2,128,128]{2,1,0:T(8,128)S(1)}, u32[]{:S(2)}, u32[]{:S(2)}) %collective-permute-start.24) | collective-permute-done | bytes 131104 | tf_op jit(solution)/shard_map/ppermute | solution.py:51
  168.8 4.7 %collective-permute-start.27 = (f32[2,64,128]{2,1,0:T(8,128)S(1)}, f32[2,64,128]{2,1,0:T(8,128)S(1)}, u32[]{:S(2)}, u32[]{:S(2)}) collective-permute-start(f32[2,64,128]{2,1,0:T(8,128)S(1)} %add_select_fusion.2), channel_id=1, source_target_pairs={{0,32},{16,48},{32,0},{48,16},{64,96},{80,112},{96,64},{112,80},{1... | collective-permute-start | bytes 196616 | tf_op jit(solution)/shard_map/ppermute | solution.py:51
  176.2 4.8 %collective-permute-start.29 = (f32[2,64,128]{2,1,0:T(8,128)S(1)}, f32[2,64,128]{2,1,0:T(8,128)S(1)}, u32[]{:S(2)}, u32[]{:S(2)}) collective-permute-start(f32[2,64,128]{2,1,0:T(8,128)S(1)} %add_select_fusion.2), channel_id=1, source_target_pairs={{0,96},{16,112},{32,64},{48,80},{64,32},{80,48},{96,0},{112,16},{1... | collective-permute-start | bytes 196616 | tf_op jit(solution)/shard_map/ppermute | solution.py:51
  184.5 4.6 %collective-permute-start.32 = (f32[2,64,128]{2,1,0:T(8,128)S(1)}, f32[2,64,128]{2,1,0:T(8,128)S(1)}, u32[]{:S(2)}, u32[]{:S(2)}) collective-permute-start(f32[2,64,128]{2,1,0:T(8,128)S(1)} %fusion.159), channel_id=1, source_target_pairs={{0,384},{16,400},{32,416},{48,432},{64,448},{80,464},{96,480},{112... | collective-permute-start | bytes 196616 | tf_op jit(solution)/shard_map/ppermute | solution.py:51
  198.8 4.4 %collective-permute-start.33 = (f32[2,64,128]{2,1,0:T(8,128)S(1)}, f32[2,64,128]{2,1,0:T(8,128)S(1)}, u32[]{:S(2)}, u32[]{:S(2)}) collective-permute-start(f32[2,64,128]{2,1,0:T(8,128)S(1)} %add_bitcast_fusion.2), channel_id=1, source_target_pairs={{0,16},{16,0},{32,48},{48,32},{64,80},{80,64},{96,112},{112,96},{1... | collective-permute-start | bytes 196616 | tf_op jit(solution)/shard_map/ppermute | solution.py:79
  209.6 6.6 %collective-permute-start.35 = (f32[2,128,128]{2,1,0:T(8,128)S(1)}, f32[2,128,128]{2,1,0:T(8,128)S(1)}, u32[]{:S(2)}, u32[]{:S(2)}) collective-permute-start(f32[2,128,128]{2,1,0:T(8,128)S(1)} %slice_select_fusion.1), channel_id=1, source_target_pairs={{0,2},{1,3},{2,0},{3,1},{4,6},{5,7},{6,4},{7,5},{8,10},{9,11},{10,... | collective-permute-start | bytes 393224 | tf_op jit(solution)/shard_map/ppermute | solution.py:51
  222.4 7.6 %collective-permute-done.36 = f32[2,128,128]{2,1,0:T(8,128)S(1)} collective-permute-done((f32[2,128,128]{2,1,0:T(8,128)S(1)}, f32[2,128,128]{2,1,0:T(8,128)S(1)}, u32[]{:S(2)}, u32[]{:S(2)}) %collective-permute-start.36) | collective-permute-done | bytes 131104 | tf_op jit(solution)/shard_map/ppermute | solution.py:51
  230.1 5.2 %collective-permute-start.38 = (f32[2,128,128]{2,1,0:T(8,128)S(1)}, f32[2,128,128]{2,1,0:T(8,128)S(1)}, u32[]{:S(2)}, u32[]{:S(2)}) collective-permute-start(f32[2,128,128]{2,1,0:T(8,128)S(1)} %fusion.157), channel_id=1, source_target_pairs={{0,8},{1,9},{2,10},{3,11},{4,12},{5,13},{6,14},{7,15},{8,0},{9,1},... | collective-permute-start | bytes 393224 | tf_op jit(solution)/shard_map/ppermute | solution.py:51
  235.4 5.5 %collective-permute-done.38 = f32[2,128,128]{2,1,0:T(8,128)S(1)} collective-permute-done((f32[2,128,128]{2,1,0:T(8,128)S(1)}, f32[2,128,128]{2,1,0:T(8,128)S(1)}, u32[]{:S(2)}, u32[]{:S(2)}) %collective-permute-start.38) | collective-permute-done | bytes 131104 | tf_op jit(solution)/shard_map/ppermute | solution.py:51
  254.4 5.8 %collective-permute-start.42 = (f32[2,64,128]{2,1,0:T(8,128)S(1)}, f32[2,64,128]{2,1,0:T(8,128)S(1)}, u32[]{:S(2)}, u32[]{:S(2)}) collective-permute-start(f32[2,64,128]{2,1,0:T(8,128)S(1)} %add_select_fusion.1), channel_id=1, source_target_pairs={{0,64},{16,80},{32,96},{48,112},{64,0},{80,16},{96,32},{112,48},{1... | collective-permute-start | bytes 196616 | tf_op jit(solution)/shard_map/ppermute | solution.py:51
  293.3 6.5 %collective-permute-start.49 = (f32[2,128,128]{2,1,0:T(8,128)S(1)}, f32[2,128,128]{2,1,0:T(8,128)S(1)}, u32[]{:S(2)}, u32[]{:S(2)}) collective-permute-start(f32[2,128,128]{2,1,0:T(8,128)S(1)} %slice_select_fusion), channel_id=1, source_target_pairs={{0,2},{1,3},{2,0},{3,1},{4,6},{5,7},{6,4},{7,5},{8,10},{9,11},{10,... | collective-permute-start | bytes 393224 | tf_op jit(solution)/shard_map/ppermute | solution.py:51
  306.1 7.6 %collective-permute-done.50 = f32[2,128,128]{2,1,0:T(8,128)S(1)} collective-permute-done((f32[2,128,128]{2,1,0:T(8,128)S(1)}, f32[2,128,128]{2,1,0:T(8,128)S(1)}, u32[]{:S(2)}, u32[]{:S(2)}) %collective-permute-start.50) | collective-permute-done | bytes 131104 | tf_op jit(solution)/shard_map/ppermute | solution.py:51
  313.8 5.3 %collective-permute-start.52 = (f32[2,128,128]{2,1,0:T(8,128)S(1)}, f32[2,128,128]{2,1,0:T(8,128)S(1)}, u32[]{:S(2)}, u32[]{:S(2)}) collective-permute-start(f32[2,128,128]{2,1,0:T(8,128)S(1)} %fusion.154), channel_id=1, source_target_pairs={{0,8},{1,9},{2,10},{3,11},{4,12},{5,13},{6,14},{7,15},{8,0},{9,1},... | collective-permute-start | bytes 393224 | tf_op jit(solution)/shard_map/ppermute | solution.py:51
  319.2 5.4 %collective-permute-done.52 = f32[2,128,128]{2,1,0:T(8,128)S(1)} collective-permute-done((f32[2,128,128]{2,1,0:T(8,128)S(1)}, f32[2,128,128]{2,1,0:T(8,128)S(1)}, u32[]{:S(2)}, u32[]{:S(2)}) %collective-permute-start.52) | collective-permute-done | bytes 131104 | tf_op jit(solution)/shard_map/ppermute | solution.py:51
  334.5 4.4 %collective-permute-start.55 = (f32[2,64,128]{2,1,0:T(8,128)S(1)}, f32[2,64,128]{2,1,0:T(8,128)S(1)}, u32[]{:S(2)}, u32[]{:S(2)}) collective-permute-start(f32[2,64,128]{2,1,0:T(8,128)S(1)} %add_select_fusion), channel_id=1, source_target_pairs={{0,32},{16,48},{32,0},{48,16},{64,96},{80,112},{96,64},{112,80},{1... | collective-permute-start | bytes 196616 | tf_op jit(solution)/shard_map/ppermute | solution.py:51
  341.9 4.8 %collective-permute-start.57 = (f32[2,64,128]{2,1,0:T(8,128)S(1)}, f32[2,64,128]{2,1,0:T(8,128)S(1)}, u32[]{:S(2)}, u32[]{:S(2)}) collective-permute-start(f32[2,64,128]{2,1,0:T(8,128)S(1)} %add_select_fusion), channel_id=1, source_target_pairs={{0,96},{16,112},{32,64},{48,80},{64,32},{80,48},{96,0},{112,16},{1... | collective-permute-start | bytes 196616 | tf_op jit(solution)/shard_map/ppermute | solution.py:51
  352.3 5.4 %collective-permute-start.59 = (f32[2,64,128]{2,1,0:T(8,128)S(1)}, f32[2,64,128]{2,1,0:T(8,128)S(1)}, u32[]{:S(2)}, u32[]{:S(2)}) collective-permute-start(f32[2,64,128]{2,1,0:T(8,128)S(1)} %fusion.153), channel_id=1, source_target_pairs={{0,256},{16,272},{32,288},{48,304},{64,320},{80,336},{96,352},{112... | collective-permute-start | bytes 196616 | tf_op jit(solution)/shard_map/ppermute | solution.py:51
  360.9 4.2 %collective-permute-done.60 = f32[2,64,128]{2,1,0:T(8,128)S(1)} collective-permute-done((f32[2,64,128]{2,1,0:T(8,128)S(1)}, f32[2,64,128]{2,1,0:T(8,128)S(1)}, u32[]{:S(2)}, u32[]{:S(2)}) %collective-permute-start.60) | collective-permute-done | bytes 65568 | tf_op jit(solution)/shard_map/ppermute | solution.py:51
  365.2 4.1 %collective-permute-start.61 = (f32[2,64,128]{2,1,0:T(8,128)S(1)}, f32[2,64,128]{2,1,0:T(8,128)S(1)}, u32[]{:S(2)}, u32[]{:S(2)}) collective-permute-start(f32[2,64,128]{2,1,0:T(8,128)S(1)} %add_bitcast_fusion), channel_id=1, source_target_pairs={{0,16},{16,0},{32,48},{48,32},{64,80},{80,64},{96,112},{112,96},{1... | collective-permute-start | bytes 196616 | tf_op jit(solution)/shard_map/ppermute | solution.py:79
  (255 shorter events, 193.6 us)
Async XLA Ops:
  15.3 12.4 %collective-permute-start.7 = (f32[2,132,128]{2,0,1:T(2,128)S(1)}, f32[2,132,128]{2,0,1:T(2,128)S(1)}, u32[]{:S(2)}, u32[]{:S(2)}) collective-permute-start(f32[2,132,128]{2,0,1:T(2,128)S(1)} %bitcast.384), channel_id=1, source_target_pairs={{0,2},{1,3},{2,0},{3,1},{4,6},{5,7},{6,4},{7,5},{8,10},{9,11},{10,... | collective-permute-start | bytes 405512 | tf_op jit(solution)/shard_map/ppermute | solution.py:51
  19.6 16.3 %collective-permute-start.8 = (f32[2,132,128]{2,0,1:T(2,128)S(1)}, f32[2,132,128]{2,0,1:T(2,128)S(1)}, u32[]{:S(2)}, u32[]{:S(2)}) collective-permute-start(f32[2,132,128]{2,0,1:T(2,128)S(1)} %bitcast.385), channel_id=1, source_target_pairs={{0,4},{1,5},{2,6},{3,7},{4,0},{5,1},{6,2},{7,3},{8,12},{9,13},{10,... | collective-permute-start | bytes 405512 | tf_op jit(solution)/shard_map/ppermute | solution.py:51
  25.7 10.2 %collective-permute-start.9 = (f32[2,132,128]{2,0,1:T(2,128)S(1)}, f32[2,132,128]{2,0,1:T(2,128)S(1)}, u32[]{:S(2)}, u32[]{:S(2)}) collective-permute-start(f32[2,132,128]{2,0,1:T(2,128)S(1)} %bitcast.386), channel_id=1, source_target_pairs={{0,6},{1,7},{2,4},{3,5},{4,2},{5,3},{6,0},{7,1},{8,14},{9,15},{10,... | collective-permute-start | bytes 405512 | tf_op jit(solution)/shard_map/ppermute | solution.py:51
  36.6 17.6 %collective-permute-start.10 = (f32[2,132,128]{2,1,0:T(8,128)S(1)}, f32[2,132,128]{2,1,0:T(8,128)S(1)}, u32[]{:S(2)}, u32[]{:S(2)}) collective-permute-start(f32[2,132,128]{2,1,0:T(8,128)S(1)} %concatenate.101), channel_id=1, source_target_pairs={{0,8},{1,9},{2,10},{3,11},{4,12},{5,13},{6,14},{7,15},{8,0},{9,1},... | collective-permute-start | bytes 405512 | tf_op jit(solution)/shard_map/ppermute | solution.py:51
  45.2 11.9 %collective-permute-start = (bf16[4,2,128,128]{3,2,1,0:T(8,128)(2,1)S(1)}, bf16[4,2,128,128]{3,2,1,0:T(8,128)(2,1)S(1)}, u32[]{:S(2)}, u32[]{:S(2)}) collective-permute-start(bf16[4,2,128,128]{3,2,1,0:T(8,128)(2,1)S(1)} %bitcast.370), channel_id=1, source_target_pairs={{0,1},{1,0},{2,3},{3,2},{4,5},{5,4},{6,7},{7,6},{8,9},{9,8},{10,11... | collective-permute-start | bytes 786440 | tf_op jit(solution)/shard_map/ppermute | solution.py:111
  47.2 12.0 %collective-permute-start.1 = (bf16[4,2,128,128]{3,2,1,0:T(8,128)(2,1)S(1)}, bf16[4,2,128,128]{3,2,1,0:T(8,128)(2,1)S(1)}, u32[]{:S(2)}, u32[]{:S(2)}) collective-permute-start(bf16[4,2,128,128]{3,2,1,0:T(8,128)(2,1)S(1)} %bitcast.371), channel_id=1, source_target_pairs={{0,2},{1,3},{2,0},{3,1},{4,6},{5,7},{6,4},{7,5},{8,10},{9,11},{10,... | collective-permute-start | bytes 786440 | tf_op jit(solution)/shard_map/ppermute | solution.py:111
  52.1 12.3 %collective-permute-start.2 = (bf16[4,2,128,128]{3,2,1,0:T(8,128)(2,1)S(1)}, bf16[4,2,128,128]{3,2,1,0:T(8,128)(2,1)S(1)}, u32[]{:S(2)}, u32[]{:S(2)}) collective-permute-start(bf16[4,2,128,128]{3,2,1,0:T(8,128)(2,1)S(1)} %bitcast.372), channel_id=1, source_target_pairs={{0,3},{1,2},{2,1},{3,0},{4,7},{5,6},{6,5},{7,4},{8,11},{9,10},{10,... | collective-permute-start | bytes 786440 | tf_op jit(solution)/shard_map/ppermute | solution.py:111
  55.1 21.7 %collective-permute-start.11 = (f32[2,132,128]{2,0,1:T(2,128)S(1)}, f32[2,132,128]{2,0,1:T(2,128)S(1)}, u32[]{:S(2)}, u32[]{:S(2)}) collective-permute-start(f32[2,132,128]{2,0,1:T(2,128)S(1)} %constant_dynamic-update-slice_fusion.16), channel_id=1, source_target_pairs={{0,1},{1,0},{2,3},{3,2},{4,5},{5,4},{6,7},{7,6},{8,9},{9,8},{10,11... | collective-permute-start | bytes 405512 | tf_op jit(solution)/shard_map/ppermute | solution.py:202
  64.5 12.9 %collective-permute-start.3 = (bf16[1,2,128,128]{3,2,1,0:T(8,128)(2,1)S(1)}, bf16[1,2,128,128]{3,2,1,0:T(8,128)(2,1)S(1)}, u32[]{:S(2)}, u32[]{:S(2)}) collective-permute-start(bf16[1,2,128,128]{3,2,1,0:T(8,128)(2,1)S(1)} %get-tuple-element.36), channel_id=1, source_target_pairs={{0,4},{1,5},{2,6},{3,7},{4,0},{5,1},{6,2},{7,3},{8,12},{9,13},{10,... | collective-permute-start | bytes 196616 | tf_op jit(solution)/shard_map/ppermute | solution.py:111
  68.8 11.0 %collective-permute-start.4 = (bf16[1,2,128,128]{3,2,1,0:T(8,128)(2,1)S(1)}, bf16[1,2,128,128]{3,2,1,0:T(8,128)(2,1)S(1)}, u32[]{:S(2)}, u32[]{:S(2)}) collective-permute-start(bf16[1,2,128,128]{3,2,1,0:T(8,128)(2,1)S(1)} %get-tuple-element.38), channel_id=1, source_target_pairs={{0,8},{1,9},{2,10},{3,11},{4,12},{5,13},{6,14},{7,15},{8,0},{9,1},... | collective-permute-start | bytes 196616 | tf_op jit(solution)/shard_map/ppermute | solution.py:111
  88.1 12.4 %collective-permute-start.13 = (f32[2,64,128]{2,1,0:T(8,128)S(1)}, f32[2,64,128]{2,1,0:T(8,128)S(1)}, u32[]{:S(2)}, u32[]{:S(2)}) collective-permute-start(f32[2,64,128]{2,1,0:T(8,128)S(1)} %add_select_fusion.3), channel_id=1, source_target_pairs={{0,32},{16,48},{32,0},{48,16},{64,96},{80,112},{96,64},{112,80},{1... | collective-permute-start | bytes 196616 | tf_op jit(solution)/shard_map/ppermute | solution.py:51
  92.6 10.4 %collective-permute-start.14 = (f32[2,64,128]{2,1,0:T(8,128)S(1)}, f32[2,64,128]{2,1,0:T(8,128)S(1)}, u32[]{:S(2)}, u32[]{:S(2)}) collective-permute-start(f32[2,64,128]{2,1,0:T(8,128)S(1)} %add_select_fusion.3), channel_id=1, source_target_pairs={{0,64},{16,80},{32,96},{48,112},{64,0},{80,16},{96,32},{112,48},{1... | collective-permute-start | bytes 196616 | tf_op jit(solution)/shard_map/ppermute | solution.py:51
  106.9 10.5 %collective-permute-start.16 = (f32[2,64,128]{2,1,0:T(8,128)S(1)}, f32[2,64,128]{2,1,0:T(8,128)S(1)}, u32[]{:S(2)}, u32[]{:S(2)}) collective-permute-start(f32[2,64,128]{2,1,0:T(8,128)S(1)} %fusion.162), channel_id=1, source_target_pairs={{0,128},{16,144},{32,160},{48,176},{64,192},{80,208},{96,224},{112... | collective-permute-start | bytes 196616 | tf_op jit(solution)/shard_map/ppermute | solution.py:51
  130.3 10.2 %collective-permute-start.21 = (f32[2,128,128]{2,1,0:T(8,128)S(1)}, f32[2,128,128]{2,1,0:T(8,128)S(1)}, u32[]{:S(2)}, u32[]{:S(2)}) collective-permute-start(f32[2,128,128]{2,1,0:T(8,128)S(1)} %slice_select_fusion.2), channel_id=1, source_target_pairs={{0,2},{1,3},{2,0},{3,1},{4,6},{5,7},{6,4},{7,5},{8,10},{9,11},{10,... | collective-permute-start | bytes 393224 | tf_op jit(solution)/shard_map/ppermute | solution.py:51
  134.1 13.8 %collective-permute-start.22 = (f32[2,128,128]{2,1,0:T(8,128)S(1)}, f32[2,128,128]{2,1,0:T(8,128)S(1)}, u32[]{:S(2)}, u32[]{:S(2)}) collective-permute-start(f32[2,128,128]{2,1,0:T(8,128)S(1)} %slice_select_fusion.2), channel_id=1, source_target_pairs={{0,4},{1,5},{2,6},{3,7},{4,0},{5,1},{6,2},{7,3},{8,12},{9,13},{10,... | collective-permute-start | bytes 393224 | tf_op jit(solution)/shard_map/ppermute | solution.py:51
  136.9 11.0 %collective-permute-start.23 = (f32[2,128,128]{2,1,0:T(8,128)S(1)}, f32[2,128,128]{2,1,0:T(8,128)S(1)}, u32[]{:S(2)}, u32[]{:S(2)}) collective-permute-start(f32[2,128,128]{2,1,0:T(8,128)S(1)} %slice_select_fusion.2), channel_id=1, source_target_pairs={{0,6},{1,7},{2,4},{3,5},{4,2},{5,3},{6,0},{7,1},{8,14},{9,15},{10,... | collective-permute-start | bytes 393224 | tf_op jit(solution)/shard_map/ppermute | solution.py:51
  148.0 10.9 %collective-permute-start.24 = (f32[2,128,128]{2,1,0:T(8,128)S(1)}, f32[2,128,128]{2,1,0:T(8,128)S(1)}, u32[]{:S(2)}, u32[]{:S(2)}) collective-permute-start(f32[2,128,128]{2,1,0:T(8,128)S(1)} %fusion.160), channel_id=1, source_target_pairs={{0,8},{1,9},{2,10},{3,11},{4,12},{5,13},{6,14},{7,15},{8,0},{9,1},... | collective-permute-start | bytes 393224 | tf_op jit(solution)/shard_map/ppermute | solution.py:51
  168.8 12.2 %collective-permute-start.27 = (f32[2,64,128]{2,1,0:T(8,128)S(1)}, f32[2,64,128]{2,1,0:T(8,128)S(1)}, u32[]{:S(2)}, u32[]{:S(2)}) collective-permute-start(f32[2,64,128]{2,1,0:T(8,128)S(1)} %add_select_fusion.2), channel_id=1, source_target_pairs={{0,32},{16,48},{32,0},{48,16},{64,96},{80,112},{96,64},{112,80},{1... | collective-permute-start | bytes 196616 | tf_op jit(solution)/shard_map/ppermute | solution.py:51
  184.5 10.5 %collective-permute-start.32 = (f32[2,64,128]{2,1,0:T(8,128)S(1)}, f32[2,64,128]{2,1,0:T(8,128)S(1)}, u32[]{:S(2)}, u32[]{:S(2)}) collective-permute-start(f32[2,64,128]{2,1,0:T(8,128)S(1)} %fusion.159), channel_id=1, source_target_pairs={{0,384},{16,400},{32,416},{48,432},{64,448},{80,464},{96,480},{112... | collective-permute-start | bytes 196616 | tf_op jit(solution)/shard_map/ppermute | solution.py:51
  209.6 12.8 %collective-permute-start.35 = (f32[2,128,128]{2,1,0:T(8,128)S(1)}, f32[2,128,128]{2,1,0:T(8,128)S(1)}, u32[]{:S(2)}, u32[]{:S(2)}) collective-permute-start(f32[2,128,128]{2,1,0:T(8,128)S(1)} %slice_select_fusion.1), channel_id=1, source_target_pairs={{0,2},{1,3},{2,0},{3,1},{4,6},{5,7},{6,4},{7,5},{8,10},{9,11},{10,... | collective-permute-start | bytes 393224 | tf_op jit(solution)/shard_map/ppermute | solution.py:51
  216.2 13.9 %collective-permute-start.36 = (f32[2,128,128]{2,1,0:T(8,128)S(1)}, f32[2,128,128]{2,1,0:T(8,128)S(1)}, u32[]{:S(2)}, u32[]{:S(2)}) collective-permute-start(f32[2,128,128]{2,1,0:T(8,128)S(1)} %slice_select_fusion.1), channel_id=1, source_target_pairs={{0,4},{1,5},{2,6},{3,7},{4,0},{5,1},{6,2},{7,3},{8,12},{9,13},{10,... | collective-permute-start | bytes 393224 | tf_op jit(solution)/shard_map/ppermute | solution.py:51
  218.5 11.5 %collective-permute-start.37 = (f32[2,128,128]{2,1,0:T(8,128)S(1)}, f32[2,128,128]{2,1,0:T(8,128)S(1)}, u32[]{:S(2)}, u32[]{:S(2)}) collective-permute-start(f32[2,128,128]{2,1,0:T(8,128)S(1)} %slice_select_fusion.1), channel_id=1, source_target_pairs={{0,6},{1,7},{2,4},{3,5},{4,2},{5,3},{6,0},{7,1},{8,14},{9,15},{10,... | collective-permute-start | bytes 393224 | tf_op jit(solution)/shard_map/ppermute | solution.py:51
  230.1 10.8 %collective-permute-start.38 = (f32[2,128,128]{2,1,0:T(8,128)S(1)}, f32[2,128,128]{2,1,0:T(8,128)S(1)}, u32[]{:S(2)}, u32[]{:S(2)}) collective-permute-start(f32[2,128,128]{2,1,0:T(8,128)S(1)} %fusion.157), channel_id=1, source_target_pairs={{0,8},{1,9},{2,10},{3,11},{4,12},{5,13},{6,14},{7,15},{8,0},{9,1},... | collective-permute-start | bytes 393224 | tf_op jit(solution)/shard_map/ppermute | solution.py:51
  250.9 12.2 %collective-permute-start.41 = (f32[2,64,128]{2,1,0:T(8,128)S(1)}, f32[2,64,128]{2,1,0:T(8,128)S(1)}, u32[]{:S(2)}, u32[]{:S(2)}) collective-permute-start(f32[2,64,128]{2,1,0:T(8,128)S(1)} %add_select_fusion.1), channel_id=1, source_target_pairs={{0,32},{16,48},{32,0},{48,16},{64,96},{80,112},{96,64},{112,80},{1... | collective-permute-start | bytes 196616 | tf_op jit(solution)/shard_map/ppermute | solution.py:51
  268.5 10.5 %collective-permute-start.44 = (f32[2,64,128]{2,1,0:T(8,128)S(1)}, f32[2,64,128]{2,1,0:T(8,128)S(1)}, u32[]{:S(2)}, u32[]{:S(2)}) collective-permute-start(f32[2,64,128]{2,1,0:T(8,128)S(1)} %fusion.156), channel_id=1, source_target_pairs={{0,128},{16,144},{32,160},{48,176},{64,192},{80,208},{96,224},{112... | collective-permute-start | bytes 196616 | tf_op jit(solution)/shard_map/ppermute | solution.py:51
  293.3 12.8 %collective-permute-start.49 = (f32[2,128,128]{2,1,0:T(8,128)S(1)}, f32[2,128,128]{2,1,0:T(8,128)S(1)}, u32[]{:S(2)}, u32[]{:S(2)}) collective-permute-start(f32[2,128,128]{2,1,0:T(8,128)S(1)} %slice_select_fusion), channel_id=1, source_target_pairs={{0,2},{1,3},{2,0},{3,1},{4,6},{5,7},{6,4},{7,5},{8,10},{9,11},{10,... | collective-permute-start | bytes 393224 | tf_op jit(solution)/shard_map/ppermute | solution.py:51
  299.9 13.9 %collective-permute-start.50 = (f32[2,128,128]{2,1,0:T(8,128)S(1)}, f32[2,128,128]{2,1,0:T(8,128)S(1)}, u32[]{:S(2)}, u32[]{:S(2)}) collective-permute-start(f32[2,128,128]{2,1,0:T(8,128)S(1)} %slice_select_fusion), channel_id=1, source_target_pairs={{0,4},{1,5},{2,6},{3,7},{4,0},{5,1},{6,2},{7,3},{8,12},{9,13},{10,... | collective-permute-start | bytes 393224 | tf_op jit(solution)/shard_map/ppermute | solution.py:51
  302.2 11.5 %collective-permute-start.51 = (f32[2,128,128]{2,1,0:T(8,128)S(1)}, f32[2,128,128]{2,1,0:T(8,128)S(1)}, u32[]{:S(2)}, u32[]{:S(2)}) collective-permute-start(f32[2,128,128]{2,1,0:T(8,128)S(1)} %slice_select_fusion), channel_id=1, source_target_pairs={{0,6},{1,7},{2,4},{3,5},{4,2},{5,3},{6,0},{7,1},{8,14},{9,15},{10,... | collective-permute-start | bytes 393224 | tf_op jit(solution)/shard_map/ppermute | solution.py:51
  313.8 10.8 %collective-permute-start.52 = (f32[2,128,128]{2,1,0:T(8,128)S(1)}, f32[2,128,128]{2,1,0:T(8,128)S(1)}, u32[]{:S(2)}, u32[]{:S(2)}) collective-permute-start(f32[2,128,128]{2,1,0:T(8,128)S(1)} %fusion.154), channel_id=1, source_target_pairs={{0,8},{1,9},{2,10},{3,11},{4,12},{5,13},{6,14},{7,15},{8,0},{9,1},... | collective-permute-start | bytes 393224 | tf_op jit(solution)/shard_map/ppermute | solution.py:51
  334.5 12.2 %collective-permute-start.55 = (f32[2,64,128]{2,1,0:T(8,128)S(1)}, f32[2,64,128]{2,1,0:T(8,128)S(1)}, u32[]{:S(2)}, u32[]{:S(2)}) collective-permute-start(f32[2,64,128]{2,1,0:T(8,128)S(1)} %add_select_fusion), channel_id=1, source_target_pairs={{0,32},{16,48},{32,0},{48,16},{64,96},{80,112},{96,64},{112,80},{1... | collective-permute-start | bytes 196616 | tf_op jit(solution)/shard_map/ppermute | solution.py:51
  338.8 10.8 %collective-permute-start.56 = (f32[2,64,128]{2,1,0:T(8,128)S(1)}, f32[2,64,128]{2,1,0:T(8,128)S(1)}, u32[]{:S(2)}, u32[]{:S(2)}) collective-permute-start(f32[2,64,128]{2,1,0:T(8,128)S(1)} %add_select_fusion), channel_id=1, source_target_pairs={{0,64},{16,80},{32,96},{48,112},{64,0},{80,16},{96,32},{112,48},{1... | collective-permute-start | bytes 196616 | tf_op jit(solution)/shard_map/ppermute | solution.py:51
  350.4 10.5 %collective-permute-start.58 = (f32[2,64,128]{2,1,0:T(8,128)S(1)}, f32[2,64,128]{2,1,0:T(8,128)S(1)}, u32[]{:S(2)}, u32[]{:S(2)}) collective-permute-start(f32[2,64,128]{2,1,0:T(8,128)S(1)} %fusion.153), channel_id=1, source_target_pairs={{0,128},{16,144},{32,160},{48,176},{64,192},{80,208},{96,224},{112... | collective-permute-start | bytes 196616 | tf_op jit(solution)/shard_map/ppermute | solution.py:51
  (34 other events, 231.3 us)

commit v7 on v6

--- a/solution.py
+++ b/solution.py
@@ -63,7 +63,7 @@
 
 
 def bit_stages(bits):
-    return [bits[b : b + 2] for b in range(0, len(bits), 2)]
+    return [[b] for b in bits]
 
 
 def group_sum(value, axis):

time: 377 us -> 377 us (level)
  waiting for transfers between devices: 125 us -> 177 us
  starting transfers between devices: 225 us -> 175 us
    ppermute x44 -> x32, waiting for transfers between devices: 84.5 us -> 136 us  [gather_bits(): got.append(lax.ppermute(value, axis, pairs))]
    ppermute x44 -> x32, starting transfers between devices: 170 us -> 126 us  [gather_bits(): got.append(lax.ppermute(value, axis, pairs))]
  transfers between devices with their start and end apart: 62 -> 50, of which waited for: 39 -> 46; matrix products, arithmetic and copies ran while one was open for 1% -> 1% of each run, Pallas kernels for 0% -> 0%
where the time goes in v7:
time: 377 us; the launch traced here: 376 us
  waiting for transfers between devices  177 us (47%)
  starting transfers between devices  175 us (46%)
  other arithmetic  11 us (3%)
  matrix products  8.78 us (2%)
    ppermute x32, waiting for transfers between devices, gather_bits(): got.append(lax.ppermute(value, axis, pairs))  136 us
    ppermute x32, starting transfers between devices, gather_bits(): got.append(lax.ppermute(value, axis, pairs))  126 us
    ppermute x6, starting transfers between devices, scatter_groups(): total = total + lax.ppermute(give, axis, pairs)  19.8 us
    ppermute x4, waiting for transfers between devices, group_sum(): other = lax.ppermute(mine, axis, pairs)  14.7 us
    ppermute x4, waiting for transfers between devices, group_sum(): arrived = lax.ppermute(jnp.where(low, second, first), axis, pairs)  13.3 us
    ppermute x4, starting transfers between devices, group_sum(): arrived = lax.ppermute(jnp.where(low, second, first), axis, pairs)  11.3 us
    ppermute x4, starting transfers between devices, group_sum(): other = lax.ppermute(mine, axis, pairs)  9.89 us
    ppermute x6, waiting for transfers between devices, scatter_groups(): total = total + lax.ppermute(give, axis, pairs)  9.71 us
  transfers between devices with their start and end apart: 50, of which 46 were waited for; matrix products, arithmetic and copies ran while one was open for 1% of the time, Pallas kernels for 0%

profile of v7, /device:TPU:6, one launch (start us, length us, event | category | flops | bytes accessed | tf_op | source)
XLA Modules:
  0.0 375.8 jit_solution(11449582973786982129)
XLA Ops:
  13.5 4.3 %collective-permute-start.7 = (f32[2,132,128]{2,0,1:T(2,128)S(1)}, f32[2,132,128]{2,0,1:T(2,128)S(1)}, u32[]{:S(2)}, u32[]{:S(2)}) collective-permute-start(f32[2,132,128]{2,0,1:T(2,128)S(1)} %bitcast.382), channel_id=1, source_target_pairs={{0,2},{1,3},{2,0},{3,1},{4,6},{5,7},{6,4},{7,5},{8,10},{9,11},{10,... | collective-permute-start | bytes 405512 | tf_op jit(solution)/shard_map/ppermute | solution.py:51
  22.6 6.1 %collective-permute-start.8 = (f32[2,132,128]{2,0,1:T(2,128)S(1)}, f32[2,132,128]{2,0,1:T(2,128)S(1)}, u32[]{:S(2)}, u32[]{:S(2)}) collective-permute-start(f32[2,132,128]{2,0,1:T(2,128)S(1)} %constant_dynamic-update-slice_fusion.16), channel_id=1, source_target_pairs={{0,4},{1,5},{2,6},{3,7},{4,0},{5,1},{6,2},{7,3},{8,12},{9,13},{10,... | collective-permute-start | bytes 405512 | tf_op jit(solution)/shard_map/ppermute | solution.py:51
  35.4 8.5 %collective-permute-start.9 = (f32[2,132,128]{2,1,0:T(8,128)S(1)}, f32[2,132,128]{2,1,0:T(8,128)S(1)}, u32[]{:S(2)}, u32[]{:S(2)}) collective-permute-start(f32[2,132,128]{2,1,0:T(8,128)S(1)} %concatenate.105), channel_id=1, source_target_pairs={{0,8},{1,9},{2,10},{3,11},{4,12},{5,13},{6,14},{7,15},{8,0},{9,1},... | collective-permute-start | bytes 405512 | tf_op jit(solution)/shard_map/ppermute | solution.py:51
  57.0 4.7 %collective-permute-done.2 = bf16[4,2,128,128]{3,2,1,0:T(8,128)(2,1)S(1)} collective-permute-done((bf16[4,2,128,128]{3,2,1,0:T(8,128)(2,1)S(1)}, bf16[4,2,128,128]{3,2,1,0:T(8,128)(2,1)S(1)}, u32[]{:S(2)}, u32[]{:S(2)}) %collective-permute-start.2) | collective-permute-done | bytes 262176 | tf_op jit(solution)/shard_map/ppermute | solution.py:111
  61.8 4.3 %collective-permute-start.3 = (bf16[1,2,128,128]{3,2,1,0:T(8,128)(2,1)S(1)}, bf16[1,2,128,128]{3,2,1,0:T(8,128)(2,1)S(1)}, u32[]{:S(2)}, u32[]{:S(2)}) collective-permute-start(bf16[1,2,128,128]{3,2,1,0:T(8,128)(2,1)S(1)} %get-tuple-element.35), channel_id=1, source_target_pairs={{0,4},{1,5},{2,6},{3,7},{4,0},{5,1},{6,2},{7,3},{8,12},{9,13},{10,... | collective-permute-start | bytes 196616 | tf_op jit(solution)/shard_map/ppermute | solution.py:111
  68.9 5.1 %collective-permute-start.5 = (bf16[1,2,128,128]{3,2,1,0:T(8,128)(2,1)S(1)}, bf16[1,2,128,128]{3,2,1,0:T(8,128)(2,1)S(1)}, u32[]{:S(2)}, u32[]{:S(2)}) collective-permute-start(bf16[1,2,128,128]{3,2,1,0:T(8,128)(2,1)S(1)} %get-tuple-element.36), channel_id=1, source_target_pairs={{0,12},{1,13},{2,14},{3,15},{4,8},{5,9},{6,10},{7,11},{8,4},{9,5},... | collective-permute-start | bytes 196616 | tf_op jit(solution)/shard_map/ppermute | solution.py:111
  84.2 4.5 %collective-permute-start.12 = (f32[2,64,128]{2,1,0:T(8,128)S(1)}, f32[2,64,128]{2,1,0:T(8,128)S(1)}, u32[]{:S(2)}, u32[]{:S(2)}) collective-permute-start(f32[2,64,128]{2,1,0:T(8,128)S(1)} %add_select_fusion.3), channel_id=1, source_target_pairs={{0,32},{16,48},{32,0},{48,16},{64,96},{80,112},{96,64},{112,80},{1... | collective-permute-start | bytes 196616 | tf_op jit(solution)/shard_map/ppermute | solution.py:51
  91.3 8.4 %collective-permute-start.13 = (f32[2,64,128]{2,1,0:T(8,128)S(1)}, f32[2,64,128]{2,1,0:T(8,128)S(1)}, u32[]{:S(2)}, u32[]{:S(2)}) collective-permute-start(f32[2,64,128]{2,1,0:T(8,128)S(1)} %bitcast.361), channel_id=1, source_target_pairs={{0,64},{16,80},{32,96},{48,112},{64,0},{80,16},{96,32},{112,48},{1... | collective-permute-start | bytes 196616 | tf_op jit(solution)/shard_map/ppermute | solution.py:51
  111.9 4.7 %collective-permute-done.15 = f32[2,64,128]{2,1,0:T(8,128)S(1)} collective-permute-done((f32[2,64,128]{2,1,0:T(8,128)S(1)}, f32[2,64,128]{2,1,0:T(8,128)S(1)}, u32[]{:S(2)}, u32[]{:S(2)}) %collective-permute-start.15) | collective-permute-done | bytes 65568 | tf_op jit(solution)/shard_map/ppermute | solution.py:51
  126.9 4.8 %collective-permute-start.18 = (f32[2,128,128]{2,1,0:T(8,128)S(1)}, f32[2,128,128]{2,1,0:T(8,128)S(1)}, u32[]{:S(2)}, u32[]{:S(2)}) collective-permute-start(f32[2,128,128]{2,1,0:T(8,128)S(1)} %slice_select_fusion.2), channel_id=1, source_target_pairs={{0,2},{1,3},{2,0},{3,1},{4,6},{5,7},{6,4},{7,5},{8,10},{9,11},{10,... | collective-permute-start | bytes 393224 | tf_op jit(solution)/shard_map/ppermute | solution.py:51
  135.5 4.9 %collective-permute-start.19 = (f32[2,128,128]{2,1,0:T(8,128)S(1)}, f32[2,128,128]{2,1,0:T(8,128)S(1)}, u32[]{:S(2)}, u32[]{:S(2)}) collective-permute-start(f32[2,128,128]{2,1,0:T(8,128)S(1)} %bitcast.354), channel_id=1, source_target_pairs={{0,4},{1,5},{2,6},{3,7},{4,0},{5,1},{6,2},{7,3},{8,12},{9,13},{10,... | collective-permute-start | bytes 393224 | tf_op jit(solution)/shard_map/ppermute | solution.py:51
  140.4 5.7 %collective-permute-done.19 = f32[2,128,128]{2,1,0:T(8,128)S(1)} collective-permute-done((f32[2,128,128]{2,1,0:T(8,128)S(1)}, f32[2,128,128]{2,1,0:T(8,128)S(1)}, u32[]{:S(2)}, u32[]{:S(2)}) %collective-permute-start.19) | collective-permute-done | bytes 131104 | tf_op jit(solution)/shard_map/ppermute | solution.py:51
  146.1 5.2 %collective-permute-start.20 = (f32[2,128,128]{2,1,0:T(8,128)S(1)}, f32[2,128,128]{2,1,0:T(8,128)S(1)}, u32[]{:S(2)}, u32[]{:S(2)}) collective-permute-start(f32[2,128,128]{2,1,0:T(8,128)S(1)} %bitcast.355), channel_id=1, source_target_pairs={{0,8},{1,9},{2,10},{3,11},{4,12},{5,13},{6,14},{7,15},{8,0},{9,1},... | collective-permute-start | bytes 393224 | tf_op jit(solution)/shard_map/ppermute | solution.py:51
  151.4 7.7 %collective-permute-done.20 = f32[2,128,128]{2,1,0:T(8,128)S(1)} collective-permute-done((f32[2,128,128]{2,1,0:T(8,128)S(1)}, f32[2,128,128]{2,1,0:T(8,128)S(1)}, u32[]{:S(2)}, u32[]{:S(2)}) %collective-permute-start.20) | collective-permute-done | bytes 131104 | tf_op jit(solution)/shard_map/ppermute | solution.py:51
  169.0 4.1 %collective-permute-start.23 = (f32[2,64,128]{2,1,0:T(8,128)S(1)}, f32[2,64,128]{2,1,0:T(8,128)S(1)}, u32[]{:S(2)}, u32[]{:S(2)}) collective-permute-start(f32[2,64,128]{2,1,0:T(8,128)S(1)} %add_select_fusion.2), channel_id=1, source_target_pairs={{0,32},{16,48},{32,0},{48,16},{64,96},{80,112},{96,64},{112,80},{1... | collective-permute-start | bytes 196616 | tf_op jit(solution)/shard_map/ppermute | solution.py:51
  176.8 7.6 %collective-permute-start.24 = (f32[2,64,128]{2,1,0:T(8,128)S(1)}, f32[2,64,128]{2,1,0:T(8,128)S(1)}, u32[]{:S(2)}, u32[]{:S(2)}) collective-permute-start(f32[2,64,128]{2,1,0:T(8,128)S(1)} %bitcast.365), channel_id=1, source_target_pairs={{0,64},{16,80},{32,96},{48,112},{64,0},{80,16},{96,32},{112,48},{1... | collective-permute-start | bytes 196616 | tf_op jit(solution)/shard_map/ppermute | solution.py:51
  189.6 4.2 %collective-permute-done.25 = f32[2,64,128]{2,1,0:T(8,128)S(1)} collective-permute-done((f32[2,64,128]{2,1,0:T(8,128)S(1)}, f32[2,64,128]{2,1,0:T(8,128)S(1)}, u32[]{:S(2)}, u32[]{:S(2)}) %collective-permute-start.25) | collective-permute-done | bytes 65568 | tf_op jit(solution)/shard_map/ppermute | solution.py:51
  196.3 5.1 %collective-permute-done.26 = f32[2,64,128]{2,1,0:T(8,128)S(1)} collective-permute-done((f32[2,64,128]{2,1,0:T(8,128)S(1)}, f32[2,64,128]{2,1,0:T(8,128)S(1)}, u32[]{:S(2)}, u32[]{:S(2)}) %collective-permute-start.26) | collective-permute-done | bytes 65568 | tf_op jit(solution)/shard_map/ppermute | solution.py:51
  213.7 5.5 %collective-permute-done.29 = f32[2,128,128]{2,1,0:T(8,128)S(1)} collective-permute-done((f32[2,128,128]{2,1,0:T(8,128)S(1)}, f32[2,128,128]{2,1,0:T(8,128)S(1)}, u32[]{:S(2)}, u32[]{:S(2)}) %collective-permute-start.29) | collective-permute-done | bytes 131104 | tf_op jit(solution)/shard_map/ppermute | solution.py:51
  222.2 7.4 %collective-permute-done.30 = f32[2,128,128]{2,1,0:T(8,128)S(1)} collective-permute-done((f32[2,128,128]{2,1,0:T(8,128)S(1)}, f32[2,128,128]{2,1,0:T(8,128)S(1)}, u32[]{:S(2)}, u32[]{:S(2)}) %collective-permute-start.30) | collective-permute-done | bytes 131104 | tf_op jit(solution)/shard_map/ppermute | solution.py:51
  229.6 4.5 %collective-permute-start.31 = (f32[2,128,128]{2,1,0:T(8,128)S(1)}, f32[2,128,128]{2,1,0:T(8,128)S(1)}, u32[]{:S(2)}, u32[]{:S(2)}) collective-permute-start(f32[2,128,128]{2,1,0:T(8,128)S(1)} %bitcast.357), channel_id=1, source_target_pairs={{0,8},{1,9},{2,10},{3,11},{4,12},{5,13},{6,14},{7,15},{8,0},{9,1},... | collective-permute-start | bytes 393224 | tf_op jit(solution)/shard_map/ppermute | solution.py:51
  234.1 8.7 %collective-permute-done.31 = f32[2,128,128]{2,1,0:T(8,128)S(1)} collective-permute-done((f32[2,128,128]{2,1,0:T(8,128)S(1)}, f32[2,128,128]{2,1,0:T(8,128)S(1)}, u32[]{:S(2)}, u32[]{:S(2)}) %collective-permute-start.31) | collective-permute-done | bytes 131104 | tf_op jit(solution)/shard_map/ppermute | solution.py:51
  260.5 7.2 %collective-permute-start.35 = (f32[2,64,128]{2,1,0:T(8,128)S(1)}, f32[2,64,128]{2,1,0:T(8,128)S(1)}, u32[]{:S(2)}, u32[]{:S(2)}) collective-permute-start(f32[2,64,128]{2,1,0:T(8,128)S(1)} %bitcast.368), channel_id=1, source_target_pairs={{0,64},{16,80},{32,96},{48,112},{64,0},{80,16},{96,32},{112,48},{1... | collective-permute-start | bytes 196616 | tf_op jit(solution)/shard_map/ppermute | solution.py:51
  279.4 5.2 %collective-permute-done.37 = f32[2,64,128]{2,1,0:T(8,128)S(1)} collective-permute-done((f32[2,64,128]{2,1,0:T(8,128)S(1)}, f32[2,64,128]{2,1,0:T(8,128)S(1)}, u32[]{:S(2)}, u32[]{:S(2)}) %collective-permute-start.37) | collective-permute-done | bytes 65568 | tf_op jit(solution)/shard_map/ppermute | solution.py:51
  297.5 5.5 %collective-permute-done.40 = f32[2,128,128]{2,1,0:T(8,128)S(1)} collective-permute-done((f32[2,128,128]{2,1,0:T(8,128)S(1)}, f32[2,128,128]{2,1,0:T(8,128)S(1)}, u32[]{:S(2)}, u32[]{:S(2)}) %collective-permute-start.40) | collective-permute-done | bytes 131104 | tf_op jit(solution)/shard_map/ppermute | solution.py:51
  306.0 7.4 %collective-permute-done.41 = f32[2,128,128]{2,1,0:T(8,128)S(1)} collective-permute-done((f32[2,128,128]{2,1,0:T(8,128)S(1)}, f32[2,128,128]{2,1,0:T(8,128)S(1)}, u32[]{:S(2)}, u32[]{:S(2)}) %collective-permute-start.41) | collective-permute-done | bytes 131104 | tf_op jit(solution)/shard_map/ppermute | solution.py:51
  313.4 5.1 %collective-permute-start.42 = (f32[2,128,128]{2,1,0:T(8,128)S(1)}, f32[2,128,128]{2,1,0:T(8,128)S(1)}, u32[]{:S(2)}, u32[]{:S(2)}) collective-permute-start(f32[2,128,128]{2,1,0:T(8,128)S(1)} %bitcast.353), channel_id=1, source_target_pairs={{0,8},{1,9},{2,10},{3,11},{4,12},{5,13},{6,14},{7,15},{8,0},{9,1},... | collective-permute-start | bytes 393224 | tf_op jit(solution)/shard_map/ppermute | solution.py:51
  318.5 8.7 %collective-permute-done.42 = f32[2,128,128]{2,1,0:T(8,128)S(1)} collective-permute-done((f32[2,128,128]{2,1,0:T(8,128)S(1)}, f32[2,128,128]{2,1,0:T(8,128)S(1)}, u32[]{:S(2)}, u32[]{:S(2)}) %collective-permute-start.42) | collective-permute-done | bytes 131104 | tf_op jit(solution)/shard_map/ppermute | solution.py:51
  340.8 4.1 %collective-permute-done.45 = f32[2,64,128]{2,1,0:T(8,128)S(1)} collective-permute-done((f32[2,64,128]{2,1,0:T(8,128)S(1)}, f32[2,64,128]{2,1,0:T(8,128)S(1)}, u32[]{:S(2)}, u32[]{:S(2)}) %collective-permute-start.45) | collective-permute-done | bytes 65568 | tf_op jit(solution)/shard_map/ppermute | solution.py:51
  344.9 7.0 %collective-permute-start.46 = (f32[2,64,128]{2,1,0:T(8,128)S(1)}, f32[2,64,128]{2,1,0:T(8,128)S(1)}, u32[]{:S(2)}, u32[]{:S(2)}) collective-permute-start(f32[2,64,128]{2,1,0:T(8,128)S(1)} %bitcast.362), channel_id=1, source_target_pairs={{0,64},{16,80},{32,96},{48,112},{64,0},{80,16},{96,32},{112,48},{1... | collective-permute-start | bytes 196616 | tf_op jit(solution)/shard_map/ppermute | solution.py:51
  356.9 4.3 %collective-permute-done.47 = f32[2,64,128]{2,1,0:T(8,128)S(1)} collective-permute-done((f32[2,64,128]{2,1,0:T(8,128)S(1)}, f32[2,64,128]{2,1,0:T(8,128)S(1)}, u32[]{:S(2)}, u32[]{:S(2)}) %collective-permute-start.47) | collective-permute-done | bytes 65568 | tf_op jit(solution)/shard_map/ppermute | solution.py:51
  363.5 5.4 %collective-permute-done.48 = f32[2,64,128]{2,1,0:T(8,128)S(1)} collective-permute-done((f32[2,64,128]{2,1,0:T(8,128)S(1)}, f32[2,64,128]{2,1,0:T(8,128)S(1)}, u32[]{:S(2)}, u32[]{:S(2)}) %collective-permute-start.48) | collective-permute-done | bytes 65568 | tf_op jit(solution)/shard_map/ppermute | solution.py:51
  (231 shorter events, 187.9 us)
Async XLA Ops:
  13.5 8.2 %collective-permute-start.7 = (f32[2,132,128]{2,0,1:T(2,128)S(1)}, f32[2,132,128]{2,0,1:T(2,128)S(1)}, u32[]{:S(2)}, u32[]{:S(2)}) collective-permute-start(f32[2,132,128]{2,0,1:T(2,128)S(1)} %bitcast.382), channel_id=1, source_target_pairs={{0,2},{1,3},{2,0},{3,1},{4,6},{5,7},{6,4},{7,5},{8,10},{9,11},{10,... | collective-permute-start | bytes 405512 | tf_op jit(solution)/shard_map/ppermute | solution.py:51
  22.6 12.3 %collective-permute-start.8 = (f32[2,132,128]{2,0,1:T(2,128)S(1)}, f32[2,132,128]{2,0,1:T(2,128)S(1)}, u32[]{:S(2)}, u32[]{:S(2)}) collective-permute-start(f32[2,132,128]{2,0,1:T(2,128)S(1)} %constant_dynamic-update-slice_fusion.16), channel_id=1, source_target_pairs={{0,4},{1,5},{2,6},{3,7},{4,0},{5,1},{6,2},{7,3},{8,12},{9,13},{10,... | collective-permute-start | bytes 405512 | tf_op jit(solution)/shard_map/ppermute | solution.py:51
  35.4 16.3 %collective-permute-start.9 = (f32[2,132,128]{2,1,0:T(8,128)S(1)}, f32[2,132,128]{2,1,0:T(8,128)S(1)}, u32[]{:S(2)}, u32[]{:S(2)}) collective-permute-start(f32[2,132,128]{2,1,0:T(8,128)S(1)} %concatenate.105), channel_id=1, source_target_pairs={{0,8},{1,9},{2,10},{3,11},{4,12},{5,13},{6,14},{7,15},{8,0},{9,1},... | collective-permute-start | bytes 405512 | tf_op jit(solution)/shard_map/ppermute | solution.py:51
  44.0 10.8 %collective-permute-start = (bf16[4,2,128,128]{3,2,1,0:T(8,128)(2,1)S(1)}, bf16[4,2,128,128]{3,2,1,0:T(8,128)(2,1)S(1)}, u32[]{:S(2)}, u32[]{:S(2)}) collective-permute-start(bf16[4,2,128,128]{3,2,1,0:T(8,128)(2,1)S(1)} %bitcast.371), channel_id=1, source_target_pairs={{0,1},{1,0},{2,3},{3,2},{4,5},{5,4},{6,7},{7,6},{8,9},{9,8},{10,11... | collective-permute-start | bytes 786440 | tf_op jit(solution)/shard_map/ppermute | solution.py:111
  45.9 11.1 %collective-permute-start.1 = (bf16[4,2,128,128]{3,2,1,0:T(8,128)(2,1)S(1)}, bf16[4,2,128,128]{3,2,1,0:T(8,128)(2,1)S(1)}, u32[]{:S(2)}, u32[]{:S(2)}) collective-permute-start(bf16[4,2,128,128]{3,2,1,0:T(8,128)(2,1)S(1)} %bitcast.372), channel_id=1, source_target_pairs={{0,2},{1,3},{2,0},{3,1},{4,6},{5,7},{6,4},{7,5},{8,10},{9,11},{10,... | collective-permute-start | bytes 786440 | tf_op jit(solution)/shard_map/ppermute | solution.py:111
  48.3 13.3 %collective-permute-start.2 = (bf16[4,2,128,128]{3,2,1,0:T(8,128)(2,1)S(1)}, bf16[4,2,128,128]{3,2,1,0:T(8,128)(2,1)S(1)}, u32[]{:S(2)}, u32[]{:S(2)}) collective-permute-start(bf16[4,2,128,128]{3,2,1,0:T(8,128)(2,1)S(1)} %bitcast.373), channel_id=1, source_target_pairs={{0,3},{1,2},{2,1},{3,0},{4,7},{5,6},{6,5},{7,4},{8,11},{9,10},{10,... | collective-permute-start | bytes 786440 | tf_op jit(solution)/shard_map/ppermute | solution.py:111
  52.6 21.4 %collective-permute-start.10 = (f32[2,132,128]{2,0,1:T(2,128)S(1)}, f32[2,132,128]{2,0,1:T(2,128)S(1)}, u32[]{:S(2)}, u32[]{:S(2)}) collective-permute-start(f32[2,132,128]{2,0,1:T(2,128)S(1)} %constant_dynamic-update-slice_fusion.20), channel_id=1, source_target_pairs={{0,1},{1,0},{2,3},{3,2},{4,5},{5,4},{6,7},{7,6},{8,9},{9,8},{10,11... | collective-permute-start | bytes 405512 | tf_op jit(solution)/shard_map/ppermute | solution.py:202
  61.8 12.9 %collective-permute-start.3 = (bf16[1,2,128,128]{3,2,1,0:T(8,128)(2,1)S(1)}, bf16[1,2,128,128]{3,2,1,0:T(8,128)(2,1)S(1)}, u32[]{:S(2)}, u32[]{:S(2)}) collective-permute-start(bf16[1,2,128,128]{3,2,1,0:T(8,128)(2,1)S(1)} %get-tuple-element.35), channel_id=1, source_target_pairs={{0,4},{1,5},{2,6},{3,7},{4,0},{5,1},{6,2},{7,3},{8,12},{9,13},{10,... | collective-permute-start | bytes 196616 | tf_op jit(solution)/shard_map/ppermute | solution.py:111
  66.1 10.2 %collective-permute-start.4 = (bf16[1,2,128,128]{3,2,1,0:T(8,128)(2,1)S(1)}, bf16[1,2,128,128]{3,2,1,0:T(8,128)(2,1)S(1)}, u32[]{:S(2)}, u32[]{:S(2)}) collective-permute-start(bf16[1,2,128,128]{3,2,1,0:T(8,128)(2,1)S(1)} %get-tuple-element.37), channel_id=1, source_target_pairs={{0,8},{1,9},{2,10},{3,11},{4,12},{5,13},{6,14},{7,15},{8,0},{9,1},... | collective-permute-start | bytes 196616 | tf_op jit(solution)/shard_map/ppermute | solution.py:111
  68.9 8.6 %collective-permute-start.5 = (bf16[1,2,128,128]{3,2,1,0:T(8,128)(2,1)S(1)}, bf16[1,2,128,128]{3,2,1,0:T(8,128)(2,1)S(1)}, u32[]{:S(2)}, u32[]{:S(2)}) collective-permute-start(bf16[1,2,128,128]{3,2,1,0:T(8,128)(2,1)S(1)} %get-tuple-element.36), channel_id=1, source_target_pairs={{0,12},{1,13},{2,14},{3,15},{4,8},{5,9},{6,10},{7,11},{8,4},{9,5},... | collective-permute-start | bytes 196616 | tf_op jit(solution)/shard_map/ppermute | solution.py:111
  84.2 7.1 %collective-permute-start.12 = (f32[2,64,128]{2,1,0:T(8,128)S(1)}, f32[2,64,128]{2,1,0:T(8,128)S(1)}, u32[]{:S(2)}, u32[]{:S(2)}) collective-permute-start(f32[2,64,128]{2,1,0:T(8,128)S(1)} %add_select_fusion.3), channel_id=1, source_target_pairs={{0,32},{16,48},{32,0},{48,16},{64,96},{80,112},{96,64},{112,80},{1... | collective-permute-start | bytes 196616 | tf_op jit(solution)/shard_map/ppermute | solution.py:51
  91.3 11.0 %collective-permute-start.13 = (f32[2,64,128]{2,1,0:T(8,128)S(1)}, f32[2,64,128]{2,1,0:T(8,128)S(1)}, u32[]{:S(2)}, u32[]{:S(2)}) collective-permute-start(f32[2,64,128]{2,1,0:T(8,128)S(1)} %bitcast.361), channel_id=1, source_target_pairs={{0,64},{16,80},{32,96},{48,112},{64,0},{80,16},{96,32},{112,48},{1... | collective-permute-start | bytes 196616 | tf_op jit(solution)/shard_map/ppermute | solution.py:51
  102.4 6.6 %collective-permute-start.14 = (f32[2,64,128]{2,1,0:T(8,128)S(1)}, f32[2,64,128]{2,1,0:T(8,128)S(1)}, u32[]{:S(2)}, u32[]{:S(2)}) collective-permute-start(f32[2,64,128]{2,1,0:T(8,128)S(1)} %bitcast.360), channel_id=1, source_target_pairs={{0,128},{16,144},{32,160},{48,176},{64,192},{80,208},{96,224},{112... | collective-permute-start | bytes 196616 | tf_op jit(solution)/shard_map/ppermute | solution.py:51
  109.0 7.7 %collective-permute-start.15 = (f32[2,64,128]{2,1,0:T(8,128)S(1)}, f32[2,64,128]{2,1,0:T(8,128)S(1)}, u32[]{:S(2)}, u32[]{:S(2)}) collective-permute-start(f32[2,64,128]{2,1,0:T(8,128)S(1)} %bitcast.359), channel_id=1, source_target_pairs={{0,256},{16,272},{32,288},{48,304},{64,320},{80,336},{96,352},{112... | collective-permute-start | bytes 196616 | tf_op jit(solution)/shard_map/ppermute | solution.py:51
  126.9 8.5 %collective-permute-start.18 = (f32[2,128,128]{2,1,0:T(8,128)S(1)}, f32[2,128,128]{2,1,0:T(8,128)S(1)}, u32[]{:S(2)}, u32[]{:S(2)}) collective-permute-start(f32[2,128,128]{2,1,0:T(8,128)S(1)} %slice_select_fusion.2), channel_id=1, source_target_pairs={{0,2},{1,3},{2,0},{3,1},{4,6},{5,7},{6,4},{7,5},{8,10},{9,11},{10,... | collective-permute-start | bytes 393224 | tf_op jit(solution)/shard_map/ppermute | solution.py:51
  135.5 10.6 %collective-permute-start.19 = (f32[2,128,128]{2,1,0:T(8,128)S(1)}, f32[2,128,128]{2,1,0:T(8,128)S(1)}, u32[]{:S(2)}, u32[]{:S(2)}) collective-permute-start(f32[2,128,128]{2,1,0:T(8,128)S(1)} %bitcast.354), channel_id=1, source_target_pairs={{0,4},{1,5},{2,6},{3,7},{4,0},{5,1},{6,2},{7,3},{8,12},{9,13},{10,... | collective-permute-start | bytes 393224 | tf_op jit(solution)/shard_map/ppermute | solution.py:51
  146.1 12.9 %collective-permute-start.20 = (f32[2,128,128]{2,1,0:T(8,128)S(1)}, f32[2,128,128]{2,1,0:T(8,128)S(1)}, u32[]{:S(2)}, u32[]{:S(2)}) collective-permute-start(f32[2,128,128]{2,1,0:T(8,128)S(1)} %bitcast.355), channel_id=1, source_target_pairs={{0,8},{1,9},{2,10},{3,11},{4,12},{5,13},{6,14},{7,15},{8,0},{9,1},... | collective-permute-start | bytes 393224 | tf_op jit(solution)/shard_map/ppermute | solution.py:51
  169.0 7.8 %collective-permute-start.23 = (f32[2,64,128]{2,1,0:T(8,128)S(1)}, f32[2,64,128]{2,1,0:T(8,128)S(1)}, u32[]{:S(2)}, u32[]{:S(2)}) collective-permute-start(f32[2,64,128]{2,1,0:T(8,128)S(1)} %add_select_fusion.2), channel_id=1, source_target_pairs={{0,32},{16,48},{32,0},{48,16},{64,96},{80,112},{96,64},{112,80},{1... | collective-permute-start | bytes 196616 | tf_op jit(solution)/shard_map/ppermute | solution.py:51
  176.8 10.6 %collective-permute-start.24 = (f32[2,64,128]{2,1,0:T(8,128)S(1)}, f32[2,64,128]{2,1,0:T(8,128)S(1)}, u32[]{:S(2)}, u32[]{:S(2)}) collective-permute-start(f32[2,64,128]{2,1,0:T(8,128)S(1)} %bitcast.365), channel_id=1, source_target_pairs={{0,64},{16,80},{32,96},{48,112},{64,0},{80,16},{96,32},{112,48},{1... | collective-permute-start | bytes 196616 | tf_op jit(solution)/shard_map/ppermute | solution.py:51
  193.8 7.7 %collective-permute-start.26 = (f32[2,64,128]{2,1,0:T(8,128)S(1)}, f32[2,64,128]{2,1,0:T(8,128)S(1)}, u32[]{:S(2)}, u32[]{:S(2)}) collective-permute-start(f32[2,64,128]{2,1,0:T(8,128)S(1)} %bitcast.367), channel_id=1, source_target_pairs={{0,256},{16,272},{32,288},{48,304},{64,320},{80,336},{96,352},{112... | collective-permute-start | bytes 196616 | tf_op jit(solution)/shard_map/ppermute | solution.py:51
  211.8 7.4 %collective-permute-start.29 = (f32[2,128,128]{2,1,0:T(8,128)S(1)}, f32[2,128,128]{2,1,0:T(8,128)S(1)}, u32[]{:S(2)}, u32[]{:S(2)}) collective-permute-start(f32[2,128,128]{2,1,0:T(8,128)S(1)} %slice_select_fusion.1), channel_id=1, source_target_pairs={{0,2},{1,3},{2,0},{3,1},{4,6},{5,7},{6,4},{7,5},{8,10},{9,11},{10,... | collective-permute-start | bytes 393224 | tf_op jit(solution)/shard_map/ppermute | solution.py:51
  219.3 10.3 %collective-permute-start.30 = (f32[2,128,128]{2,1,0:T(8,128)S(1)}, f32[2,128,128]{2,1,0:T(8,128)S(1)}, u32[]{:S(2)}, u32[]{:S(2)}) collective-permute-start(f32[2,128,128]{2,1,0:T(8,128)S(1)} %bitcast.356), channel_id=1, source_target_pairs={{0,4},{1,5},{2,6},{3,7},{4,0},{5,1},{6,2},{7,3},{8,12},{9,13},{10,... | collective-permute-start | bytes 393224 | tf_op jit(solution)/shard_map/ppermute | solution.py:51
  229.6 13.3 %collective-permute-start.31 = (f32[2,128,128]{2,1,0:T(8,128)S(1)}, f32[2,128,128]{2,1,0:T(8,128)S(1)}, u32[]{:S(2)}, u32[]{:S(2)}) collective-permute-start(f32[2,128,128]{2,1,0:T(8,128)S(1)} %bitcast.357), channel_id=1, source_target_pairs={{0,8},{1,9},{2,10},{3,11},{4,12},{5,13},{6,14},{7,15},{8,0},{9,1},... | collective-permute-start | bytes 393224 | tf_op jit(solution)/shard_map/ppermute | solution.py:51
  252.7 7.8 %collective-permute-start.34 = (f32[2,64,128]{2,1,0:T(8,128)S(1)}, f32[2,64,128]{2,1,0:T(8,128)S(1)}, u32[]{:S(2)}, u32[]{:S(2)}) collective-permute-start(f32[2,64,128]{2,1,0:T(8,128)S(1)} %add_select_fusion.1), channel_id=1, source_target_pairs={{0,32},{16,48},{32,0},{48,16},{64,96},{80,112},{96,64},{112,80},{1... | collective-permute-start | bytes 196616 | tf_op jit(solution)/shard_map/ppermute | solution.py:51
  260.5 10.2 %collective-permute-start.35 = (f32[2,64,128]{2,1,0:T(8,128)S(1)}, f32[2,64,128]{2,1,0:T(8,128)S(1)}, u32[]{:S(2)}, u32[]{:S(2)}) collective-permute-start(f32[2,64,128]{2,1,0:T(8,128)S(1)} %bitcast.368), channel_id=1, source_target_pairs={{0,64},{16,80},{32,96},{48,112},{64,0},{80,16},{96,32},{112,48},{1... | collective-permute-start | bytes 196616 | tf_op jit(solution)/shard_map/ppermute | solution.py:51
  277.0 7.7 %collective-permute-start.37 = (f32[2,64,128]{2,1,0:T(8,128)S(1)}, f32[2,64,128]{2,1,0:T(8,128)S(1)}, u32[]{:S(2)}, u32[]{:S(2)}) collective-permute-start(f32[2,64,128]{2,1,0:T(8,128)S(1)} %bitcast.370), channel_id=1, source_target_pairs={{0,256},{16,272},{32,288},{48,304},{64,320},{80,336},{96,352},{112... | collective-permute-start | bytes 196616 | tf_op jit(solution)/shard_map/ppermute | solution.py:51
  295.6 7.4 %collective-permute-start.40 = (f32[2,128,128]{2,1,0:T(8,128)S(1)}, f32[2,128,128]{2,1,0:T(8,128)S(1)}, u32[]{:S(2)}, u32[]{:S(2)}) collective-permute-start(f32[2,128,128]{2,1,0:T(8,128)S(1)} %slice_select_fusion), channel_id=1, source_target_pairs={{0,2},{1,3},{2,0},{3,1},{4,6},{5,7},{6,4},{7,5},{8,10},{9,11},{10,... | collective-permute-start | bytes 393224 | tf_op jit(solution)/shard_map/ppermute | solution.py:51
  303.1 10.3 %collective-permute-start.41 = (f32[2,128,128]{2,1,0:T(8,128)S(1)}, f32[2,128,128]{2,1,0:T(8,128)S(1)}, u32[]{:S(2)}, u32[]{:S(2)}) collective-permute-start(f32[2,128,128]{2,1,0:T(8,128)S(1)} %bitcast.352), channel_id=1, source_target_pairs={{0,4},{1,5},{2,6},{3,7},{4,0},{5,1},{6,2},{7,3},{8,12},{9,13},{10,... | collective-permute-start | bytes 393224 | tf_op jit(solution)/shard_map/ppermute | solution.py:51
  313.4 13.8 %collective-permute-start.42 = (f32[2,128,128]{2,1,0:T(8,128)S(1)}, f32[2,128,128]{2,1,0:T(8,128)S(1)}, u32[]{:S(2)}, u32[]{:S(2)}) collective-permute-start(f32[2,128,128]{2,1,0:T(8,128)S(1)} %bitcast.353), channel_id=1, source_target_pairs={{0,8},{1,9},{2,10},{3,11},{4,12},{5,13},{6,14},{7,15},{8,0},{9,1},... | collective-permute-start | bytes 393224 | tf_op jit(solution)/shard_map/ppermute | solution.py:51
  337.1 7.8 %collective-permute-start.45 = (f32[2,64,128]{2,1,0:T(8,128)S(1)}, f32[2,64,128]{2,1,0:T(8,128)S(1)}, u32[]{:S(2)}, u32[]{:S(2)}) collective-permute-start(f32[2,64,128]{2,1,0:T(8,128)S(1)} %add_select_fusion), channel_id=1, source_target_pairs={{0,32},{16,48},{32,0},{48,16},{64,96},{80,112},{96,64},{112,80},{1... | collective-permute-start | bytes 196616 | tf_op jit(solution)/shard_map/ppermute | solution.py:51
  344.9 10.1 %collective-permute-start.46 = (f32[2,64,128]{2,1,0:T(8,128)S(1)}, f32[2,64,128]{2,1,0:T(8,128)S(1)}, u32[]{:S(2)}, u32[]{:S(2)}) collective-permute-start(f32[2,64,128]{2,1,0:T(8,128)S(1)} %bitcast.362), channel_id=1, source_target_pairs={{0,64},{16,80},{32,96},{48,112},{64,0},{80,16},{96,32},{112,48},{1... | collective-permute-start | bytes 196616 | tf_op jit(solution)/shard_map/ppermute | solution.py:51
  361.2 7.7 %collective-permute-start.48 = (f32[2,64,128]{2,1,0:T(8,128)S(1)}, f32[2,64,128]{2,1,0:T(8,128)S(1)}, u32[]{:S(2)}, u32[]{:S(2)}) collective-permute-start(f32[2,64,128]{2,1,0:T(8,128)S(1)} %bitcast.364), channel_id=1, source_target_pairs={{0,256},{16,272},{32,288},{48,304},{64,320},{80,336},{96,352},{112... | collective-permute-start | bytes 196616 | tf_op jit(solution)/shard_map/ppermute | solution.py:51
  (22 other events, 137.1 us)

commit v8 on v7

--- a/solution.py
+++ b/solution.py
@@ -186,16 +186,19 @@
     cdenom = jnp.sum(cweights, axis=-1)
 
     stat_bits = (col_devices.bit_length() - 1) if isinstance(col_devices, int) else 4
-    packed = pack(numer, peak, denom, cpeak, cdenom)
-    members = gather_bits(packed, "kv", [0])
-    numer, peak, denom, cpeak, cdenom = combine_members(members, query_rows)
     half = query_rows // 2
     low = (me_kv & 1) == 0
     halves = [
         pack(*(a[:, :half] for a in (numer, peak, denom, cpeak, cdenom))),
         pack(*(a[:, half:] for a in (numer, peak, denom, cpeak, cdenom))),
     ]
-    packed = jnp.where(low, halves[0], halves[1])
+    keep = jnp.where(low, halves[0], halves[1])
+    arrived = lax.ppermute(
+        jnp.where(low, halves[1], halves[0]), "kv", [(s, s ^ 1) for s in range(col_devices)]
+    )
+    packed = pack(
+        *combine_members([jnp.where(low, keep, arrived), jnp.where(low, arrived, keep)], half)
+    )
     for bits in bit_stages(list(range(1, stat_bits))):
         members = gather_bits(packed, "kv", bits)
         packed = pack(*combine_members(members, half))
@@ -218,7 +221,7 @@
     rhs = group_sum(rhs_part, "pb") * weighting
 
     def gram_times(vec):
-        across = pair_split_sum(split_dot("hqa,had->hqd", probs, vec), "kv", 1)
+        across = group_sum(split_dot("hqa,had->hqd", probs, vec), "kv")
         back = group_sum(split_dot("hqa,hqd->had", probs, across), "pb")
         return back * weighting + ridge_weight * vec
 

time: 377 us -> 376 us (level)
    ppermute x32 -> x28, starting transfers between devices: 126 us -> 118 us  [gather_bits(): got.append(lax.ppermute(value, axis, pairs))]
    ppermute x4 -> x7, starting transfers between devices: 11.3 us -> 16.9 us  [group_sum(): arrived = lax.ppermute(jnp.where(low, second, first), axis, pairs)]
    ppermute x4 -> x7, starting transfers between devices: 9.89 us -> 15.5 us  [group_sum(): other = lax.ppermute(mine, axis, pairs)]
    ppermute x32 -> x28, waiting for transfers between devices: 136 us -> 130 us  [gather_bits(): got.append(lax.ppermute(value, axis, pairs))]
    ppermute x4 -> x7, waiting for transfers between devices: 14.7 us -> 18.8 us  [group_sum(): other = lax.ppermute(mine, axis, pairs)]
    ppermute x4 -> x7, waiting for transfers between devices: 13.3 us -> 17.4 us  [group_sum(): arrived = lax.ppermute(jnp.where(low, second, first), axis, pairs)]
    ppermute x3 -> x1, starting transfers between devices: 5.78 us -> 1.92 us  [per_device(): lax.ppermute(jnp.where(low, halves[1], halves[0]), 'kv', [(s, s ^ 1) for...]
where the time goes in v8:
time: 376 us; the launch traced here: 374 us
  waiting for transfers between devices  177 us (47%)
  starting transfers between devices  174 us (46%)
  other arithmetic  10.5 us (3%)
  matrix products  8.74 us (2%)
    ppermute x28, waiting for transfers between devices, gather_bits(): got.append(lax.ppermute(value, axis, pairs))  130 us
    ppermute x28, starting transfers between devices, gather_bits(): got.append(lax.ppermute(value, axis, pairs))  118 us
    ppermute x6, starting transfers between devices, scatter_groups(): total = total + lax.ppermute(give, axis, pairs)  19.8 us
    ppermute x7, waiting for transfers between devices, group_sum(): other = lax.ppermute(mine, axis, pairs)  18.8 us
    ppermute x7, waiting for transfers between devices, group_sum(): arrived = lax.ppermute(jnp.where(low, second, first), axis, pairs)  17.4 us
    ppermute x7, starting transfers between devices, group_sum(): arrived = lax.ppermute(jnp.where(low, second, first), axis, pairs)  16.9 us
    ppermute x7, starting transfers between devices, group_sum(): other = lax.ppermute(mine, axis, pairs)  15.5 us
    ppermute x6, waiting for transfers between devices, scatter_groups(): total = total + lax.ppermute(give, axis, pairs)  9.09 us
  transfers between devices with their start and end apart: 50, of which 46 were waited for; matrix products, arithmetic and copies ran while one was open for 1% of the time, Pallas kernels for 0%

profile of v8, /device:TPU:6, one launch (start us, length us, event | category | flops | bytes accessed | tf_op | source)
XLA Modules:
  0.0 373.9 jit_solution(13333759151080123323)
XLA Ops:
  12.4 4.3 %collective-permute-start.7 = (f32[2,132,128]{2,0,1:T(2,128)S(1)}, f32[2,132,128]{2,0,1:T(2,128)S(1)}, u32[]{:S(2)}, u32[]{:S(2)}) collective-permute-start(f32[2,132,128]{2,0,1:T(2,128)S(1)} %constant_dynamic-update-slice_fusion.8), channel_id=1, source_target_pairs={{0,2},{1,3},{2,0},{3,1},{4,6},{5,7},{6,4},{7,5},{8,10},{9,11},{10,... | collective-permute-start | bytes 405512 | tf_op jit(solution)/shard_map/ppermute | solution.py:51
  21.5 6.1 %collective-permute-start.8 = (f32[2,132,128]{2,0,1:T(2,128)S(1)}, f32[2,132,128]{2,0,1:T(2,128)S(1)}, u32[]{:S(2)}, u32[]{:S(2)}) collective-permute-start(f32[2,132,128]{2,0,1:T(2,128)S(1)} %constant_dynamic-update-slice_fusion.12), channel_id=1, source_target_pairs={{0,4},{1,5},{2,6},{3,7},{4,0},{5,1},{6,2},{7,3},{8,12},{9,13},{10,... | collective-permute-start | bytes 405512 | tf_op jit(solution)/shard_map/ppermute | solution.py:51
  34.3 8.4 %collective-permute-start.9 = (f32[2,132,128]{2,1,0:T(8,128)S(1)}, f32[2,132,128]{2,1,0:T(8,128)S(1)}, u32[]{:S(2)}, u32[]{:S(2)}) collective-permute-start(f32[2,132,128]{2,1,0:T(8,128)S(1)} %concatenate.55), channel_id=1, source_target_pairs={{0,8},{1,9},{2,10},{3,11},{4,12},{5,13},{6,14},{7,15},{8,0},{9,1},... | collective-permute-start | bytes 405512 | tf_op jit(solution)/shard_map/ppermute | solution.py:51
  55.9 4.7 %collective-permute-done.2 = bf16[4,2,128,128]{3,2,1,0:T(8,128)(2,1)S(1)} collective-permute-done((bf16[4,2,128,128]{3,2,1,0:T(8,128)(2,1)S(1)}, bf16[4,2,128,128]{3,2,1,0:T(8,128)(2,1)S(1)}, u32[]{:S(2)}, u32[]{:S(2)}) %collective-permute-start.2) | collective-permute-done | bytes 262176 | tf_op jit(solution)/shard_map/ppermute | solution.py:111
  60.7 4.3 %collective-permute-start.3 = (bf16[1,2,128,128]{3,2,1,0:T(8,128)(2,1)S(1)}, bf16[1,2,128,128]{3,2,1,0:T(8,128)(2,1)S(1)}, u32[]{:S(2)}, u32[]{:S(2)}) collective-permute-start(bf16[1,2,128,128]{3,2,1,0:T(8,128)(2,1)S(1)} %get-tuple-element.36), channel_id=1, source_target_pairs={{0,4},{1,5},{2,6},{3,7},{4,0},{5,1},{6,2},{7,3},{8,12},{9,13},{10,... | collective-permute-start | bytes 196616 | tf_op jit(solution)/shard_map/ppermute | solution.py:111
  67.8 5.1 %collective-permute-start.5 = (bf16[1,2,128,128]{3,2,1,0:T(8,128)(2,1)S(1)}, bf16[1,2,128,128]{3,2,1,0:T(8,128)(2,1)S(1)}, u32[]{:S(2)}, u32[]{:S(2)}) collective-permute-start(bf16[1,2,128,128]{3,2,1,0:T(8,128)(2,1)S(1)} %get-tuple-element.37), channel_id=1, source_target_pairs={{0,12},{1,13},{2,14},{3,15},{4,8},{5,9},{6,10},{7,11},{8,4},{9,5},... | collective-permute-start | bytes 196616 | tf_op jit(solution)/shard_map/ppermute | solution.py:111
  83.0 4.5 %collective-permute-start.12 = (f32[2,64,128]{2,1,0:T(8,128)S(1)}, f32[2,64,128]{2,1,0:T(8,128)S(1)}, u32[]{:S(2)}, u32[]{:S(2)}) collective-permute-start(f32[2,64,128]{2,1,0:T(8,128)S(1)} %add_select_fusion.6), channel_id=1, source_target_pairs={{0,32},{16,48},{32,0},{48,16},{64,96},{80,112},{96,64},{112,80},{1... | collective-permute-start | bytes 196616 | tf_op jit(solution)/shard_map/ppermute | solution.py:51
  90.1 8.4 %collective-permute-start.13 = (f32[2,64,128]{2,1,0:T(8,128)S(1)}, f32[2,64,128]{2,1,0:T(8,128)S(1)}, u32[]{:S(2)}, u32[]{:S(2)}) collective-permute-start(f32[2,64,128]{2,1,0:T(8,128)S(1)} %bitcast.288), channel_id=1, source_target_pairs={{0,64},{16,80},{32,96},{48,112},{64,0},{80,16},{96,32},{112,48},{1... | collective-permute-start | bytes 196616 | tf_op jit(solution)/shard_map/ppermute | solution.py:51
  110.7 4.7 %collective-permute-done.15 = f32[2,64,128]{2,1,0:T(8,128)S(1)} collective-permute-done((f32[2,64,128]{2,1,0:T(8,128)S(1)}, f32[2,64,128]{2,1,0:T(8,128)S(1)}, u32[]{:S(2)}, u32[]{:S(2)}) %collective-permute-start.15) | collective-permute-done | bytes 65568 | tf_op jit(solution)/shard_map/ppermute | solution.py:51
  125.4 4.7 %collective-permute-start.18 = (f32[2,128,128]{2,1,0:T(8,128)S(1)}, f32[2,128,128]{2,1,0:T(8,128)S(1)}, u32[]{:S(2)}, u32[]{:S(2)}) collective-permute-start(f32[2,128,128]{2,1,0:T(8,128)S(1)} %add_select_fusion.2), channel_id=1, source_target_pairs={{0,2},{1,3},{2,0},{3,1},{4,6},{5,7},{6,4},{7,5},{8,10},{9,11},{10,... | collective-permute-start | bytes 393224 | tf_op jit(solution)/shard_map/ppermute | solution.py:51
  134.0 4.9 %collective-permute-start.19 = (f32[2,128,128]{2,1,0:T(8,128)S(1)}, f32[2,128,128]{2,1,0:T(8,128)S(1)}, u32[]{:S(2)}, u32[]{:S(2)}) collective-permute-start(f32[2,128,128]{2,1,0:T(8,128)S(1)} %bitcast.281), channel_id=1, source_target_pairs={{0,4},{1,5},{2,6},{3,7},{4,0},{5,1},{6,2},{7,3},{8,12},{9,13},{10,... | collective-permute-start | bytes 393224 | tf_op jit(solution)/shard_map/ppermute | solution.py:51
  138.9 5.7 %collective-permute-done.19 = f32[2,128,128]{2,1,0:T(8,128)S(1)} collective-permute-done((f32[2,128,128]{2,1,0:T(8,128)S(1)}, f32[2,128,128]{2,1,0:T(8,128)S(1)}, u32[]{:S(2)}, u32[]{:S(2)}) %collective-permute-start.19) | collective-permute-done | bytes 131104 | tf_op jit(solution)/shard_map/ppermute | solution.py:51
  144.7 5.2 %collective-permute-start.20 = (f32[2,128,128]{2,1,0:T(8,128)S(1)}, f32[2,128,128]{2,1,0:T(8,128)S(1)}, u32[]{:S(2)}, u32[]{:S(2)}) collective-permute-start(f32[2,128,128]{2,1,0:T(8,128)S(1)} %bitcast.282), channel_id=1, source_target_pairs={{0,8},{1,9},{2,10},{3,11},{4,12},{5,13},{6,14},{7,15},{8,0},{9,1},... | collective-permute-start | bytes 393224 | tf_op jit(solution)/shard_map/ppermute | solution.py:51
  149.9 7.7 %collective-permute-done.20 = f32[2,128,128]{2,1,0:T(8,128)S(1)} collective-permute-done((f32[2,128,128]{2,1,0:T(8,128)S(1)}, f32[2,128,128]{2,1,0:T(8,128)S(1)}, u32[]{:S(2)}, u32[]{:S(2)}) %collective-permute-start.20) | collective-permute-done | bytes 131104 | tf_op jit(solution)/shard_map/ppermute | solution.py:51
  175.3 7.6 %collective-permute-start.24 = (f32[2,64,128]{2,1,0:T(8,128)S(1)}, f32[2,64,128]{2,1,0:T(8,128)S(1)}, u32[]{:S(2)}, u32[]{:S(2)}) collective-permute-start(f32[2,64,128]{2,1,0:T(8,128)S(1)} %bitcast.292), channel_id=1, source_target_pairs={{0,64},{16,80},{32,96},{48,112},{64,0},{80,16},{96,32},{112,48},{1... | collective-permute-start | bytes 196616 | tf_op jit(solution)/shard_map/ppermute | solution.py:51
  188.2 4.2 %collective-permute-done.25 = f32[2,64,128]{2,1,0:T(8,128)S(1)} collective-permute-done((f32[2,64,128]{2,1,0:T(8,128)S(1)}, f32[2,64,128]{2,1,0:T(8,128)S(1)}, u32[]{:S(2)}, u32[]{:S(2)}) %collective-permute-start.25) | collective-permute-done | bytes 65568 | tf_op jit(solution)/shard_map/ppermute | solution.py:51
  194.9 5.1 %collective-permute-done.26 = f32[2,64,128]{2,1,0:T(8,128)S(1)} collective-permute-done((f32[2,64,128]{2,1,0:T(8,128)S(1)}, f32[2,64,128]{2,1,0:T(8,128)S(1)}, u32[]{:S(2)}, u32[]{:S(2)}) %collective-permute-start.26) | collective-permute-done | bytes 65568 | tf_op jit(solution)/shard_map/ppermute | solution.py:51
  212.2 5.3 %collective-permute-done.29 = f32[2,128,128]{2,1,0:T(8,128)S(1)} collective-permute-done((f32[2,128,128]{2,1,0:T(8,128)S(1)}, f32[2,128,128]{2,1,0:T(8,128)S(1)}, u32[]{:S(2)}, u32[]{:S(2)}) %collective-permute-start.29) | collective-permute-done | bytes 131104 | tf_op jit(solution)/shard_map/ppermute | solution.py:51
  220.5 7.4 %collective-permute-done.30 = f32[2,128,128]{2,1,0:T(8,128)S(1)} collective-permute-done((f32[2,128,128]{2,1,0:T(8,128)S(1)}, f32[2,128,128]{2,1,0:T(8,128)S(1)}, u32[]{:S(2)}, u32[]{:S(2)}) %collective-permute-start.30) | collective-permute-done | bytes 131104 | tf_op jit(solution)/shard_map/ppermute | solution.py:51
  227.9 4.5 %collective-permute-start.31 = (f32[2,128,128]{2,1,0:T(8,128)S(1)}, f32[2,128,128]{2,1,0:T(8,128)S(1)}, u32[]{:S(2)}, u32[]{:S(2)}) collective-permute-start(f32[2,128,128]{2,1,0:T(8,128)S(1)} %bitcast.285), channel_id=1, source_target_pairs={{0,8},{1,9},{2,10},{3,11},{4,12},{5,13},{6,14},{7,15},{8,0},{9,1},... | collective-permute-start | bytes 393224 | tf_op jit(solution)/shard_map/ppermute | solution.py:51
  232.5 8.7 %collective-permute-done.31 = f32[2,128,128]{2,1,0:T(8,128)S(1)} collective-permute-done((f32[2,128,128]{2,1,0:T(8,128)S(1)}, f32[2,128,128]{2,1,0:T(8,128)S(1)}, u32[]{:S(2)}, u32[]{:S(2)}) %collective-permute-start.31) | collective-permute-done | bytes 131104 | tf_op jit(solution)/shard_map/ppermute | solution.py:51
  254.7 4.1 %collective-permute-done.34 = f32[2,64,128]{2,1,0:T(8,128)S(1)} collective-permute-done((f32[2,64,128]{2,1,0:T(8,128)S(1)}, f32[2,64,128]{2,1,0:T(8,128)S(1)}, u32[]{:S(2)}, u32[]{:S(2)}) %collective-permute-start.34) | collective-permute-done | bytes 65568 | tf_op jit(solution)/shard_map/ppermute | solution.py:51
  258.9 7.1 %collective-permute-start.35 = (f32[2,64,128]{2,1,0:T(8,128)S(1)}, f32[2,64,128]{2,1,0:T(8,128)S(1)}, u32[]{:S(2)}, u32[]{:S(2)}) collective-permute-start(f32[2,64,128]{2,1,0:T(8,128)S(1)} %bitcast.295), channel_id=1, source_target_pairs={{0,64},{16,80},{32,96},{48,112},{64,0},{80,16},{96,32},{112,48},{1... | collective-permute-start | bytes 196616 | tf_op jit(solution)/shard_map/ppermute | solution.py:51
  277.8 5.2 %collective-permute-done.37 = f32[2,64,128]{2,1,0:T(8,128)S(1)} collective-permute-done((f32[2,64,128]{2,1,0:T(8,128)S(1)}, f32[2,64,128]{2,1,0:T(8,128)S(1)}, u32[]{:S(2)}, u32[]{:S(2)}) %collective-permute-start.37) | collective-permute-done | bytes 65568 | tf_op jit(solution)/shard_map/ppermute | solution.py:51
  295.6 5.5 %collective-permute-done.40 = f32[2,128,128]{2,1,0:T(8,128)S(1)} collective-permute-done((f32[2,128,128]{2,1,0:T(8,128)S(1)}, f32[2,128,128]{2,1,0:T(8,128)S(1)}, u32[]{:S(2)}, u32[]{:S(2)}) %collective-permute-start.40) | collective-permute-done | bytes 131104 | tf_op jit(solution)/shard_map/ppermute | solution.py:51
  304.0 7.4 %collective-permute-done.41 = f32[2,128,128]{2,1,0:T(8,128)S(1)} collective-permute-done((f32[2,128,128]{2,1,0:T(8,128)S(1)}, f32[2,128,128]{2,1,0:T(8,128)S(1)}, u32[]{:S(2)}, u32[]{:S(2)}) %collective-permute-start.41) | collective-permute-done | bytes 131104 | tf_op jit(solution)/shard_map/ppermute | solution.py:51
  311.5 5.1 %collective-permute-start.42 = (f32[2,128,128]{2,1,0:T(8,128)S(1)}, f32[2,128,128]{2,1,0:T(8,128)S(1)}, u32[]{:S(2)}, u32[]{:S(2)}) collective-permute-start(f32[2,128,128]{2,1,0:T(8,128)S(1)} %bitcast.278), channel_id=1, source_target_pairs={{0,8},{1,9},{2,10},{3,11},{4,12},{5,13},{6,14},{7,15},{8,0},{9,1},... | collective-permute-start | bytes 393224 | tf_op jit(solution)/shard_map/ppermute | solution.py:51
  316.6 8.7 %collective-permute-done.42 = f32[2,128,128]{2,1,0:T(8,128)S(1)} collective-permute-done((f32[2,128,128]{2,1,0:T(8,128)S(1)}, f32[2,128,128]{2,1,0:T(8,128)S(1)}, u32[]{:S(2)}, u32[]{:S(2)}) %collective-permute-start.42) | collective-permute-done | bytes 131104 | tf_op jit(solution)/shard_map/ppermute | solution.py:51
  338.8 4.2 %collective-permute-done.45 = f32[2,64,128]{2,1,0:T(8,128)S(1)} collective-permute-done((f32[2,64,128]{2,1,0:T(8,128)S(1)}, f32[2,64,128]{2,1,0:T(8,128)S(1)}, u32[]{:S(2)}, u32[]{:S(2)}) %collective-permute-start.45) | collective-permute-done | bytes 65568 | tf_op jit(solution)/shard_map/ppermute | solution.py:51
  343.0 7.0 %collective-permute-start.46 = (f32[2,64,128]{2,1,0:T(8,128)S(1)}, f32[2,64,128]{2,1,0:T(8,128)S(1)}, u32[]{:S(2)}, u32[]{:S(2)}) collective-permute-start(f32[2,64,128]{2,1,0:T(8,128)S(1)} %bitcast.289), channel_id=1, source_target_pairs={{0,64},{16,80},{32,96},{48,112},{64,0},{80,16},{96,32},{112,48},{1... | collective-permute-start | bytes 196616 | tf_op jit(solution)/shard_map/ppermute | solution.py:51
  355.0 4.3 %collective-permute-done.47 = f32[2,64,128]{2,1,0:T(8,128)S(1)} collective-permute-done((f32[2,64,128]{2,1,0:T(8,128)S(1)}, f32[2,64,128]{2,1,0:T(8,128)S(1)}, u32[]{:S(2)}, u32[]{:S(2)}) %collective-permute-start.47) | collective-permute-done | bytes 65568 | tf_op jit(solution)/shard_map/ppermute | solution.py:51
  361.6 5.4 %collective-permute-done.48 = f32[2,64,128]{2,1,0:T(8,128)S(1)} collective-permute-done((f32[2,64,128]{2,1,0:T(8,128)S(1)}, f32[2,64,128]{2,1,0:T(8,128)S(1)}, u32[]{:S(2)}, u32[]{:S(2)}) %collective-permute-start.48) | collective-permute-done | bytes 65568 | tf_op jit(solution)/shard_map/ppermute | solution.py:51
  (212 shorter events, 186.2 us)
Async XLA Ops:
  12.4 8.2 %collective-permute-start.7 = (f32[2,132,128]{2,0,1:T(2,128)S(1)}, f32[2,132,128]{2,0,1:T(2,128)S(1)}, u32[]{:S(2)}, u32[]{:S(2)}) collective-permute-start(f32[2,132,128]{2,0,1:T(2,128)S(1)} %constant_dynamic-update-slice_fusion.8), channel_id=1, source_target_pairs={{0,2},{1,3},{2,0},{3,1},{4,6},{5,7},{6,4},{7,5},{8,10},{9,11},{10,... | collective-permute-start | bytes 405512 | tf_op jit(solution)/shard_map/ppermute | solution.py:51
  21.5 12.3 %collective-permute-start.8 = (f32[2,132,128]{2,0,1:T(2,128)S(1)}, f32[2,132,128]{2,0,1:T(2,128)S(1)}, u32[]{:S(2)}, u32[]{:S(2)}) collective-permute-start(f32[2,132,128]{2,0,1:T(2,128)S(1)} %constant_dynamic-update-slice_fusion.12), channel_id=1, source_target_pairs={{0,4},{1,5},{2,6},{3,7},{4,0},{5,1},{6,2},{7,3},{8,12},{9,13},{10,... | collective-permute-start | bytes 405512 | tf_op jit(solution)/shard_map/ppermute | solution.py:51
  34.3 16.3 %collective-permute-start.9 = (f32[2,132,128]{2,1,0:T(8,128)S(1)}, f32[2,132,128]{2,1,0:T(8,128)S(1)}, u32[]{:S(2)}, u32[]{:S(2)}) collective-permute-start(f32[2,132,128]{2,1,0:T(8,128)S(1)} %concatenate.55), channel_id=1, source_target_pairs={{0,8},{1,9},{2,10},{3,11},{4,12},{5,13},{6,14},{7,15},{8,0},{9,1},... | collective-permute-start | bytes 405512 | tf_op jit(solution)/shard_map/ppermute | solution.py:51
  42.9 10.8 %collective-permute-start = (bf16[4,2,128,128]{3,2,1,0:T(8,128)(2,1)S(1)}, bf16[4,2,128,128]{3,2,1,0:T(8,128)(2,1)S(1)}, u32[]{:S(2)}, u32[]{:S(2)}) collective-permute-start(bf16[4,2,128,128]{3,2,1,0:T(8,128)(2,1)S(1)} %bitcast.298), channel_id=1, source_target_pairs={{0,1},{1,0},{2,3},{3,2},{4,5},{5,4},{6,7},{7,6},{8,9},{9,8},{10,11... | collective-permute-start | bytes 786440 | tf_op jit(solution)/shard_map/ppermute | solution.py:111
  44.8 11.1 %collective-permute-start.1 = (bf16[4,2,128,128]{3,2,1,0:T(8,128)(2,1)S(1)}, bf16[4,2,128,128]{3,2,1,0:T(8,128)(2,1)S(1)}, u32[]{:S(2)}, u32[]{:S(2)}) collective-permute-start(bf16[4,2,128,128]{3,2,1,0:T(8,128)(2,1)S(1)} %bitcast.299), channel_id=1, source_target_pairs={{0,2},{1,3},{2,0},{3,1},{4,6},{5,7},{6,4},{7,5},{8,10},{9,11},{10,... | collective-permute-start | bytes 786440 | tf_op jit(solution)/shard_map/ppermute | solution.py:111
  47.2 13.3 %collective-permute-start.2 = (bf16[4,2,128,128]{3,2,1,0:T(8,128)(2,1)S(1)}, bf16[4,2,128,128]{3,2,1,0:T(8,128)(2,1)S(1)}, u32[]{:S(2)}, u32[]{:S(2)}) collective-permute-start(bf16[4,2,128,128]{3,2,1,0:T(8,128)(2,1)S(1)} %bitcast.300), channel_id=1, source_target_pairs={{0,3},{1,2},{2,1},{3,0},{4,7},{5,6},{6,5},{7,4},{8,11},{9,10},{10,... | collective-permute-start | bytes 786440 | tf_op jit(solution)/shard_map/ppermute | solution.py:111
  51.5 21.4 %collective-permute-start.10 = (f32[2,132,128]{2,0,1:T(2,128)S(1)}, f32[2,132,128]{2,0,1:T(2,128)S(1)}, u32[]{:S(2)}, u32[]{:S(2)}) collective-permute-start(f32[2,132,128]{2,0,1:T(2,128)S(1)} %constant_dynamic-update-slice_fusion.16), channel_id=1, source_target_pairs={{0,1},{1,0},{2,3},{3,2},{4,5},{5,4},{6,7},{7,6},{8,9},{9,8},{10,11... | collective-permute-start | bytes 405512 | tf_op jit(solution)/shard_map/ppermute | solution.py:205
  60.7 13.5 %collective-permute-start.3 = (bf16[1,2,128,128]{3,2,1,0:T(8,128)(2,1)S(1)}, bf16[1,2,128,128]{3,2,1,0:T(8,128)(2,1)S(1)}, u32[]{:S(2)}, u32[]{:S(2)}) collective-permute-start(bf16[1,2,128,128]{3,2,1,0:T(8,128)(2,1)S(1)} %get-tuple-element.36), channel_id=1, source_target_pairs={{0,4},{1,5},{2,6},{3,7},{4,0},{5,1},{6,2},{7,3},{8,12},{9,13},{10,... | collective-permute-start | bytes 196616 | tf_op jit(solution)/shard_map/ppermute | solution.py:111
  65.0 10.2 %collective-permute-start.4 = (bf16[1,2,128,128]{3,2,1,0:T(8,128)(2,1)S(1)}, bf16[1,2,128,128]{3,2,1,0:T(8,128)(2,1)S(1)}, u32[]{:S(2)}, u32[]{:S(2)}) collective-permute-start(bf16[1,2,128,128]{3,2,1,0:T(8,128)(2,1)S(1)} %get-tuple-element.38), channel_id=1, source_target_pairs={{0,8},{1,9},{2,10},{3,11},{4,12},{5,13},{6,14},{7,15},{8,0},{9,1},... | collective-permute-start | bytes 196616 | tf_op jit(solution)/shard_map/ppermute | solution.py:111
  67.8 8.6 %collective-permute-start.5 = (bf16[1,2,128,128]{3,2,1,0:T(8,128)(2,1)S(1)}, bf16[1,2,128,128]{3,2,1,0:T(8,128)(2,1)S(1)}, u32[]{:S(2)}, u32[]{:S(2)}) collective-permute-start(bf16[1,2,128,128]{3,2,1,0:T(8,128)(2,1)S(1)} %get-tuple-element.37), channel_id=1, source_target_pairs={{0,12},{1,13},{2,14},{3,15},{4,8},{5,9},{6,10},{7,11},{8,4},{9,5},... | collective-permute-start | bytes 196616 | tf_op jit(solution)/shard_map/ppermute | solution.py:111
  83.0 7.1 %collective-permute-start.12 = (f32[2,64,128]{2,1,0:T(8,128)S(1)}, f32[2,64,128]{2,1,0:T(8,128)S(1)}, u32[]{:S(2)}, u32[]{:S(2)}) collective-permute-start(f32[2,64,128]{2,1,0:T(8,128)S(1)} %add_select_fusion.6), channel_id=1, source_target_pairs={{0,32},{16,48},{32,0},{48,16},{64,96},{80,112},{96,64},{112,80},{1... | collective-permute-start | bytes 196616 | tf_op jit(solution)/shard_map/ppermute | solution.py:51
  90.1 11.0 %collective-permute-start.13 = (f32[2,64,128]{2,1,0:T(8,128)S(1)}, f32[2,64,128]{2,1,0:T(8,128)S(1)}, u32[]{:S(2)}, u32[]{:S(2)}) collective-permute-start(f32[2,64,128]{2,1,0:T(8,128)S(1)} %bitcast.288), channel_id=1, source_target_pairs={{0,64},{16,80},{32,96},{48,112},{64,0},{80,16},{96,32},{112,48},{1... | collective-permute-start | bytes 196616 | tf_op jit(solution)/shard_map/ppermute | solution.py:51
  101.2 6.6 %collective-permute-start.14 = (f32[2,64,128]{2,1,0:T(8,128)S(1)}, f32[2,64,128]{2,1,0:T(8,128)S(1)}, u32[]{:S(2)}, u32[]{:S(2)}) collective-permute-start(f32[2,64,128]{2,1,0:T(8,128)S(1)} %bitcast.287), channel_id=1, source_target_pairs={{0,128},{16,144},{32,160},{48,176},{64,192},{80,208},{96,224},{112... | collective-permute-start | bytes 196616 | tf_op jit(solution)/shard_map/ppermute | solution.py:51
  107.8 7.7 %collective-permute-start.15 = (f32[2,64,128]{2,1,0:T(8,128)S(1)}, f32[2,64,128]{2,1,0:T(8,128)S(1)}, u32[]{:S(2)}, u32[]{:S(2)}) collective-permute-start(f32[2,64,128]{2,1,0:T(8,128)S(1)} %bitcast.286), channel_id=1, source_target_pairs={{0,256},{16,272},{32,288},{48,304},{64,320},{80,336},{96,352},{112... | collective-permute-start | bytes 196616 | tf_op jit(solution)/shard_map/ppermute | solution.py:51
  125.4 8.5 %collective-permute-start.18 = (f32[2,128,128]{2,1,0:T(8,128)S(1)}, f32[2,128,128]{2,1,0:T(8,128)S(1)}, u32[]{:S(2)}, u32[]{:S(2)}) collective-permute-start(f32[2,128,128]{2,1,0:T(8,128)S(1)} %add_select_fusion.2), channel_id=1, source_target_pairs={{0,2},{1,3},{2,0},{3,1},{4,6},{5,7},{6,4},{7,5},{8,10},{9,11},{10,... | collective-permute-start | bytes 393224 | tf_op jit(solution)/shard_map/ppermute | solution.py:51
  134.0 10.7 %collective-permute-start.19 = (f32[2,128,128]{2,1,0:T(8,128)S(1)}, f32[2,128,128]{2,1,0:T(8,128)S(1)}, u32[]{:S(2)}, u32[]{:S(2)}) collective-permute-start(f32[2,128,128]{2,1,0:T(8,128)S(1)} %bitcast.281), channel_id=1, source_target_pairs={{0,4},{1,5},{2,6},{3,7},{4,0},{5,1},{6,2},{7,3},{8,12},{9,13},{10,... | collective-permute-start | bytes 393224 | tf_op jit(solution)/shard_map/ppermute | solution.py:51
  144.7 12.9 %collective-permute-start.20 = (f32[2,128,128]{2,1,0:T(8,128)S(1)}, f32[2,128,128]{2,1,0:T(8,128)S(1)}, u32[]{:S(2)}, u32[]{:S(2)}) collective-permute-start(f32[2,128,128]{2,1,0:T(8,128)S(1)} %bitcast.282), channel_id=1, source_target_pairs={{0,8},{1,9},{2,10},{3,11},{4,12},{5,13},{6,14},{7,15},{8,0},{9,1},... | collective-permute-start | bytes 393224 | tf_op jit(solution)/shard_map/ppermute | solution.py:51
  167.5 7.8 %collective-permute-start.23 = (f32[2,64,128]{2,1,0:T(8,128)S(1)}, f32[2,64,128]{2,1,0:T(8,128)S(1)}, u32[]{:S(2)}, u32[]{:S(2)}) collective-permute-start(f32[2,64,128]{2,1,0:T(8,128)S(1)} %add_select_fusion.5), channel_id=1, source_target_pairs={{0,32},{16,48},{32,0},{48,16},{64,96},{80,112},{96,64},{112,80},{1... | collective-permute-start | bytes 196616 | tf_op jit(solution)/shard_map/ppermute | solution.py:51
  175.3 10.6 %collective-permute-start.24 = (f32[2,64,128]{2,1,0:T(8,128)S(1)}, f32[2,64,128]{2,1,0:T(8,128)S(1)}, u32[]{:S(2)}, u32[]{:S(2)}) collective-permute-start(f32[2,64,128]{2,1,0:T(8,128)S(1)} %bitcast.292), channel_id=1, source_target_pairs={{0,64},{16,80},{32,96},{48,112},{64,0},{80,16},{96,32},{112,48},{1... | collective-permute-start | bytes 196616 | tf_op jit(solution)/shard_map/ppermute | solution.py:51
  192.4 7.7 %collective-permute-start.26 = (f32[2,64,128]{2,1,0:T(8,128)S(1)}, f32[2,64,128]{2,1,0:T(8,128)S(1)}, u32[]{:S(2)}, u32[]{:S(2)}) collective-permute-start(f32[2,64,128]{2,1,0:T(8,128)S(1)} %bitcast.294), channel_id=1, source_target_pairs={{0,256},{16,272},{32,288},{48,304},{64,320},{80,336},{96,352},{112... | collective-permute-start | bytes 196616 | tf_op jit(solution)/shard_map/ppermute | solution.py:51
  210.1 7.4 %collective-permute-start.29 = (f32[2,128,128]{2,1,0:T(8,128)S(1)}, f32[2,128,128]{2,1,0:T(8,128)S(1)}, u32[]{:S(2)}, u32[]{:S(2)}) collective-permute-start(f32[2,128,128]{2,1,0:T(8,128)S(1)} %add_select_fusion.1), channel_id=1, source_target_pairs={{0,2},{1,3},{2,0},{3,1},{4,6},{5,7},{6,4},{7,5},{8,10},{9,11},{10,... | collective-permute-start | bytes 393224 | tf_op jit(solution)/shard_map/ppermute | solution.py:51
  217.6 10.3 %collective-permute-start.30 = (f32[2,128,128]{2,1,0:T(8,128)S(1)}, f32[2,128,128]{2,1,0:T(8,128)S(1)}, u32[]{:S(2)}, u32[]{:S(2)}) collective-permute-start(f32[2,128,128]{2,1,0:T(8,128)S(1)} %bitcast.284), channel_id=1, source_target_pairs={{0,4},{1,5},{2,6},{3,7},{4,0},{5,1},{6,2},{7,3},{8,12},{9,13},{10,... | collective-permute-start | bytes 393224 | tf_op jit(solution)/shard_map/ppermute | solution.py:51
  227.9 13.3 %collective-permute-start.31 = (f32[2,128,128]{2,1,0:T(8,128)S(1)}, f32[2,128,128]{2,1,0:T(8,128)S(1)}, u32[]{:S(2)}, u32[]{:S(2)}) collective-permute-start(f32[2,128,128]{2,1,0:T(8,128)S(1)} %bitcast.285), channel_id=1, source_target_pairs={{0,8},{1,9},{2,10},{3,11},{4,12},{5,13},{6,14},{7,15},{8,0},{9,1},... | collective-permute-start | bytes 393224 | tf_op jit(solution)/shard_map/ppermute | solution.py:51
  251.1 7.8 %collective-permute-start.34 = (f32[2,64,128]{2,1,0:T(8,128)S(1)}, f32[2,64,128]{2,1,0:T(8,128)S(1)}, u32[]{:S(2)}, u32[]{:S(2)}) collective-permute-start(f32[2,64,128]{2,1,0:T(8,128)S(1)} %add_select_fusion.4), channel_id=1, source_target_pairs={{0,32},{16,48},{32,0},{48,16},{64,96},{80,112},{96,64},{112,80},{1... | collective-permute-start | bytes 196616 | tf_op jit(solution)/shard_map/ppermute | solution.py:51
  258.9 10.2 %collective-permute-start.35 = (f32[2,64,128]{2,1,0:T(8,128)S(1)}, f32[2,64,128]{2,1,0:T(8,128)S(1)}, u32[]{:S(2)}, u32[]{:S(2)}) collective-permute-start(f32[2,64,128]{2,1,0:T(8,128)S(1)} %bitcast.295), channel_id=1, source_target_pairs={{0,64},{16,80},{32,96},{48,112},{64,0},{80,16},{96,32},{112,48},{1... | collective-permute-start | bytes 196616 | tf_op jit(solution)/shard_map/ppermute | solution.py:51
  275.3 7.7 %collective-permute-start.37 = (f32[2,64,128]{2,1,0:T(8,128)S(1)}, f32[2,64,128]{2,1,0:T(8,128)S(1)}, u32[]{:S(2)}, u32[]{:S(2)}) collective-permute-start(f32[2,64,128]{2,1,0:T(8,128)S(1)} %bitcast.297), channel_id=1, source_target_pairs={{0,256},{16,272},{32,288},{48,304},{64,320},{80,336},{96,352},{112... | collective-permute-start | bytes 196616 | tf_op jit(solution)/shard_map/ppermute | solution.py:51
  293.7 7.4 %collective-permute-start.40 = (f32[2,128,128]{2,1,0:T(8,128)S(1)}, f32[2,128,128]{2,1,0:T(8,128)S(1)}, u32[]{:S(2)}, u32[]{:S(2)}) collective-permute-start(f32[2,128,128]{2,1,0:T(8,128)S(1)} %add_select_fusion), channel_id=1, source_target_pairs={{0,2},{1,3},{2,0},{3,1},{4,6},{5,7},{6,4},{7,5},{8,10},{9,11},{10,... | collective-permute-start | bytes 393224 | tf_op jit(solution)/shard_map/ppermute | solution.py:51
  301.2 10.3 %collective-permute-start.41 = (f32[2,128,128]{2,1,0:T(8,128)S(1)}, f32[2,128,128]{2,1,0:T(8,128)S(1)}, u32[]{:S(2)}, u32[]{:S(2)}) collective-permute-start(f32[2,128,128]{2,1,0:T(8,128)S(1)} %bitcast.277), channel_id=1, source_target_pairs={{0,4},{1,5},{2,6},{3,7},{4,0},{5,1},{6,2},{7,3},{8,12},{9,13},{10,... | collective-permute-start | bytes 393224 | tf_op jit(solution)/shard_map/ppermute | solution.py:51
  311.5 13.8 %collective-permute-start.42 = (f32[2,128,128]{2,1,0:T(8,128)S(1)}, f32[2,128,128]{2,1,0:T(8,128)S(1)}, u32[]{:S(2)}, u32[]{:S(2)}) collective-permute-start(f32[2,128,128]{2,1,0:T(8,128)S(1)} %bitcast.278), channel_id=1, source_target_pairs={{0,8},{1,9},{2,10},{3,11},{4,12},{5,13},{6,14},{7,15},{8,0},{9,1},... | collective-permute-start | bytes 393224 | tf_op jit(solution)/shard_map/ppermute | solution.py:51
  335.2 7.8 %collective-permute-start.45 = (f32[2,64,128]{2,1,0:T(8,128)S(1)}, f32[2,64,128]{2,1,0:T(8,128)S(1)}, u32[]{:S(2)}, u32[]{:S(2)}) collective-permute-start(f32[2,64,128]{2,1,0:T(8,128)S(1)} %add_select_fusion.3), channel_id=1, source_target_pairs={{0,32},{16,48},{32,0},{48,16},{64,96},{80,112},{96,64},{112,80},{1... | collective-permute-start | bytes 196616 | tf_op jit(solution)/shard_map/ppermute | solution.py:51
  343.0 10.1 %collective-permute-start.46 = (f32[2,64,128]{2,1,0:T(8,128)S(1)}, f32[2,64,128]{2,1,0:T(8,128)S(1)}, u32[]{:S(2)}, u32[]{:S(2)}) collective-permute-start(f32[2,64,128]{2,1,0:T(8,128)S(1)} %bitcast.289), channel_id=1, source_target_pairs={{0,64},{16,80},{32,96},{48,112},{64,0},{80,16},{96,32},{112,48},{1... | collective-permute-start | bytes 196616 | tf_op jit(solution)/shard_map/ppermute | solution.py:51
  359.3 7.7 %collective-permute-start.48 = (f32[2,64,128]{2,1,0:T(8,128)S(1)}, f32[2,64,128]{2,1,0:T(8,128)S(1)}, u32[]{:S(2)}, u32[]{:S(2)}) collective-permute-start(f32[2,64,128]{2,1,0:T(8,128)S(1)} %bitcast.291), channel_id=1, source_target_pairs={{0,256},{16,272},{32,288},{48,304},{64,320},{80,336},{96,352},{112... | collective-permute-start | bytes 196616 | tf_op jit(solution)/shard_map/ppermute | solution.py:51
  (22 other events, 143.6 us)

commit v9 on v8

--- a/solution.py
+++ b/solution.py
@@ -97,10 +97,12 @@
     )
 
 
-def scatter_groups(blocks, axis):
+def scatter_groups(blocks, axis, hold):
     size = lax.axis_size(axis)
     me = lax.axis_index(axis)
-    for stride, radix in digit_groups(size):
+    for level, (stride, radix) in enumerate(digit_groups(size)):
+        if level == 1:
+            blocks, hold = lax.optimization_barrier((blocks, hold))
         digit = (me // stride) % radix
         rest = blocks.shape[0] // radix
         split = blocks.reshape((rest, radix) + blocks.shape[1:])
@@ -110,7 +112,7 @@
             give = lax.dynamic_index_in_dim(split, digit ^ k, 1, False)
             total = total + lax.ppermute(give, axis, pairs)
         blocks = total
-    return blocks[0]
+    return blocks[0], hold
 
 
 def split_dot(spec, low, wide):
@@ -166,7 +168,7 @@
     ).astype(BF16)
     kept_mask = jnp.any(owned, axis=1)
     blocks = picked.reshape(head_count, col_devices, col_len, head_width).transpose(1, 0, 2, 3)
-    chosen_block = scatter_groups(blocks, "kv")
+    chosen_block, queries = scatter_groups(blocks, "kv", queries)
 
     scores = (
         jnp.einsum("hqd,hkd->hqk", queries, cache_keys, preferred_element_type=F32) * score_scale

time: 376 us -> 386 us (1.027)
  waiting for transfers between devices: 177 us -> 192 us
  starting transfers between devices: 174 us -> 169 us
    ppermute x28, waiting for transfers between devices: 130 us -> 143 us  [gather_bits(): got.append(lax.ppermute(value, axis, pairs))]
    ppermute x28, starting transfers between devices: 118 us -> 113 us  [gather_bits(): got.append(lax.ppermute(value, axis, pairs))]
where the time goes in v9:
time: 386 us; the launch traced here: 384 us
  waiting for transfers between devices  192 us (50%)
  starting transfers between devices  169 us (44%)
  other arithmetic  9.58 us (2%)
  matrix products  8.59 us (2%)
    ppermute x28, waiting for transfers between devices, gather_bits(): got.append(lax.ppermute(value, axis, pairs))  143 us
    ppermute x28, starting transfers between devices, gather_bits(): got.append(lax.ppermute(value, axis, pairs))  113 us
    ppermute x6, starting transfers between devices, scatter_groups(): total = total + lax.ppermute(give, axis, pairs)  20.4 us
    ppermute x7, waiting for transfers between devices, group_sum(): other = lax.ppermute(mine, axis, pairs)  19 us
    ppermute x7, waiting for transfers between devices, group_sum(): arrived = lax.ppermute(jnp.where(low, second, first), axis, pairs)  17.5 us
    ppermute x7, starting transfers between devices, group_sum(): arrived = lax.ppermute(jnp.where(low, second, first), axis, pairs)  16.8 us
    ppermute x7, starting transfers between devices, group_sum(): other = lax.ppermute(mine, axis, pairs)  15.3 us
    ppermute x6, waiting for transfers between devices, scatter_groups(): total = total + lax.ppermute(give, axis, pairs)  11.4 us
  transfers between devices with their start and end apart: 50, of which 46 were waited for; matrix products, arithmetic and copies ran while one was open for 1% of the time, Pallas kernels for 0%

profile of v9, /device:TPU:6, one launch (start us, length us, event | category | flops | bytes accessed | tf_op | source)
XLA Modules:
  0.0 384.4 jit_solution(12123685999696618460)
XLA Ops:
  7.7 4.3 %collective-permute-start.1 = (bf16[4,2,128,128]{3,2,1,0:T(8,128)(2,1)S(1)}, bf16[4,2,128,128]{3,2,1,0:T(8,128)(2,1)S(1)}, u32[]{:S(2)}, u32[]{:S(2)}) collective-permute-start(bf16[4,2,128,128]{3,2,1,0:T(8,128)(2,1)S(1)} %bitcast.299), channel_id=1, source_target_pairs={{0,2},{1,3},{2,0},{3,1},{4,6},{5,7},{6,4},{7,5},{8,10},{9,11},{10,... | collective-permute-start | bytes 786440 | tf_op jit(solution)/shard_map/ppermute | solution.py:113
  19.1 5.2 %collective-permute-done.2 = bf16[4,2,128,128]{3,2,1,0:T(8,128)(2,1)S(1)} collective-permute-done((bf16[4,2,128,128]{3,2,1,0:T(8,128)(2,1)S(1)}, bf16[4,2,128,128]{3,2,1,0:T(8,128)(2,1)S(1)}, u32[]{:S(2)}, u32[]{:S(2)}) %collective-permute-start.2) | collective-permute-done | bytes 262176 | tf_op jit(solution)/shard_map/ppermute | solution.py:113
  35.2 4.1 %collective-permute-done.7 = f32[2,132,128]{2,0,1:T(2,128)S(1)} collective-permute-done((f32[2,132,128]{2,0,1:T(2,128)S(1)}, f32[2,132,128]{2,0,1:T(2,128)S(1)}, u32[]{:S(2)}, u32[]{:S(2)}) %collective-permute-start.7) | collective-permute-done | bytes 135200 | tf_op jit(solution)/shard_map/ppermute | solution.py:51
  40.3 6.1 %collective-permute-start.8 = (f32[2,132,128]{2,0,1:T(2,128)S(1)}, f32[2,132,128]{2,0,1:T(2,128)S(1)}, u32[]{:S(2)}, u32[]{:S(2)}) collective-permute-start(f32[2,132,128]{2,0,1:T(2,128)S(1)} %constant_dynamic-update-slice_fusion.12), channel_id=1, source_target_pairs={{0,4},{1,5},{2,6},{3,7},{4,0},{5,1},{6,2},{7,3},{8,12},{9,13},{10,... | collective-permute-start | bytes 405512 | tf_op jit(solution)/shard_map/ppermute | solution.py:51
  46.4 5.9 %collective-permute-done.8 = f32[2,132,128]{2,0,1:T(2,128)S(1)} collective-permute-done((f32[2,132,128]{2,0,1:T(2,128)S(1)}, f32[2,132,128]{2,0,1:T(2,128)S(1)}, u32[]{:S(2)}, u32[]{:S(2)}) %collective-permute-start.8) | collective-permute-done | bytes 135200 | tf_op jit(solution)/shard_map/ppermute | solution.py:51
  52.8 8.8 %collective-permute-start.9 = (f32[2,132,128]{2,1,0:T(8,128)S(1)}, f32[2,132,128]{2,1,0:T(8,128)S(1)}, u32[]{:S(2)}, u32[]{:S(2)}) collective-permute-start(f32[2,132,128]{2,1,0:T(8,128)S(1)} %concatenate.55), channel_id=1, source_target_pairs={{0,8},{1,9},{2,10},{3,11},{4,12},{5,13},{6,14},{7,15},{8,0},{9,1},... | collective-permute-start | bytes 405512 | tf_op jit(solution)/shard_map/ppermute | solution.py:51
  61.6 5.5 %collective-permute-done.9 = f32[2,132,128]{2,1,0:T(8,128)S(1)} collective-permute-done((f32[2,132,128]{2,1,0:T(8,128)S(1)}, f32[2,132,128]{2,1,0:T(8,128)S(1)}, u32[]{:S(2)}, u32[]{:S(2)}) %collective-permute-start.9) | collective-permute-done | bytes 135200 | tf_op jit(solution)/shard_map/ppermute | solution.py:51
  71.9 6.6 %collective-permute-start.4 = (bf16[1,2,128,128]{3,2,1,0:T(8,128)(2,1)S(1)}, bf16[1,2,128,128]{3,2,1,0:T(8,128)(2,1)S(1)}, u32[]{:S(2)}, u32[]{:S(2)}) collective-permute-start(bf16[1,2,128,128]{3,2,1,0:T(8,128)(2,1)S(1)} %get-tuple-element.42), channel_id=1, source_target_pairs={{0,8},{1,9},{2,10},{3,11},{4,12},{5,13},{6,14},{7,15},{8,0},{9,1},... | collective-permute-start | bytes 196616 | tf_op jit(solution)/shard_map/ppermute | solution.py:113
  93.9 5.4 %collective-permute-start.12 = (f32[2,64,128]{2,1,0:T(8,128)S(1)}, f32[2,64,128]{2,1,0:T(8,128)S(1)}, u32[]{:S(2)}, u32[]{:S(2)}) collective-permute-start(f32[2,64,128]{2,1,0:T(8,128)S(1)} %add_select_fusion.6), channel_id=1, source_target_pairs={{0,32},{16,48},{32,0},{48,16},{64,96},{80,112},{96,64},{112,80},{1... | collective-permute-start | bytes 196616 | tf_op jit(solution)/shard_map/ppermute | solution.py:51
  101.5 7.2 %collective-permute-start.13 = (f32[2,64,128]{2,1,0:T(8,128)S(1)}, f32[2,64,128]{2,1,0:T(8,128)S(1)}, u32[]{:S(2)}, u32[]{:S(2)}) collective-permute-start(f32[2,64,128]{2,1,0:T(8,128)S(1)} %bitcast.288), channel_id=1, source_target_pairs={{0,64},{16,80},{32,96},{48,112},{64,0},{80,16},{96,32},{112,48},{1... | collective-permute-start | bytes 196616 | tf_op jit(solution)/shard_map/ppermute | solution.py:51
  121.6 4.8 %collective-permute-done.15 = f32[2,64,128]{2,1,0:T(8,128)S(1)} collective-permute-done((f32[2,64,128]{2,1,0:T(8,128)S(1)}, f32[2,64,128]{2,1,0:T(8,128)S(1)}, u32[]{:S(2)}, u32[]{:S(2)}) %collective-permute-start.15) | collective-permute-done | bytes 65568 | tf_op jit(solution)/shard_map/ppermute | solution.py:51
  136.2 4.8 %collective-permute-start.18 = (f32[2,128,128]{2,1,0:T(8,128)S(1)}, f32[2,128,128]{2,1,0:T(8,128)S(1)}, u32[]{:S(2)}, u32[]{:S(2)}) collective-permute-start(f32[2,128,128]{2,1,0:T(8,128)S(1)} %add_select_fusion.2), channel_id=1, source_target_pairs={{0,2},{1,3},{2,0},{3,1},{4,6},{5,7},{6,4},{7,5},{8,10},{9,11},{10,... | collective-permute-start | bytes 393224 | tf_op jit(solution)/shard_map/ppermute | solution.py:51
  148.4 7.0 %collective-permute-done.19 = f32[2,128,128]{2,1,0:T(8,128)S(1)} collective-permute-done((f32[2,128,128]{2,1,0:T(8,128)S(1)}, f32[2,128,128]{2,1,0:T(8,128)S(1)}, u32[]{:S(2)}, u32[]{:S(2)}) %collective-permute-start.19) | collective-permute-done | bytes 131104 | tf_op jit(solution)/shard_map/ppermute | solution.py:51
  155.4 5.0 %collective-permute-start.20 = (f32[2,128,128]{2,1,0:T(8,128)S(1)}, f32[2,128,128]{2,1,0:T(8,128)S(1)}, u32[]{:S(2)}, u32[]{:S(2)}) collective-permute-start(f32[2,128,128]{2,1,0:T(8,128)S(1)} %bitcast.282), channel_id=1, source_target_pairs={{0,8},{1,9},{2,10},{3,11},{4,12},{5,13},{6,14},{7,15},{8,0},{9,1},... | collective-permute-start | bytes 393224 | tf_op jit(solution)/shard_map/ppermute | solution.py:51
  160.4 8.0 %collective-permute-done.20 = f32[2,128,128]{2,1,0:T(8,128)S(1)} collective-permute-done((f32[2,128,128]{2,1,0:T(8,128)S(1)}, f32[2,128,128]{2,1,0:T(8,128)S(1)}, u32[]{:S(2)}, u32[]{:S(2)}) %collective-permute-start.20) | collective-permute-done | bytes 131104 | tf_op jit(solution)/shard_map/ppermute | solution.py:51
  186.2 7.0 %collective-permute-start.24 = (f32[2,64,128]{2,1,0:T(8,128)S(1)}, f32[2,64,128]{2,1,0:T(8,128)S(1)}, u32[]{:S(2)}, u32[]{:S(2)}) collective-permute-start(f32[2,64,128]{2,1,0:T(8,128)S(1)} %bitcast.292), channel_id=1, source_target_pairs={{0,64},{16,80},{32,96},{48,112},{64,0},{80,16},{96,32},{112,48},{1... | collective-permute-start | bytes 196616 | tf_op jit(solution)/shard_map/ppermute | solution.py:51
  205.4 5.2 %collective-permute-done.26 = f32[2,64,128]{2,1,0:T(8,128)S(1)} collective-permute-done((f32[2,64,128]{2,1,0:T(8,128)S(1)}, f32[2,64,128]{2,1,0:T(8,128)S(1)}, u32[]{:S(2)}, u32[]{:S(2)}) %collective-permute-start.26) | collective-permute-done | bytes 65568 | tf_op jit(solution)/shard_map/ppermute | solution.py:51
  222.6 5.3 %collective-permute-done.29 = f32[2,128,128]{2,1,0:T(8,128)S(1)} collective-permute-done((f32[2,128,128]{2,1,0:T(8,128)S(1)}, f32[2,128,128]{2,1,0:T(8,128)S(1)}, u32[]{:S(2)}, u32[]{:S(2)}) %collective-permute-start.29) | collective-permute-done | bytes 131104 | tf_op jit(solution)/shard_map/ppermute | solution.py:51
  231.2 7.1 %collective-permute-done.30 = f32[2,128,128]{2,1,0:T(8,128)S(1)} collective-permute-done((f32[2,128,128]{2,1,0:T(8,128)S(1)}, f32[2,128,128]{2,1,0:T(8,128)S(1)}, u32[]{:S(2)}, u32[]{:S(2)}) %collective-permute-start.30) | collective-permute-done | bytes 131104 | tf_op jit(solution)/shard_map/ppermute | solution.py:51
  238.3 4.7 %collective-permute-start.31 = (f32[2,128,128]{2,1,0:T(8,128)S(1)}, f32[2,128,128]{2,1,0:T(8,128)S(1)}, u32[]{:S(2)}, u32[]{:S(2)}) collective-permute-start(f32[2,128,128]{2,1,0:T(8,128)S(1)} %bitcast.285), channel_id=1, source_target_pairs={{0,8},{1,9},{2,10},{3,11},{4,12},{5,13},{6,14},{7,15},{8,0},{9,1},... | collective-permute-start | bytes 393224 | tf_op jit(solution)/shard_map/ppermute | solution.py:51
  243.1 8.4 %collective-permute-done.31 = f32[2,128,128]{2,1,0:T(8,128)S(1)} collective-permute-done((f32[2,128,128]{2,1,0:T(8,128)S(1)}, f32[2,128,128]{2,1,0:T(8,128)S(1)}, u32[]{:S(2)}, u32[]{:S(2)}) %collective-permute-start.31) | collective-permute-done | bytes 131104 | tf_op jit(solution)/shard_map/ppermute | solution.py:51
  269.3 6.1 %collective-permute-start.35 = (f32[2,64,128]{2,1,0:T(8,128)S(1)}, f32[2,64,128]{2,1,0:T(8,128)S(1)}, u32[]{:S(2)}, u32[]{:S(2)}) collective-permute-start(f32[2,64,128]{2,1,0:T(8,128)S(1)} %bitcast.295), channel_id=1, source_target_pairs={{0,64},{16,80},{32,96},{48,112},{64,0},{80,16},{96,32},{112,48},{1... | collective-permute-start | bytes 196616 | tf_op jit(solution)/shard_map/ppermute | solution.py:51
  281.9 4.4 %collective-permute-done.36 = f32[2,64,128]{2,1,0:T(8,128)S(1)} collective-permute-done((f32[2,64,128]{2,1,0:T(8,128)S(1)}, f32[2,64,128]{2,1,0:T(8,128)S(1)}, u32[]{:S(2)}, u32[]{:S(2)}) %collective-permute-start.36) | collective-permute-done | bytes 65568 | tf_op jit(solution)/shard_map/ppermute | solution.py:51
  288.3 5.7 %collective-permute-done.37 = f32[2,64,128]{2,1,0:T(8,128)S(1)} collective-permute-done((f32[2,64,128]{2,1,0:T(8,128)S(1)}, f32[2,64,128]{2,1,0:T(8,128)S(1)}, u32[]{:S(2)}, u32[]{:S(2)}) %collective-permute-start.37) | collective-permute-done | bytes 65568 | tf_op jit(solution)/shard_map/ppermute | solution.py:51
  306.5 5.5 %collective-permute-done.40 = f32[2,128,128]{2,1,0:T(8,128)S(1)} collective-permute-done((f32[2,128,128]{2,1,0:T(8,128)S(1)}, f32[2,128,128]{2,1,0:T(8,128)S(1)}, u32[]{:S(2)}, u32[]{:S(2)}) %collective-permute-start.40) | collective-permute-done | bytes 131104 | tf_op jit(solution)/shard_map/ppermute | solution.py:51
  315.4 7.0 %collective-permute-done.41 = f32[2,128,128]{2,1,0:T(8,128)S(1)} collective-permute-done((f32[2,128,128]{2,1,0:T(8,128)S(1)}, f32[2,128,128]{2,1,0:T(8,128)S(1)}, u32[]{:S(2)}, u32[]{:S(2)}) %collective-permute-start.41) | collective-permute-done | bytes 131104 | tf_op jit(solution)/shard_map/ppermute | solution.py:51
  322.4 4.6 %collective-permute-start.42 = (f32[2,128,128]{2,1,0:T(8,128)S(1)}, f32[2,128,128]{2,1,0:T(8,128)S(1)}, u32[]{:S(2)}, u32[]{:S(2)}) collective-permute-start(f32[2,128,128]{2,1,0:T(8,128)S(1)} %bitcast.278), channel_id=1, source_target_pairs={{0,8},{1,9},{2,10},{3,11},{4,12},{5,13},{6,14},{7,15},{8,0},{9,1},... | collective-permute-start | bytes 393224 | tf_op jit(solution)/shard_map/ppermute | solution.py:51
  327.0 8.7 %collective-permute-done.42 = f32[2,128,128]{2,1,0:T(8,128)S(1)} collective-permute-done((f32[2,128,128]{2,1,0:T(8,128)S(1)}, f32[2,128,128]{2,1,0:T(8,128)S(1)}, u32[]{:S(2)}, u32[]{:S(2)}) %collective-permute-start.42) | collective-permute-done | bytes 131104 | tf_op jit(solution)/shard_map/ppermute | solution.py:51
  348.9 4.4 %collective-permute-done.45 = f32[2,64,128]{2,1,0:T(8,128)S(1)} collective-permute-done((f32[2,64,128]{2,1,0:T(8,128)S(1)}, f32[2,64,128]{2,1,0:T(8,128)S(1)}, u32[]{:S(2)}, u32[]{:S(2)}) %collective-permute-start.45) | collective-permute-done | bytes 65568 | tf_op jit(solution)/shard_map/ppermute | solution.py:51
  353.3 5.8 %collective-permute-start.46 = (f32[2,64,128]{2,1,0:T(8,128)S(1)}, f32[2,64,128]{2,1,0:T(8,128)S(1)}, u32[]{:S(2)}, u32[]{:S(2)}) collective-permute-start(f32[2,64,128]{2,1,0:T(8,128)S(1)} %bitcast.289), channel_id=1, source_target_pairs={{0,64},{16,80},{32,96},{48,112},{64,0},{80,16},{96,32},{112,48},{1... | collective-permute-start | bytes 196616 | tf_op jit(solution)/shard_map/ppermute | solution.py:51
  359.2 4.4 %collective-permute-done.46 = f32[2,64,128]{2,1,0:T(8,128)S(1)} collective-permute-done((f32[2,64,128]{2,1,0:T(8,128)S(1)}, f32[2,64,128]{2,1,0:T(8,128)S(1)}, u32[]{:S(2)}, u32[]{:S(2)}) %collective-permute-start.46) | collective-permute-done | bytes 65568 | tf_op jit(solution)/shard_map/ppermute | solution.py:51
  371.7 5.7 %collective-permute-done.48 = f32[2,64,128]{2,1,0:T(8,128)S(1)} collective-permute-done((f32[2,64,128]{2,1,0:T(8,128)S(1)}, f32[2,64,128]{2,1,0:T(8,128)S(1)}, u32[]{:S(2)}, u32[]{:S(2)}) %collective-permute-start.48) | collective-permute-done | bytes 65568 | tf_op jit(solution)/shard_map/ppermute | solution.py:51
  (212 shorter events, 193.8 us)
Async XLA Ops:
  5.7 10.9 %collective-permute-start = (bf16[4,2,128,128]{3,2,1,0:T(8,128)(2,1)S(1)}, bf16[4,2,128,128]{3,2,1,0:T(8,128)(2,1)S(1)}, u32[]{:S(2)}, u32[]{:S(2)}) collective-permute-start(bf16[4,2,128,128]{3,2,1,0:T(8,128)(2,1)S(1)} %bitcast.298), channel_id=1, source_target_pairs={{0,1},{1,0},{2,3},{3,2},{4,5},{5,4},{6,7},{7,6},{8,9},{9,8},{10,11... | collective-permute-start | bytes 786440 | tf_op jit(solution)/shard_map/ppermute | solution.py:113
  7.7 11.4 %collective-permute-start.1 = (bf16[4,2,128,128]{3,2,1,0:T(8,128)(2,1)S(1)}, bf16[4,2,128,128]{3,2,1,0:T(8,128)(2,1)S(1)}, u32[]{:S(2)}, u32[]{:S(2)}) collective-permute-start(bf16[4,2,128,128]{3,2,1,0:T(8,128)(2,1)S(1)} %bitcast.299), channel_id=1, source_target_pairs={{0,2},{1,3},{2,0},{3,1},{4,6},{5,7},{6,4},{7,5},{8,10},{9,11},{10,... | collective-permute-start | bytes 786440 | tf_op jit(solution)/shard_map/ppermute | solution.py:113
  12.0 12.3 %collective-permute-start.2 = (bf16[4,2,128,128]{3,2,1,0:T(8,128)(2,1)S(1)}, bf16[4,2,128,128]{3,2,1,0:T(8,128)(2,1)S(1)}, u32[]{:S(2)}, u32[]{:S(2)}) collective-permute-start(bf16[4,2,128,128]{3,2,1,0:T(8,128)(2,1)S(1)} %bitcast.300), channel_id=1, source_target_pairs={{0,3},{1,2},{2,1},{3,0},{4,7},{5,6},{6,5},{7,4},{8,11},{9,10},{10,... | collective-permute-start | bytes 786440 | tf_op jit(solution)/shard_map/ppermute | solution.py:113
  31.8 7.5 %collective-permute-start.7 = (f32[2,132,128]{2,0,1:T(2,128)S(1)}, f32[2,132,128]{2,0,1:T(2,128)S(1)}, u32[]{:S(2)}, u32[]{:S(2)}) collective-permute-start(f32[2,132,128]{2,0,1:T(2,128)S(1)} %constant_dynamic-update-slice_fusion.8), channel_id=1, source_target_pairs={{0,2},{1,3},{2,0},{3,1},{4,6},{5,7},{6,4},{7,5},{8,10},{9,11},{10,... | collective-permute-start | bytes 405512 | tf_op jit(solution)/shard_map/ppermute | solution.py:51
  40.3 12.0 %collective-permute-start.8 = (f32[2,132,128]{2,0,1:T(2,128)S(1)}, f32[2,132,128]{2,0,1:T(2,128)S(1)}, u32[]{:S(2)}, u32[]{:S(2)}) collective-permute-start(f32[2,132,128]{2,0,1:T(2,128)S(1)} %constant_dynamic-update-slice_fusion.12), channel_id=1, source_target_pairs={{0,4},{1,5},{2,6},{3,7},{4,0},{5,1},{6,2},{7,3},{8,12},{9,13},{10,... | collective-permute-start | bytes 405512 | tf_op jit(solution)/shard_map/ppermute | solution.py:51
  52.8 14.3 %collective-permute-start.9 = (f32[2,132,128]{2,1,0:T(8,128)S(1)}, f32[2,132,128]{2,1,0:T(8,128)S(1)}, u32[]{:S(2)}, u32[]{:S(2)}) collective-permute-start(f32[2,132,128]{2,1,0:T(8,128)S(1)} %concatenate.55), channel_id=1, source_target_pairs={{0,8},{1,9},{2,10},{3,11},{4,12},{5,13},{6,14},{7,15},{8,0},{9,1},... | collective-permute-start | bytes 405512 | tf_op jit(solution)/shard_map/ppermute | solution.py:51
  68.0 14.3 %collective-permute-start.10 = (f32[2,132,128]{2,0,1:T(2,128)S(1)}, f32[2,132,128]{2,0,1:T(2,128)S(1)}, u32[]{:S(2)}, u32[]{:S(2)}) collective-permute-start(f32[2,132,128]{2,0,1:T(2,128)S(1)} %constant_dynamic-update-slice_fusion.16), channel_id=1, source_target_pairs={{0,1},{1,0},{2,3},{3,2},{4,5},{5,4},{6,7},{7,6},{8,9},{9,8},{10,11... | collective-permute-start | bytes 405512 | tf_op jit(solution)/shard_map/ppermute | solution.py:207
  70.0 13.5 %collective-permute-start.3 = (bf16[1,2,128,128]{3,2,1,0:T(8,128)(2,1)S(1)}, bf16[1,2,128,128]{3,2,1,0:T(8,128)(2,1)S(1)}, u32[]{:S(2)}, u32[]{:S(2)}) collective-permute-start(bf16[1,2,128,128]{3,2,1,0:T(8,128)(2,1)S(1)} %get-tuple-element.40), channel_id=1, source_target_pairs={{0,4},{1,5},{2,6},{3,7},{4,0},{5,1},{6,2},{7,3},{8,12},{9,13},{10,... | collective-permute-start | bytes 196616 | tf_op jit(solution)/shard_map/ppermute | solution.py:113
  71.9 11.6 %collective-permute-start.4 = (bf16[1,2,128,128]{3,2,1,0:T(8,128)(2,1)S(1)}, bf16[1,2,128,128]{3,2,1,0:T(8,128)(2,1)S(1)}, u32[]{:S(2)}, u32[]{:S(2)}) collective-permute-start(bf16[1,2,128,128]{3,2,1,0:T(8,128)(2,1)S(1)} %get-tuple-element.42), channel_id=1, source_target_pairs={{0,8},{1,9},{2,10},{3,11},{4,12},{5,13},{6,14},{7,15},{8,0},{9,1},... | collective-permute-start | bytes 196616 | tf_op jit(solution)/shard_map/ppermute | solution.py:113
  78.5 8.7 %collective-permute-start.5 = (bf16[1,2,128,128]{3,2,1,0:T(8,128)(2,1)S(1)}, bf16[1,2,128,128]{3,2,1,0:T(8,128)(2,1)S(1)}, u32[]{:S(2)}, u32[]{:S(2)}) collective-permute-start(bf16[1,2,128,128]{3,2,1,0:T(8,128)(2,1)S(1)} %get-tuple-element.41), channel_id=1, source_target_pairs={{0,12},{1,13},{2,14},{3,15},{4,8},{5,9},{6,10},{7,11},{8,4},{9,5},... | collective-permute-start | bytes 196616 | tf_op jit(solution)/shard_map/ppermute | solution.py:113
  93.9 7.6 %collective-permute-start.12 = (f32[2,64,128]{2,1,0:T(8,128)S(1)}, f32[2,64,128]{2,1,0:T(8,128)S(1)}, u32[]{:S(2)}, u32[]{:S(2)}) collective-permute-start(f32[2,64,128]{2,1,0:T(8,128)S(1)} %add_select_fusion.6), channel_id=1, source_target_pairs={{0,32},{16,48},{32,0},{48,16},{64,96},{80,112},{96,64},{112,80},{1... | collective-permute-start | bytes 196616 | tf_op jit(solution)/shard_map/ppermute | solution.py:51
  101.5 10.3 %collective-permute-start.13 = (f32[2,64,128]{2,1,0:T(8,128)S(1)}, f32[2,64,128]{2,1,0:T(8,128)S(1)}, u32[]{:S(2)}, u32[]{:S(2)}) collective-permute-start(f32[2,64,128]{2,1,0:T(8,128)S(1)} %bitcast.288), channel_id=1, source_target_pairs={{0,64},{16,80},{32,96},{48,112},{64,0},{80,16},{96,32},{112,48},{1... | collective-permute-start | bytes 196616 | tf_op jit(solution)/shard_map/ppermute | solution.py:51
  118.7 7.7 %collective-permute-start.15 = (f32[2,64,128]{2,1,0:T(8,128)S(1)}, f32[2,64,128]{2,1,0:T(8,128)S(1)}, u32[]{:S(2)}, u32[]{:S(2)}) collective-permute-start(f32[2,64,128]{2,1,0:T(8,128)S(1)} %bitcast.286), channel_id=1, source_target_pairs={{0,256},{16,272},{32,288},{48,304},{64,320},{80,336},{96,352},{112... | collective-permute-start | bytes 196616 | tf_op jit(solution)/shard_map/ppermute | solution.py:51
  136.2 8.6 %collective-permute-start.18 = (f32[2,128,128]{2,1,0:T(8,128)S(1)}, f32[2,128,128]{2,1,0:T(8,128)S(1)}, u32[]{:S(2)}, u32[]{:S(2)}) collective-permute-start(f32[2,128,128]{2,1,0:T(8,128)S(1)} %add_select_fusion.2), channel_id=1, source_target_pairs={{0,2},{1,3},{2,0},{3,1},{4,6},{5,7},{6,4},{7,5},{8,10},{9,11},{10,... | collective-permute-start | bytes 393224 | tf_op jit(solution)/shard_map/ppermute | solution.py:51
  144.8 10.6 %collective-permute-start.19 = (f32[2,128,128]{2,1,0:T(8,128)S(1)}, f32[2,128,128]{2,1,0:T(8,128)S(1)}, u32[]{:S(2)}, u32[]{:S(2)}) collective-permute-start(f32[2,128,128]{2,1,0:T(8,128)S(1)} %bitcast.281), channel_id=1, source_target_pairs={{0,4},{1,5},{2,6},{3,7},{4,0},{5,1},{6,2},{7,3},{8,12},{9,13},{10,... | collective-permute-start | bytes 393224 | tf_op jit(solution)/shard_map/ppermute | solution.py:51
  155.4 13.0 %collective-permute-start.20 = (f32[2,128,128]{2,1,0:T(8,128)S(1)}, f32[2,128,128]{2,1,0:T(8,128)S(1)}, u32[]{:S(2)}, u32[]{:S(2)}) collective-permute-start(f32[2,128,128]{2,1,0:T(8,128)S(1)} %bitcast.282), channel_id=1, source_target_pairs={{0,8},{1,9},{2,10},{3,11},{4,12},{5,13},{6,14},{7,15},{8,0},{9,1},... | collective-permute-start | bytes 393224 | tf_op jit(solution)/shard_map/ppermute | solution.py:51
  178.4 7.8 %collective-permute-start.23 = (f32[2,64,128]{2,1,0:T(8,128)S(1)}, f32[2,64,128]{2,1,0:T(8,128)S(1)}, u32[]{:S(2)}, u32[]{:S(2)}) collective-permute-start(f32[2,64,128]{2,1,0:T(8,128)S(1)} %add_select_fusion.5), channel_id=1, source_target_pairs={{0,32},{16,48},{32,0},{48,16},{64,96},{80,112},{96,64},{112,80},{1... | collective-permute-start | bytes 196616 | tf_op jit(solution)/shard_map/ppermute | solution.py:51
  186.2 10.1 %collective-permute-start.24 = (f32[2,64,128]{2,1,0:T(8,128)S(1)}, f32[2,64,128]{2,1,0:T(8,128)S(1)}, u32[]{:S(2)}, u32[]{:S(2)}) collective-permute-start(f32[2,64,128]{2,1,0:T(8,128)S(1)} %bitcast.292), channel_id=1, source_target_pairs={{0,64},{16,80},{32,96},{48,112},{64,0},{80,16},{96,32},{112,48},{1... | collective-permute-start | bytes 196616 | tf_op jit(solution)/shard_map/ppermute | solution.py:51
  202.9 7.7 %collective-permute-start.26 = (f32[2,64,128]{2,1,0:T(8,128)S(1)}, f32[2,64,128]{2,1,0:T(8,128)S(1)}, u32[]{:S(2)}, u32[]{:S(2)}) collective-permute-start(f32[2,64,128]{2,1,0:T(8,128)S(1)} %bitcast.294), channel_id=1, source_target_pairs={{0,256},{16,272},{32,288},{48,304},{64,320},{80,336},{96,352},{112... | collective-permute-start | bytes 196616 | tf_op jit(solution)/shard_map/ppermute | solution.py:51
  220.5 7.4 %collective-permute-start.29 = (f32[2,128,128]{2,1,0:T(8,128)S(1)}, f32[2,128,128]{2,1,0:T(8,128)S(1)}, u32[]{:S(2)}, u32[]{:S(2)}) collective-permute-start(f32[2,128,128]{2,1,0:T(8,128)S(1)} %add_select_fusion.1), channel_id=1, source_target_pairs={{0,2},{1,3},{2,0},{3,1},{4,6},{5,7},{6,4},{7,5},{8,10},{9,11},{10,... | collective-permute-start | bytes 393224 | tf_op jit(solution)/shard_map/ppermute | solution.py:51
  228.0 10.3 %collective-permute-start.30 = (f32[2,128,128]{2,1,0:T(8,128)S(1)}, f32[2,128,128]{2,1,0:T(8,128)S(1)}, u32[]{:S(2)}, u32[]{:S(2)}) collective-permute-start(f32[2,128,128]{2,1,0:T(8,128)S(1)} %bitcast.284), channel_id=1, source_target_pairs={{0,4},{1,5},{2,6},{3,7},{4,0},{5,1},{6,2},{7,3},{8,12},{9,13},{10,... | collective-permute-start | bytes 393224 | tf_op jit(solution)/shard_map/ppermute | solution.py:51
  238.3 13.2 %collective-permute-start.31 = (f32[2,128,128]{2,1,0:T(8,128)S(1)}, f32[2,128,128]{2,1,0:T(8,128)S(1)}, u32[]{:S(2)}, u32[]{:S(2)}) collective-permute-start(f32[2,128,128]{2,1,0:T(8,128)S(1)} %bitcast.285), channel_id=1, source_target_pairs={{0,8},{1,9},{2,10},{3,11},{4,12},{5,13},{6,14},{7,15},{8,0},{9,1},... | collective-permute-start | bytes 393224 | tf_op jit(solution)/shard_map/ppermute | solution.py:51
  261.5 7.8 %collective-permute-start.34 = (f32[2,64,128]{2,1,0:T(8,128)S(1)}, f32[2,64,128]{2,1,0:T(8,128)S(1)}, u32[]{:S(2)}, u32[]{:S(2)}) collective-permute-start(f32[2,64,128]{2,1,0:T(8,128)S(1)} %add_select_fusion.4), channel_id=1, source_target_pairs={{0,32},{16,48},{32,0},{48,16},{64,96},{80,112},{96,64},{112,80},{1... | collective-permute-start | bytes 196616 | tf_op jit(solution)/shard_map/ppermute | solution.py:51
  269.3 10.1 %collective-permute-start.35 = (f32[2,64,128]{2,1,0:T(8,128)S(1)}, f32[2,64,128]{2,1,0:T(8,128)S(1)}, u32[]{:S(2)}, u32[]{:S(2)}) collective-permute-start(f32[2,64,128]{2,1,0:T(8,128)S(1)} %bitcast.295), channel_id=1, source_target_pairs={{0,64},{16,80},{32,96},{48,112},{64,0},{80,16},{96,32},{112,48},{1... | collective-permute-start | bytes 196616 | tf_op jit(solution)/shard_map/ppermute | solution.py:51
  279.5 6.8 %collective-permute-start.36 = (f32[2,64,128]{2,1,0:T(8,128)S(1)}, f32[2,64,128]{2,1,0:T(8,128)S(1)}, u32[]{:S(2)}, u32[]{:S(2)}) collective-permute-start(f32[2,64,128]{2,1,0:T(8,128)S(1)} %bitcast.296), channel_id=1, source_target_pairs={{0,128},{16,144},{32,160},{48,176},{64,192},{80,208},{96,224},{112... | collective-permute-start | bytes 196616 | tf_op jit(solution)/shard_map/ppermute | solution.py:51
  286.3 7.7 %collective-permute-start.37 = (f32[2,64,128]{2,1,0:T(8,128)S(1)}, f32[2,64,128]{2,1,0:T(8,128)S(1)}, u32[]{:S(2)}, u32[]{:S(2)}) collective-permute-start(f32[2,64,128]{2,1,0:T(8,128)S(1)} %bitcast.297), channel_id=1, source_target_pairs={{0,256},{16,272},{32,288},{48,304},{64,320},{80,336},{96,352},{112... | collective-permute-start | bytes 196616 | tf_op jit(solution)/shard_map/ppermute | solution.py:51
  304.6 7.4 %collective-permute-start.40 = (f32[2,128,128]{2,1,0:T(8,128)S(1)}, f32[2,128,128]{2,1,0:T(8,128)S(1)}, u32[]{:S(2)}, u32[]{:S(2)}) collective-permute-start(f32[2,128,128]{2,1,0:T(8,128)S(1)} %add_select_fusion), channel_id=1, source_target_pairs={{0,2},{1,3},{2,0},{3,1},{4,6},{5,7},{6,4},{7,5},{8,10},{9,11},{10,... | collective-permute-start | bytes 393224 | tf_op jit(solution)/shard_map/ppermute | solution.py:51
  312.1 10.3 %collective-permute-start.41 = (f32[2,128,128]{2,1,0:T(8,128)S(1)}, f32[2,128,128]{2,1,0:T(8,128)S(1)}, u32[]{:S(2)}, u32[]{:S(2)}) collective-permute-start(f32[2,128,128]{2,1,0:T(8,128)S(1)} %bitcast.277), channel_id=1, source_target_pairs={{0,4},{1,5},{2,6},{3,7},{4,0},{5,1},{6,2},{7,3},{8,12},{9,13},{10,... | collective-permute-start | bytes 393224 | tf_op jit(solution)/shard_map/ppermute | solution.py:51
  322.4 13.3 %collective-permute-start.42 = (f32[2,128,128]{2,1,0:T(8,128)S(1)}, f32[2,128,128]{2,1,0:T(8,128)S(1)}, u32[]{:S(2)}, u32[]{:S(2)}) collective-permute-start(f32[2,128,128]{2,1,0:T(8,128)S(1)} %bitcast.278), channel_id=1, source_target_pairs={{0,8},{1,9},{2,10},{3,11},{4,12},{5,13},{6,14},{7,15},{8,0},{9,1},... | collective-permute-start | bytes 393224 | tf_op jit(solution)/shard_map/ppermute | solution.py:51
  345.7 7.6 %collective-permute-start.45 = (f32[2,64,128]{2,1,0:T(8,128)S(1)}, f32[2,64,128]{2,1,0:T(8,128)S(1)}, u32[]{:S(2)}, u32[]{:S(2)}) collective-permute-start(f32[2,64,128]{2,1,0:T(8,128)S(1)} %add_select_fusion.3), channel_id=1, source_target_pairs={{0,32},{16,48},{32,0},{48,16},{64,96},{80,112},{96,64},{112,80},{1... | collective-permute-start | bytes 196616 | tf_op jit(solution)/shard_map/ppermute | solution.py:51
  353.3 10.2 %collective-permute-start.46 = (f32[2,64,128]{2,1,0:T(8,128)S(1)}, f32[2,64,128]{2,1,0:T(8,128)S(1)}, u32[]{:S(2)}, u32[]{:S(2)}) collective-permute-start(f32[2,64,128]{2,1,0:T(8,128)S(1)} %bitcast.289), channel_id=1, source_target_pairs={{0,64},{16,80},{32,96},{48,112},{64,0},{80,16},{96,32},{112,48},{1... | collective-permute-start | bytes 196616 | tf_op jit(solution)/shard_map/ppermute | solution.py:51
  369.8 7.7 %collective-permute-start.48 = (f32[2,64,128]{2,1,0:T(8,128)S(1)}, f32[2,64,128]{2,1,0:T(8,128)S(1)}, u32[]{:S(2)}, u32[]{:S(2)}) collective-permute-start(f32[2,64,128]{2,1,0:T(8,128)S(1)} %bitcast.291), channel_id=1, source_target_pairs={{0,256},{16,272},{32,288},{48,304},{64,320},{80,336},{96,352},{112... | collective-permute-start | bytes 196616 | tf_op jit(solution)/shard_map/ppermute | solution.py:51
  (22 other events, 130.8 us)

commit v10 on v8

--- a/solution.py
+++ b/solution.py
@@ -68,16 +68,25 @@
 
 def group_sum(value, axis):
     count = lax.axis_size(axis).bit_length() - 1
-    pairs = [(s, s ^ 1) for s in range(lax.axis_size(axis))]
-    low = (lax.axis_index(axis) & 1) == 0
-    half = value.shape[1] // 2
-    first = value[:, :half]
-    second = value[:, half:]
-    arrived = lax.ppermute(jnp.where(low, second, first), axis, pairs)
-    mine = jnp.where(low, first + arrived, arrived + second)
-    mine = sum_over_bits(mine, axis, bit_stages(list(range(1, count))))
-    other = lax.ppermute(mine, axis, pairs)
-    return jnp.concatenate([jnp.where(low, mine, other), jnp.where(low, other, mine)], axis=1)
+    me = lax.axis_index(axis)
+    depth = 2
+    for bit in range(depth):
+        pairs = [(s, s ^ (1 << bit)) for s in range(lax.axis_size(axis))]
+        low = ((me >> bit) & 1) == 0
+        half = value.shape[1] // 2
+        first = value[:, :half]
+        second = value[:, half:]
+        arrived = lax.ppermute(jnp.where(low, second, first), axis, pairs)
+        value = jnp.where(low, first + arrived, arrived + second)
+    value = sum_over_bits(value, axis, bit_stages(list(range(depth, count))))
+    for bit in reversed(range(depth)):
+        pairs = [(s, s ^ (1 << bit)) for s in range(lax.axis_size(axis))]
+        low = ((me >> bit) & 1) == 0
+        other = lax.ppermute(value, axis, pairs)
+        value = jnp.concatenate(
+            [jnp.where(low, value, other), jnp.where(low, other, value)], axis=1
+        )
+    return value
 
 
 def pair_split_sum(value, axis, split_axis):

time: 376 us -> 391 us (1.040)
  starting transfers between devices: 174 us -> 207 us
  waiting for transfers between devices: 177 us -> 160 us
    ppermute x28 -> x21, waiting for transfers between devices: 130 us -> 68.8 us  [gather_bits(): got.append(lax.ppermute(value, axis, pairs))]
    ppermute x7 -> x14, starting transfers between devices: 16.9 us -> 42.9 us  [group_sum(): arrived = lax.ppermute(jnp.where(low, second, first), axis, pairs)]
    ppermute x7 -> x14, waiting for transfers between devices: 18.8 us -> 42.6 us  [group_sum(): other = lax.ppermute(value, axis, pairs)]
    ppermute x7 -> x14, starting transfers between devices: 15.5 us -> 38 us  [group_sum(): other = lax.ppermute(value, axis, pairs)]
    ppermute x7 -> x14, waiting for transfers between devices: 17.4 us -> 37.9 us  [group_sum(): arrived = lax.ppermute(jnp.where(low, second, first), axis, pairs)]
    ppermute x28 -> x21, starting transfers between devices: 118 us -> 102 us  [gather_bits(): got.append(lax.ppermute(value, axis, pairs))]
  transfers between devices with their start and end apart: 50 -> 57, of which waited for: 46 -> 53; matrix products, arithmetic and copies ran while one was open for 1% -> 1% of each run, Pallas kernels for 0% -> 0%
where the time goes in v10:
time: 391 us; the launch traced here: 389 us
  starting transfers between devices  207 us (53%)
  waiting for transfers between devices  160 us (41%)
  other arithmetic  10.2 us (3%)
  matrix products  8.76 us (2%)
    ppermute x21, starting transfers between devices, gather_bits(): got.append(lax.ppermute(value, axis, pairs))  102 us
    ppermute x21, waiting for transfers between devices, gather_bits(): got.append(lax.ppermute(value, axis, pairs))  68.8 us
    ppermute x14, starting transfers between devices, group_sum(): arrived = lax.ppermute(jnp.where(low, second, first), axis, pairs)  42.9 us
    ppermute x14, waiting for transfers between devices, group_sum(): other = lax.ppermute(value, axis, pairs)  42.6 us
    ppermute x14, starting transfers between devices, group_sum(): other = lax.ppermute(value, axis, pairs)  38 us
    ppermute x14, waiting for transfers between devices, group_sum(): arrived = lax.ppermute(jnp.where(low, second, first), axis, pairs)  37.9 us
    ppermute x6, starting transfers between devices, scatter_groups(): total = total + lax.ppermute(give, axis, pairs)  19.8 us
    ppermute x6, waiting for transfers between devices, scatter_groups(): total = total + lax.ppermute(give, axis, pairs)  9.09 us
  transfers between devices with their start and end apart: 57, of which 53 were waited for; matrix products, arithmetic and copies ran while one was open for 1% of the time, Pallas kernels for 0%

profile of v10, /device:TPU:6, one launch (start us, length us, event | category | flops | bytes accessed | tf_op | source)
XLA Modules:
  0.0 389.2 jit_solution(9194891853605772189)
XLA Ops:
  12.4 4.3 %collective-permute-start.7 = (f32[2,132,128]{2,0,1:T(2,128)S(1)}, f32[2,132,128]{2,0,1:T(2,128)S(1)}, u32[]{:S(2)}, u32[]{:S(2)}) collective-permute-start(f32[2,132,128]{2,0,1:T(2,128)S(1)} %constant_dynamic-update-slice_fusion.8), channel_id=1, source_target_pairs={{0,2},{1,3},{2,0},{3,1},{4,6},{5,7},{6,4},{7,5},{8,10},{9,11},{10,... | collective-permute-start | bytes 405512 | tf_op jit(solution)/shard_map/ppermute | solution.py:51
  21.5 6.1 %collective-permute-start.8 = (f32[2,132,128]{2,0,1:T(2,128)S(1)}, f32[2,132,128]{2,0,1:T(2,128)S(1)}, u32[]{:S(2)}, u32[]{:S(2)}) collective-permute-start(f32[2,132,128]{2,0,1:T(2,128)S(1)} %constant_dynamic-update-slice_fusion.12), channel_id=1, source_target_pairs={{0,4},{1,5},{2,6},{3,7},{4,0},{5,1},{6,2},{7,3},{8,12},{9,13},{10,... | collective-permute-start | bytes 405512 | tf_op jit(solution)/shard_map/ppermute | solution.py:51
  34.3 8.4 %collective-permute-start.9 = (f32[2,132,128]{2,1,0:T(8,128)S(1)}, f32[2,132,128]{2,1,0:T(8,128)S(1)}, u32[]{:S(2)}, u32[]{:S(2)}) collective-permute-start(f32[2,132,128]{2,1,0:T(8,128)S(1)} %concatenate.76), channel_id=1, source_target_pairs={{0,8},{1,9},{2,10},{3,11},{4,12},{5,13},{6,14},{7,15},{8,0},{9,1},... | collective-permute-start | bytes 405512 | tf_op jit(solution)/shard_map/ppermute | solution.py:51
  55.9 4.7 %collective-permute-done.2 = bf16[4,2,128,128]{3,2,1,0:T(8,128)(2,1)S(1)} collective-permute-done((bf16[4,2,128,128]{3,2,1,0:T(8,128)(2,1)S(1)}, bf16[4,2,128,128]{3,2,1,0:T(8,128)(2,1)S(1)}, u32[]{:S(2)}, u32[]{:S(2)}) %collective-permute-start.2) | collective-permute-done | bytes 262176 | tf_op jit(solution)/shard_map/ppermute | solution.py:120
  60.7 4.3 %collective-permute-start.3 = (bf16[1,2,128,128]{3,2,1,0:T(8,128)(2,1)S(1)}, bf16[1,2,128,128]{3,2,1,0:T(8,128)(2,1)S(1)}, u32[]{:S(2)}, u32[]{:S(2)}) collective-permute-start(bf16[1,2,128,128]{3,2,1,0:T(8,128)(2,1)S(1)} %get-tuple-element.36), channel_id=1, source_target_pairs={{0,4},{1,5},{2,6},{3,7},{4,0},{5,1},{6,2},{7,3},{8,12},{9,13},{10,... | collective-permute-start | bytes 196616 | tf_op jit(solution)/shard_map/ppermute | solution.py:120
  67.8 5.1 %collective-permute-start.5 = (bf16[1,2,128,128]{3,2,1,0:T(8,128)(2,1)S(1)}, bf16[1,2,128,128]{3,2,1,0:T(8,128)(2,1)S(1)}, u32[]{:S(2)}, u32[]{:S(2)}) collective-permute-start(bf16[1,2,128,128]{3,2,1,0:T(8,128)(2,1)S(1)} %get-tuple-element.37), channel_id=1, source_target_pairs={{0,12},{1,13},{2,14},{3,15},{4,8},{5,9},{6,10},{7,11},{8,4},{9,5},... | collective-permute-start | bytes 196616 | tf_op jit(solution)/shard_map/ppermute | solution.py:120
  83.1 4.5 %collective-permute-start.12 = (f32[2,32,128]{2,1,0:T(8,128)S(1)}, f32[2,32,128]{2,1,0:T(8,128)S(1)}, u32[]{:S(2)}, u32[]{:S(2)}) collective-permute-start(f32[2,32,128]{2,1,0:T(8,128)S(1)} %slice_select_fusion.13), channel_id=1, source_target_pairs={{0,32},{16,48},{32,0},{48,16},{64,96},{80,112},{96,64},{112,80},{1... | collective-permute-start | bytes 98312 | tf_op jit(solution)/shard_map/ppermute | solution.py:79
  89.8 8.1 %collective-permute-start.13 = (f32[2,32,128]{2,1,0:T(8,128)S(1)}, f32[2,32,128]{2,1,0:T(8,128)S(1)}, u32[]{:S(2)}, u32[]{:S(2)}) collective-permute-start(f32[2,32,128]{2,1,0:T(8,128)S(1)} %add_select_fusion.13), channel_id=1, source_target_pairs={{0,64},{16,80},{32,96},{48,112},{64,0},{80,16},{96,32},{112,48},{1... | collective-permute-start | bytes 98312 | tf_op jit(solution)/shard_map/ppermute | solution.py:51
  109.3 4.0 %collective-permute-done.15 = f32[2,32,128]{2,1,0:T(8,128)S(1)} collective-permute-done((f32[2,32,128]{2,1,0:T(8,128)S(1)}, f32[2,32,128]{2,1,0:T(8,128)S(1)}, u32[]{:S(2)}, u32[]{:S(2)}) %collective-permute-start.15) | collective-permute-done | bytes 32800 | tf_op jit(solution)/shard_map/ppermute | solution.py:51
  113.3 4.0 %collective-permute-start.16 = (f32[2,32,128]{2,1,0:T(8,128)S(1)}, f32[2,32,128]{2,1,0:T(8,128)S(1)}, u32[]{:S(2)}, u32[]{:S(2)}) collective-permute-start(f32[2,32,128]{2,1,0:T(8,128)S(1)} %fusion.114), channel_id=1, source_target_pairs={{0,32},{16,48},{32,0},{48,16},{64,96},{80,112},{96,64},{112,80},{1... | collective-permute-start | bytes 98312 | tf_op jit(solution)/shard_map/ppermute | solution.py:85
  130.0 4.4 %collective-permute-start.19 = (f32[2,64,128]{2,1,0:T(8,128)S(1)}, f32[2,64,128]{2,1,0:T(8,128)S(1)}, u32[]{:S(2)}, u32[]{:S(2)}) collective-permute-start(f32[2,64,128]{2,1,0:T(8,128)S(1)} %slice_select_fusion.8), channel_id=1, source_target_pairs={{0,2},{1,3},{2,0},{3,1},{4,6},{5,7},{6,4},{7,5},{8,10},{9,11},{10,... | collective-permute-start | bytes 196616 | tf_op jit(solution)/shard_map/ppermute | solution.py:79
  136.8 5.1 %collective-permute-start.20 = (f32[2,64,128]{2,1,0:T(8,128)S(1)}, f32[2,64,128]{2,1,0:T(8,128)S(1)}, u32[]{:S(2)}, u32[]{:S(2)}) collective-permute-start(f32[2,64,128]{2,1,0:T(8,128)S(1)} %add_select_fusion.8), channel_id=1, source_target_pairs={{0,4},{1,5},{2,6},{3,7},{4,0},{5,1},{6,2},{7,3},{8,12},{9,13},{10,... | collective-permute-start | bytes 196616 | tf_op jit(solution)/shard_map/ppermute | solution.py:51
  144.1 5.8 %collective-permute-start.21 = (f32[2,64,128]{2,1,0:T(8,128)S(1)}, f32[2,64,128]{2,1,0:T(8,128)S(1)}, u32[]{:S(2)}, u32[]{:S(2)}) collective-permute-start(f32[2,64,128]{2,1,0:T(8,128)S(1)} %bitcast.264), channel_id=1, source_target_pairs={{0,8},{1,9},{2,10},{3,11},{4,12},{5,13},{6,14},{7,15},{8,0},{9,1},... | collective-permute-start | bytes 196616 | tf_op jit(solution)/shard_map/ppermute | solution.py:51
  149.9 4.3 %collective-permute-done.21 = f32[2,64,128]{2,1,0:T(8,128)S(1)} collective-permute-done((f32[2,64,128]{2,1,0:T(8,128)S(1)}, f32[2,64,128]{2,1,0:T(8,128)S(1)}, u32[]{:S(2)}, u32[]{:S(2)}) %collective-permute-start.21) | collective-permute-done | bytes 65568 | tf_op jit(solution)/shard_map/ppermute | solution.py:51
  170.3 4.3 %collective-permute-start.25 = (f32[2,32,128]{2,1,0:T(8,128)S(1)}, f32[2,32,128]{2,1,0:T(8,128)S(1)}, u32[]{:S(2)}, u32[]{:S(2)}) collective-permute-start(f32[2,32,128]{2,1,0:T(8,128)S(1)} %slice_select_fusion.12), channel_id=1, source_target_pairs={{0,32},{16,48},{32,0},{48,16},{64,96},{80,112},{96,64},{112,80},{1... | collective-permute-start | bytes 98312 | tf_op jit(solution)/shard_map/ppermute | solution.py:79
  177.0 8.1 %collective-permute-start.26 = (f32[2,32,128]{2,1,0:T(8,128)S(1)}, f32[2,32,128]{2,1,0:T(8,128)S(1)}, u32[]{:S(2)}, u32[]{:S(2)}) collective-permute-start(f32[2,32,128]{2,1,0:T(8,128)S(1)} %add_select_fusion.12), channel_id=1, source_target_pairs={{0,64},{16,80},{32,96},{48,112},{64,0},{80,16},{96,32},{112,48},{1... | collective-permute-start | bytes 98312 | tf_op jit(solution)/shard_map/ppermute | solution.py:51
  196.5 4.1 %collective-permute-done.28 = f32[2,32,128]{2,1,0:T(8,128)S(1)} collective-permute-done((f32[2,32,128]{2,1,0:T(8,128)S(1)}, f32[2,32,128]{2,1,0:T(8,128)S(1)}, u32[]{:S(2)}, u32[]{:S(2)}) %collective-permute-start.28) | collective-permute-done | bytes 32800 | tf_op jit(solution)/shard_map/ppermute | solution.py:51
  224.0 4.9 %collective-permute-start.33 = (f32[2,64,128]{2,1,0:T(8,128)S(1)}, f32[2,64,128]{2,1,0:T(8,128)S(1)}, u32[]{:S(2)}, u32[]{:S(2)}) collective-permute-start(f32[2,64,128]{2,1,0:T(8,128)S(1)} %add_select_fusion.6), channel_id=1, source_target_pairs={{0,4},{1,5},{2,6},{3,7},{4,0},{5,1},{6,2},{7,3},{8,12},{9,13},{10,... | collective-permute-start | bytes 196616 | tf_op jit(solution)/shard_map/ppermute | solution.py:51
  231.2 5.7 %collective-permute-start.34 = (f32[2,64,128]{2,1,0:T(8,128)S(1)}, f32[2,64,128]{2,1,0:T(8,128)S(1)}, u32[]{:S(2)}, u32[]{:S(2)}) collective-permute-start(f32[2,64,128]{2,1,0:T(8,128)S(1)} %bitcast.265), channel_id=1, source_target_pairs={{0,8},{1,9},{2,10},{3,11},{4,12},{5,13},{6,14},{7,15},{8,0},{9,1},... | collective-permute-start | bytes 196616 | tf_op jit(solution)/shard_map/ppermute | solution.py:51
  236.9 4.3 %collective-permute-done.34 = f32[2,64,128]{2,1,0:T(8,128)S(1)} collective-permute-done((f32[2,64,128]{2,1,0:T(8,128)S(1)}, f32[2,64,128]{2,1,0:T(8,128)S(1)}, u32[]{:S(2)}, u32[]{:S(2)}) %collective-permute-start.34) | collective-permute-done | bytes 65568 | tf_op jit(solution)/shard_map/ppermute | solution.py:51
  264.4 7.2 %collective-permute-start.39 = (f32[2,32,128]{2,1,0:T(8,128)S(1)}, f32[2,32,128]{2,1,0:T(8,128)S(1)}, u32[]{:S(2)}, u32[]{:S(2)}) collective-permute-start(f32[2,32,128]{2,1,0:T(8,128)S(1)} %add_select_fusion.11), channel_id=1, source_target_pairs={{0,64},{16,80},{32,96},{48,112},{64,0},{80,16},{96,32},{112,48},{1... | collective-permute-start | bytes 98312 | tf_op jit(solution)/shard_map/ppermute | solution.py:51
  283.0 4.2 %collective-permute-done.41 = f32[2,32,128]{2,1,0:T(8,128)S(1)} collective-permute-done((f32[2,32,128]{2,1,0:T(8,128)S(1)}, f32[2,32,128]{2,1,0:T(8,128)S(1)}, u32[]{:S(2)}, u32[]{:S(2)}) %collective-permute-start.41) | collective-permute-done | bytes 32800 | tf_op jit(solution)/shard_map/ppermute | solution.py:51
  290.4 4.0 %collective-permute-done.42 = f32[2,32,128]{2,1,0:T(8,128)S(1)} collective-permute-done((f32[2,32,128]{2,1,0:T(8,128)S(1)}, f32[2,32,128]{2,1,0:T(8,128)S(1)}, u32[]{:S(2)}, u32[]{:S(2)}) %collective-permute-start.42) | collective-permute-done | bytes 32800 | tf_op jit(solution)/shard_map/ppermute | solution.py:85
  311.3 5.0 %collective-permute-start.46 = (f32[2,64,128]{2,1,0:T(8,128)S(1)}, f32[2,64,128]{2,1,0:T(8,128)S(1)}, u32[]{:S(2)}, u32[]{:S(2)}) collective-permute-start(f32[2,64,128]{2,1,0:T(8,128)S(1)} %add_select_fusion.4), channel_id=1, source_target_pairs={{0,4},{1,5},{2,6},{3,7},{4,0},{5,1},{6,2},{7,3},{8,12},{9,13},{10,... | collective-permute-start | bytes 196616 | tf_op jit(solution)/shard_map/ppermute | solution.py:51
  319.2 5.2 %collective-permute-start.47 = (f32[2,64,128]{2,1,0:T(8,128)S(1)}, f32[2,64,128]{2,1,0:T(8,128)S(1)}, u32[]{:S(2)}, u32[]{:S(2)}) collective-permute-start(f32[2,64,128]{2,1,0:T(8,128)S(1)} %bitcast.263), channel_id=1, source_target_pairs={{0,8},{1,9},{2,10},{3,11},{4,12},{5,13},{6,14},{7,15},{8,0},{9,1},... | collective-permute-start | bytes 196616 | tf_op jit(solution)/shard_map/ppermute | solution.py:51
  324.4 4.9 %collective-permute-done.47 = f32[2,64,128]{2,1,0:T(8,128)S(1)} collective-permute-done((f32[2,64,128]{2,1,0:T(8,128)S(1)}, f32[2,64,128]{2,1,0:T(8,128)S(1)}, u32[]{:S(2)}, u32[]{:S(2)}) %collective-permute-start.47) | collective-permute-done | bytes 65568 | tf_op jit(solution)/shard_map/ppermute | solution.py:51
  331.6 4.0 %collective-permute-done.48 = f32[2,64,128]{2,1,0:T(8,128)S(1)} collective-permute-done((f32[2,64,128]{2,1,0:T(8,128)S(1)}, f32[2,64,128]{2,1,0:T(8,128)S(1)}, u32[]{:S(2)}, u32[]{:S(2)}) %collective-permute-start.48) | collective-permute-done | bytes 65568 | tf_op jit(solution)/shard_map/ppermute | solution.py:85
  348.3 4.0 %collective-permute-done.51 = f32[2,32,128]{2,1,0:T(8,128)S(1)} collective-permute-done((f32[2,32,128]{2,1,0:T(8,128)S(1)}, f32[2,32,128]{2,1,0:T(8,128)S(1)}, u32[]{:S(2)}, u32[]{:S(2)}) %collective-permute-start.51) | collective-permute-done | bytes 32800 | tf_op jit(solution)/shard_map/ppermute | solution.py:79
  352.4 6.9 %collective-permute-start.52 = (f32[2,32,128]{2,1,0:T(8,128)S(1)}, f32[2,32,128]{2,1,0:T(8,128)S(1)}, u32[]{:S(2)}, u32[]{:S(2)}) collective-permute-start(f32[2,32,128]{2,1,0:T(8,128)S(1)} %add_select_fusion.10), channel_id=1, source_target_pairs={{0,64},{16,80},{32,96},{48,112},{64,0},{80,16},{96,32},{112,48},{1... | collective-permute-start | bytes 98312 | tf_op jit(solution)/shard_map/ppermute | solution.py:51
  364.0 3.9 %collective-permute-done.53 = f32[2,32,128]{2,1,0:T(8,128)S(1)} collective-permute-done((f32[2,32,128]{2,1,0:T(8,128)S(1)}, f32[2,32,128]{2,1,0:T(8,128)S(1)}, u32[]{:S(2)}, u32[]{:S(2)}) %collective-permute-start.53) | collective-permute-done | bytes 32800 | tf_op jit(solution)/shard_map/ppermute | solution.py:51
  370.0 5.3 %collective-permute-done.54 = f32[2,32,128]{2,1,0:T(8,128)S(1)} collective-permute-done((f32[2,32,128]{2,1,0:T(8,128)S(1)}, f32[2,32,128]{2,1,0:T(8,128)S(1)}, u32[]{:S(2)}, u32[]{:S(2)}) %collective-permute-start.54) | collective-permute-done | bytes 32800 | tf_op jit(solution)/shard_map/ppermute | solution.py:51
  378.0 4.4 %collective-permute-done.55 = f32[2,32,128]{2,1,0:T(8,128)S(1)} collective-permute-done((f32[2,32,128]{2,1,0:T(8,128)S(1)}, f32[2,32,128]{2,1,0:T(8,128)S(1)}, u32[]{:S(2)}, u32[]{:S(2)}) %collective-permute-start.55) | collective-permute-done | bytes 32800 | tf_op jit(solution)/shard_map/ppermute | solution.py:85
  (247 shorter events, 223.6 us)
Async XLA Ops:
  12.4 8.2 %collective-permute-start.7 = (f32[2,132,128]{2,0,1:T(2,128)S(1)}, f32[2,132,128]{2,0,1:T(2,128)S(1)}, u32[]{:S(2)}, u32[]{:S(2)}) collective-permute-start(f32[2,132,128]{2,0,1:T(2,128)S(1)} %constant_dynamic-update-slice_fusion.8), channel_id=1, source_target_pairs={{0,2},{1,3},{2,0},{3,1},{4,6},{5,7},{6,4},{7,5},{8,10},{9,11},{10,... | collective-permute-start | bytes 405512 | tf_op jit(solution)/shard_map/ppermute | solution.py:51
  21.5 12.3 %collective-permute-start.8 = (f32[2,132,128]{2,0,1:T(2,128)S(1)}, f32[2,132,128]{2,0,1:T(2,128)S(1)}, u32[]{:S(2)}, u32[]{:S(2)}) collective-permute-start(f32[2,132,128]{2,0,1:T(2,128)S(1)} %constant_dynamic-update-slice_fusion.12), channel_id=1, source_target_pairs={{0,4},{1,5},{2,6},{3,7},{4,0},{5,1},{6,2},{7,3},{8,12},{9,13},{10,... | collective-permute-start | bytes 405512 | tf_op jit(solution)/shard_map/ppermute | solution.py:51
  34.3 16.3 %collective-permute-start.9 = (f32[2,132,128]{2,1,0:T(8,128)S(1)}, f32[2,132,128]{2,1,0:T(8,128)S(1)}, u32[]{:S(2)}, u32[]{:S(2)}) collective-permute-start(f32[2,132,128]{2,1,0:T(8,128)S(1)} %concatenate.76), channel_id=1, source_target_pairs={{0,8},{1,9},{2,10},{3,11},{4,12},{5,13},{6,14},{7,15},{8,0},{9,1},... | collective-permute-start | bytes 405512 | tf_op jit(solution)/shard_map/ppermute | solution.py:51
  42.9 10.8 %collective-permute-start = (bf16[4,2,128,128]{3,2,1,0:T(8,128)(2,1)S(1)}, bf16[4,2,128,128]{3,2,1,0:T(8,128)(2,1)S(1)}, u32[]{:S(2)}, u32[]{:S(2)}) collective-permute-start(bf16[4,2,128,128]{3,2,1,0:T(8,128)(2,1)S(1)} %bitcast.266), channel_id=1, source_target_pairs={{0,1},{1,0},{2,3},{3,2},{4,5},{5,4},{6,7},{7,6},{8,9},{9,8},{10,11... | collective-permute-start | bytes 786440 | tf_op jit(solution)/shard_map/ppermute | solution.py:120
  44.8 11.1 %collective-permute-start.1 = (bf16[4,2,128,128]{3,2,1,0:T(8,128)(2,1)S(1)}, bf16[4,2,128,128]{3,2,1,0:T(8,128)(2,1)S(1)}, u32[]{:S(2)}, u32[]{:S(2)}) collective-permute-start(bf16[4,2,128,128]{3,2,1,0:T(8,128)(2,1)S(1)} %bitcast.267), channel_id=1, source_target_pairs={{0,2},{1,3},{2,0},{3,1},{4,6},{5,7},{6,4},{7,5},{8,10},{9,11},{10,... | collective-permute-start | bytes 786440 | tf_op jit(solution)/shard_map/ppermute | solution.py:120
  47.2 13.3 %collective-permute-start.2 = (bf16[4,2,128,128]{3,2,1,0:T(8,128)(2,1)S(1)}, bf16[4,2,128,128]{3,2,1,0:T(8,128)(2,1)S(1)}, u32[]{:S(2)}, u32[]{:S(2)}) collective-permute-start(bf16[4,2,128,128]{3,2,1,0:T(8,128)(2,1)S(1)} %bitcast.268), channel_id=1, source_target_pairs={{0,3},{1,2},{2,1},{3,0},{4,7},{5,6},{6,5},{7,4},{8,11},{9,10},{10,... | collective-permute-start | bytes 786440 | tf_op jit(solution)/shard_map/ppermute | solution.py:120
  51.5 21.4 %collective-permute-start.10 = (f32[2,132,128]{2,0,1:T(2,128)S(1)}, f32[2,132,128]{2,0,1:T(2,128)S(1)}, u32[]{:S(2)}, u32[]{:S(2)}) collective-permute-start(f32[2,132,128]{2,0,1:T(2,128)S(1)} %constant_dynamic-update-slice_fusion.16), channel_id=1, source_target_pairs={{0,1},{1,0},{2,3},{3,2},{4,5},{5,4},{6,7},{7,6},{8,9},{9,8},{10,11... | collective-permute-start | bytes 405512 | tf_op jit(solution)/shard_map/ppermute | solution.py:214
  60.7 13.5 %collective-permute-start.3 = (bf16[1,2,128,128]{3,2,1,0:T(8,128)(2,1)S(1)}, bf16[1,2,128,128]{3,2,1,0:T(8,128)(2,1)S(1)}, u32[]{:S(2)}, u32[]{:S(2)}) collective-permute-start(bf16[1,2,128,128]{3,2,1,0:T(8,128)(2,1)S(1)} %get-tuple-element.36), channel_id=1, source_target_pairs={{0,4},{1,5},{2,6},{3,7},{4,0},{5,1},{6,2},{7,3},{8,12},{9,13},{10,... | collective-permute-start | bytes 196616 | tf_op jit(solution)/shard_map/ppermute | solution.py:120
  65.0 10.2 %collective-permute-start.4 = (bf16[1,2,128,128]{3,2,1,0:T(8,128)(2,1)S(1)}, bf16[1,2,128,128]{3,2,1,0:T(8,128)(2,1)S(1)}, u32[]{:S(2)}, u32[]{:S(2)}) collective-permute-start(bf16[1,2,128,128]{3,2,1,0:T(8,128)(2,1)S(1)} %get-tuple-element.38), channel_id=1, source_target_pairs={{0,8},{1,9},{2,10},{3,11},{4,12},{5,13},{6,14},{7,15},{8,0},{9,1},... | collective-permute-start | bytes 196616 | tf_op jit(solution)/shard_map/ppermute | solution.py:120
  67.8 8.6 %collective-permute-start.5 = (bf16[1,2,128,128]{3,2,1,0:T(8,128)(2,1)S(1)}, bf16[1,2,128,128]{3,2,1,0:T(8,128)(2,1)S(1)}, u32[]{:S(2)}, u32[]{:S(2)}) collective-permute-start(bf16[1,2,128,128]{3,2,1,0:T(8,128)(2,1)S(1)} %get-tuple-element.37), channel_id=1, source_target_pairs={{0,12},{1,13},{2,14},{3,15},{4,8},{5,9},{6,10},{7,11},{8,4},{9,5},... | collective-permute-start | bytes 196616 | tf_op jit(solution)/shard_map/ppermute | solution.py:120
  83.1 6.7 %collective-permute-start.12 = (f32[2,32,128]{2,1,0:T(8,128)S(1)}, f32[2,32,128]{2,1,0:T(8,128)S(1)}, u32[]{:S(2)}, u32[]{:S(2)}) collective-permute-start(f32[2,32,128]{2,1,0:T(8,128)S(1)} %slice_select_fusion.13), channel_id=1, source_target_pairs={{0,32},{16,48},{32,0},{48,16},{64,96},{80,112},{96,64},{112,80},{1... | collective-permute-start | bytes 98312 | tf_op jit(solution)/shard_map/ppermute | solution.py:79
  89.8 10.3 %collective-permute-start.13 = (f32[2,32,128]{2,1,0:T(8,128)S(1)}, f32[2,32,128]{2,1,0:T(8,128)S(1)}, u32[]{:S(2)}, u32[]{:S(2)}) collective-permute-start(f32[2,32,128]{2,1,0:T(8,128)S(1)} %add_select_fusion.13), channel_id=1, source_target_pairs={{0,64},{16,80},{32,96},{48,112},{64,0},{80,16},{96,32},{112,48},{1... | collective-permute-start | bytes 98312 | tf_op jit(solution)/shard_map/ppermute | solution.py:51
  105.9 7.3 %collective-permute-start.15 = (f32[2,32,128]{2,1,0:T(8,128)S(1)}, f32[2,32,128]{2,1,0:T(8,128)S(1)}, u32[]{:S(2)}, u32[]{:S(2)}) collective-permute-start(f32[2,32,128]{2,1,0:T(8,128)S(1)} %bitcast.278), channel_id=1, source_target_pairs={{0,256},{16,272},{32,288},{48,304},{64,320},{80,336},{96,352},{112... | collective-permute-start | bytes 98312 | tf_op jit(solution)/shard_map/ppermute | solution.py:51
  113.3 6.7 %collective-permute-start.16 = (f32[2,32,128]{2,1,0:T(8,128)S(1)}, f32[2,32,128]{2,1,0:T(8,128)S(1)}, u32[]{:S(2)}, u32[]{:S(2)}) collective-permute-start(f32[2,32,128]{2,1,0:T(8,128)S(1)} %fusion.114), channel_id=1, source_target_pairs={{0,32},{16,48},{32,0},{48,16},{64,96},{80,112},{96,64},{112,80},{1... | collective-permute-start | bytes 98312 | tf_op jit(solution)/shard_map/ppermute | solution.py:85
  130.0 6.8 %collective-permute-start.19 = (f32[2,64,128]{2,1,0:T(8,128)S(1)}, f32[2,64,128]{2,1,0:T(8,128)S(1)}, u32[]{:S(2)}, u32[]{:S(2)}) collective-permute-start(f32[2,64,128]{2,1,0:T(8,128)S(1)} %slice_select_fusion.8), channel_id=1, source_target_pairs={{0,2},{1,3},{2,0},{3,1},{4,6},{5,7},{6,4},{7,5},{8,10},{9,11},{10,... | collective-permute-start | bytes 196616 | tf_op jit(solution)/shard_map/ppermute | solution.py:79
  136.8 7.3 %collective-permute-start.20 = (f32[2,64,128]{2,1,0:T(8,128)S(1)}, f32[2,64,128]{2,1,0:T(8,128)S(1)}, u32[]{:S(2)}, u32[]{:S(2)}) collective-permute-start(f32[2,64,128]{2,1,0:T(8,128)S(1)} %add_select_fusion.8), channel_id=1, source_target_pairs={{0,4},{1,5},{2,6},{3,7},{4,0},{5,1},{6,2},{7,3},{8,12},{9,13},{10,... | collective-permute-start | bytes 196616 | tf_op jit(solution)/shard_map/ppermute | solution.py:51
  144.1 10.1 %collective-permute-start.21 = (f32[2,64,128]{2,1,0:T(8,128)S(1)}, f32[2,64,128]{2,1,0:T(8,128)S(1)}, u32[]{:S(2)}, u32[]{:S(2)}) collective-permute-start(f32[2,64,128]{2,1,0:T(8,128)S(1)} %bitcast.264), channel_id=1, source_target_pairs={{0,8},{1,9},{2,10},{3,11},{4,12},{5,13},{6,14},{7,15},{8,0},{9,1},... | collective-permute-start | bytes 196616 | tf_op jit(solution)/shard_map/ppermute | solution.py:51
  177.0 10.3 %collective-permute-start.26 = (f32[2,32,128]{2,1,0:T(8,128)S(1)}, f32[2,32,128]{2,1,0:T(8,128)S(1)}, u32[]{:S(2)}, u32[]{:S(2)}) collective-permute-start(f32[2,32,128]{2,1,0:T(8,128)S(1)} %add_select_fusion.12), channel_id=1, source_target_pairs={{0,64},{16,80},{32,96},{48,112},{64,0},{80,16},{96,32},{112,48},{1... | collective-permute-start | bytes 98312 | tf_op jit(solution)/shard_map/ppermute | solution.py:51
  193.4 7.3 %collective-permute-start.28 = (f32[2,32,128]{2,1,0:T(8,128)S(1)}, f32[2,32,128]{2,1,0:T(8,128)S(1)}, u32[]{:S(2)}, u32[]{:S(2)}) collective-permute-start(f32[2,32,128]{2,1,0:T(8,128)S(1)} %bitcast.283), channel_id=1, source_target_pairs={{0,256},{16,272},{32,288},{48,304},{64,320},{80,336},{96,352},{112... | collective-permute-start | bytes 98312 | tf_op jit(solution)/shard_map/ppermute | solution.py:51
  200.7 7.1 %collective-permute-start.29 = (f32[2,32,128]{2,1,0:T(8,128)S(1)}, f32[2,32,128]{2,1,0:T(8,128)S(1)}, u32[]{:S(2)}, u32[]{:S(2)}) collective-permute-start(f32[2,32,128]{2,1,0:T(8,128)S(1)} %fusion.104), channel_id=1, source_target_pairs={{0,32},{16,48},{32,0},{48,16},{64,96},{80,112},{96,64},{112,80},{1... | collective-permute-start | bytes 98312 | tf_op jit(solution)/shard_map/ppermute | solution.py:85
  224.0 7.2 %collective-permute-start.33 = (f32[2,64,128]{2,1,0:T(8,128)S(1)}, f32[2,64,128]{2,1,0:T(8,128)S(1)}, u32[]{:S(2)}, u32[]{:S(2)}) collective-permute-start(f32[2,64,128]{2,1,0:T(8,128)S(1)} %add_select_fusion.6), channel_id=1, source_target_pairs={{0,4},{1,5},{2,6},{3,7},{4,0},{5,1},{6,2},{7,3},{8,12},{9,13},{10,... | collective-permute-start | bytes 196616 | tf_op jit(solution)/shard_map/ppermute | solution.py:51
  231.2 10.1 %collective-permute-start.34 = (f32[2,64,128]{2,1,0:T(8,128)S(1)}, f32[2,64,128]{2,1,0:T(8,128)S(1)}, u32[]{:S(2)}, u32[]{:S(2)}) collective-permute-start(f32[2,64,128]{2,1,0:T(8,128)S(1)} %bitcast.265), channel_id=1, source_target_pairs={{0,8},{1,9},{2,10},{3,11},{4,12},{5,13},{6,14},{7,15},{8,0},{9,1},... | collective-permute-start | bytes 196616 | tf_op jit(solution)/shard_map/ppermute | solution.py:51
  257.4 7.0 %collective-permute-start.38 = (f32[2,32,128]{2,1,0:T(8,128)S(1)}, f32[2,32,128]{2,1,0:T(8,128)S(1)}, u32[]{:S(2)}, u32[]{:S(2)}) collective-permute-start(f32[2,32,128]{2,1,0:T(8,128)S(1)} %slice_select_fusion.11), channel_id=1, source_target_pairs={{0,32},{16,48},{32,0},{48,16},{64,96},{80,112},{96,64},{112,80},{1... | collective-permute-start | bytes 98312 | tf_op jit(solution)/shard_map/ppermute | solution.py:79
  264.4 9.7 %collective-permute-start.39 = (f32[2,32,128]{2,1,0:T(8,128)S(1)}, f32[2,32,128]{2,1,0:T(8,128)S(1)}, u32[]{:S(2)}, u32[]{:S(2)}) collective-permute-start(f32[2,32,128]{2,1,0:T(8,128)S(1)} %add_select_fusion.11), channel_id=1, source_target_pairs={{0,64},{16,80},{32,96},{48,112},{64,0},{80,16},{96,32},{112,48},{1... | collective-permute-start | bytes 98312 | tf_op jit(solution)/shard_map/ppermute | solution.py:51
  280.0 7.3 %collective-permute-start.41 = (f32[2,32,128]{2,1,0:T(8,128)S(1)}, f32[2,32,128]{2,1,0:T(8,128)S(1)}, u32[]{:S(2)}, u32[]{:S(2)}) collective-permute-start(f32[2,32,128]{2,1,0:T(8,128)S(1)} %bitcast.285), channel_id=1, source_target_pairs={{0,256},{16,272},{32,288},{48,304},{64,320},{80,336},{96,352},{112... | collective-permute-start | bytes 98312 | tf_op jit(solution)/shard_map/ppermute | solution.py:51
  287.3 7.1 %collective-permute-start.42 = (f32[2,32,128]{2,1,0:T(8,128)S(1)}, f32[2,32,128]{2,1,0:T(8,128)S(1)}, u32[]{:S(2)}, u32[]{:S(2)}) collective-permute-start(f32[2,32,128]{2,1,0:T(8,128)S(1)} %fusion.94), channel_id=1, source_target_pairs={{0,32},{16,48},{32,0},{48,16},{64,96},{80,112},{96,64},{112,80},{1... | collective-permute-start | bytes 98312 | tf_op jit(solution)/shard_map/ppermute | solution.py:85
  311.3 7.9 %collective-permute-start.46 = (f32[2,64,128]{2,1,0:T(8,128)S(1)}, f32[2,64,128]{2,1,0:T(8,128)S(1)}, u32[]{:S(2)}, u32[]{:S(2)}) collective-permute-start(f32[2,64,128]{2,1,0:T(8,128)S(1)} %add_select_fusion.4), channel_id=1, source_target_pairs={{0,4},{1,5},{2,6},{3,7},{4,0},{5,1},{6,2},{7,3},{8,12},{9,13},{10,... | collective-permute-start | bytes 196616 | tf_op jit(solution)/shard_map/ppermute | solution.py:51
  319.2 10.2 %collective-permute-start.47 = (f32[2,64,128]{2,1,0:T(8,128)S(1)}, f32[2,64,128]{2,1,0:T(8,128)S(1)}, u32[]{:S(2)}, u32[]{:S(2)}) collective-permute-start(f32[2,64,128]{2,1,0:T(8,128)S(1)} %bitcast.263), channel_id=1, source_target_pairs={{0,8},{1,9},{2,10},{3,11},{4,12},{5,13},{6,14},{7,15},{8,0},{9,1},... | collective-permute-start | bytes 196616 | tf_op jit(solution)/shard_map/ppermute | solution.py:51
  345.4 6.9 %collective-permute-start.51 = (f32[2,32,128]{2,1,0:T(8,128)S(1)}, f32[2,32,128]{2,1,0:T(8,128)S(1)}, u32[]{:S(2)}, u32[]{:S(2)}) collective-permute-start(f32[2,32,128]{2,1,0:T(8,128)S(1)} %slice_select_fusion.10), channel_id=1, source_target_pairs={{0,32},{16,48},{32,0},{48,16},{64,96},{80,112},{96,64},{112,80},{1... | collective-permute-start | bytes 98312 | tf_op jit(solution)/shard_map/ppermute | solution.py:79
  352.4 9.7 %collective-permute-start.52 = (f32[2,32,128]{2,1,0:T(8,128)S(1)}, f32[2,32,128]{2,1,0:T(8,128)S(1)}, u32[]{:S(2)}, u32[]{:S(2)}) collective-permute-start(f32[2,32,128]{2,1,0:T(8,128)S(1)} %add_select_fusion.10), channel_id=1, source_target_pairs={{0,64},{16,80},{32,96},{48,112},{64,0},{80,16},{96,32},{112,48},{1... | collective-permute-start | bytes 98312 | tf_op jit(solution)/shard_map/ppermute | solution.py:51
  368.0 7.3 %collective-permute-start.54 = (f32[2,32,128]{2,1,0:T(8,128)S(1)}, f32[2,32,128]{2,1,0:T(8,128)S(1)}, u32[]{:S(2)}, u32[]{:S(2)}) collective-permute-start(f32[2,32,128]{2,1,0:T(8,128)S(1)} %bitcast.281), channel_id=1, source_target_pairs={{0,256},{16,272},{32,288},{48,304},{64,320},{80,336},{96,352},{112... | collective-permute-start | bytes 98312 | tf_op jit(solution)/shard_map/ppermute | solution.py:51
  375.3 7.1 %collective-permute-start.55 = (f32[2,32,128]{2,1,0:T(8,128)S(1)}, f32[2,32,128]{2,1,0:T(8,128)S(1)}, u32[]{:S(2)}, u32[]{:S(2)}) collective-permute-start(f32[2,32,128]{2,1,0:T(8,128)S(1)} %fusion.84), channel_id=1, source_target_pairs={{0,32},{16,48},{32,0},{48,16},{64,96},{80,112},{96,64},{112,80},{1... | collective-permute-start | bytes 98312 | tf_op jit(solution)/shard_map/ppermute | solution.py:85
  (29 other events, 185.8 us)
